TPU v7x, 128 devices: a whole 4x4x4 slice. The times are simulated.
128 devices in a mesh: gx: 4 (over x_lo, core), gy: 8 (over y, x_hi), gz: 4 (over z).
Axes of the slice: x: 4 (x_hi: 2, x_lo: 2; x = x_hi * 2 + x_lo), y: 4, z: 4, core: 2. Of those that a mesh axis runs over, the one named last changes fastest.
Arguments:
- state: float32 [4, 96, 128, 2048], P(None, 'gz', 'gx', 'gy'), may hold values from -5 to 5
- mixing: float32 [2, 96, 128, 2048], P(None, 'gz', 'gx', 'gy'), may hold values from 0.1 to 1000
- depth_levels: int32 [128, 2048], replicated, may hold values from 0 to 96
- wind: float32 [2, 128, 2048], P(None, 'gx', 'gy'), may hold values from -3 to 3
Outputs:
- state_next: float32 [4, 96, 128, 2048], P(None, 'gz', 'gx', 'gy')
Inputs may be any that keep to these rules, and one draw needn't show every extreme that they name: `depth_levels`: levels at or beyond a column's count are land.
All inputs are finite; a program needn't handle non-finite values.
Results may differ from a plain program's by a relative error of at most 0.0003.
Values sent between devices are 32-bit elements; how exact they have to be, the bound alone decides.
No kernel may reach another device: no remote copies, remote signals or barrier semaphores. Data moves between devices by JAX's collectives and lax.ppermute only.
A program may use at most 192 MiB of HBM per device.

v0:
```python
import jax
import jax.numpy as jnp
from jax import lax
from jax.sharding import PartitionSpec as P


def padded_2(array, sides, width):
    for axis, dim in sides:
        peers, length = (lax.axis_size(axis), array.shape[dim])
        up = [(i, (i + 1) % peers) for i in range(peers)]
        down = [(j, i) for i, j in up]
        last = lax.slice_in_dim(array, length - width, length, axis=dim)
        initial = lax.slice_in_dim(array, 0, width, axis=dim)
        before = lax.ppermute(last, axis, up)
        after = lax.ppermute(initial, axis, down)
        array = jnp.concatenate([before, array, after], axis=dim)
    return array


def carried_in(part, axis, combine, identity):
    place = lax.axis_index(axis)
    gathered = lax.all_gather(part, axis)
    state = jnp.zeros_like(part) + jnp.asarray(identity, part.dtype)

    def one(turn, state):
        return combine(state, lax.dynamic_index_in_dim(gathered, turn, 0, False))

    return lax.fori_loop(0, place, one, state)


def density_of(fields, wet_mask):
    return (-0.3 * fields[0] + 0.7 * fields[1] - 0.05 * fields[0] * fields[0]) * wet_mask


def advance(padded, wet_pad, pressure, wall_face, coriolis):
    wet_x = wet_pad[:, :-1, 1:-1] * wet_pad[:, 1:, 1:-1]
    wet_y = wet_pad[:, 1:-1, :-1] * wet_pad[:, 1:-1, 1:] * wall_face
    east_vel = 0.5 * (padded[2, :, :-1, 1:-1] + padded[2, :, 1:, 1:-1]) * wet_x
    north_vel = 0.5 * (padded[3, :, 1:-1, :-1] + padded[3, :, 1:-1, 1:]) * wet_y
    west_side = padded[:, :, :-1, 1:-1]
    east_side = padded[:, :, 1:, 1:-1]
    flux_x = 0.25 * (
        jnp.maximum(east_vel, 0.0) * west_side + jnp.minimum(east_vel, 0.0) * east_side
    ) - 0.08 * wet_x * (east_side - west_side)
    south_side = padded[:, :, 1:-1, :-1]
    north_side = padded[:, :, 1:-1, 1:]
    flux_y = 0.25 * (
        jnp.maximum(north_vel, 0.0) * south_side + jnp.minimum(north_vel, 0.0) * north_side
    ) - 0.08 * wet_y * (north_side - south_side)
    interior = padded[:, :, 1:-1, 1:-1]
    moved = interior - (
        flux_x[:, :, 1:] - flux_x[:, :, :-1] + flux_y[:, :, :, 1:] - flux_y[:, :, :, :-1]
    )
    centre = pressure[:, 1:-1, 1:-1]
    grad_x = 0.5 * (
        wet_x[:, 1:] * (pressure[:, 2:, 1:-1] - centre)
        + wet_x[:, :-1] * (centre - pressure[:, :-2, 1:-1])
    )
    grad_y = 0.5 * (
        wet_y[:, :, 1:] * (pressure[:, 1:-1, 2:] - centre)
        + wet_y[:, :, :-1] * (centre - pressure[:, 1:-1, :-2])
    )
    east_new = moved[2] + 0.3 * coriolis * interior[3] - grad_x
    north_new = moved[3] - 0.3 * coriolis * interior[2] - grad_y
    wet_inner = wet_pad[:, 1:-1, 1:-1]
    return jnp.stack([moved[0], moved[1], east_new, north_new]) * wet_inner


def thomas(rhs_lev, below_lev, above_lev):

    def forward(carry, item):
        ratio_prev, value_prev = carry
        rhs_here, below_here, above_here = item
        divisor = 1.0 + above_here * (1.0 - ratio_prev) + below_here
        ratio = below_here / divisor
        value = (rhs_here + above_here * value_prev) / divisor
        return ((ratio, value), (ratio, value))

    zero_level = jnp.zeros_like(rhs_lev[0])
    ratio_start = jnp.zeros_like(below_lev[0] * rhs_lev[0])
    _, (ratios, values) = lax.scan(
        forward, (ratio_start, zero_level), (rhs_lev, below_lev, above_lev), unroll=8
    )

    def backward(later, item):
        ratio, value = item
        result = value + ratio * later
        return (result, result)

    _, solved = lax.scan(backward, zero_level, (ratios, values), reverse=True, unroll=8)
    return solved


def tridiagonal(forced, coupling):
    below = jnp.repeat(coupling, 2, axis=0)
    above = jnp.concatenate([jnp.zeros_like(below[:, :1]), below[:, :-1]], axis=1)
    solved = thomas(
        jnp.moveaxis(forced, 1, 0), jnp.moveaxis(below, 1, 0), jnp.moveaxis(above, 1, 0)
    )
    return jnp.moveaxis(solved, 0, 1)


def add_totals(earlier, later):
    return earlier + later


def per_device(state, mixing, depth_levels, wind):
    fields, lev_count, col_x, col_y = state.shape
    total_x, total_y = depth_levels.shape
    start_x = lax.axis_index("gx") * col_x
    start_y = lax.axis_index("gy") * col_y
    start_z = lax.axis_index("gz") * lev_count
    padded = padded_2(state, (("gx", 2), ("gy", 3)), 1)
    row_index = (start_x - 1 + jnp.arange(col_x + 2, dtype=jnp.int32)) % total_x
    col_index = (start_y - 1 + jnp.arange(col_y + 2, dtype=jnp.int32)) % total_y
    depth_pad = jnp.take(jnp.take(depth_levels, row_index, axis=0), col_index, axis=1)
    levels = start_z + jnp.arange(lev_count, dtype=jnp.int32)
    wet_pad = (levels[:, None, None] < depth_pad[None]).astype(jnp.float32)
    density_field = density_of(padded, wet_pad)
    inclusive = jnp.cumsum(density_field, axis=0)
    column_total = inclusive[-1]
    shallower = carried_in(column_total, "gz", add_totals, jnp.zeros_like(column_total))
    pressure = 0.03 * (shallower[None] + inclusive - 0.5 * density_field)
    face_row = start_y - 1 + jnp.arange(col_y + 1, dtype=jnp.int32)
    wall_face = ((face_row >= 0) & (face_row <= total_y - 2)).astype(jnp.float32)
    row_global = start_y + jnp.arange(col_y, dtype=jnp.int32)
    coriolis = 0.5 + (row_global.astype(jnp.float32) + 0.5) / total_y
    forced = advance(padded, wet_pad, pressure, wall_face, coriolis)
    wet_inner = wet_pad[:, 1:-1, 1:-1]
    depth_inner = depth_pad[1:-1, 1:-1]
    wet_next = ((levels + 1)[:, None, None] < depth_inner[None]).astype(jnp.float32)
    top_level = (levels == 0).astype(jnp.float32)
    forced = forced.at[2:].add(wind[:, None] * top_level[None, :, None, None] * wet_inner[None])
    coupling = mixing * (wet_inner * wet_next)[None]
    whole_forced, whole_coupling = (
        lax.all_gather(forced, "gz", axis=1, tiled=True),
        lax.all_gather(coupling, "gz", axis=1, tiled=True),
    )
    solved = tridiagonal(whole_forced, whole_coupling)
    result = lax.dynamic_slice_in_dim(solved, start_z, lev_count, 1)
    return result


def solution(mesh):
    return jax.shard_map(
        per_device,
        mesh=mesh,
        in_specs=(P(None, "gz", "gx", "gy"), P(None, "gz", "gx", "gy"), P(), P(None, "gx", "gy")),
        out_specs=P(None, "gz", "gx", "gy"),
        check_vma=False,
    )
```

profile of v0, /device:TPU:0, one launch (start us, length us, event | category | flops | bytes accessed | tf_op | source)
XLA Modules:
  0.0 404.1 jit_solution(3733420670964093776)
XLA Ops:
  13.1 2.9 broadcast_multiply_fusion
  16.9 1.7 collective-permute-start.1
  19.2 1.9 constant_dynamic-update-slice_fusion
  22.4 2.6 fusion.103
  25.0 2.3 copy.21
  27.3 3.2 collective-permute-start.2
  30.5 2.5 copy.23
  32.9 2.8 collective-permute-start.3
  35.8 2.8 dynamic-update-slice.28
  38.5 2.8 broadcast_maximum_fusion.1
  43.8 2.9 multiply_subtract_fusion.1
  46.7 2.1 copy.22
  48.8 2.9 copy.24
  51.7 3.1 compare_select_fusion
  54.9 5.1 %fusion.106 = f32[24,34,258]{2,1,0:T(8,128)S(1)} fusion(f32[24,34,258]{2,1,0:T(8,128)S(1)} %compare_select_fusion), kind=kOutput, calls=%fused_computation.238 | output fusion | flops 4842144 | bytes 1684224 | tf_op jit(solution)/shard_map/jit(cumsum)/reduce_window_sum | solution.py:120
  62.1 2.9 multiply_subtract_fusion
  65.0 3.1 fusion.43
  68.9 15.0 %all_gather.10 = f32[4,34,258]{2,1,0:T(8,128)S(1)} all-gather(f32[1,34,258]{2,1,0:T(8,128)S(1)} %slice-done.1), channel_id=1, replica_groups=mesh['gx'=4,'gy'=8,'gz'=4] {'gz'}, dimensions={0}, use_global_device_ids=true | all-gather | bytes 175440 | tf_op jit(solution)/shard_map/all_gather | solution.py:22
  84.1 2.2 subtract_multiply_fusion
  86.5 2.6 fusion.69
  90.4 1.7 copy-done.8
  92.1 3.9 copy.20
  96.0 8.0 %broadcast_in_dim.186 = f32[2,2,96,32,256]{4,3,1,0,2:T(8,128)} broadcast(f32[2,96,32,256]{3,2,0,1:T(8,128)S(1)} %copy.20), dimensions={0,2,3,4} | broadcast | bytes 18874368 | tf_op jit(solution)/shard_map/broadcast_in_dim | solution.py:95
  104.0 12.8 %slice.499 = f32[4,95,32,256]{3,2,0,1:T(8,128)} slice(f32[4,96,32,256]{3,2,0,1:T(8,128)} %bitcast.484), slice={[0:4], [0:95], [0:32], [0:256]} | slice | bytes 24903680 | tf_op jit(solution)/shard_map/slice | solution.py:96
  116.9 12.1 %concatenate.42 = f32[4,96,32,256]{3,2,0,1:T(8,128)} pad(f32[4,95,32,256]{3,2,0,1:T(8,128)} %slice.499, f32[]{:T(128)} %constant.186.clone.1), padding=0_0x1_0x0_0x0_0 | pad | bytes 25034756 | tf_op jit(solution)/shard_map/concatenate | solution.py:96
  128.9 81.3 %all-gather.5.cloned.1.call-done = f32[4,96,32,256]{3,2,1,0:T(8,128)} async-done(((f32[4,24,32,256]{3,2,1,0:T(8,128)}), f32[4,96,32,256]{3,2,1,0:T(8,128)}) %all-gather.5.cloned.1.call-update) | async-done | bytes 12582928 | tf_op jit(solution)/shard_map/all_gather | solution.py:136
  210.3 141.2 %while.46 = (s32[]{:T(128)}, f32[4,32,256]{2,1,0:T(8,128)S(1)}, f32[4,32,256]{2,1,0:T(8,128)S(1)}, f32[12,8,4,32,256]{4,3,2,1,0:T(8,128)}, f32[12,8,4,32,256]{4,...) while((s32[]{:T(128)}, f32[4,32,256]{2,1,0:T(8,128)S(1)}, ...), condition=%wide.region_4.5_spmd.clone, body=%wide.region_3.4_spmd.clone.sunk | while | flops 2162696 | bytes 14943063 | solution.py:81
  255.8 1.5 bitcast_dynamic-update-slice_fusion.53
  267.6 1.5 bitcast_dynamic-update-slice_fusion.53
  279.4 1.5 bitcast_dynamic-update-slice_fusion.53
  291.2 1.5 bitcast_dynamic-update-slice_fusion.53
  314.7 1.5 bitcast_dynamic-update-slice_fusion.53
  338.2 1.5 bitcast_dynamic-update-slice_fusion.53
  351.4 6.2 %broadcast.313.clone = f32[12,8,4,32,256]{4,3,1,0,2:T(8,128)} broadcast(f32[]{:T(128)} %constant.186.clone.1), dimensions={} | broadcast | bytes 12582916 | tf_op jit(solution)/shard_map/broadcast.15
  357.6 35.6 %while.47 = (s32[]{:T(128)}, f32[4,32,256]{2,1,0:T(8,128)S(1)}, f32[12,8,4,32,256]{4,3,1,0,2:T(8,128)}, f32[12,8,4,32,256]{4,3,2,1,0:T(8,128)}, f32[12,8,4,32,25...) while((s32[]{:T(128)}, f32[4,32,256]{2,1,0:T(8,128)S(1)}, ...), condition=%wide.region_6.7_spmd.clone, body=%wide.region_5.6_spmd.clone.sunk | while | flops 557066 | bytes 7340315 | solution.py:90
  357.6 1.8 bitcast_dynamic-update-slice_fusion.54
  360.6 1.8 bitcast_dynamic-update-slice_fusion.54
  363.6 1.8 bitcast_dynamic-update-slice_fusion.54
  366.5 1.8 bitcast_dynamic-update-slice_fusion.54
  369.5 1.8 bitcast_dynamic-update-slice_fusion.54
  372.4 1.8 bitcast_dynamic-update-slice_fusion.54
  375.4 1.8 bitcast_dynamic-update-slice_fusion.54
  378.3 1.8 bitcast_dynamic-update-slice_fusion.54
  381.3 1.8 bitcast_dynamic-update-slice_fusion.54
  384.3 1.8 bitcast_dynamic-update-slice_fusion.54
  387.2 1.8 bitcast_dynamic-update-slice_fusion.54
  390.2 1.8 bitcast_dynamic-update-slice_fusion.54
  393.2 4.1 %dynamic-slice_bitcast_fusion.40 = f32[4,24,32,256]{3,2,1,0:T(8,128)} fusion(f32[96,4,32,256]{3,2,0,1:T(8,128)} %bitcast.487, s32[]{:T(128)S(6)} %select_n.96), kind=kLoop, calls=%fused_computation.139 | loop fusion | bytes 6291460 | tf_op jit(solution)/shard_map/dynamic_slice | solution.py:140
  (302 shorter events, 161.4 us)
Async XLA Ops:
  6.5 1.2 copy-start
  6.5 85.6 %all-gather.3.cloned.1.call-start = ((), (), s32[]{:S(2)}) async-start(), calls=%async_computation | async-start | bytes 7864320 | tf_op jit(solution)/shard_map/all_gather | solution.py:137
  10.3 0.5 copy-start.18
  10.8 1.1 copy-start.5
  13.1 3.0 copy-start.2
  16.1 194.2 %all-gather.5.cloned.1.call-start = ((), (), s32[]{:S(2)}) async-start(), calls=%async_computation.1 | async-start | bytes 15728640 | tf_op jit(solution)/shard_map/all_gather | solution.py:136
  16.9 4.8 %collective-permute-start = (f32[4,24,1,256]{3,2,1,0:T(1,128)}, f32[4,24,1,256]{3,2,1,0:T(1,128)S(1)}, u32[]{:S(2)}, u32[]{:S(2)}) collective-permute-start(f32[4,24,1,256]{3,2,1,0:T(1,128)} %get-tuple-element.347), channel_id=1, source_target_pairs={{0,32},{32,64},{64,96},{96,0},{1,33},{33,65},{65,97},{97,1},{2,34}... | collective-permute-start | bytes 294920 | tf_op jit(solution)/shard_map/ppermute | solution.py:14
  16.9 4.8 %collective-permute-start.1 = (f32[4,24,1,256]{3,2,1,0:T(1,128)S(1)}, f32[4,24,1,256]{3,2,1,0:T(1,128)S(1)}, u32[]{:S(2)}, u32[]{:S(2)}) collective-permute-start(f32[4,24,1,256]{3,2,1,0:T(1,128)S(1)} %get-tuple-element.348), channel_id=1, source_target_pairs={{32,0},{64,32},{96,64},{0,96},{33,1},{65,33},{97,65},{1,97},{34,2}... | collective-permute-start | bytes 294920 | tf_op jit(solution)/shard_map/ppermute | solution.py:15
  27.3 19.4 %collective-permute-start.2 = (f32[4,24,34,1]{2,1,3,0:T(8,128)S(1)}, f32[4,24,34,1]{2,1,3,0:T(8,128)S(1)}, u32[]{:S(2)}, u32[]{:S(2)}) collective-permute-start(f32[4,24,34,1]{2,1,3,0:T(8,128)S(1)} %copy.21), channel_id=1, source_target_pairs={{0,4},{4,8},{8,12},{12,16},{16,20},{20,24},{24,28},{28,0},{1,5},{5... | collective-permute-start | bytes 39176 | tf_op jit(solution)/shard_map/ppermute | solution.py:14
  32.9 15.9 %collective-permute-start.3 = (f32[4,24,34,1]{2,1,3,0:T(8,128)S(1)}, f32[4,24,34,1]{2,1,3,0:T(8,128)}, u32[]{:S(2)}, u32[]{:S(2)}) collective-permute-start(f32[4,24,34,1]{2,1,3,0:T(8,128)S(1)} %copy.23), channel_id=1, source_target_pairs={{4,0},{8,4},{12,8},{16,12},{20,16},{24,20},{28,24},{0,28},{5,1},{9... | collective-permute-start | bytes 39176 | tf_op jit(solution)/shard_map/ppermute | solution.py:15
  41.3 1.0 copy-start.13
  41.3 2.5 copy-start.9
  46.7 5.0 %copy-start.19 = (s32[24]{0:T(128)S(1)}, s32[24]{0:T(128)}, u32[]{:S(2)}) copy-start(s32[24]{0:T(128)} %copy-done.18) | copy-start | bytes 292
  51.7 8.3 %copy-start.4 = (f32[4,24,34,1]{3,2,1,0:T(8,128)S(1)}, f32[4,24,34,1]{3,2,1,0:T(8,128)}, u32[]{:S(2)}) copy-start(f32[4,24,34,1]{3,2,1,0:T(8,128)} %copy.24) | copy-start | bytes 39172
  51.7 8.3 %copy-start.6 = (f32[24,34,258]{2,1,0:T(8,128)S(1)}, f32[24,34,258]{2,1,0:T(8,128)}, u32[]{:S(2)}) copy-start(f32[24,34,258]{2,1,0:T(8,128)} %copy-done.5) | copy-start | bytes 2526340
  54.8 6.1 %copy-start.10 = (f32[24,34,258]{2,1,0:T(8,128)}, f32[24,34,258]{2,1,0:T(8,128)S(1)}, u32[]{:S(2)}) copy-start(f32[24,34,258]{2,1,0:T(8,128)S(1)} %compare_select_fusion) | copy-start | bytes 2526340
  54.9 5.1 %copy-start.3 = (f32[4,24,34,1]{3,2,1,0:T(8,128)S(1)}, f32[4,24,34,1]{3,2,1,0:T(8,128)}, u32[]{:S(2)}) copy-start(f32[4,24,34,1]{3,2,1,0:T(8,128)} %copy.22) | copy-start | bytes 39172
  59.9 1.1 copy-start.16
  61.1 1.0 copy-start.11
  62.1 2.9 copy-start.7
  68.1 0.8 slice-start.1
  68.9 17.3 %copy-start.20 = (f32[256]{0:T(256)S(1)}, f32[256]{0:T(256)}, u32[]{:S(2)}) copy-start(f32[256]{0:T(256)} %add_multiply_fusion) | copy-start | bytes 3076
  84.1 2.2 copy-start.12
  84.1 2.4 copy-start.14
  86.5 2.6 slice-start
  86.5 2.6 copy-start.15
  89.2 0.8 copy-start.17
  89.2 0.8 copy-start.21
  90.4 1.7 copy-start.8
  393.2 4.1 %copy-start.1 = (s32[128,2048]{1,0:T(8,128)S(1)}, s32[128,2048]{1,0:T(8,128)}, u32[]{:S(2)}) copy-start(s32[128,2048]{1,0:T(8,128)} %param.14) | copy-start | bytes 3145732
Sparse Core Ops, SparseCore 0:
  16.2 70.3 all-gather.2
  92.2 118.0 all-gather.4
where the time goes:
time: 408 us; the launch traced here: 404 us
  other arithmetic  177 us (43%)
  local copies, waits for them, and re-layouts  108 us (26%)
  waiting for transfers between devices  81.4 us (20%)
  blocking collectives  15 us (4%)
  between operations  13.8 us (3%)
  starting transfers between devices  7.8 us (2%)
    while x96, other arithmetic  118 us
    all_gather x1, waiting for transfers between devices, per_device(): lax.all_gather(forced, 'gz', axis=1, tiled=True)  81.3 us
    dynamic_update_slice x24, local copies, waits for them, and re-layouts, thomas(): lax.scan(forward, (ratio_start, zero_level), (rhs_lev, below_lev, above_l...  30.6 us
    concatenate x24, other arithmetic, thomas(): lax.scan(forward, (ratio_start, zero_level), (rhs_lev, below_lev, above_l...  25.3 us
    all_gather x1, blocking collectives, carried_in(): gathered = lax.all_gather(part, axis)  15 us
    slice x1, local copies, waits for them, and re-layouts, tridiagonal(): below[:, :-1]  12.8 us
    concatenate x1, local copies, waits for them, and re-layouts, tridiagonal(): jnp.concatenate([jnp.zeros_like(below[:, :1]), below[:, :-1]], axis=1)  12.1 us
    unnamed x45, local copies, waits for them, and re-layouts  9.9 us
  transfers between devices with their start and end apart: 6, of which 1 were waited for; matrix products, arithmetic and copies ran while one was open for 21% of the time, Pallas kernels for 0%

commit v1 on v0

--- a/solution.py
+++ b/solution.py
@@ -1,6 +1,8 @@
 import jax
 import jax.numpy as jnp
 from jax import lax
+from jax.experimental import pallas as pl
+from jax.experimental.pallas import tpu as pltpu
 from jax.sharding import PartitionSpec as P
 
 
@@ -15,17 +17,6 @@
         after = lax.ppermute(initial, axis, down)
         array = jnp.concatenate([before, array, after], axis=dim)
     return array
-
-
-def carried_in(part, axis, combine, identity):
-    place = lax.axis_index(axis)
-    gathered = lax.all_gather(part, axis)
-    state = jnp.zeros_like(part) + jnp.asarray(identity, part.dtype)
-
-    def one(turn, state):
-        return combine(state, lax.dynamic_index_in_dim(gathered, turn, 0, False))
-
-    return lax.fori_loop(0, place, one, state)
 
 
 def density_of(fields, wet_mask):
@@ -66,50 +57,120 @@
     return jnp.stack([moved[0], moved[1], east_new, north_new]) * wet_inner
 
 
-def thomas(rhs_lev, below_lev, above_lev):
-
-    def forward(carry, item):
-        ratio_prev, value_prev = carry
-        rhs_here, below_here, above_here = item
-        divisor = 1.0 + above_here * (1.0 - ratio_prev) + below_here
-        ratio = below_here / divisor
-        value = (rhs_here + above_here * value_prev) / divisor
-        return ((ratio, value), (ratio, value))
-
-    zero_level = jnp.zeros_like(rhs_lev[0])
-    ratio_start = jnp.zeros_like(below_lev[0] * rhs_lev[0])
-    _, (ratios, values) = lax.scan(
-        forward, (ratio_start, zero_level), (rhs_lev, below_lev, above_lev), unroll=8
-    )
-
-    def backward(later, item):
-        ratio, value = item
-        result = value + ratio * later
-        return (result, result)
-
-    _, solved = lax.scan(backward, zero_level, (ratios, values), reverse=True, unroll=8)
-    return solved
-
-
-def tridiagonal(forced, coupling):
-    below = jnp.repeat(coupling, 2, axis=0)
-    above = jnp.concatenate([jnp.zeros_like(below[:, :1]), below[:, :-1]], axis=1)
-    solved = thomas(
-        jnp.moveaxis(forced, 1, 0), jnp.moveaxis(below, 1, 0), jnp.moveaxis(above, 1, 0)
-    )
-    return jnp.moveaxis(solved, 0, 1)
-
-
-def add_totals(earlier, later):
-    return earlier + later
+def local_solve_kernel(f_ref, c_ref, ctop_ref, y_ref, u_ref, v_ref, ratio_s):
+    levels = f_ref.shape[1]
+    ctop = ctop_ref[...]
+    ratio_prev = None
+    vy_prev = None
+    vu_prev = None
+    for k in range(levels):
+        above = ctop if k == 0 else c_ref[:, k - 1]
+        below = c_ref[:, k]
+        if k == 0:
+            divisor = 1.0 + above + below
+        else:
+            divisor = 1.0 + above * (1.0 - ratio_prev) + below
+        inv = 1.0 / divisor
+        ratio = below * inv
+        rhs = f_ref[:, k]
+        if k == 0:
+            vy = rhs * jnp.repeat(inv, 2, axis=0)
+            vu = ctop * inv
+        else:
+            vy = (rhs + jnp.repeat(above, 2, axis=0) * vy_prev) * jnp.repeat(inv, 2, axis=0)
+            vu = above * vu_prev * inv
+        ratio_s[:, k] = ratio
+        y_ref[:, k] = vy
+        u_ref[:, k] = vu
+        ratio_prev, vy_prev, vu_prev = ratio, vy, vu
+    y_later = vy_prev
+    u_later = vu_prev
+    v_later = ratio_prev
+    v_ref[:, levels - 1] = v_later
+    for k in range(levels - 2, -1, -1):
+        ratio = ratio_s[:, k]
+        y_later = y_ref[:, k] + jnp.repeat(ratio, 2, axis=0) * y_later
+        u_later = u_ref[:, k] + ratio * u_later
+        v_later = ratio * v_later
+        y_ref[:, k] = y_later
+        u_ref[:, k] = u_later
+        v_ref[:, k] = v_later
+
+
+def local_solve(forced, coupling, ctop):
+    fields, levels, cols_x, cols_y = forced.shape
+    pairs = coupling.shape[0]
+    bx = 8 if cols_x % 8 == 0 else cols_x
+    grid = (cols_x // bx,)
+    fspec = pl.BlockSpec((fields, levels, bx, cols_y), lambda i: (0, 0, i, 0))
+    cspec = pl.BlockSpec((pairs, levels, bx, cols_y), lambda i: (0, 0, i, 0))
+    tspec = pl.BlockSpec((pairs, bx, cols_y), lambda i: (0, i, 0))
+    return pl.pallas_call(
+        local_solve_kernel,
+        grid=grid,
+        in_specs=[fspec, cspec, tspec],
+        out_specs=[fspec, cspec, cspec],
+        out_shape=[
+            jax.ShapeDtypeStruct(forced.shape, jnp.float32),
+            jax.ShapeDtypeStruct(coupling.shape, jnp.float32),
+            jax.ShapeDtypeStruct(coupling.shape, jnp.float32),
+        ],
+        scratch_shapes=[pltpu.VMEM((pairs, levels, bx, cols_y), jnp.float32)],
+    )(forced, coupling, ctop)
+
+
+def interface_values(summary, place, peers):
+    fields = 4
+    y0 = summary[:, 0:fields]
+    y1 = summary[:, fields:2 * fields]
+    rest = jnp.repeat(summary[:, 2 * fields:], 2, axis=1)
+    u0 = rest[:, 0:4]
+    u1 = rest[:, 4:8]
+    v0 = rest[:, 8:12]
+    v1 = rest[:, 12:16]
+    pt, qt, pb, qb = [], [], [], []
+    for q in range(peers):
+        if q == 0:
+            pt_q, qt_q = y0[q], v0[q]
+            pb_q, qb_q = y1[q], v1[q]
+        else:
+            d = 1.0 - u0[q] * qb[-1]
+            inv = 1.0 / d
+            pt_q = (y0[q] + u0[q] * pb[-1]) * inv
+            qt_q = v0[q] * inv
+            pb_q = y1[q] + u1[q] * (pb[-1] + qb[-1] * pt_q)
+            qb_q = v1[q] + u1[q] * qb[-1] * qt_q
+        pt.append(pt_q)
+        qt.append(qt_q)
+        pb.append(pb_q)
+        qb.append(qb_q)
+    tops = [None] * peers
+    bots = [None] * peers
+    t_next = jnp.zeros_like(pt[0])
+    for q in range(peers - 1, -1, -1):
+        tops[q] = pt[q] + qt[q] * t_next
+        bots[q] = pb[q] + qb[q] * t_next
+        t_next = tops[q]
+    above = jnp.zeros_like(pt[0])
+    below = jnp.zeros_like(pt[0])
+    for q in range(peers):
+        if q >= 1:
+            above = jnp.where(place == q, bots[q - 1], above)
+        if q <= peers - 2:
+            below = jnp.where(place == q, tops[q + 1], below)
+    return above, below
 
 
 def per_device(state, mixing, depth_levels, wind):
     fields, lev_count, col_x, col_y = state.shape
     total_x, total_y = depth_levels.shape
+    peers_z = lax.axis_size("gz")
+    place_z = lax.axis_index("gz")
     start_x = lax.axis_index("gx") * col_x
     start_y = lax.axis_index("gy") * col_y
-    start_z = lax.axis_index("gz") * lev_count
+    start_z = place_z * lev_count
+    down_z = [(i, i + 1) for i in range(peers_z - 1)]
+    mix_above = lax.ppermute(mixing[:, lev_count - 1], "gz", down_z)
     padded = padded_2(state, (("gx", 2), ("gy", 3)), 1)
     row_index = (start_x - 1 + jnp.arange(col_x + 2, dtype=jnp.int32)) % total_x
     col_index = (start_y - 1 + jnp.arange(col_y + 2, dtype=jnp.int32)) % total_y
@@ -119,7 +180,10 @@
     density_field = density_of(padded, wet_pad)
     inclusive = jnp.cumsum(density_field, axis=0)
     column_total = inclusive[-1]
-    shallower = carried_in(column_total, "gz", add_totals, jnp.zeros_like(column_total))
+    gathered = lax.all_gather(column_total, "gz")
+    shallower = jnp.zeros_like(column_total)
+    for q in range(peers_z):
+        shallower = shallower + jnp.where(q < place_z, gathered[q], 0.0)
     pressure = 0.03 * (shallower[None] + inclusive - 0.5 * density_field)
     face_row = start_y - 1 + jnp.arange(col_y + 1, dtype=jnp.int32)
     wall_face = ((face_row >= 0) & (face_row <= total_y - 2)).astype(jnp.float32)
@@ -132,13 +196,19 @@
     top_level = (levels == 0).astype(jnp.float32)
     forced = forced.at[2:].add(wind[:, None] * top_level[None, :, None, None] * wet_inner[None])
     coupling = mixing * (wet_inner * wet_next)[None]
-    whole_forced, whole_coupling = (
-        lax.all_gather(forced, "gz", axis=1, tiled=True),
-        lax.all_gather(coupling, "gz", axis=1, tiled=True),
-    )
-    solved = tridiagonal(whole_forced, whole_coupling)
-    result = lax.dynamic_slice_in_dim(solved, start_z, lev_count, 1)
-    return result
+    wet_up = ((start_z - 1) < depth_inner).astype(jnp.float32)
+    ctop = mix_above * (wet_up * wet_inner[0])[None]
+    ctop = jnp.where(place_z > 0, ctop, 0.0)
+    y, u, v = local_solve(forced, coupling, ctop)
+    last = lev_count - 1
+    summary = jnp.concatenate(
+        [y[:, 0], y[:, last], u[:, 0], u[:, last], v[:, 0], v[:, last]], axis=0
+    )
+    gathered_ends = lax.all_gather(summary, "gz")
+    x_above, x_below = interface_values(gathered_ends, place_z, peers_z)
+    u4 = jnp.repeat(u, 2, axis=0)
+    v4 = jnp.repeat(v, 2, axis=0)
+    return y + x_above[:, None] * u4 + x_below[:, None] * v4
 
 
 def solution(mesh):

time: 408 us -> 157 us (0.38)
  other arithmetic: 177 us -> 48.3 us
  local copies, waits for them, and re-layouts: 108 us -> 34.1 us
  waiting for transfers between devices: 81.4 us -> 28.7 us
  Pallas kernels: 0 us -> 6.13 us
    while x96 -> x0, other arithmetic: 118 us -> none
    all_gather x2 -> x1, waiting for transfers between devices: 81.4 us -> 28.7 us  [per_device(): gathered_ends = lax.all_gather(summary, 'gz')]
    dynamic_update_slice x24 -> x0, local copies, waits for them, and re-layouts: 30.6 us -> none  [thomas(): lax.scan(forward, (ratio_start, zero_level), (rhs_lev, below_lev, above_l...]
    concatenate x24 -> x0, other arithmetic: 25.3 us -> none  [thomas(): lax.scan(forward, (ratio_start, zero_level), (rhs_lev, below_lev, above_l...]
    slice x1, local copies, waits for them, and re-layouts: 12.8 us -> 1.44 us  [interface_values(): rest = jnp.repeat(summary[:, 2 * fields:], 2, axis=1)]
    concatenate x13 -> x1, local copies, waits for them, and re-layouts: 12.2 us -> 0.84 us  [per_device(): jnp.concatenate([y[:, 0], y[:, last], u[:, 0], u[:, last], v[:, 0], v[:,...]
    broadcast_in_dim x2 -> x1, local copies, waits for them, and re-layouts: 8 us -> 0.24 us  [interface_values(): rest = jnp.repeat(summary[:, 2 * fields:], 2, axis=1)]
    unnamed x45 -> x38, local copies, waits for them, and re-layouts: 9.9 us -> 16.2 us
  transfers between devices with their start and end apart: 6 -> 6, of which waited for: 1 -> 1; matrix products, arithmetic and copies ran while one was open for 21% -> 14% of each run, Pallas kernels for 0% -> 0%
where the time goes in v1:
time: 157 us; the launch traced here: 155 us
  other arithmetic  48.3 us (31%)
  local copies, waits for them, and re-layouts  34.1 us (22%)
  waiting for transfers between devices  28.7 us (18%)
  between operations  13.7 us (9%)
  blocking collectives  13.5 us (9%)
  starting transfers between devices  10.7 us (7%)
  Pallas kernels  6.13 us (4%)
    all_gather x1, waiting for transfers between devices, per_device(): gathered_ends = lax.all_gather(summary, 'gz')  28.7 us
    unnamed x38, local copies, waits for them, and re-layouts  16.2 us
    all_gather x1, blocking collectives, per_device(): gathered = lax.all_gather(column_total, 'gz')  13.5 us
    sub x1, other arithmetic, advance(): interior - (flux_x[:, :, 1:] - flux_x[:, :, :-1] + flux_y[:, :, :, 1:] -...  6.57 us
    pallas_call x1, Pallas kernels, local_solve(): pl.pallas_call(local_solve_kernel, grid=grid, in_specs=[fspec, cspec, tsp...  6.13 us
    slice x3, local copies, waits for them, and re-layouts, padded_2(): last = lax.slice_in_dim(array, length - width, length, axis=dim)  5.81 us
    sub x1, other arithmetic, advance(): 0.25 * (jnp.maximum(east_vel, 0.0) * west_side + jnp.minimum(east_vel, 0....  5.75 us
    another operation x1, other arithmetic, per_device(): inclusive = jnp.cumsum(density_field, axis=0)  5.06 us
  transfers between devices with their start and end apart: 6, of which 1 were waited for; matrix products, arithmetic and copies ran while one was open for 14% of the time, Pallas kernels for 0%

profile of v1, /device:TPU:0, one launch (start us, length us, event | category | flops | bytes accessed | tf_op | source)
XLA Modules:
  0.0 155.1 jit_solution(10120468274463298533)
XLA Ops:
  6.5 1.6 %fusion.66 = (f32[4,24,1,256]{3,2,1,0:T(1,128)S(1)}, f32[4,24,1,256]{3,2,1,0:T(1,128)S(1)}) fusion(f32[4,24,32,256]{3,2,1,0:T(8,128)} %param.6), kind=kLoop, calls=%fused_computation.176 | loop fusion | bytes 393216 | tf_op jit(solution)/shard_map/slice | solution.py:14
  8.1 1.1 collective-permute-start.1
  9.3 0.8 slice_bitcast_fusion.20
  10.1 3.8 %collective-permute-start.4 = (f32[2,32,256]{2,1,0:T(8,128)S(1)}, f32[2,32,256]{2,1,0:T(8,128)S(1)}, u32[]{:S(2)}, u32[]{:S(2)}) collective-permute-start(f32[2,32,256]{2,1,0:T(8,128)S(1)} %slice_bitcast_fusion.20), channel_id=1, source_target_pairs={{0,1},{1,2},{2,3},{4,5},{5,6},{6,7},{8,9},{9,10},{10,11},{12,13},{... | collective-permute-start | bytes 196616 | tf_op jit(solution)/shard_map/ppermute | solution.py:173
  14.0 4.0 %constant_dynamic-update-slice_fusion = f32[4,24,33,256]{3,2,1,0:T(8,128)} fusion(f32[4,24,32,256]{3,2,1,0:T(8,128)} %param.6), kind=kLoop, calls=%fused_computation.139 | loop fusion | bytes 6291456
  18.0 0.7 gather_fusion
  19.2 1.0 gather_fusion.1
  20.7 1.2 compare_select_fusion.1
  22.0 2.8 %broadcast_multiply_fusion.c_ref = f32[2,24,32,256]{3,2,1,0:T(8,128)} fusion(f32[2,24,32,256]{3,2,1,0:T(8,128)} %param.7, f32[24,32,256]{2,1,0:T(8,128)S(1)} %get-tuple-element.35), kind=kLoop, calls=%fused_computation.72 | loop fusion | flops 393216 | bytes 3932160 | tf_op jit(solution)/shard_map/mul | solution.py:198
  24.8 0.6 multiply_select_fusion.ctop_ref
  25.4 2.8 %dynamic-update-slice.10 = f32[4,24,33,256]{3,2,1,0:T(8,128)} dynamic-update-slice(f32[4,24,33,256]{3,2,1,0:T(8,128)} %constant_dynamic-update-slice_fusion, f32[4,24,1,256]{3,2,1,0:T(1,128)S(1)} %collective-permute-done.1, s32[]{} %constant.159, s32[]{} %constant.159, s32[]{} %constant.170, s32[]{} %constant.159) | dynamic-update-slice | bytes 196612 | tf_op jit(solution)/shard_map/concatenate | solution.py:18
  28.2 3.0 %broadcast_maximum_fusion.1 = (f32[24,33,256]{2,1,0:T(8,128)}, f32[24,33,256]{2,1,0:T(8,128)S(1)}, f32[24,33,256]{2,1,0:T(8,128)S(1)}) fusion(f32[4,24,33,256]{3,2,1,0:T(8,128)} %dynamic-update-slice.10, f32[4,24,32,256]{3,2,1,0:T(8,128)} %param.6, f32[4,24,1,256]{3,2,1,0:T(1,128)S(1)} %collective-permute-done, f32[24,34,258]{2,1,0:T(8,128)S(1)} %compare_convert_fusion), kind=kLoop, calls=%fused_computation.79 | loop fusion | flops 1216512 | bytes 8110080 | tf_op jit(solution)/shard_map/max | solution.py:34
  31.2 1.1 broadcast_multiply_fusion.2
  32.3 1.0 broadcast_minimum_fusion.1
  33.8 0.7 pad_maximum_fusion.7
  34.5 1.9 %fusion.65 = (f32[4,24,34,1]{3,2,1,0:T(8,128)}, f32[4,24,34,1]{3,2,1,0:T(8,128)S(1)}) fusion(f32[4,24,34,256]{3,2,1,0:T(8,128)S(1)} %pad_maximum_fusion.7), kind=kLoop, calls=%fused_computation.175 | loop fusion | bytes 52224 | tf_op jit(solution)/shard_map/slice | solution.py:14
  36.4 2.3 %copy.15 = f32[4,24,34,1]{2,1,3,0:T(8,128)S(1)} copy(f32[4,24,34,1]{3,2,1,0:T(8,128)} %get-tuple-element.31) | data formatting | bytes 26112 | tf_op jit(solution)/shard_map/slice | solution.py:14
  38.7 2.8 %collective-permute-start.2 = (f32[4,24,34,1]{2,1,3,0:T(8,128)S(1)}, f32[4,24,34,1]{2,1,3,0:T(8,128)S(1)}, u32[]{:S(2)}, u32[]{:S(2)}) collective-permute-start(f32[4,24,34,1]{2,1,3,0:T(8,128)S(1)} %copy.15), channel_id=1, source_target_pairs={{0,4},{4,8},{8,12},{12,16},{16,20},{20,24},{24,28},{28,0},{1,5},{5... | collective-permute-start | bytes 39176 | tf_op jit(solution)/shard_map/ppermute | solution.py:16
  41.5 0.8 copy.17
  42.3 3.0 %collective-permute-start.3 = (f32[4,24,34,1]{2,1,3,0:T(8,128)S(1)}, f32[4,24,34,1]{2,1,3,0:T(8,128)S(1)}, u32[]{:S(2)}, u32[]{:S(2)}) collective-permute-start(f32[4,24,34,1]{2,1,3,0:T(8,128)S(1)} %copy.17), channel_id=1, source_target_pairs={{4,0},{8,4},{12,8},{16,12},{20,16},{24,20},{28,24},{0,28},{5,1},{9... | collective-permute-start | bytes 39176 | tf_op jit(solution)/shard_map/ppermute | solution.py:17
  45.2 5.7 %multiply_subtract_fusion.1 = f32[4,24,33,256]{3,2,1,0:T(8,128)} fusion(f32[4,24,33,256]{3,2,1,0:T(8,128)} %dynamic-update-slice.10, f32[4,24,32,256]{3,2,1,0:T(8,128)} %param.6, f32[4,24,1,256]{3,2,1,0:T(1,128)S(1)} %collective-permute-done, f32[24,33,256]{2,1,0:T(8,128)} %broadcast_multiply_fusion.2, f32[24,33,256]{2,1,0:T(8,128)} %broadcast_minimum_fusion.1, ...), kind=kLoop, calls=%fused_computation.13 | loop fusion | flops 6488064 | bytes 12165120 | tf_op jit(solution)/shard_map/sub | solution.py:33
  51.0 0.8 copy.16
  51.8 2.1 %copy.18 = f32[4,24,34,1]{3,2,1,0:T(8,128)} copy(f32[4,24,34,1]{2,1,3,0:T(8,128)S(1)} %collective-permute-done.3) | data formatting | bytes 26112 | tf_op jit(solution)/shard_map/ppermute | solution.py:17
  53.9 3.4 %broadcast_maximum_fusion = (f32[24,32,257]{2,1,0:T(8,128)S(1)}, f32[24,32,257]{2,1,0:T(8,128)S(1)}, f32[24,32,257]{2,1,0:T(8,128)S(1)}) fusion(f32[4,24,34,1]{3,2,1,0:T(8,128)} %copy.18, f32[4,24,1,256]{3,2,1,0:T(1,128)S(1)} %collective-permute-done.1, f32[4,24,32,256]{3,2,1,0:T(8,128)} %param.6, f32[4,24,1,256]{3,2,1,0:T(1,128)S(1)} %collective-permute-done, ...), kind=kLoop, calls=%fused_computation.76 | loop fusion | flops 2368512 | bytes 7316996 | tf_op jit(solution)/shard_map/max | solution.py:39
  57.4 0.9 copy-done.7
  58.4 1.2 copy-done.3
  59.6 1.6 %compare_select_fusion = f32[24,34,258]{2,1,0:T(8,128)S(1)} fusion(f32[4,24,34,1]{3,2,1,0:T(8,128)S(1)} %copy-done.4, f32[4,24,34,1]{3,2,1,0:T(8,128)S(1)} %copy.16, f32[4,24,1,256]{3,2,1,0:T(1,128)S(1)} %collective-permute-done.1, f32[4,24,32,256]{3,2,1,0:T(8,128)S(1)} %copy-done.3, f32[4,24,1,256]{3,2,1,0:T(1,128)S(1)} %collective-permute-done, ...), kind=kLoop, calls=%fused_computation.24 | loop fusion | flops 3368448 | bytes 4245744 | tf_op jit(solution)/shard_map/mul | solution.py:23
  61.2 5.1 %fusion.67 = f32[24,34,258]{2,1,0:T(8,128)S(1)} fusion(f32[24,34,258]{2,1,0:T(8,128)S(1)} %compare_select_fusion), kind=kOutput, calls=%fused_computation.177 | output fusion | flops 4842144 | bytes 1684224 | tf_op jit(solution)/shard_map/jit(cumsum)/reduce_window_sum | solution.py:181
  66.2 13.5 %all_gather.9 = f32[4,34,258]{2,1,0:T(8,128)S(1)} all-gather(f32[1,34,258]{2,1,0:T(8,128)S(1)} %slice.362), channel_id=1, replica_groups=mesh['gx'=4,'gy'=8,'gz'=4] {'gz'}, dimensions={0}, use_global_device_ids=true | all-gather | bytes 175440 | tf_op jit(solution)/shard_map/all_gather | solution.py:183
  80.0 4.2 %multiply_subtract_fusion = f32[4,24,32,257]{3,2,1,0:T(8,128)} fusion(f32[4,24,34,1]{3,2,1,0:T(8,128)S(1)} %copy-done.4, f32[4,24,1,256]{3,2,1,0:T(1,128)S(1)} %collective-permute-done.1, f32[4,24,32,256]{3,2,1,0:T(8,128)S(1)} %copy-done.3, f32[4,24,1,256]{3,2,1,0:T(1,128)S(1)} %collective-permute-done, f32[4,24,34,1]{3,2,1,0:T(8,128)S(1)} %copy.16, ...), kind=kLoop, calls=%fused_computation.10 | loop fusion | flops 10263552 | bytes 8894976 | tf_op jit(solution)/shard_map/sub | solution.py:38
  84.2 6.6 %fusion = f32[4,24,32,256]{3,2,1,0:T(8,128)} fusion(f32[4,24,32,256]{3,2,1,0:T(8,128)S(1)} %copy-done.3, f32[4,24,32,257]{3,2,1,0:T(8,128)} %multiply_subtract_fusion, f32[4,24,33,256]{3,2,1,0:T(8,128)S(1)} %copy-done.6), kind=kLoop, calls=%fused_computation.15 | loop fusion | flops 3145728 | bytes 18874368 | tf_op jit(solution)/shard_map/sub | solution.py:42
  90.8 1.3 copy-done.8
  92.1 2.6 %fusion.28 = (f32[1,24,32,256]{3,2,1,0:T(8,128)S(1)}, f32[1,24,32,256]{3,2,1,0:T(8,128)S(1)}) fusion(f32[24,34,258]{2,1,0:T(8,128)S(1)} %subtract_multiply_fusion, f32[24,33,256]{2,1,0:T(8,128)S(1)} %get-tuple-element.25, f32[4,24,32,256]{3,2,1,0:T(8,128)} %fusion, f32[4,24,32,256]{3,2,1,0:T(8,128)S(1)} %copy-done.3, f32[256]{0:T(256)S(1)} %add_multiply_fusion, ...), kind=kLoop, calls=%fused_computation.65 | loop fusion | flops 3538944 | bytes 11797504 | tf_op jit(solution)/shard_map/stack | solution.py:57
  94.7 2.1 %maximum_multiply_fusion = f32[4,24,32,256]{3,2,1,0:T(8,128)} fusion(f32[1,24,32,256]{3,2,1,0:T(8,128)S(1)} %get-tuple-element.30, f32[1,24,32,256]{3,2,1,0:T(8,128)S(1)} %get-tuple-element.29, f32[2,24,32,256]{3,2,1,0:T(8,128)S(1)} %slice-done, f32[24,32,256]{2,1,0:T(8,128)S(1)} %copy-done.9), kind=kLoop, calls=%fused_computation.18 | loop fusion | flops 2359296 | bytes 7077888 | tf_op jit(solution)/shard_map/mul | solution.py:57
  96.8 2.8 %fusion.3.f_ref = f32[4,24,32,256]{3,2,1,0:T(8,128)} fusion(f32[4,24,32,256]{3,2,1,0:T(8,128)} %maximum_multiply_fusion, f32[24,32,256]{2,1,0:T(8,128)S(1)} %copy-done.9, f32[24]{0:T(128)S(1)} %compare_convert_fusion.1, f32[2,32,256]{2,1,0:T(8,128)S(1)} %copy-done.15), kind=kLoop, calls=%fused_computation.27 | loop fusion | flops 1179648 | bytes 3997792 | tf_op jit(solution)/shard_map/scatter-add | solution.py:197
  99.6 6.1 %shard_map.46 = (f32[4,24,32,256]{3,2,1,0:T(8,128)}, f32[2,24,32,256]{3,2,1,0:T(8,128)}, f32[2,24,32,256]{3,2,1,0:T(8,128)}) custom-call(f32[4,24,32,256]{3,2,1,0:T(8,128)} %fusion.3.f_ref, f32[2,24,32,256]{3,2,1,0:T(8,128)} %broadcast_multiply_fusion.c_ref, f32[2,32,256]{2,1,0:T(8,128)} %multiply_select_fusion.ctop_ref), custom_call_target="tpu_custom_call" | custom-call | tf_op jit(solution)/shard_map/pallas_call | solution.py:108
  105.7 0.9 fusion.46
  106.6 0.9 bitcast_dynamic-update-slice_fusion
  107.5 0.9 bitcast_dynamic-update-slice_fusion.4
  108.4 0.8 bitcast_dynamic-update-slice_fusion.3
  109.2 0.8 bitcast_dynamic-update-slice_fusion.2
  110.1 0.8 bitcast_dynamic-update-slice_fusion.1
  110.9 0.8 copy-done.14
  111.8 28.7 %all-gather.3.cloned.1.call-done = f32[64,32,256]{2,1,0:T(8,128)} async-done(((f32[16,32,256]{2,1,0:T(8,128)}), f32[64,32,256]{2,1,0:T(8,128)}) %all-gather.3.cloned.1.call-update) | async-done | bytes 2097168 | tf_op jit(solution)/shard_map/all_gather | solution.py:207
  140.4 1.4 slice.382
  142.1 1.3 copy-done.11
  144.0 1.4 copy-done.10
  145.8 2.5 %fusion.1 = f32[4,24,32,256]{3,2,1,0:T(8,128)} fusion(f32[4,24,32,256]{3,2,1,0:T(8,128)S(1)} %copy-done.10, f32[2,24,32,256]{3,2,1,0:T(8,128)S(1)} %copy-done.13, f32[4,32,256]{2,1,0:T(8,128)S(1)} %select_select_fusion, f32[2,24,32,256]{3,2,1,0:T(8,128)S(1)} %copy-done.12, f32[4,32,256]{2,1,0:T(8,128)S(1)} %select_select_fusion.1), kind=kLoop, calls=%fused_computation.20 | loop fusion | flops 3145728 | bytes 9699328 | tf_op jit(solution)/shard_map/add | solution.py:211
  (61 shorter events, 3.2 us)
Async XLA Ops:
  6.5 11.5 %copy-start = (s32[128,2048]{1,0:T(8,128)S(1)}, s32[128,2048]{1,0:T(8,128)}, u32[]{:S(2)}) copy-start(s32[128,2048]{1,0:T(8,128)} %param.8) | copy-start | bytes 3145732
  6.5 133.9 %all-gather.3.cloned.1.call-start = ((), (), s32[]{:S(2)}) async-start(), calls=%async_computation | async-start | bytes 2621440 | tf_op jit(solution)/shard_map/all_gather | solution.py:207
  8.1 17.3 %collective-permute-start.1 = (f32[4,24,1,256]{3,2,1,0:T(1,128)S(1)}, f32[4,24,1,256]{3,2,1,0:T(1,128)S(1)}, u32[]{:S(2)}, u32[]{:S(2)}) collective-permute-start(f32[4,24,1,256]{3,2,1,0:T(1,128)S(1)} %get-tuple-element.34), channel_id=1, source_target_pairs={{32,0},{64,32},{96,64},{0,96},{33,1},{65,33},{97,65},{1,97},{34,2}... | collective-permute-start | bytes 294920 | tf_op jit(solution)/shard_map/ppermute | solution.py:17
  9.3 19.0 %collective-permute-start = (f32[4,24,1,256]{3,2,1,0:T(1,128)S(1)}, f32[4,24,1,256]{3,2,1,0:T(1,128)S(1)}, u32[]{:S(2)}, u32[]{:S(2)}) collective-permute-start(f32[4,24,1,256]{3,2,1,0:T(1,128)S(1)} %get-tuple-element.33), channel_id=1, source_target_pairs={{0,32},{32,64},{64,96},{96,0},{1,33},{33,65},{65,97},{97,1},{2,34}... | collective-permute-start | bytes 294920 | tf_op jit(solution)/shard_map/ppermute | solution.py:16
  10.1 14.7 %collective-permute-start.4 = (f32[2,32,256]{2,1,0:T(8,128)S(1)}, f32[2,32,256]{2,1,0:T(8,128)S(1)}, u32[]{:S(2)}, u32[]{:S(2)}) collective-permute-start(f32[2,32,256]{2,1,0:T(8,128)S(1)} %slice_bitcast_fusion.20), channel_id=1, source_target_pairs={{0,1},{1,2},{2,3},{4,5},{5,6},{6,7},{8,9},{9,10},{10,11},{12,13},{... | collective-permute-start | bytes 196616 | tf_op jit(solution)/shard_map/ppermute | solution.py:173
  20.6 7.6 %copy-start.5 = (f32[24,34,258]{2,1,0:T(8,128)}, f32[24,34,258]{2,1,0:T(8,128)S(1)}, u32[]{:S(2)}) copy-start(f32[24,34,258]{2,1,0:T(8,128)S(1)} %compare_convert_fusion) | copy-start | bytes 2526340
  31.2 2.6 %copy-start.2 = (f32[4,24,32,256]{3,2,1,0:T(8,128)S(1)}, f32[4,24,32,256]{3,2,1,0:T(8,128)}, u32[]{:S(2)}) copy-start(f32[4,24,32,256]{3,2,1,0:T(8,128)} %param.6) | copy-start | bytes 9437188
  38.7 12.3 %collective-permute-start.2 = (f32[4,24,34,1]{2,1,3,0:T(8,128)S(1)}, f32[4,24,34,1]{2,1,3,0:T(8,128)S(1)}, u32[]{:S(2)}, u32[]{:S(2)}) collective-permute-start(f32[4,24,34,1]{2,1,3,0:T(8,128)S(1)} %copy.15), channel_id=1, source_target_pairs={{0,4},{4,8},{8,12},{12,16},{16,20},{20,24},{24,28},{28,0},{1,5},{5... | collective-permute-start | bytes 39176 | tf_op jit(solution)/shard_map/ppermute | solution.py:16
  42.3 9.5 %collective-permute-start.3 = (f32[4,24,34,1]{2,1,3,0:T(8,128)S(1)}, f32[4,24,34,1]{2,1,3,0:T(8,128)S(1)}, u32[]{:S(2)}, u32[]{:S(2)}) collective-permute-start(f32[4,24,34,1]{2,1,3,0:T(8,128)S(1)} %copy.17), channel_id=1, source_target_pairs={{4,0},{8,4},{12,8},{16,12},{20,16},{24,20},{28,24},{0,28},{5,1},{9... | collective-permute-start | bytes 39176 | tf_op jit(solution)/shard_map/ppermute | solution.py:17
  53.9 4.5 %copy-start.4 = (f32[4,24,34,1]{3,2,1,0:T(8,128)S(1)}, f32[4,24,34,1]{3,2,1,0:T(8,128)}, u32[]{:S(2)}) copy-start(f32[4,24,34,1]{3,2,1,0:T(8,128)} %copy.18) | copy-start | bytes 39172
  57.3 1.0 copy-start.7
  57.3 2.3 %copy-start.3 = (f32[4,24,32,256]{3,2,1,0:T(8,128)S(1)}, f32[4,24,32,256]{3,2,1,0:T(8,128)}, u32[]{:S(2)}) copy-start(f32[4,24,32,256]{3,2,1,0:T(8,128)} %param.6) | copy-start | bytes 9437188
  80.0 4.2 %copy-start.6 = (f32[4,24,33,256]{3,2,1,0:T(8,128)S(1)}, f32[4,24,33,256]{3,2,1,0:T(8,128)}, u32[]{:S(2)}) copy-start(f32[4,24,33,256]{3,2,1,0:T(8,128)} %multiply_subtract_fusion.1) | copy-start | bytes 9732100
  90.8 1.3 copy-start.8
  92.1 2.6 %slice-start = ((f32[4,24,32,256]{3,2,1,0:T(8,128)}), f32[2,24,32,256]{3,2,1,0:T(8,128)S(1)}, s32[]{:S(2)}) async-start(f32[4,24,32,256]{3,2,1,0:T(8,128)} %fusion), calls=%async_computation.1 | async-start | bytes 3145728 | tf_op jit(solution)/shard_map/slice | solution.py:57
  92.1 2.6 %copy-start.9 = (f32[24,32,256]{2,1,0:T(8,128)S(1)}, f32[24,32,256]{2,1,0:T(8,128)}, u32[]{:S(2)}) copy-start(f32[24,32,256]{2,1,0:T(8,128)} %get-tuple-element.36) | copy-start | bytes 2359300
  94.7 2.1 %copy-start.15 = (f32[2,32,256]{2,1,0:T(8,128)S(1)}, f32[2,32,256]{2,1,0:T(8,128)}, u32[]{:S(2)}) copy-start(f32[2,32,256]{2,1,0:T(8,128)} %param.9) | copy-start | bytes 196612
  110.9 0.8 copy-start.14
  140.4 3.5 %copy-start.13 = (f32[2,24,32,256]{3,2,1,0:T(8,128)S(1)}, f32[2,24,32,256]{3,2,1,0:T(8,128)}, u32[]{:S(2)}) copy-start(f32[2,24,32,256]{3,2,1,0:T(8,128)} %get-tuple-element.22) | copy-start | bytes 4718596
  141.9 1.6 %copy-start.11 = (f32[64,32,256]{2,1,0:T(8,128)S(1)}, f32[64,32,256]{2,1,0:T(8,128)}, u32[]{:S(2)}) copy-start(f32[64,32,256]{2,1,0:T(8,128)} %all-gather.3.cloned.1.call-done) | copy-start | bytes 6291460
  143.5 1.9 %copy-start.10 = (f32[4,24,32,256]{3,2,1,0:T(8,128)S(1)}, f32[4,24,32,256]{3,2,1,0:T(8,128)}, u32[]{:S(2)}) copy-start(f32[4,24,32,256]{3,2,1,0:T(8,128)} %get-tuple-element.20) | copy-start | bytes 9437188
  143.5 2.4 %copy-start.12 = (f32[2,24,32,256]{3,2,1,0:T(8,128)S(1)}, f32[2,24,32,256]{3,2,1,0:T(8,128)}, u32[]{:S(2)}) copy-start(f32[2,24,32,256]{3,2,1,0:T(8,128)} %get-tuple-element.21) | copy-start | bytes 4718596
  145.8 2.5 %copy-start.1 = (s32[128,2048]{1,0:T(8,128)S(1)}, s32[128,2048]{1,0:T(8,128)}, u32[]{:S(2)}) copy-start(s32[128,2048]{1,0:T(8,128)} %param.8) | copy-start | bytes 3145732
Sparse Core Ops, SparseCore 0:
  111.9 28.5 all-gather.2

commit v2 on v1

--- a/solution.py
+++ b/solution.py
@@ -57,11 +57,10 @@
     return jnp.stack([moved[0], moved[1], east_new, north_new]) * wet_inner
 
 
-def local_solve_kernel(f_ref, c_ref, ctop_ref, y_ref, u_ref, v_ref, ratio_s):
-    levels = f_ref.shape[1]
+def coupling_kernel(c_ref, ctop_ref, ratio_ref, inv_ref, u_ref, v_ref, ends_ref):
+    levels = c_ref.shape[1]
     ctop = ctop_ref[...]
     ratio_prev = None
-    vy_prev = None
     vu_prev = None
     for k in range(levels):
         above = ctop if k == 0 else c_ref[:, k - 1]
@@ -72,58 +71,93 @@
             divisor = 1.0 + above * (1.0 - ratio_prev) + below
         inv = 1.0 / divisor
         ratio = below * inv
+        vu = ctop * inv if k == 0 else above * vu_prev * inv
+        ratio_ref[:, k] = ratio
+        inv_ref[:, k] = inv
+        u_ref[:, k] = vu
+        ratio_prev, vu_prev = ratio, vu
+    u_later = vu_prev
+    v_later = ratio_prev
+    pairs = c_ref.shape[0]
+    ends_ref[pairs:2 * pairs] = u_later
+    ends_ref[3 * pairs:4 * pairs] = v_later
+    v_ref[:, levels - 1] = v_later
+    for k in range(levels - 2, -1, -1):
+        ratio = ratio_ref[:, k]
+        u_later = u_ref[:, k] + ratio * u_later
+        v_later = ratio * v_later
+        u_ref[:, k] = u_later
+        v_ref[:, k] = v_later
+    ends_ref[0:pairs] = u_later
+    ends_ref[2 * pairs:3 * pairs] = v_later
+
+
+def field_kernel(f_ref, c_ref, ctop_ref, ratio_ref, inv_ref, y_ref, ends_ref):
+    levels = f_ref.shape[1]
+    fields = f_ref.shape[0]
+    vy = None
+    for k in range(levels):
+        inv = jnp.repeat(inv_ref[:, k], 2, axis=0)
         rhs = f_ref[:, k]
         if k == 0:
-            vy = rhs * jnp.repeat(inv, 2, axis=0)
-            vu = ctop * inv
+            vy = rhs * inv
         else:
-            vy = (rhs + jnp.repeat(above, 2, axis=0) * vy_prev) * jnp.repeat(inv, 2, axis=0)
-            vu = above * vu_prev * inv
-        ratio_s[:, k] = ratio
+            above = jnp.repeat(c_ref[:, k - 1], 2, axis=0)
+            vy = (rhs + above * vy) * inv
         y_ref[:, k] = vy
-        u_ref[:, k] = vu
-        ratio_prev, vy_prev, vu_prev = ratio, vy, vu
-    y_later = vy_prev
-    u_later = vu_prev
-    v_later = ratio_prev
-    v_ref[:, levels - 1] = v_later
+    y_later = vy
+    ends_ref[fields:2 * fields] = y_later
     for k in range(levels - 2, -1, -1):
-        ratio = ratio_s[:, k]
-        y_later = y_ref[:, k] + jnp.repeat(ratio, 2, axis=0) * y_later
-        u_later = u_ref[:, k] + ratio * u_later
-        v_later = ratio * v_later
+        ratio = jnp.repeat(ratio_ref[:, k], 2, axis=0)
+        y_later = y_ref[:, k] + ratio * y_later
         y_ref[:, k] = y_later
-        u_ref[:, k] = u_later
-        v_ref[:, k] = v_later
-
-
-def local_solve(forced, coupling, ctop):
+    ends_ref[0:fields] = y_later
+
+
+def _specs(lead, levels, bx, cols_y):
+    return pl.BlockSpec((lead, levels, bx, cols_y), lambda i: (0, 0, i, 0))
+
+
+def _plane_spec(lead, bx, cols_y):
+    return pl.BlockSpec((lead, bx, cols_y), lambda i: (0, i, 0))
+
+
+def coupling_solve(coupling, ctop):
+    pairs, levels, cols_x, cols_y = coupling.shape
+    bx = 8 if cols_x % 8 == 0 else cols_x
+    cspec = _specs(pairs, levels, bx, cols_y)
+    full = jax.ShapeDtypeStruct(coupling.shape, jnp.float32)
+    return pl.pallas_call(
+        coupling_kernel,
+        grid=(cols_x // bx,),
+        in_specs=[cspec, _plane_spec(pairs, bx, cols_y)],
+        out_specs=[cspec, cspec, cspec, cspec, _plane_spec(4 * pairs, bx, cols_y)],
+        out_shape=[full, full, full, full,
+                   jax.ShapeDtypeStruct((4 * pairs, cols_x, cols_y), jnp.float32)],
+    )(coupling, ctop)
+
+
+def field_solve(forced, coupling, ctop, ratio, inv):
     fields, levels, cols_x, cols_y = forced.shape
     pairs = coupling.shape[0]
     bx = 8 if cols_x % 8 == 0 else cols_x
-    grid = (cols_x // bx,)
-    fspec = pl.BlockSpec((fields, levels, bx, cols_y), lambda i: (0, 0, i, 0))
-    cspec = pl.BlockSpec((pairs, levels, bx, cols_y), lambda i: (0, 0, i, 0))
-    tspec = pl.BlockSpec((pairs, bx, cols_y), lambda i: (0, i, 0))
+    fspec = _specs(fields, levels, bx, cols_y)
+    cspec = _specs(pairs, levels, bx, cols_y)
     return pl.pallas_call(
-        local_solve_kernel,
-        grid=grid,
-        in_specs=[fspec, cspec, tspec],
-        out_specs=[fspec, cspec, cspec],
-        out_shape=[
-            jax.ShapeDtypeStruct(forced.shape, jnp.float32),
-            jax.ShapeDtypeStruct(coupling.shape, jnp.float32),
-            jax.ShapeDtypeStruct(coupling.shape, jnp.float32),
-        ],
-        scratch_shapes=[pltpu.VMEM((pairs, levels, bx, cols_y), jnp.float32)],
-    )(forced, coupling, ctop)
-
-
-def interface_values(summary, place, peers):
+        field_kernel,
+        grid=(cols_x // bx,),
+        in_specs=[fspec, cspec, _plane_spec(pairs, bx, cols_y), cspec, cspec],
+        out_specs=[fspec, _plane_spec(2 * fields, bx, cols_y)],
+        out_shape=[jax.ShapeDtypeStruct(forced.shape, jnp.float32),
+                   jax.ShapeDtypeStruct((2 * fields, cols_x, cols_y), jnp.float32)],
+    )(forced, coupling, ctop, ratio, inv)
+
+
+def interface_values(y_ends, uv_ends, place, peers):
     fields = 4
-    y0 = summary[:, 0:fields]
-    y1 = summary[:, fields:2 * fields]
-    rest = jnp.repeat(summary[:, 2 * fields:], 2, axis=1)
+    y0 = y_ends[:, 0:fields]
+    y1 = y_ends[:, fields:2 * fields]
+    rest = jnp.repeat(uv_ends, 2, axis=1)
     u0 = rest[:, 0:4]
     u1 = rest[:, 4:8]
     v0 = rest[:, 8:12]
@@ -134,8 +168,7 @@
             pt_q, qt_q = y0[q], v0[q]
             pb_q, qb_q = y1[q], v1[q]
         else:
-            d = 1.0 - u0[q] * qb[-1]
-            inv = 1.0 / d
+            inv = 1.0 / (1.0 - u0[q] * qb[-1])
             pt_q = (y0[q] + u0[q] * pb[-1]) * inv
             qt_q = v0[q] * inv
             pb_q = y1[q] + u1[q] * (pb[-1] + qb[-1] * pt_q)
@@ -171,19 +204,28 @@
     start_z = place_z * lev_count
     down_z = [(i, i + 1) for i in range(peers_z - 1)]
     mix_above = lax.ppermute(mixing[:, lev_count - 1], "gz", down_z)
+    levels = start_z + jnp.arange(lev_count, dtype=jnp.int32)
+    depth_inner = lax.dynamic_slice(depth_levels, (start_x, start_y), (col_x, col_y))
+    wet_here = (levels[:, None, None] < depth_inner[None]).astype(jnp.float32)
+    wet_next = ((levels + 1)[:, None, None] < depth_inner[None]).astype(jnp.float32)
+    coupling = mixing * (wet_here * wet_next)[None]
+    wet_up = ((start_z - 1) < depth_inner).astype(jnp.float32)
+    ctop = mix_above * (wet_up * wet_here[0])[None]
+    ctop = jnp.where(place_z > 0, ctop, 0.0)
+    ratio, inv, u, v, uv_ends = coupling_solve(coupling, ctop)
+    uv_all = lax.all_gather(uv_ends, "gz")
     padded = padded_2(state, (("gx", 2), ("gy", 3)), 1)
     row_index = (start_x - 1 + jnp.arange(col_x + 2, dtype=jnp.int32)) % total_x
     col_index = (start_y - 1 + jnp.arange(col_y + 2, dtype=jnp.int32)) % total_y
     depth_pad = jnp.take(jnp.take(depth_levels, row_index, axis=0), col_index, axis=1)
-    levels = start_z + jnp.arange(lev_count, dtype=jnp.int32)
     wet_pad = (levels[:, None, None] < depth_pad[None]).astype(jnp.float32)
     density_field = density_of(padded, wet_pad)
     inclusive = jnp.cumsum(density_field, axis=0)
     column_total = inclusive[-1]
-    gathered = lax.all_gather(column_total, "gz")
     shallower = jnp.zeros_like(column_total)
-    for q in range(peers_z):
-        shallower = shallower + jnp.where(q < place_z, gathered[q], 0.0)
+    for hop in range(1, peers_z):
+        pairs_z = [(i, i + hop) for i in range(peers_z - hop)]
+        shallower = shallower + lax.ppermute(column_total, "gz", pairs_z)
     pressure = 0.03 * (shallower[None] + inclusive - 0.5 * density_field)
     face_row = start_y - 1 + jnp.arange(col_y + 1, dtype=jnp.int32)
     wall_face = ((face_row >= 0) & (face_row <= total_y - 2)).astype(jnp.float32)
@@ -191,21 +233,11 @@
     coriolis = 0.5 + (row_global.astype(jnp.float32) + 0.5) / total_y
     forced = advance(padded, wet_pad, pressure, wall_face, coriolis)
     wet_inner = wet_pad[:, 1:-1, 1:-1]
-    depth_inner = depth_pad[1:-1, 1:-1]
-    wet_next = ((levels + 1)[:, None, None] < depth_inner[None]).astype(jnp.float32)
     top_level = (levels == 0).astype(jnp.float32)
     forced = forced.at[2:].add(wind[:, None] * top_level[None, :, None, None] * wet_inner[None])
-    coupling = mixing * (wet_inner * wet_next)[None]
-    wet_up = ((start_z - 1) < depth_inner).astype(jnp.float32)
-    ctop = mix_above * (wet_up * wet_inner[0])[None]
-    ctop = jnp.where(place_z > 0, ctop, 0.0)
-    y, u, v = local_solve(forced, coupling, ctop)
-    last = lev_count - 1
-    summary = jnp.concatenate(
-        [y[:, 0], y[:, last], u[:, 0], u[:, last], v[:, 0], v[:, last]], axis=0
-    )
-    gathered_ends = lax.all_gather(summary, "gz")
-    x_above, x_below = interface_values(gathered_ends, place_z, peers_z)
+    y, y_ends = field_solve(forced, coupling, ctop, ratio, inv)
+    y_all = lax.all_gather(y_ends, "gz")
+    x_above, x_below = interface_values(y_all, uv_all, place_z, peers_z)
     u4 = jnp.repeat(u, 2, axis=0)
     v4 = jnp.repeat(v, 2, axis=0)
     return y + x_above[:, None] * u4 + x_below[:, None] * v4

time: 157 us -> 139 us (0.89)
  blocking collectives: 13.5 us -> 0 us
  other arithmetic: 48.3 us -> 36 us
  starting transfers between devices: 10.7 us -> 19.5 us
  waiting for transfers between devices: 28.7 us -> 21 us
  Pallas kernels: 6.13 us -> 10.7 us
  local copies, waits for them, and re-layouts: 34.1 us -> 37.5 us
    all_gather x1 -> x0, blocking collectives: 13.5 us -> none  [per_device(): gathered = lax.all_gather(column_total, 'gz')]
    ppermute x0 -> x3, starting transfers between devices: none -> 8.27 us  [per_device(): shallower = shallower + lax.ppermute(column_total, 'gz', pairs_z)]
    all_gather x1 -> x2, waiting for transfers between devices: 28.7 us -> 21 us  [the longest x1 21 us: per_device(): y_all = lax.all_gather(y_ends, 'gz')]
    pallas_call x1 -> x2, Pallas kernels: 6.13 us -> 10.7 us  [the longest x1 5.59 us: field_solve(): pl.pallas_call(field_kernel, grid=(cols_x // bx,), in_specs=[fspec, cspec...]
    sub x1, other arithmetic: 6.57 us -> 3.1 us  [advance(): interior - (flux_x[:, :, 1:] - flux_x[:, :, :-1] + flux_y[:, :, :, 1:] -...]
    sub x1, other arithmetic: 5.75 us -> 2.91 us  [advance(): 0.25 * (jnp.maximum(east_vel, 0.0) * west_side + jnp.minimum(east_vel, 0....]
    unnamed x38 -> x49, local copies, waits for them, and re-layouts: 16.2 us -> 13.7 us
    max x1, other arithmetic: 3.41 us -> 0.97 us  [advance(): jnp.maximum(north_vel, 0.0) * south_side]
  transfers between devices with their start and end apart: 6 -> 10, of which waited for: 1 -> 1; matrix products, arithmetic and copies ran while one was open for 14% -> 41% of each run, Pallas kernels for 0% -> 8%
where the time goes in v2:
time: 139 us
  local copies, waits for them, and re-layouts  37.5 us (27%)
  other arithmetic  36 us (26%)
  waiting for transfers between devices  21 us (15%)
  starting transfers between devices  19.5 us (14%)
  between operations  13.9 us (10%)
  Pallas kernels  10.7 us (8%)
    all_gather x1, waiting for transfers between devices, per_device(): y_all = lax.all_gather(y_ends, 'gz')  21 us
    unnamed x49, local copies, waits for them, and re-layouts  13.7 us
    ppermute x3, starting transfers between devices, per_device(): shallower = shallower + lax.ppermute(column_total, 'gz', pairs_z)  8.27 us
    slice x3, local copies, waits for them, and re-layouts, padded_2(): last = lax.slice_in_dim(array, length - width, length, axis=dim)  7.04 us
    pallas_call x1, Pallas kernels, field_solve(): pl.pallas_call(field_kernel, grid=(cols_x // bx,), in_specs=[fspec, cspec...  5.59 us
    pallas_call x1, Pallas kernels, coupling_solve(): pl.pallas_call(coupling_kernel, grid=(cols_x // bx,), in_specs=[cspec, _p...  5.07 us
    another operation x1, other arithmetic, per_device(): inclusive = jnp.cumsum(density_field, axis=0)  5.06 us
    ppermute x1, starting transfers between devices, per_device(): mix_above = lax.ppermute(mixing[:, lev_count - 1], 'gz', down_z)  4.43 us
  transfers between devices with their start and end apart: 10, of which 1 were waited for; matrix products, arithmetic and copies ran while one was open for 41% of the time, Pallas kernels for 8%

profile of v2, /device:TPU:0, one launch (start us, length us, event | category | flops | bytes accessed | tf_op | source)
XLA Modules:
  0.0 138.6 jit_solution(6893034038882027724)
XLA Ops:
  6.5 2.2 %fusion.61 = (f32[4,24,1,256]{3,2,1,0:T(1,128)S(1)}, f32[4,24,1,256]{3,2,1,0:T(1,128)}) fusion(f32[4,24,32,256]{3,2,1,0:T(8,128)} %param.6), kind=kLoop, calls=%fused_computation.164 | loop fusion | bytes 393216 | tf_op jit(solution)/shard_map/slice | solution.py:14
  8.7 1.0 collective-permute-start.1
  9.7 1.5 %slice_bitcast_fusion.19 = f32[2,32,256]{2,1,0:T(8,128)} fusion(f32[2,24,32,256]{3,2,1,0:T(8,128)} %param.7), kind=kLoop, calls=%fused_computation.122 | loop fusion | bytes 131072 | tf_op jit(solution)/shard_map/squeeze | solution.py:206
  11.2 4.4 %collective-permute-start.7 = (f32[2,32,256]{2,1,0:T(8,128)}, f32[2,32,256]{2,1,0:T(8,128)}, u32[]{:S(2)}, u32[]{:S(2)}) collective-permute-start(f32[2,32,256]{2,1,0:T(8,128)} %slice_bitcast_fusion.19), channel_id=1, source_target_pairs={{0,1},{1,2},{2,3},{4,5},{5,6},{6,7},{8,9},{9,10},{10,11},{12,13},{... | collective-permute-start | bytes 196616 | tf_op jit(solution)/shard_map/ppermute | solution.py:206
  15.7 4.1 %constant_dynamic-update-slice_fusion = f32[4,24,33,256]{3,2,1,0:T(8,128)} fusion(f32[4,24,32,256]{3,2,1,0:T(8,128)} %param.6), kind=kLoop, calls=%fused_computation.144 | loop fusion | bytes 6291456
  19.8 0.6 fusion.51
  20.4 0.6 add_multiply_fusion
  21.0 0.7 gather_fusion
  22.1 1.0 gather_fusion.1
  23.6 1.1 copy-done.3
  24.7 1.2 slice.323
  26.2 2.9 %broadcast_multiply_fusion.c_ref = f32[2,24,32,256]{3,2,1,0:T(8,128)} fusion(f32[2,24,32,256]{3,2,1,0:T(8,128)} %param.7, f32[24,32,256]{2,1,0:T(8,128)S(1)} %compare_select_fusion.1), kind=kLoop, calls=%fused_computation.72 | loop fusion | flops 393216 | bytes 3932160 | tf_op jit(solution)/shard_map/mul | solution.py:211
  29.1 0.8 fusion.46
  29.9 0.5 compare_convert_fusion.2
  30.4 1.5 %multiply_select_fusion.ctop_ref = f32[2,32,256]{2,1,0:T(8,128)} fusion(f32[2,32,256]{2,1,0:T(8,128)} %collective-permute-done.7, f32[32,256]{1,0:T(8,128)S(1)} %fusion.46, pred[]{:T(512)S(6)} %gt.3), kind=kLoop, calls=%fused_computation.121 | loop fusion | flops 32768 | bytes 163841 | tf_op jit(solution)/shard_map/jit(_where)/select_n | solution.py:214
  31.9 5.1 %shard_map.46 = (f32[2,24,32,256]{3,2,1,0:T(8,128)}, f32[2,24,32,256]{3,2,1,0:T(8,128)}, f32[2,24,32,256]{3,2,1,0:T(8,128)}, f32[2,24,32,256]{3,2,1,0:T(8,128)}, f32[8,32,256]{2,1,0:T(8,128)}) custom-call(f32[2,24,32,256]{3,2,1,0:T(8,128)} %broadcast_multiply_fusion.c_ref, f32[2,32,256]{2,1,0:T(8,128)} %multiply_select_fusion.ctop_ref), custom_call_target="tpu_custom_call" | custom-call | tf_op jit(solution)/shard_map/pallas_call | solution.py:130
  37.1 0.7 pad_maximum_fusion.7
  37.7 2.6 %fusion.60 = (f32[4,24,34,1]{3,2,1,0:T(8,128)}, f32[4,24,34,1]{3,2,1,0:T(8,128)}) fusion(f32[4,24,34,256]{3,2,1,0:T(8,128)S(1)} %pad_maximum_fusion.7), kind=kLoop, calls=%fused_computation.163 | loop fusion | bytes 52224 | tf_op jit(solution)/shard_map/slice | solution.py:14
  40.3 2.3 %copy.13 = f32[4,24,34,1]{2,1,3,0:T(8,128)S(1)} copy(f32[4,24,34,1]{3,2,1,0:T(8,128)} %get-tuple-element.39) | data formatting | bytes 26112 | tf_op jit(solution)/shard_map/slice | solution.py:14
  42.6 2.8 %collective-permute-start.2 = (f32[4,24,34,1]{2,1,3,0:T(8,128)S(1)}, f32[4,24,34,1]{2,1,3,0:T(8,128)S(1)}, u32[]{:S(2)}, u32[]{:S(2)}) collective-permute-start(f32[4,24,34,1]{2,1,3,0:T(8,128)S(1)} %copy.13), channel_id=1, source_target_pairs={{0,4},{4,8},{8,12},{12,16},{16,20},{20,24},{24,28},{28,0},{1,5},{5... | collective-permute-start | bytes 39176 | tf_op jit(solution)/shard_map/ppermute | solution.py:16
  45.4 2.3 %copy.15 = f32[4,24,34,1]{2,1,3,0:T(8,128)S(1)} copy(f32[4,24,34,1]{3,2,1,0:T(8,128)} %get-tuple-element.40) | data formatting | bytes 26112 | tf_op jit(solution)/shard_map/slice | solution.py:15
  47.7 3.0 %collective-permute-start.3 = (f32[4,24,34,1]{2,1,3,0:T(8,128)S(1)}, f32[4,24,34,1]{2,1,3,0:T(8,128)}, u32[]{:S(2)}, u32[]{:S(2)}) collective-permute-start(f32[4,24,34,1]{2,1,3,0:T(8,128)S(1)} %copy.15), channel_id=1, source_target_pairs={{4,0},{8,4},{12,8},{16,12},{20,16},{24,20},{28,24},{0,28},{5,1},{9... | collective-permute-start | bytes 39176 | tf_op jit(solution)/shard_map/ppermute | solution.py:17
  50.7 2.8 %dynamic-update-slice.4 = f32[4,24,33,256]{3,2,1,0:T(8,128)} dynamic-update-slice(f32[4,24,33,256]{3,2,1,0:T(8,128)} %constant_dynamic-update-slice_fusion, f32[4,24,1,256]{3,2,1,0:T(1,128)S(1)} %collective-permute-done.1, s32[]{} %constant.164, s32[]{} %constant.164, s32[]{} %constant.165, s32[]{} %constant.164) | dynamic-update-slice | bytes 196612 | tf_op jit(solution)/shard_map/concatenate | solution.py:18
  53.4 2.7 %broadcast_maximum_fusion.1 = (f32[24,33,256]{2,1,0:T(8,128)S(1)}, f32[24,33,256]{2,1,0:T(8,128)S(1)}, f32[24,33,256]{2,1,0:T(8,128)S(1)}) fusion(f32[4,24,33,256]{3,2,1,0:T(8,128)} %dynamic-update-slice.4, f32[4,24,32,256]{3,2,1,0:T(8,128)S(1)} %copy-done, f32[4,24,1,256]{3,2,1,0:T(1,128)S(1)} %collective-permute-done, f32[24,34,258]{2,1,0:T(8,128)} %copy-done.3), kind=kLoop, calls=%fused_computation.80 | loop fusion | flops 1216512 | bytes 8110080 | tf_op jit(solution)/shard_map/max | solution.py:34
  56.4 0.7 copy-done.10
  57.1 1.6 %copy-done.7 = f32[4,24,33,256]{3,2,1,0:T(8,128)S(1)} copy-done((f32[4,24,33,256]{3,2,1,0:T(8,128)S(1)}, f32[4,24,33,256]{3,2,1,0:T(8,128)}, u32[]{:S(2)}) %copy-start.7) | copy-done | bytes 3244056
  58.7 2.9 %multiply_subtract_fusion.1 = f32[4,24,33,256]{3,2,1,0:T(8,128)} fusion(f32[4,24,33,256]{3,2,1,0:T(8,128)S(1)} %copy-done.7, f32[4,24,32,256]{3,2,1,0:T(8,128)S(1)} %copy-done, f32[4,24,1,256]{3,2,1,0:T(1,128)S(1)} %collective-permute-done, f32[24,33,256]{2,1,0:T(8,128)S(1)} %get-tuple-element.43, f32[24,33,256]{2,1,0:T(8,128)S(1)} %get-tuple-element.44, ...), kind=kLoop, calls=%fused_computation.13 | loop fusion | flops 6488064 | bytes 12165120 | tf_op jit(solution)/shard_map/sub | solution.py:33
  61.6 2.1 %copy.14 = f32[4,24,34,1]{3,2,1,0:T(8,128)} copy(f32[4,24,34,1]{2,1,3,0:T(8,128)S(1)} %collective-permute-done.2) | data formatting | bytes 26112 | tf_op jit(solution)/shard_map/ppermute | solution.py:16
  63.8 2.9 %copy.16 = f32[4,24,34,1]{3,2,1,0:T(8,128)} copy(f32[4,24,34,1]{2,1,3,0:T(8,128)} %collective-permute-done.3) | data formatting | bytes 26112 | tf_op jit(solution)/shard_map/ppermute | solution.py:17
  66.6 3.1 %compare_select_fusion = f32[24,34,258]{2,1,0:T(8,128)S(1)} fusion(f32[4,24,34,1]{3,2,1,0:T(8,128)} %copy.16, f32[4,24,34,1]{3,2,1,0:T(8,128)} %copy.14, f32[4,24,1,256]{3,2,1,0:T(1,128)S(1)} %collective-permute-done.1, f32[4,24,32,256]{3,2,1,0:T(8,128)S(1)} %copy-done, f32[4,24,1,256]{3,2,1,0:T(1,128)S(1)} %collective-permute-done, s32[34,258]{1,0:T(8,128)S(1)} %copy.12, ...), kind=kLoop, calls=%fused_computation.24 | loop fusion | flops 3368448 | bytes 4245744 | tf_op jit(solution)/shard_map/mul | solution.py:23
  69.7 5.1 %fusion.62 = f32[24,34,258]{2,1,0:T(8,128)S(1)} fusion(f32[24,34,258]{2,1,0:T(8,128)S(1)} %compare_select_fusion), kind=kOutput, calls=%fused_computation.165 | output fusion | flops 4842144 | bytes 1684224 | tf_op jit(solution)/shard_map/jit(cumsum)/reduce_window_sum | solution.py:223
  74.8 3.2 %collective-permute-start.4 = (f32[34,258]{1,0:T(8,128)S(1)}, f32[34,258]{1,0:T(8,128)S(1)}, u32[]{:S(2)}, u32[]{:S(2)}) collective-permute-start(f32[34,258]{1,0:T(8,128)S(1)} %slice_bitcast_fusion.20), channel_id=1, source_target_pairs={{0,1},{1,2},{2,3},{4,5},{5,6},{6,7},{8,9},{9,10},{10,11},{12,13},{... | collective-permute-start | bytes 105272 | tf_op jit(solution)/shard_map/ppermute | solution.py:228
  78.1 3.6 %collective-permute-start.5 = (f32[34,258]{1,0:T(8,128)S(1)}, f32[34,258]{1,0:T(8,128)S(1)}, u32[]{:S(2)}, u32[]{:S(2)}) collective-permute-start(f32[34,258]{1,0:T(8,128)S(1)} %slice_bitcast_fusion.20), channel_id=1, source_target_pairs={{0,2},{1,3},{4,6},{5,7},{8,10},{9,11},{12,14},{13,15},{16,18},{17,... | collective-permute-start | bytes 105272 | tf_op jit(solution)/shard_map/ppermute | solution.py:228
  81.7 1.5 %collective-permute-start.6 = (f32[34,258]{1,0:T(8,128)S(1)}, f32[34,258]{1,0:T(8,128)S(1)}, u32[]{:S(2)}, u32[]{:S(2)}) collective-permute-start(f32[34,258]{1,0:T(8,128)S(1)} %slice_bitcast_fusion.20), channel_id=1, source_target_pairs={{0,3},{4,7},{8,11},{12,15},{16,19},{20,23},{24,27},{28,31},{32,35}... | collective-permute-start | bytes 105272 | tf_op jit(solution)/shard_map/ppermute | solution.py:228
  83.2 1.0 broadcast_maximum_fusion
  84.4 0.7 copy-done.8
  85.2 2.9 %multiply_subtract_fusion = f32[4,24,32,257]{3,2,1,0:T(8,128)S(1)} fusion(f32[4,24,34,1]{3,2,1,0:T(8,128)S(1)} %copy-done.2, f32[4,24,1,256]{3,2,1,0:T(1,128)S(1)} %collective-permute-done.1, f32[4,24,32,256]{3,2,1,0:T(8,128)S(1)} %copy-done, f32[4,24,1,256]{3,2,1,0:T(1,128)S(1)} %collective-permute-done, f32[4,24,34,1]{3,2,1,0:T(8,128)S(1)} %copy-done.1, ...), kind=kLoop, calls=%fused_computation.10 | loop fusion | flops 10263552 | bytes 8894976 | tf_op jit(solution)/shard_map/sub | solution.py:38
  88.1 3.1 %fusion = f32[4,24,32,256]{3,2,1,0:T(8,128)} fusion(f32[4,24,32,256]{3,2,1,0:T(8,128)S(1)} %copy-done, f32[4,24,32,257]{3,2,1,0:T(8,128)S(1)} %multiply_subtract_fusion, f32[4,24,33,256]{3,2,1,0:T(8,128)S(1)} %copy-done.5), kind=kLoop, calls=%fused_computation.15 | loop fusion | flops 3145728 | bytes 18874368 | tf_op jit(solution)/shard_map/sub | solution.py:42
  91.3 1.7 %subtract_multiply_fusion = f32[24,34,258]{2,1,0:T(8,128)S(1)} fusion(f32[24,34,258]{2,1,0:T(8,128)S(1)} %compare_select_fusion, f32[24,34,258]{2,1,0:T(8,128)} %copy-done.15, f32[34,258]{1,0:T(8,128)S(1)} %add_add_fusion), kind=kLoop, calls=%fused_computation.37 | loop fusion | flops 842112 | bytes 2561424 | tf_op jit(solution)/shard_map/mul | solution.py:229
  93.0 0.5 copy-done.12
  94.2 1.1 fusion.28
  97.0 1.7 %copy-done.6 = f32[4,24,32,256]{3,2,1,0:T(8,128)} copy-done((f32[4,24,32,256]{3,2,1,0:T(8,128)}, f32[4,24,32,256]{3,2,1,0:T(8,128)S(1)}, u32[]{:S(2)}) %copy-start.6) | copy-done | bytes 3145752
  98.6 5.6 %shard_map.47 = (f32[4,24,32,256]{3,2,1,0:T(8,128)}, f32[8,32,256]{2,1,0:T(8,128)}) custom-call(f32[4,24,32,256]{3,2,1,0:T(8,128)} %copy-done.6, f32[2,24,32,256]{3,2,1,0:T(8,128)} %broadcast_multiply_fusion.c_ref, f32[2,32,256]{2,1,0:T(8,128)} %multiply_select_fusion.ctop_ref, f32[2,24,32,256]{3,2,1,0:T(8,128)} %get-tuple-element.24.ratio_ref, ...), custom_call_target="tpu_custom_call" | custom-call | tf_op jit(solution)/shard_map/pallas_call | solution.py:146
  104.3 21.0 %all-gather.5.cloned.1.call-done = f32[32,32,256]{2,1,0:T(8,128)} async-done(((f32[8,32,256]{2,1,0:T(8,128)}), f32[32,32,256]{2,1,0:T(8,128)}) %all-gather.5.cloned.1.call-update) | async-done | bytes 1048592 | tf_op jit(solution)/shard_map/all_gather | solution.py:239
  125.3 1.6 %broadcast_in_dim.35 = f32[4,8,2,32,256]{4,3,2,1,0:T(8,128)S(1)} broadcast(f32[4,8,32,256]{3,2,1,0:T(8,128)} %bitcast.278), dimensions={0,1,3,4} | broadcast | bytes 3145728 | tf_op jit(solution)/shard_map/broadcast_in_dim | solution.py:160
  127.4 1.5 %copy-done.16 = f32[4,24,32,256]{3,2,1,0:T(8,128)S(1)} copy-done((f32[4,24,32,256]{3,2,1,0:T(8,128)S(1)}, f32[4,24,32,256]{3,2,1,0:T(8,128)}, u32[]{:S(2)}) %copy-start.16) | copy-done | bytes 3145752
  128.9 0.5 copy-done.18
  129.3 2.5 %fusion.1 = f32[4,24,32,256]{3,2,1,0:T(8,128)} fusion(f32[4,24,32,256]{3,2,1,0:T(8,128)S(1)} %copy-done.16, f32[2,24,32,256]{3,2,1,0:T(8,128)S(1)} %copy-done.19, f32[4,32,256]{2,1,0:T(8,128)S(1)} %select_select_fusion, f32[2,24,32,256]{3,2,1,0:T(8,128)S(1)} %copy-done.18, f32[4,32,256]{2,1,0:T(8,128)S(1)} %select_select_fusion.1), kind=kLoop, calls=%fused_computation.20 | loop fusion | flops 3145728 | bytes 9699328 | tf_op jit(solution)/shard_map/add | solution.py:243
  (80 shorter events, 4.6 us)
Async XLA Ops:
  6.5 97.8 %all-gather.7.cloned.1.call-start = ((), (), s32[]{:S(2)}) async-start(), calls=%async_computation.1 | async-start | bytes 1310720 | tf_op jit(solution)/shard_map/all_gather | solution.py:216
  8.7 28.3 %collective-permute-start.1 = (f32[4,24,1,256]{3,2,1,0:T(1,128)}, f32[4,24,1,256]{3,2,1,0:T(1,128)S(1)}, u32[]{:S(2)}, u32[]{:S(2)}) collective-permute-start(f32[4,24,1,256]{3,2,1,0:T(1,128)} %get-tuple-element.42), channel_id=1, source_target_pairs={{32,0},{64,32},{96,64},{0,96},{33,1},{65,33},{97,65},{1,97},{34,2}... | collective-permute-start | bytes 294920 | tf_op jit(solution)/shard_map/ppermute | solution.py:17
  9.7 27.3 %collective-permute-start = (f32[4,24,1,256]{3,2,1,0:T(1,128)S(1)}, f32[4,24,1,256]{3,2,1,0:T(1,128)S(1)}, u32[]{:S(2)}, u32[]{:S(2)}) collective-permute-start(f32[4,24,1,256]{3,2,1,0:T(1,128)S(1)} %get-tuple-element.41), channel_id=1, source_target_pairs={{0,32},{32,64},{64,96},{96,0},{1,33},{33,65},{65,97},{97,1},{2,34}... | collective-permute-start | bytes 294920 | tf_op jit(solution)/shard_map/ppermute | solution.py:16
  11.2 19.2 %collective-permute-start.7 = (f32[2,32,256]{2,1,0:T(8,128)}, f32[2,32,256]{2,1,0:T(8,128)}, u32[]{:S(2)}, u32[]{:S(2)}) collective-permute-start(f32[2,32,256]{2,1,0:T(8,128)} %slice_bitcast_fusion.19), channel_id=1, source_target_pairs={{0,1},{1,2},{2,3},{4,5},{5,6},{6,7},{8,9},{9,10},{10,11},{12,13},{... | collective-permute-start | bytes 196616 | tf_op jit(solution)/shard_map/ppermute | solution.py:206
  15.7 5.2 %copy-start.14 = (s32[128,2048]{1,0:T(8,128)S(1)}, s32[128,2048]{1,0:T(8,128)}, u32[]{:S(2)}) copy-start(s32[128,2048]{1,0:T(8,128)} %param.8) | copy-start | bytes 3145732
  23.6 1.1 copy-start.3
  26.2 10.8 %copy-start = (f32[4,24,32,256]{3,2,1,0:T(8,128)S(1)}, f32[4,24,32,256]{3,2,1,0:T(8,128)}, u32[]{:S(2)}) copy-start(f32[4,24,32,256]{3,2,1,0:T(8,128)} %param.6) | copy-start | bytes 9437188
  37.0 88.3 %all-gather.5.cloned.1.call-start = ((), (), s32[]{:S(2)}) async-start(), calls=%async_computation | async-start | bytes 1310720 | tf_op jit(solution)/shard_map/all_gather | solution.py:239
  42.6 19.0 %collective-permute-start.2 = (f32[4,24,34,1]{2,1,3,0:T(8,128)S(1)}, f32[4,24,34,1]{2,1,3,0:T(8,128)S(1)}, u32[]{:S(2)}, u32[]{:S(2)}) collective-permute-start(f32[4,24,34,1]{2,1,3,0:T(8,128)S(1)} %copy.13), channel_id=1, source_target_pairs={{0,4},{4,8},{8,12},{12,16},{16,20},{20,24},{24,28},{28,0},{1,5},{5... | collective-permute-start | bytes 39176 | tf_op jit(solution)/shard_map/ppermute | solution.py:16
  47.7 16.0 %collective-permute-start.3 = (f32[4,24,34,1]{2,1,3,0:T(8,128)S(1)}, f32[4,24,34,1]{2,1,3,0:T(8,128)}, u32[]{:S(2)}, u32[]{:S(2)}) collective-permute-start(f32[4,24,34,1]{2,1,3,0:T(8,128)S(1)} %copy.15), channel_id=1, source_target_pairs={{4,0},{8,4},{12,8},{16,12},{20,16},{24,20},{28,24},{0,28},{5,1},{9... | collective-permute-start | bytes 39176 | tf_op jit(solution)/shard_map/ppermute | solution.py:17
  56.2 0.9 copy-start.10
  56.2 2.5 %copy-start.7 = (f32[4,24,33,256]{3,2,1,0:T(8,128)S(1)}, f32[4,24,33,256]{3,2,1,0:T(8,128)}, u32[]{:S(2)}) copy-start(f32[4,24,33,256]{3,2,1,0:T(8,128)} %dynamic-update-slice.4) | copy-start | bytes 9732100
  66.6 16.5 %copy-start.2 = (f32[4,24,34,1]{3,2,1,0:T(8,128)S(1)}, f32[4,24,34,1]{3,2,1,0:T(8,128)}, u32[]{:S(2)}) copy-start(f32[4,24,34,1]{3,2,1,0:T(8,128)} %copy.16) | copy-start | bytes 39172
  66.6 16.5 %copy-start.4 = (f32[24,34,258]{2,1,0:T(8,128)S(1)}, f32[24,34,258]{2,1,0:T(8,128)}, u32[]{:S(2)}) copy-start(f32[24,34,258]{2,1,0:T(8,128)} %copy-done.3) | copy-start | bytes 2526340
  69.7 13.4 %copy-start.1 = (f32[4,24,34,1]{3,2,1,0:T(8,128)S(1)}, f32[4,24,34,1]{3,2,1,0:T(8,128)}, u32[]{:S(2)}) copy-start(f32[4,24,34,1]{3,2,1,0:T(8,128)} %copy.14) | copy-start | bytes 39172
  69.7 13.4 %copy-start.21 = (f32[257]{0:T(512)S(1)}, f32[257]{0:T(512)}, u32[]{:S(2)}) copy-start(f32[257]{0:T(512)} %fusion.51) | copy-start | bytes 3088
  74.8 6.8 %copy-start.15 = (f32[24,34,258]{2,1,0:T(8,128)}, f32[24,34,258]{2,1,0:T(8,128)S(1)}, u32[]{:S(2)}) copy-start(f32[24,34,258]{2,1,0:T(8,128)S(1)} %fusion.62) | copy-start | bytes 2526340
  74.8 16.4 %collective-permute-start.4 = (f32[34,258]{1,0:T(8,128)S(1)}, f32[34,258]{1,0:T(8,128)S(1)}, u32[]{:S(2)}, u32[]{:S(2)}) collective-permute-start(f32[34,258]{1,0:T(8,128)S(1)} %slice_bitcast_fusion.20), channel_id=1, source_target_pairs={{0,1},{1,2},{2,3},{4,5},{5,6},{6,7},{8,9},{9,10},{10,11},{12,13},{... | collective-permute-start | bytes 105272 | tf_op jit(solution)/shard_map/ppermute | solution.py:228
  78.1 13.1 %collective-permute-start.5 = (f32[34,258]{1,0:T(8,128)S(1)}, f32[34,258]{1,0:T(8,128)S(1)}, u32[]{:S(2)}, u32[]{:S(2)}) collective-permute-start(f32[34,258]{1,0:T(8,128)S(1)} %slice_bitcast_fusion.20), channel_id=1, source_target_pairs={{0,2},{1,3},{4,6},{5,7},{8,10},{9,11},{12,14},{13,15},{16,18},{17,... | collective-permute-start | bytes 105272 | tf_op jit(solution)/shard_map/ppermute | solution.py:228
  81.7 9.6 %collective-permute-start.6 = (f32[34,258]{1,0:T(8,128)S(1)}, f32[34,258]{1,0:T(8,128)S(1)}, u32[]{:S(2)}, u32[]{:S(2)}) collective-permute-start(f32[34,258]{1,0:T(8,128)S(1)} %slice_bitcast_fusion.20), channel_id=1, source_target_pairs={{0,3},{4,7},{8,11},{12,15},{16,19},{20,23},{24,27},{28,31},{32,35}... | collective-permute-start | bytes 105272 | tf_op jit(solution)/shard_map/ppermute | solution.py:228
  84.1 1.0 copy-start.8
  85.2 2.9 %copy-start.5 = (f32[4,24,33,256]{3,2,1,0:T(8,128)S(1)}, f32[4,24,33,256]{3,2,1,0:T(8,128)}, u32[]{:S(2)}) copy-start(f32[4,24,33,256]{3,2,1,0:T(8,128)} %multiply_subtract_fusion.1) | copy-start | bytes 9732100
  91.2 2.3 %copy-start.12 = (f32[4,24,32,256]{3,2,1,0:T(8,128)S(1)}, f32[4,24,32,256]{3,2,1,0:T(8,128)}, u32[]{:S(2)}) copy-start(f32[4,24,32,256]{3,2,1,0:T(8,128)} %fusion) | copy-start | bytes 9437188
  91.2 2.6 %copy-start.9 = (f32[24,32,257]{2,1,0:T(8,128)S(1)}, f32[24,32,257]{2,1,0:T(8,128)}, u32[]{:S(2)}) copy-start(f32[24,32,257]{2,1,0:T(8,128)} %copy-done.8) | copy-start | bytes 2368516
  91.3 2.9 %copy-start.11 = (f32[24,33,256]{2,1,0:T(8,128)S(1)}, f32[24,33,256]{2,1,0:T(8,128)}, u32[]{:S(2)}) copy-start(f32[24,33,256]{2,1,0:T(8,128)} %copy-done.10) | copy-start | bytes 2433028
  91.3 2.9 %copy-start.22 = (f32[256]{0:T(256)S(1)}, f32[256]{0:T(256)}, u32[]{:S(2)}) copy-start(f32[256]{0:T(256)} %add_multiply_fusion) | copy-start | bytes 3076
  94.2 1.4 %slice-start = ((f32[4,24,32,256]{3,2,1,0:T(8,128)}), f32[2,24,32,256]{3,2,1,0:T(8,128)S(1)}, s32[]{:S(2)}) async-start(f32[4,24,32,256]{3,2,1,0:T(8,128)} %fusion), calls=%async_computation.2 | async-start | bytes 3145728 | tf_op jit(solution)/shard_map/slice | solution.py:57
  94.2 1.6 %copy-start.13 = (f32[24,32,256]{2,1,0:T(8,128)S(1)}, f32[24,32,256]{2,1,0:T(8,128)}, u32[]{:S(2)}) copy-start(f32[24,32,256]{2,1,0:T(8,128)} %slice.323) | copy-start | bytes 2359300
  95.8 0.8 copy-start.20
  95.8 0.8 copy-start.23
  97.0 1.7 %copy-start.6 = (f32[4,24,32,256]{3,2,1,0:T(8,128)}, f32[4,24,32,256]{3,2,1,0:T(8,128)S(1)}, u32[]{:S(2)}) copy-start(f32[4,24,32,256]{3,2,1,0:T(8,128)S(1)} %fusion.3.f_ref) | copy-start | bytes 9437188
  125.3 1.6 %copy-start.17 = (f32[32,32,256]{2,1,0:T(8,128)S(1)}, f32[32,32,256]{2,1,0:T(8,128)}, u32[]{:S(2)}) copy-start(f32[32,32,256]{2,1,0:T(8,128)} %all-gather.5.cloned.1.call-done) | copy-start | bytes 3145732
  125.3 2.1 %copy-start.19 = (f32[2,24,32,256]{3,2,1,0:T(8,128)S(1)}, f32[2,24,32,256]{3,2,1,0:T(8,128)}, u32[]{:S(2)}) copy-start(f32[2,24,32,256]{3,2,1,0:T(8,128)} %get-tuple-element.30) | copy-start | bytes 4718596
  126.9 2.0 %copy-start.16 = (f32[4,24,32,256]{3,2,1,0:T(8,128)S(1)}, f32[4,24,32,256]{3,2,1,0:T(8,128)}, u32[]{:S(2)}) copy-start(f32[4,24,32,256]{3,2,1,0:T(8,128)} %get-tuple-element.26) | copy-start | bytes 9437188
  126.9 2.4 %copy-start.18 = (f32[2,24,32,256]{3,2,1,0:T(8,128)S(1)}, f32[2,24,32,256]{3,2,1,0:T(8,128)}, u32[]{:S(2)}) copy-start(f32[2,24,32,256]{3,2,1,0:T(8,128)} %get-tuple-element.29) | copy-start | bytes 4718596
Sparse Core Ops, SparseCore 0:
  37.1 25.6 all-gather.6
  104.4 20.8 all-gather.4

commit v3 on v2

--- a/solution.py
+++ b/solution.py
@@ -192,6 +192,20 @@
         if q <= peers - 2:
             below = jnp.where(place == q, tops[q + 1], below)
     return above, below
+
+
+def gather_by_permutes(part, axis, place, peers):
+    received = [part]
+    for hop in range(1, peers):
+        shift = [(i, (i + hop) % peers) for i in range(peers)]
+        received.append(lax.ppermute(part, axis, shift))
+    rows = []
+    for q in range(peers):
+        row = received[0]
+        for hop in range(1, peers):
+            row = jnp.where((place - hop) % peers == q, received[hop], row)
+        rows.append(row)
+    return jnp.stack(rows)
 
 
 def per_device(state, mixing, depth_levels, wind):
@@ -236,7 +250,7 @@
     top_level = (levels == 0).astype(jnp.float32)
     forced = forced.at[2:].add(wind[:, None] * top_level[None, :, None, None] * wet_inner[None])
     y, y_ends = field_solve(forced, coupling, ctop, ratio, inv)
-    y_all = lax.all_gather(y_ends, "gz")
+    y_all = gather_by_permutes(y_ends, "gz", place_z, peers_z)
     x_above, x_below = interface_values(y_all, uv_all, place_z, peers_z)
     u4 = jnp.repeat(u, 2, axis=0)
     v4 = jnp.repeat(v, 2, axis=0)

time: 139 us -> 134 us (0.964)
  waiting for transfers between devices: 21 us -> 11.7 us
  starting transfers between devices: 19.5 us -> 22.7 us
    all_gather x1 -> x0, waiting for transfers between devices: 21 us -> none  [per_device(): y_all = lax.all_gather(y_ends, 'gz')]
    ppermute x0 -> x3, waiting for transfers between devices: none -> 11.7 us  [gather_by_permutes(): received.append(lax.ppermute(part, axis, shift))]
    ppermute x0 -> x3, starting transfers between devices: none -> 3.24 us  [gather_by_permutes(): received.append(lax.ppermute(part, axis, shift))]
    unnamed x49 -> x47, local copies, waits for them, and re-layouts: 13.7 us -> 13.6 us
  transfers between devices with their start and end apart: 10 -> 12, of which waited for: 1 -> 1; matrix products, arithmetic and copies ran while one was open for 41% -> 43% of each run, Pallas kernels for 8% -> 8%
where the time goes in v3:
time: 134 us
  local copies, waits for them, and re-layouts  37.4 us (28%)
  other arithmetic  37.1 us (28%)
  starting transfers between devices  22.7 us (17%)
  between operations  13.9 us (10%)
  waiting for transfers between devices  11.7 us (9%)
  Pallas kernels  10.7 us (8%)
    unnamed x47, local copies, waits for them, and re-layouts  13.6 us
    ppermute x3, waiting for transfers between devices, gather_by_permutes(): received.append(lax.ppermute(part, axis, shift))  11.7 us
    ppermute x3, starting transfers between devices, per_device(): shallower = shallower + lax.ppermute(column_total, 'gz', pairs_z)  8.27 us
    slice x3, local copies, waits for them, and re-layouts, padded_2(): last = lax.slice_in_dim(array, length - width, length, axis=dim)  7.05 us
    pallas_call x1, Pallas kernels, field_solve(): pl.pallas_call(field_kernel, grid=(cols_x // bx,), in_specs=[fspec, cspec...  5.59 us
    pallas_call x1, Pallas kernels, coupling_solve(): pl.pallas_call(coupling_kernel, grid=(cols_x // bx,), in_specs=[cspec, _p...  5.08 us
    another operation x1, other arithmetic, per_device(): inclusive = jnp.cumsum(density_field, axis=0)  5.06 us
    ppermute x1, starting transfers between devices, per_device(): mix_above = lax.ppermute(mixing[:, lev_count - 1], 'gz', down_z)  4.43 us
  transfers between devices with their start and end apart: 12, of which 1 were waited for; matrix products, arithmetic and copies ran while one was open for 43% of the time, Pallas kernels for 8%

profile of v3, /device:TPU:0, one launch (start us, length us, event | category | flops | bytes accessed | tf_op | source)
XLA Modules:
  0.0 133.6 jit_solution(5018955216431456918)
XLA Ops:
  6.5 2.2 %fusion.61 = (f32[4,24,1,256]{3,2,1,0:T(1,128)S(1)}, f32[4,24,1,256]{3,2,1,0:T(1,128)}) fusion(f32[4,24,32,256]{3,2,1,0:T(8,128)} %param.6), kind=kLoop, calls=%fused_computation.168 | loop fusion | bytes 393216 | tf_op jit(solution)/shard_map/slice | solution.py:14
  8.7 1.0 collective-permute-start.1
  9.7 1.5 %slice_bitcast_fusion.19 = f32[2,32,256]{2,1,0:T(8,128)} fusion(f32[2,24,32,256]{3,2,1,0:T(8,128)} %param.7), kind=kLoop, calls=%fused_computation.126 | loop fusion | bytes 131072 | tf_op jit(solution)/shard_map/squeeze | solution.py:220
  11.2 4.4 %collective-permute-start.7 = (f32[2,32,256]{2,1,0:T(8,128)}, f32[2,32,256]{2,1,0:T(8,128)}, u32[]{:S(2)}, u32[]{:S(2)}) collective-permute-start(f32[2,32,256]{2,1,0:T(8,128)} %slice_bitcast_fusion.19), channel_id=1, source_target_pairs={{0,1},{1,2},{2,3},{4,5},{5,6},{6,7},{8,9},{9,10},{10,11},{12,13},{... | collective-permute-start | bytes 196616 | tf_op jit(solution)/shard_map/ppermute | solution.py:220
  15.7 4.1 %constant_dynamic-update-slice_fusion = f32[4,24,33,256]{3,2,1,0:T(8,128)} fusion(f32[4,24,32,256]{3,2,1,0:T(8,128)} %param.6), kind=kLoop, calls=%fused_computation.148 | loop fusion | bytes 6291456
  19.8 0.6 fusion.51
  20.4 0.6 add_multiply_fusion
  21.0 0.7 gather_fusion
  22.1 1.0 gather_fusion.1
  23.6 1.1 copy-done.3
  24.7 1.2 slice.329
  26.2 2.9 %broadcast_multiply_fusion.c_ref = f32[2,24,32,256]{3,2,1,0:T(8,128)} fusion(f32[2,24,32,256]{3,2,1,0:T(8,128)} %param.7, f32[24,32,256]{2,1,0:T(8,128)S(1)} %compare_select_fusion.1), kind=kLoop, calls=%fused_computation.72 | loop fusion | flops 393216 | bytes 3932160 | tf_op jit(solution)/shard_map/mul | solution.py:225
  29.1 0.8 fusion.46
  30.4 1.5 %multiply_select_fusion.ctop_ref = f32[2,32,256]{2,1,0:T(8,128)} fusion(f32[2,32,256]{2,1,0:T(8,128)} %collective-permute-done.7, f32[32,256]{1,0:T(8,128)S(1)} %fusion.46, pred[]{:T(512)S(6)} %gt.3), kind=kLoop, calls=%fused_computation.125 | loop fusion | flops 32768 | bytes 163841 | tf_op jit(solution)/shard_map/jit(_where)/select_n | solution.py:228
  31.9 5.1 %shard_map.46 = (f32[2,24,32,256]{3,2,1,0:T(8,128)}, f32[2,24,32,256]{3,2,1,0:T(8,128)}, f32[2,24,32,256]{3,2,1,0:T(8,128)}, f32[2,24,32,256]{3,2,1,0:T(8,128)}, f32[8,32,256]{2,1,0:T(8,128)}) custom-call(f32[2,24,32,256]{3,2,1,0:T(8,128)} %broadcast_multiply_fusion.c_ref, f32[2,32,256]{2,1,0:T(8,128)} %multiply_select_fusion.ctop_ref), custom_call_target="tpu_custom_call" | custom-call | tf_op jit(solution)/shard_map/pallas_call | solution.py:130
  37.0 0.7 pad_maximum_fusion.7
  37.7 2.6 %fusion.60 = (f32[4,24,34,1]{3,2,1,0:T(8,128)}, f32[4,24,34,1]{3,2,1,0:T(8,128)}) fusion(f32[4,24,34,256]{3,2,1,0:T(8,128)S(1)} %pad_maximum_fusion.7), kind=kLoop, calls=%fused_computation.167 | loop fusion | bytes 52224 | tf_op jit(solution)/shard_map/slice | solution.py:14
  40.3 2.3 %copy.13 = f32[4,24,34,1]{2,1,3,0:T(8,128)S(1)} copy(f32[4,24,34,1]{3,2,1,0:T(8,128)} %get-tuple-element.39) | data formatting | bytes 26112 | tf_op jit(solution)/shard_map/slice | solution.py:14
  42.6 2.8 %collective-permute-start.2 = (f32[4,24,34,1]{2,1,3,0:T(8,128)S(1)}, f32[4,24,34,1]{2,1,3,0:T(8,128)S(1)}, u32[]{:S(2)}, u32[]{:S(2)}) collective-permute-start(f32[4,24,34,1]{2,1,3,0:T(8,128)S(1)} %copy.13), channel_id=1, source_target_pairs={{0,4},{4,8},{8,12},{12,16},{16,20},{20,24},{24,28},{28,0},{1,5},{5... | collective-permute-start | bytes 39176 | tf_op jit(solution)/shard_map/ppermute | solution.py:16
  45.4 2.3 %copy.15 = f32[4,24,34,1]{2,1,3,0:T(8,128)S(1)} copy(f32[4,24,34,1]{3,2,1,0:T(8,128)} %get-tuple-element.40) | data formatting | bytes 26112 | tf_op jit(solution)/shard_map/slice | solution.py:15
  47.7 3.0 %collective-permute-start.3 = (f32[4,24,34,1]{2,1,3,0:T(8,128)S(1)}, f32[4,24,34,1]{2,1,3,0:T(8,128)}, u32[]{:S(2)}, u32[]{:S(2)}) collective-permute-start(f32[4,24,34,1]{2,1,3,0:T(8,128)S(1)} %copy.15), channel_id=1, source_target_pairs={{4,0},{8,4},{12,8},{16,12},{20,16},{24,20},{28,24},{0,28},{5,1},{9... | collective-permute-start | bytes 39176 | tf_op jit(solution)/shard_map/ppermute | solution.py:17
  50.7 2.8 %dynamic-update-slice.4 = f32[4,24,33,256]{3,2,1,0:T(8,128)} dynamic-update-slice(f32[4,24,33,256]{3,2,1,0:T(8,128)} %constant_dynamic-update-slice_fusion, f32[4,24,1,256]{3,2,1,0:T(1,128)S(1)} %collective-permute-done.1, s32[]{} %constant.206, s32[]{} %constant.206, s32[]{} %constant.207, s32[]{} %constant.206) | dynamic-update-slice | bytes 196612 | tf_op jit(solution)/shard_map/concatenate | solution.py:18
  53.4 2.7 %broadcast_maximum_fusion.1 = (f32[24,33,256]{2,1,0:T(8,128)S(1)}, f32[24,33,256]{2,1,0:T(8,128)S(1)}, f32[24,33,256]{2,1,0:T(8,128)S(1)}) fusion(f32[4,24,33,256]{3,2,1,0:T(8,128)} %dynamic-update-slice.4, f32[4,24,32,256]{3,2,1,0:T(8,128)S(1)} %copy-done, f32[4,24,1,256]{3,2,1,0:T(1,128)S(1)} %collective-permute-done, f32[24,34,258]{2,1,0:T(8,128)} %copy-done.3), kind=kLoop, calls=%fused_computation.80 | loop fusion | flops 1216512 | bytes 8110080 | tf_op jit(solution)/shard_map/max | solution.py:34
  56.4 0.7 copy-done.10
  57.1 1.6 %copy-done.7 = f32[4,24,33,256]{3,2,1,0:T(8,128)S(1)} copy-done((f32[4,24,33,256]{3,2,1,0:T(8,128)S(1)}, f32[4,24,33,256]{3,2,1,0:T(8,128)}, u32[]{:S(2)}) %copy-start.7) | copy-done | bytes 3244056
  58.7 2.9 %multiply_subtract_fusion.1 = f32[4,24,33,256]{3,2,1,0:T(8,128)} fusion(f32[4,24,33,256]{3,2,1,0:T(8,128)S(1)} %copy-done.7, f32[4,24,32,256]{3,2,1,0:T(8,128)S(1)} %copy-done, f32[4,24,1,256]{3,2,1,0:T(1,128)S(1)} %collective-permute-done, f32[24,33,256]{2,1,0:T(8,128)S(1)} %get-tuple-element.47, f32[24,33,256]{2,1,0:T(8,128)S(1)} %get-tuple-element.48, ...), kind=kLoop, calls=%fused_computation.13 | loop fusion | flops 6488064 | bytes 12165120 | tf_op jit(solution)/shard_map/sub | solution.py:33
  61.6 2.1 %copy.14 = f32[4,24,34,1]{3,2,1,0:T(8,128)} copy(f32[4,24,34,1]{2,1,3,0:T(8,128)S(1)} %collective-permute-done.2) | data formatting | bytes 26112 | tf_op jit(solution)/shard_map/ppermute | solution.py:16
  63.7 2.9 %copy.16 = f32[4,24,34,1]{3,2,1,0:T(8,128)} copy(f32[4,24,34,1]{2,1,3,0:T(8,128)} %collective-permute-done.3) | data formatting | bytes 26112 | tf_op jit(solution)/shard_map/ppermute | solution.py:17
  66.6 3.1 %compare_select_fusion = f32[24,34,258]{2,1,0:T(8,128)S(1)} fusion(f32[4,24,34,1]{3,2,1,0:T(8,128)} %copy.16, f32[4,24,34,1]{3,2,1,0:T(8,128)} %copy.14, f32[4,24,1,256]{3,2,1,0:T(1,128)S(1)} %collective-permute-done.1, f32[4,24,32,256]{3,2,1,0:T(8,128)S(1)} %copy-done, f32[4,24,1,256]{3,2,1,0:T(1,128)S(1)} %collective-permute-done, s32[34,258]{1,0:T(8,128)S(1)} %copy.12, ...), kind=kLoop, calls=%fused_computation.24 | loop fusion | flops 3368448 | bytes 4245744 | tf_op jit(solution)/shard_map/mul | solution.py:23
  69.7 5.1 %fusion.62 = f32[24,34,258]{2,1,0:T(8,128)S(1)} fusion(f32[24,34,258]{2,1,0:T(8,128)S(1)} %compare_select_fusion), kind=kOutput, calls=%fused_computation.169 | output fusion | flops 4842144 | bytes 1684224 | tf_op jit(solution)/shard_map/jit(cumsum)/reduce_window_sum | solution.py:237
  74.8 3.2 %collective-permute-start.4 = (f32[34,258]{1,0:T(8,128)S(1)}, f32[34,258]{1,0:T(8,128)S(1)}, u32[]{:S(2)}, u32[]{:S(2)}) collective-permute-start(f32[34,258]{1,0:T(8,128)S(1)} %slice_bitcast_fusion.20), channel_id=1, source_target_pairs={{0,1},{1,2},{2,3},{4,5},{5,6},{6,7},{8,9},{9,10},{10,11},{12,13},{... | collective-permute-start | bytes 105272 | tf_op jit(solution)/shard_map/ppermute | solution.py:242
  78.0 3.6 %collective-permute-start.5 = (f32[34,258]{1,0:T(8,128)S(1)}, f32[34,258]{1,0:T(8,128)S(1)}, u32[]{:S(2)}, u32[]{:S(2)}) collective-permute-start(f32[34,258]{1,0:T(8,128)S(1)} %slice_bitcast_fusion.20), channel_id=1, source_target_pairs={{0,2},{1,3},{4,6},{5,7},{8,10},{9,11},{12,14},{13,15},{16,18},{17,... | collective-permute-start | bytes 105272 | tf_op jit(solution)/shard_map/ppermute | solution.py:242
  81.6 1.5 %collective-permute-start.6 = (f32[34,258]{1,0:T(8,128)S(1)}, f32[34,258]{1,0:T(8,128)S(1)}, u32[]{:S(2)}, u32[]{:S(2)}) collective-permute-start(f32[34,258]{1,0:T(8,128)S(1)} %slice_bitcast_fusion.20), channel_id=1, source_target_pairs={{0,3},{4,7},{8,11},{12,15},{16,19},{20,23},{24,27},{28,31},{32,35}... | collective-permute-start | bytes 105272 | tf_op jit(solution)/shard_map/ppermute | solution.py:242
  83.2 1.0 broadcast_maximum_fusion
  84.4 0.7 copy-done.8
  85.1 2.9 %multiply_subtract_fusion = f32[4,24,32,257]{3,2,1,0:T(8,128)S(1)} fusion(f32[4,24,34,1]{3,2,1,0:T(8,128)S(1)} %copy-done.2, f32[4,24,1,256]{3,2,1,0:T(1,128)S(1)} %collective-permute-done.1, f32[4,24,32,256]{3,2,1,0:T(8,128)S(1)} %copy-done, f32[4,24,1,256]{3,2,1,0:T(1,128)S(1)} %collective-permute-done, f32[4,24,34,1]{3,2,1,0:T(8,128)S(1)} %copy-done.1, ...), kind=kLoop, calls=%fused_computation.10 | loop fusion | flops 10263552 | bytes 8894976 | tf_op jit(solution)/shard_map/sub | solution.py:38
  88.1 3.1 %fusion = f32[4,24,32,256]{3,2,1,0:T(8,128)} fusion(f32[4,24,32,256]{3,2,1,0:T(8,128)S(1)} %copy-done, f32[4,24,32,257]{3,2,1,0:T(8,128)S(1)} %multiply_subtract_fusion, f32[4,24,33,256]{3,2,1,0:T(8,128)S(1)} %copy-done.5), kind=kLoop, calls=%fused_computation.15 | loop fusion | flops 3145728 | bytes 18874368 | tf_op jit(solution)/shard_map/sub | solution.py:42
  91.2 1.7 %subtract_multiply_fusion = f32[24,34,258]{2,1,0:T(8,128)S(1)} fusion(f32[24,34,258]{2,1,0:T(8,128)S(1)} %compare_select_fusion, f32[24,34,258]{2,1,0:T(8,128)} %copy-done.15, f32[34,258]{1,0:T(8,128)S(1)} %add_add_fusion), kind=kLoop, calls=%fused_computation.37 | loop fusion | flops 842112 | bytes 2561424 | tf_op jit(solution)/shard_map/mul | solution.py:243
  93.0 0.5 copy-done.12
  94.1 1.1 fusion.28
  97.0 1.7 %copy-done.6 = f32[4,24,32,256]{3,2,1,0:T(8,128)} copy-done((f32[4,24,32,256]{3,2,1,0:T(8,128)}, f32[4,24,32,256]{3,2,1,0:T(8,128)S(1)}, u32[]{:S(2)}) %copy-start.6) | copy-done | bytes 3145752
  98.6 5.6 %shard_map.47 = (f32[4,24,32,256]{3,2,1,0:T(8,128)}, f32[8,32,256]{2,1,0:T(8,128)}) custom-call(f32[4,24,32,256]{3,2,1,0:T(8,128)} %copy-done.6, f32[2,24,32,256]{3,2,1,0:T(8,128)} %broadcast_multiply_fusion.c_ref, f32[2,32,256]{2,1,0:T(8,128)} %multiply_select_fusion.ctop_ref, f32[2,24,32,256]{3,2,1,0:T(8,128)} %get-tuple-element.24.ratio_ref, ...), custom_call_target="tpu_custom_call" | custom-call | tf_op jit(solution)/shard_map/pallas_call | solution.py:146
  104.2 3.2 %collective-permute-start.8 = (f32[8,32,256]{2,1,0:T(8,128)}, f32[8,32,256]{2,1,0:T(8,128)S(1)}, u32[]{:S(2)}, u32[]{:S(2)}) collective-permute-start(f32[8,32,256]{2,1,0:T(8,128)} %get-tuple-element.27), channel_id=1, source_target_pairs={{0,3},{1,0},{2,1},{3,2},{4,7},{5,4},{6,5},{7,6},{8,11},{9,8},{10,9... | collective-permute-start | bytes 786440 | tf_op jit(solution)/shard_map/ppermute | solution.py:201
  107.4 11.7 %collective-permute-done.10 = f32[8,32,256]{2,1,0:T(8,128)S(1)} collective-permute-done((f32[8,32,256]{2,1,0:T(8,128)}, f32[8,32,256]{2,1,0:T(8,128)S(1)}, u32[]{:S(2)}, u32[]{:S(2)}) %collective-permute-start.10) | collective-permute-done | bytes 262176 | tf_op jit(solution)/shard_map/ppermute | solution.py:201
  119.1 1.1 select_bitcast_fusion.2
  120.3 1.6 %broadcast_in_dim.35 = f32[4,8,2,32,256]{4,3,2,1,0:T(8,128)S(1)} broadcast(f32[4,8,32,256]{3,2,1,0:T(8,128)} %bitcast.283), dimensions={0,1,3,4} | broadcast | bytes 3145728 | tf_op jit(solution)/shard_map/broadcast_in_dim | solution.py:160
  122.4 1.4 %copy-done.16 = f32[4,24,32,256]{3,2,1,0:T(8,128)S(1)} copy-done((f32[4,24,32,256]{3,2,1,0:T(8,128)S(1)}, f32[4,24,32,256]{3,2,1,0:T(8,128)}, u32[]{:S(2)}) %copy-start.16) | copy-done | bytes 3145752
  124.2 2.5 %fusion.1 = f32[4,24,32,256]{3,2,1,0:T(8,128)} fusion(f32[4,24,32,256]{3,2,1,0:T(8,128)S(1)} %copy-done.16, f32[2,24,32,256]{3,2,1,0:T(8,128)S(1)} %copy-done.18, f32[4,32,256]{2,1,0:T(8,128)S(1)} %select_select_fusion, f32[2,24,32,256]{3,2,1,0:T(8,128)S(1)} %copy-done.17, f32[4,32,256]{2,1,0:T(8,128)S(1)} %select_select_fusion.1), kind=kLoop, calls=%fused_computation.20 | loop fusion | flops 3145728 | bytes 9699328 | tf_op jit(solution)/shard_map/add | solution.py:257
  (82 shorter events, 5.6 us)
Async XLA Ops:
  6.5 113.7 %all-gather.3.cloned.1.call-start = ((), (), s32[]{:S(2)}) async-start(), calls=%async_computation | async-start | bytes 1310720 | tf_op jit(solution)/shard_map/all_gather | solution.py:230
  8.7 28.3 %collective-permute-start.1 = (f32[4,24,1,256]{3,2,1,0:T(1,128)}, f32[4,24,1,256]{3,2,1,0:T(1,128)S(1)}, u32[]{:S(2)}, u32[]{:S(2)}) collective-permute-start(f32[4,24,1,256]{3,2,1,0:T(1,128)} %get-tuple-element.42), channel_id=1, source_target_pairs={{32,0},{64,32},{96,64},{0,96},{33,1},{65,33},{97,65},{1,97},{34,2}... | collective-permute-start | bytes 294920 | tf_op jit(solution)/shard_map/ppermute | solution.py:17
  9.7 27.3 %collective-permute-start = (f32[4,24,1,256]{3,2,1,0:T(1,128)S(1)}, f32[4,24,1,256]{3,2,1,0:T(1,128)S(1)}, u32[]{:S(2)}, u32[]{:S(2)}) collective-permute-start(f32[4,24,1,256]{3,2,1,0:T(1,128)S(1)} %get-tuple-element.41), channel_id=1, source_target_pairs={{0,32},{32,64},{64,96},{96,0},{1,33},{33,65},{65,97},{97,1},{2,34}... | collective-permute-start | bytes 294920 | tf_op jit(solution)/shard_map/ppermute | solution.py:16
  11.2 19.2 %collective-permute-start.7 = (f32[2,32,256]{2,1,0:T(8,128)}, f32[2,32,256]{2,1,0:T(8,128)}, u32[]{:S(2)}, u32[]{:S(2)}) collective-permute-start(f32[2,32,256]{2,1,0:T(8,128)} %slice_bitcast_fusion.19), channel_id=1, source_target_pairs={{0,1},{1,2},{2,3},{4,5},{5,6},{6,7},{8,9},{9,10},{10,11},{12,13},{... | collective-permute-start | bytes 196616 | tf_op jit(solution)/shard_map/ppermute | solution.py:220
  15.7 5.2 %copy-start.14 = (s32[128,2048]{1,0:T(8,128)S(1)}, s32[128,2048]{1,0:T(8,128)}, u32[]{:S(2)}) copy-start(s32[128,2048]{1,0:T(8,128)} %param.8) | copy-start | bytes 3145732
  23.6 1.1 copy-start.3
  26.2 10.8 %copy-start = (f32[4,24,32,256]{3,2,1,0:T(8,128)S(1)}, f32[4,24,32,256]{3,2,1,0:T(8,128)}, u32[]{:S(2)}) copy-start(f32[4,24,32,256]{3,2,1,0:T(8,128)} %param.6) | copy-start | bytes 9437188
  42.6 19.0 %collective-permute-start.2 = (f32[4,24,34,1]{2,1,3,0:T(8,128)S(1)}, f32[4,24,34,1]{2,1,3,0:T(8,128)S(1)}, u32[]{:S(2)}, u32[]{:S(2)}) collective-permute-start(f32[4,24,34,1]{2,1,3,0:T(8,128)S(1)} %copy.13), channel_id=1, source_target_pairs={{0,4},{4,8},{8,12},{12,16},{16,20},{20,24},{24,28},{28,0},{1,5},{5... | collective-permute-start | bytes 39176 | tf_op jit(solution)/shard_map/ppermute | solution.py:16
  47.7 16.0 %collective-permute-start.3 = (f32[4,24,34,1]{2,1,3,0:T(8,128)S(1)}, f32[4,24,34,1]{2,1,3,0:T(8,128)}, u32[]{:S(2)}, u32[]{:S(2)}) collective-permute-start(f32[4,24,34,1]{2,1,3,0:T(8,128)S(1)} %copy.15), channel_id=1, source_target_pairs={{4,0},{8,4},{12,8},{16,12},{20,16},{24,20},{28,24},{0,28},{5,1},{9... | collective-permute-start | bytes 39176 | tf_op jit(solution)/shard_map/ppermute | solution.py:17
  56.2 0.9 copy-start.10
  56.2 2.5 %copy-start.7 = (f32[4,24,33,256]{3,2,1,0:T(8,128)S(1)}, f32[4,24,33,256]{3,2,1,0:T(8,128)}, u32[]{:S(2)}) copy-start(f32[4,24,33,256]{3,2,1,0:T(8,128)} %dynamic-update-slice.4) | copy-start | bytes 9732100
  66.6 16.5 %copy-start.2 = (f32[4,24,34,1]{3,2,1,0:T(8,128)S(1)}, f32[4,24,34,1]{3,2,1,0:T(8,128)}, u32[]{:S(2)}) copy-start(f32[4,24,34,1]{3,2,1,0:T(8,128)} %copy.16) | copy-start | bytes 39172
  66.6 16.5 %copy-start.4 = (f32[24,34,258]{2,1,0:T(8,128)S(1)}, f32[24,34,258]{2,1,0:T(8,128)}, u32[]{:S(2)}) copy-start(f32[24,34,258]{2,1,0:T(8,128)} %copy-done.3) | copy-start | bytes 2526340
  69.7 13.4 %copy-start.1 = (f32[4,24,34,1]{3,2,1,0:T(8,128)S(1)}, f32[4,24,34,1]{3,2,1,0:T(8,128)}, u32[]{:S(2)}) copy-start(f32[4,24,34,1]{3,2,1,0:T(8,128)} %copy.14) | copy-start | bytes 39172
  69.7 13.4 %copy-start.20 = (f32[257]{0:T(512)S(1)}, f32[257]{0:T(512)}, u32[]{:S(2)}) copy-start(f32[257]{0:T(512)} %fusion.51) | copy-start | bytes 3088
  74.8 6.8 %copy-start.15 = (f32[24,34,258]{2,1,0:T(8,128)}, f32[24,34,258]{2,1,0:T(8,128)S(1)}, u32[]{:S(2)}) copy-start(f32[24,34,258]{2,1,0:T(8,128)S(1)} %fusion.62) | copy-start | bytes 2526340
  74.8 16.4 %collective-permute-start.4 = (f32[34,258]{1,0:T(8,128)S(1)}, f32[34,258]{1,0:T(8,128)S(1)}, u32[]{:S(2)}, u32[]{:S(2)}) collective-permute-start(f32[34,258]{1,0:T(8,128)S(1)} %slice_bitcast_fusion.20), channel_id=1, source_target_pairs={{0,1},{1,2},{2,3},{4,5},{5,6},{6,7},{8,9},{9,10},{10,11},{12,13},{... | collective-permute-start | bytes 105272 | tf_op jit(solution)/shard_map/ppermute | solution.py:242
  78.0 13.1 %collective-permute-start.5 = (f32[34,258]{1,0:T(8,128)S(1)}, f32[34,258]{1,0:T(8,128)S(1)}, u32[]{:S(2)}, u32[]{:S(2)}) collective-permute-start(f32[34,258]{1,0:T(8,128)S(1)} %slice_bitcast_fusion.20), channel_id=1, source_target_pairs={{0,2},{1,3},{4,6},{5,7},{8,10},{9,11},{12,14},{13,15},{16,18},{17,... | collective-permute-start | bytes 105272 | tf_op jit(solution)/shard_map/ppermute | solution.py:242
  81.6 9.6 %collective-permute-start.6 = (f32[34,258]{1,0:T(8,128)S(1)}, f32[34,258]{1,0:T(8,128)S(1)}, u32[]{:S(2)}, u32[]{:S(2)}) collective-permute-start(f32[34,258]{1,0:T(8,128)S(1)} %slice_bitcast_fusion.20), channel_id=1, source_target_pairs={{0,3},{4,7},{8,11},{12,15},{16,19},{20,23},{24,27},{28,31},{32,35}... | collective-permute-start | bytes 105272 | tf_op jit(solution)/shard_map/ppermute | solution.py:242
  84.1 1.0 copy-start.8
  85.1 2.9 %copy-start.5 = (f32[4,24,33,256]{3,2,1,0:T(8,128)S(1)}, f32[4,24,33,256]{3,2,1,0:T(8,128)}, u32[]{:S(2)}) copy-start(f32[4,24,33,256]{3,2,1,0:T(8,128)} %multiply_subtract_fusion.1) | copy-start | bytes 9732100
  91.2 2.3 %copy-start.12 = (f32[4,24,32,256]{3,2,1,0:T(8,128)S(1)}, f32[4,24,32,256]{3,2,1,0:T(8,128)}, u32[]{:S(2)}) copy-start(f32[4,24,32,256]{3,2,1,0:T(8,128)} %fusion) | copy-start | bytes 9437188
  91.2 2.6 %copy-start.9 = (f32[24,32,257]{2,1,0:T(8,128)S(1)}, f32[24,32,257]{2,1,0:T(8,128)}, u32[]{:S(2)}) copy-start(f32[24,32,257]{2,1,0:T(8,128)} %copy-done.8) | copy-start | bytes 2368516
  91.2 2.9 %copy-start.11 = (f32[24,33,256]{2,1,0:T(8,128)S(1)}, f32[24,33,256]{2,1,0:T(8,128)}, u32[]{:S(2)}) copy-start(f32[24,33,256]{2,1,0:T(8,128)} %copy-done.10) | copy-start | bytes 2433028
  91.2 2.9 %copy-start.21 = (f32[256]{0:T(256)S(1)}, f32[256]{0:T(256)}, u32[]{:S(2)}) copy-start(f32[256]{0:T(256)} %add_multiply_fusion) | copy-start | bytes 3076
  94.1 1.4 %slice-start = ((f32[4,24,32,256]{3,2,1,0:T(8,128)}), f32[2,24,32,256]{3,2,1,0:T(8,128)S(1)}, s32[]{:S(2)}) async-start(f32[4,24,32,256]{3,2,1,0:T(8,128)} %fusion), calls=%async_computation.1 | async-start | bytes 3145728 | tf_op jit(solution)/shard_map/slice | solution.py:57
  94.1 1.6 %copy-start.13 = (f32[24,32,256]{2,1,0:T(8,128)S(1)}, f32[24,32,256]{2,1,0:T(8,128)}, u32[]{:S(2)}) copy-start(f32[24,32,256]{2,1,0:T(8,128)} %slice.329) | copy-start | bytes 2359300
  95.7 0.8 copy-start.19
  95.7 0.8 copy-start.22
  96.9 1.7 %copy-start.6 = (f32[4,24,32,256]{3,2,1,0:T(8,128)}, f32[4,24,32,256]{3,2,1,0:T(8,128)S(1)}, u32[]{:S(2)}) copy-start(f32[4,24,32,256]{3,2,1,0:T(8,128)S(1)} %fusion.3.f_ref) | copy-start | bytes 9437188
  104.2 14.9 %collective-permute-start.10 = (f32[8,32,256]{2,1,0:T(8,128)}, f32[8,32,256]{2,1,0:T(8,128)S(1)}, u32[]{:S(2)}, u32[]{:S(2)}) collective-permute-start(f32[8,32,256]{2,1,0:T(8,128)} %get-tuple-element.27), channel_id=1, source_target_pairs={{0,1},{1,2},{2,3},{3,0},{4,5},{5,6},{6,7},{7,4},{8,9},{9,10},{10,1... | collective-permute-start | bytes 786440 | tf_op jit(solution)/shard_map/ppermute | solution.py:201
  104.2 14.9 %collective-permute-start.8 = (f32[8,32,256]{2,1,0:T(8,128)}, f32[8,32,256]{2,1,0:T(8,128)S(1)}, u32[]{:S(2)}, u32[]{:S(2)}) collective-permute-start(f32[8,32,256]{2,1,0:T(8,128)} %get-tuple-element.27), channel_id=1, source_target_pairs={{0,3},{1,0},{2,1},{3,2},{4,7},{5,4},{6,5},{7,6},{8,11},{9,8},{10,9... | collective-permute-start | bytes 786440 | tf_op jit(solution)/shard_map/ppermute | solution.py:201
  107.4 11.7 %collective-permute-start.9 = (f32[8,32,256]{2,1,0:T(8,128)}, f32[8,32,256]{2,1,0:T(8,128)S(1)}, u32[]{:S(2)}, u32[]{:S(2)}) collective-permute-start(f32[8,32,256]{2,1,0:T(8,128)} %get-tuple-element.27), channel_id=1, source_target_pairs={{0,2},{1,3},{2,0},{3,1},{4,6},{5,7},{6,4},{7,5},{8,10},{9,11},{10,... | collective-permute-start | bytes 786440 | tf_op jit(solution)/shard_map/ppermute | solution.py:201
  120.3 2.1 %copy-start.18 = (f32[2,24,32,256]{3,2,1,0:T(8,128)S(1)}, f32[2,24,32,256]{3,2,1,0:T(8,128)}, u32[]{:S(2)}) copy-start(f32[2,24,32,256]{3,2,1,0:T(8,128)} %get-tuple-element.30) | copy-start | bytes 4718596
  121.9 1.9 %copy-start.16 = (f32[4,24,32,256]{3,2,1,0:T(8,128)S(1)}, f32[4,24,32,256]{3,2,1,0:T(8,128)}, u32[]{:S(2)}) copy-start(f32[4,24,32,256]{3,2,1,0:T(8,128)} %get-tuple-element.26) | copy-start | bytes 9437188
  121.9 2.4 %copy-start.17 = (f32[2,24,32,256]{3,2,1,0:T(8,128)S(1)}, f32[2,24,32,256]{3,2,1,0:T(8,128)}, u32[]{:S(2)}) copy-start(f32[2,24,32,256]{3,2,1,0:T(8,128)} %get-tuple-element.29) | copy-start | bytes 4718596
Sparse Core Ops, SparseCore 0:
  37.1 25.6 all-gather.2

commit v4 on v3

--- a/solution.py
+++ b/solution.py
@@ -208,48 +208,227 @@
     return jnp.stack(rows)
 
 
+def _density(t, s, w):
+    return (-0.3 * t + 0.7 * s - 0.05 * t * t) * w
+
+
+def _flux(vel, lo, hi, w):
+    return 0.25 * (jnp.maximum(vel, 0.0) * lo + jnp.minimum(vel, 0.0) * hi) - 0.08 * w * (hi - lo)
+
+
+def fused_kernel(st_ref, xw_ref, xe_ref, ys_ref, yn_ref,
+                 dc_ref, de_ref, dw_ref, dn_ref, ds_ref,
+                 dxw_ref, dxe_ref, dys_ref, dyn_ref,
+                 sc_ref, sxw_ref, sxe_ref, sys_ref, syn_ref,
+                 lane_ref, wind_ref, c_ref, inv_ref, ratio_ref,
+                 y_ref, ends_ref):
+    fields, levels, nx, ny = st_ref.shape
+    row = lax.broadcasted_iota(jnp.int32, (nx, ny), 0)
+    lane = lax.broadcasted_iota(jnp.int32, (nx, ny), 1)
+    wall_n = lane_ref[0:1]
+    wall_s = lane_ref[1:2]
+    cor03 = lane_ref[2:3]
+    d_c, d_e, d_w, d_n, d_s = dc_ref[...], de_ref[...], dw_ref[...], dn_ref[...], ds_ref[...]
+    d_xw, d_xe, d_ys, d_yn = dxw_ref[...], dxe_ref[...], dys_ref[...], dyn_ref[...]
+
+    def east(r, h):
+        return jnp.where(row == nx - 1, h, pltpu.roll(r, nx - 1, 0))
+
+    def west(r, h):
+        return jnp.where(row == 0, h, pltpu.roll(r, 1, 0))
+
+    def north(r, h):
+        return jnp.where(lane == ny - 1, h, pltpu.roll(r, ny - 1, 1))
+
+    def south(r, h):
+        return jnp.where(lane == 0, h, pltpu.roll(r, 1, 1))
+
+    def level(k, run, vy_prev):
+        wc = (k < d_c).astype(jnp.float32)
+        we = (k < d_e).astype(jnp.float32)
+        ww = (k < d_w).astype(jnp.float32)
+        wn = (k < d_n).astype(jnp.float32)
+        ws = (k < d_s).astype(jnp.float32)
+        wxw = (k < d_xw).astype(jnp.float32)
+        wxe = (k < d_xe).astype(jnp.float32)
+        wys = (k < d_ys).astype(jnp.float32)
+        wyn = (k < d_yn).astype(jnp.float32)
+        cen = [st_ref[f, k] for f in range(fields)]
+        hxw = [xw_ref[f, k] for f in range(fields)]
+        hxe = [xe_ref[f, k] for f in range(fields)]
+        hys = [ys_ref[f, k] for f in range(fields)]
+        hyn = [yn_ref[f, k] for f in range(fields)]
+        run_c, run_xw, run_xe, run_ys, run_yn = run
+        den_c = _density(cen[0], cen[1], wc)
+        den_xw = _density(hxw[0], hxw[1], wxw)
+        den_xe = _density(hxe[0], hxe[1], wxe)
+        den_ys = _density(hys[0], hys[1], wys)
+        den_yn = _density(hyn[0], hyn[1], wyn)
+        run_c = run_c + den_c
+        run_xw = run_xw + den_xw
+        run_xe = run_xe + den_xe
+        run_ys = run_ys + den_ys
+        run_yn = run_yn + den_yn
+        p_c = 0.03 * (sc_ref[...] + run_c - 0.5 * den_c)
+        p_xw = 0.03 * (sxw_ref[...] + run_xw - 0.5 * den_xw)
+        p_xe = 0.03 * (sxe_ref[...] + run_xe - 0.5 * den_xe)
+        p_ys = 0.03 * (sys_ref[...] + run_ys - 0.5 * den_ys)
+        p_yn = 0.03 * (syn_ref[...] + run_yn - 0.5 * den_yn)
+        p_e = east(p_c, p_xe)
+        p_w = west(p_c, p_xw)
+        p_n = north(p_c, p_yn)
+        p_s = south(p_c, p_ys)
+        face_e = wc * we
+        face_w = ww * wc
+        face_n = wc * wn * wall_n
+        face_s = ws * wc * wall_s
+        nbr_e = [east(cen[f], hxe[f]) for f in range(fields)]
+        nbr_w = [west(cen[f], hxw[f]) for f in range(fields)]
+        nbr_n = [north(cen[f], hyn[f]) for f in range(fields)]
+        nbr_s = [south(cen[f], hys[f]) for f in range(fields)]
+        vel_e = 0.5 * (cen[2] + nbr_e[2]) * face_e
+        vel_w = 0.5 * (nbr_w[2] + cen[2]) * face_w
+        vel_n = 0.5 * (cen[3] + nbr_n[3]) * face_n
+        vel_s = 0.5 * (nbr_s[3] + cen[3]) * face_s
+        moved = []
+        for f in range(fields):
+            fe = _flux(vel_e, cen[f], nbr_e[f], face_e)
+            fw = _flux(vel_w, nbr_w[f], cen[f], face_w)
+            fn = _flux(vel_n, cen[f], nbr_n[f], face_n)
+            fs = _flux(vel_s, nbr_s[f], cen[f], face_s)
+            moved.append(cen[f] - (fe - fw + fn - fs))
+        grad_x = 0.5 * (face_e * (p_e - p_c) + face_w * (p_c - p_w))
+        grad_y = 0.5 * (face_n * (p_n - p_c) + face_s * (p_c - p_s))
+        east_new = moved[2] + cor03 * cen[3] - grad_x
+        north_new = moved[3] - cor03 * cen[2] - grad_y
+        forced = [moved[0] * wc, moved[1] * wc, east_new * wc, north_new * wc]
+        if isinstance(k, int) and k == 0:
+            forced[2] = forced[2] + wind_ref[0] * wc
+            forced[3] = forced[3] + wind_ref[1] * wc
+        vy = []
+        for f in range(fields):
+            m = f // 2
+            inv = inv_ref[m, k]
+            if vy_prev is None:
+                val = forced[f] * inv
+            else:
+                val = (forced[f] + c_ref[m, k - 1] * vy_prev[f]) * inv
+            y_ref[f, k] = val
+            vy.append(val)
+        return (run_c, run_xw, run_xe, run_ys, run_yn), vy
+
+    run0 = (jnp.zeros((nx, ny), jnp.float32), jnp.zeros((1, ny), jnp.float32),
+            jnp.zeros((1, ny), jnp.float32), jnp.zeros((nx, 1), jnp.float32),
+            jnp.zeros((nx, 1), jnp.float32))
+    run, vy = level(0, run0, None)
+
+    def step(k, carry):
+        run, vy = carry
+        run, vy = level(k, run, vy)
+        return run, vy
+
+    run, vy = lax.fori_loop(1, levels, step, (run, vy), unroll=2)
+    for f in range(fields):
+        ends_ref[fields + f] = vy[f]
+
+    def back(j, later):
+        k = levels - 2 - j
+        out = []
+        for f in range(fields):
+            val = y_ref[f, k] + ratio_ref[f // 2, k] * later[f]
+            y_ref[f, k] = val
+            out.append(val)
+        return out
+
+    later = lax.fori_loop(0, levels - 1, back, vy, unroll=2)
+    for f in range(fields):
+        ends_ref[f] = later[f]
+
+
+def fused_solve(*operands):
+    st = operands[0]
+    fields, levels, nx, ny = st.shape
+    vmem = pl.BlockSpec(memory_space=pltpu.VMEM)
+    return pl.pallas_call(
+        fused_kernel,
+        in_specs=[vmem] * len(operands),
+        out_specs=[vmem, vmem],
+        out_shape=[jax.ShapeDtypeStruct(st.shape, jnp.float32),
+                   jax.ShapeDtypeStruct((2 * fields, nx, ny), jnp.float32)],
+        compiler_params=pltpu.CompilerParams(vmem_limit_bytes=60 * 1024 * 1024),
+    )(*operands)
+
+
 def per_device(state, mixing, depth_levels, wind):
     fields, lev_count, col_x, col_y = state.shape
     total_x, total_y = depth_levels.shape
     peers_z = lax.axis_size("gz")
     place_z = lax.axis_index("gz")
+    peers_x = lax.axis_size("gx")
+    peers_y = lax.axis_size("gy")
     start_x = lax.axis_index("gx") * col_x
     start_y = lax.axis_index("gy") * col_y
     start_z = place_z * lev_count
     down_z = [(i, i + 1) for i in range(peers_z - 1)]
     mix_above = lax.ppermute(mixing[:, lev_count - 1], "gz", down_z)
+    up_x = [(i, (i + 1) % peers_x) for i in range(peers_x)]
+    dn_x = [(j, i) for i, j in up_x]
+    up_y = [(i, (i + 1) % peers_y) for i in range(peers_y)]
+    dn_y = [(j, i) for i, j in up_y]
+    halo_xw = lax.ppermute(state[:, :, col_x - 1:], "gx", up_x)
+    halo_xe = lax.ppermute(state[:, :, :1], "gx", dn_x)
+    halo_ys = lax.ppermute(state[:, :, :, col_y - 1:], "gy", up_y)
+    halo_yn = lax.ppermute(state[:, :, :, :1], "gy", dn_y)
     levels = start_z + jnp.arange(lev_count, dtype=jnp.int32)
-    depth_inner = lax.dynamic_slice(depth_levels, (start_x, start_y), (col_x, col_y))
-    wet_here = (levels[:, None, None] < depth_inner[None]).astype(jnp.float32)
-    wet_next = ((levels + 1)[:, None, None] < depth_inner[None]).astype(jnp.float32)
+    row_index = (start_x - 1 + jnp.arange(col_x + 2, dtype=jnp.int32)) % total_x
+    col_index = (start_y - 1 + jnp.arange(col_y + 2, dtype=jnp.int32)) % total_y
+    depth_pad = jnp.take(jnp.take(depth_levels, row_index, axis=0), col_index, axis=1) - start_z
+    d_c = depth_pad[1:-1, 1:-1]
+    d_e = depth_pad[2:, 1:-1]
+    d_w = depth_pad[:-2, 1:-1]
+    d_n = depth_pad[1:-1, 2:]
+    d_s = depth_pad[1:-1, :-2]
+    d_xw = depth_pad[0:1, 1:-1]
+    d_xe = depth_pad[col_x + 1:, 1:-1]
+    d_ys = depth_pad[1:-1, 0:1]
+    d_yn = depth_pad[1:-1, col_y + 1:]
+    local = jnp.arange(lev_count, dtype=jnp.int32)
+    wet_here = (local[:, None, None] < d_c[None]).astype(jnp.float32)
+    wet_next = ((local + 1)[:, None, None] < d_c[None]).astype(jnp.float32)
     coupling = mixing * (wet_here * wet_next)[None]
-    wet_up = ((start_z - 1) < depth_inner).astype(jnp.float32)
+    wet_up = (-1 < d_c).astype(jnp.float32)
     ctop = mix_above * (wet_up * wet_here[0])[None]
     ctop = jnp.where(place_z > 0, ctop, 0.0)
     ratio, inv, u, v, uv_ends = coupling_solve(coupling, ctop)
     uv_all = lax.all_gather(uv_ends, "gz")
-    padded = padded_2(state, (("gx", 2), ("gy", 3)), 1)
-    row_index = (start_x - 1 + jnp.arange(col_x + 2, dtype=jnp.int32)) % total_x
-    col_index = (start_y - 1 + jnp.arange(col_y + 2, dtype=jnp.int32)) % total_y
-    depth_pad = jnp.take(jnp.take(depth_levels, row_index, axis=0), col_index, axis=1)
-    wet_pad = (levels[:, None, None] < depth_pad[None]).astype(jnp.float32)
-    density_field = density_of(padded, wet_pad)
-    inclusive = jnp.cumsum(density_field, axis=0)
-    column_total = inclusive[-1]
-    shallower = jnp.zeros_like(column_total)
+    lev3 = local[:, None, None]
+    tot_c = jnp.sum(density_of(state, (lev3 < d_c[None]).astype(jnp.float32)), axis=0)
+    tot_xw = jnp.sum(density_of(halo_xw, (lev3 < d_xw[None]).astype(jnp.float32)), axis=0)
+    tot_xe = jnp.sum(density_of(halo_xe, (lev3 < d_xe[None]).astype(jnp.float32)), axis=0)
+    tot_ys = jnp.sum(density_of(halo_ys, (lev3 < d_ys[None]).astype(jnp.float32)), axis=0)
+    tot_yn = jnp.sum(density_of(halo_yn, (lev3 < d_yn[None]).astype(jnp.float32)), axis=0)
+    side = jnp.zeros((2, col_y), jnp.float32)
+    side = side.at[0, :col_x].set(tot_ys[:, 0]).at[1, :col_x].set(tot_yn[:, 0])
+    pack = jnp.concatenate([tot_c, tot_xw, tot_xe, side], axis=0)
+    shallower = jnp.zeros_like(pack)
     for hop in range(1, peers_z):
         pairs_z = [(i, i + hop) for i in range(peers_z - hop)]
-        shallower = shallower + lax.ppermute(column_total, "gz", pairs_z)
-    pressure = 0.03 * (shallower[None] + inclusive - 0.5 * density_field)
-    face_row = start_y - 1 + jnp.arange(col_y + 1, dtype=jnp.int32)
-    wall_face = ((face_row >= 0) & (face_row <= total_y - 2)).astype(jnp.float32)
-    row_global = start_y + jnp.arange(col_y, dtype=jnp.int32)
-    coriolis = 0.5 + (row_global.astype(jnp.float32) + 0.5) / total_y
-    forced = advance(padded, wet_pad, pressure, wall_face, coriolis)
-    wet_inner = wet_pad[:, 1:-1, 1:-1]
-    top_level = (levels == 0).astype(jnp.float32)
-    forced = forced.at[2:].add(wind[:, None] * top_level[None, :, None, None] * wet_inner[None])
-    y, y_ends = field_solve(forced, coupling, ctop, ratio, inv)
+        shallower = shallower + lax.ppermute(pack, "gz", pairs_z)
+    s_c = shallower[:col_x]
+    s_xw = shallower[col_x:col_x + 1]
+    s_xe = shallower[col_x + 1:col_x + 2]
+    s_ys = shallower[col_x + 2, :col_x][:, None]
+    s_yn = shallower[col_x + 3, :col_x][:, None]
+    face_row = start_y + jnp.arange(col_y, dtype=jnp.int32)
+    wall_n = (face_row <= total_y - 2).astype(jnp.float32)
+    wall_s = (face_row - 1 >= 0).astype(jnp.float32)
+    coriolis = 0.5 + (face_row.astype(jnp.float32) + 0.5) / total_y
+    lanes = jnp.stack([wall_n, wall_s, 0.3 * coriolis] + [jnp.zeros_like(wall_n)] * 5)
+    wind_top = jnp.where(place_z == 0, wind, 0.0)
+    y, y_ends = fused_solve(state, halo_xw, halo_xe, halo_ys, halo_yn,
+                            d_c, d_e, d_w, d_n, d_s, d_xw, d_xe, d_ys, d_yn,
+                            s_c, s_xw, s_xe, s_ys, s_yn, lanes, wind_top,
+                            coupling, inv, ratio)
     y_all = gather_by_permutes(y_ends, "gz", place_z, peers_z)
     x_above, x_below = interface_values(y_all, uv_all, place_z, peers_z)
     u4 = jnp.repeat(u, 2, axis=0)

time: 134 us -> 102 us (0.76)
  other arithmetic: 37.1 us -> 8.97 us
  local copies, waits for them, and re-layouts: 37.4 us -> 23 us
  Pallas kernels: 10.7 us -> 20.2 us
    pallas_call x1, Pallas kernels: 5.59 us -> 15.1 us  [fused_solve(): pl.pallas_call(fused_kernel, in_specs=[vmem] * len(operands), out_specs=[...]
    unnamed x47 -> x24, local copies, waits for them, and re-layouts: 13.6 us -> 4.56 us
    sub x3 -> x1, other arithmetic: 8.93 us -> 0.02 us  [per_device(): jnp.take(jnp.take(depth_levels, row_index, axis=0), col_index, axis=1)]
    mul x6 -> x1, other arithmetic: 6.21 us -> 0.01 us  [per_device(): 0.3 * coriolis]
    another operation x2 -> x0, other arithmetic: 6.16 us -> none  [the longest x1 5.06 us: per_device(): inclusive = jnp.cumsum(density_field, axis=0)]
    max x2 -> x0, other arithmetic: 3.71 us -> none  [the longest x1 2.74 us: advance(): jnp.maximum(east_vel, 0.0) * west_side]
    slice x7, local copies, waits for them, and re-layouts: 10.9 us -> 7.99 us  [the longest x1 3.7 us: per_device(): halo_yn = lax.ppermute(state[:, :, :, :1], 'gy', dn_y)]
    concatenate x1 -> x0, local copies, waits for them, and re-layouts: 2.77 us -> none  [padded_2(): array = jnp.concatenate([before, array, after], axis=dim)]
  transfers between devices with their start and end apart: 12 -> 12, of which waited for: 1 -> 1; matrix products, arithmetic and copies ran while one was open for 43% -> 20% of each run, Pallas kernels for 8% -> 20%
where the time goes in v4:
time: 102 us; the launch traced here: 101 us
  local copies, waits for them, and re-layouts  23 us (23%)
  starting transfers between devices  22.2 us (22%)
  Pallas kernels  20.2 us (20%)
  between operations  13.7 us (13%)
  waiting for transfers between devices  12.7 us (12%)
  other arithmetic  8.97 us (9%)
    pallas_call x1, Pallas kernels, fused_solve(): pl.pallas_call(fused_kernel, in_specs=[vmem] * len(operands), out_specs=[...  15.1 us
    ppermute x3, waiting for transfers between devices, gather_by_permutes(): received.append(lax.ppermute(part, axis, shift))  12.6 us
    ppermute x3, starting transfers between devices, per_device(): shallower = shallower + lax.ppermute(pack, 'gz', pairs_z)  8.7 us
    pallas_call x1, Pallas kernels, coupling_solve(): pl.pallas_call(coupling_kernel, grid=(cols_x // bx,), in_specs=[cspec, _p...  5.11 us
    unnamed x24, local copies, waits for them, and re-layouts  4.56 us
    ppermute x1, starting transfers between devices, per_device(): mix_above = lax.ppermute(mixing[:, lev_count - 1], 'gz', down_z)  3.92 us
    slice x1, local copies, waits for them, and re-layouts, per_device(): halo_yn = lax.ppermute(state[:, :, :, :1], 'gy', dn_y)  3.7 us
    ppermute x3, starting transfers between devices, gather_by_permutes(): received.append(lax.ppermute(part, axis, shift))  3.28 us
  transfers between devices with their start and end apart: 12, of which 1 were waited for; matrix products, arithmetic and copies ran while one was open for 20% of the time, Pallas kernels for 20%

profile of v4, /device:TPU:0, one launch (start us, length us, event | category | flops | bytes accessed | tf_op | source)
XLA Modules:
  0.0 100.8 jit_solution(13089963758366842355)
XLA Ops:
  6.5 3.7 %fusion.46 = (f32[4,24,32,1]{3,2,1,0:T(8,128)S(1)}, f32[4,24,32,1]{3,2,1,0:T(8,128)}) fusion(f32[4,24,32,256]{3,2,1,0:T(8,128)} %st_ref.1), kind=kLoop, calls=%fused_computation.136 | loop fusion | bytes 49152 | tf_op jit(solution)/shard_map/slice | solution.py:381
  10.2 2.0 %copy.48 = f32[4,24,32,1]{2,1,3,0:T(8,128)S(1)} copy(f32[4,24,32,1]{3,2,1,0:T(8,128)} %get-tuple-element.46) | data formatting | bytes 24576
  12.3 3.2 %collective-permute-start.2 = (f32[4,24,32,1]{2,1,3,0:T(8,128)S(1)}, f32[4,24,32,1]{2,1,3,0:T(8,128)S(1)}, u32[]{:S(2)}, u32[]{:S(2)}) collective-permute-start(f32[4,24,32,1]{2,1,3,0:T(8,128)S(1)} %copy.48), channel_id=1, source_target_pairs={{0,4},{4,8},{8,12},{12,16},{16,20},{20,24},{24,28},{28,0},{1,5},{5... | collective-permute-start | bytes 36872 | tf_op jit(solution)/shard_map/ppermute | solution.py:380
  15.5 0.6 copy.49
  16.1 2.6 %collective-permute-start.3 = (f32[4,24,32,1]{2,1,3,0:T(8,128)S(1)}, f32[4,24,32,1]{2,1,3,0:T(8,128)S(1)}, u32[]{:S(2)}, u32[]{:S(2)}) collective-permute-start(f32[4,24,32,1]{2,1,3,0:T(8,128)S(1)} %copy.49), channel_id=1, source_target_pairs={{4,0},{8,4},{12,8},{16,12},{20,16},{24,20},{28,24},{0,28},{5,1},{9... | collective-permute-start | bytes 36872 | tf_op jit(solution)/shard_map/ppermute | solution.py:381
  18.6 1.5 %fusion.47 = (f32[4,24,1,256]{3,2,1,0:T(1,128)S(1)}, f32[4,24,1,256]{3,2,1,0:T(1,128)S(1)}) fusion(f32[4,24,32,256]{3,2,1,0:T(8,128)} %st_ref.1), kind=kLoop, calls=%fused_computation.137 | loop fusion | bytes 393216 | tf_op jit(solution)/shard_map/slice | solution.py:379
  20.2 0.6 collective-permute-start.1
  20.7 0.8 slice_bitcast_fusion.17
  21.6 3.9 %collective-permute-start.7 = (f32[2,32,256]{2,1,0:T(8,128)S(1)}, f32[2,32,256]{2,1,0:T(8,128)S(1)}, u32[]{:S(2)}, u32[]{:S(2)}) collective-permute-start(f32[2,32,256]{2,1,0:T(8,128)S(1)} %slice_bitcast_fusion.17), channel_id=1, source_target_pairs={{0,1},{1,2},{2,3},{4,5},{5,6},{6,7},{8,9},{9,10},{10,11},{12,13},{... | collective-permute-start | bytes 196616 | tf_op jit(solution)/shard_map/ppermute | solution.py:373
  25.6 0.7 gather_fusion
  26.3 0.1 broadcast_select_fusion
  26.4 0.4 copy.41
  26.8 1.0 %gather_fusion.1 = s32[258,34]{1,0:T(8,128)S(1)} fusion(s32[34,2048]{0,1:T(8,128)S(1)} %copy.41, s32[1024]{0:T(1024)S(1)} %pad_clamp_fusion), kind=kCustom, calls=%fused_computation.1 | custom fusion | bytes 71208 | tf_op jit(solution)/shard_map/jit(_take)/gather | solution.py:385
  27.8 0.1 copy.42
  28.0 0.8 slice_reduce_fusion
  28.8 0.7 fusion.49
  29.5 0.1 fusion.48
  29.6 0.1 fusion.5
  29.7 1.7 %compare_select_fusion = (f32[24,32,256]{2,1,0:T(8,128)S(1)}, f32[32,256]{1,0:T(8,128)S(1)}) fusion(s32[32,256]{1,0:T(8,128)S(1)} %get-tuple-element.61.dc_ref, s32[24]{0:T(128)S(1)} %iota_add_fusion.1, f32[4,24,32,256]{3,2,1,0:T(8,128)} %st_ref.1), kind=kLoop, calls=%fused_computation.15 | loop fusion | flops 2351104 | bytes 2424928 | tf_op jit(solution)/shard_map/mul | solution.py:398
  31.4 0.1 fusion.21
  31.5 1.3 %broadcast_multiply_fusion.c_ref = f32[2,24,32,256]{3,2,1,0:T(8,128)} fusion(f32[2,24,32,256]{3,2,1,0:T(8,128)S(1)} %copy-done.2, f32[24,32,256]{2,1,0:T(8,128)S(1)} %get-tuple-element.66), kind=kLoop, calls=%fused_computation.12 | loop fusion | flops 393216 | bytes 3932160 | tf_op jit(solution)/shard_map/mul | solution.py:398
  32.8 0.6 broadcast_select_fusion.1.wind_ref
  33.5 0.2 scatter.9
  33.7 0.6 multiply_select_fusion.ctop_ref
  34.3 5.1 %shard_map.46 = (f32[2,24,32,256]{3,2,1,0:T(8,128)}, f32[2,24,32,256]{3,2,1,0:T(8,128)}, f32[2,24,32,256]{3,2,1,0:T(8,128)}, f32[2,24,32,256]{3,2,1,0:T(8,128)}, f32[8,32,256]{2,1,0:T(8,128)}) custom-call(f32[2,24,32,256]{3,2,1,0:T(8,128)} %broadcast_multiply_fusion.c_ref, f32[2,32,256]{2,1,0:T(8,128)} %multiply_select_fusion.ctop_ref), custom_call_target="tpu_custom_call" | custom-call | tf_op jit(solution)/shard_map/pallas_call | solution.py:130
  39.5 0.1 fusion.29
  39.6 0.1 fusion.28
  39.7 3.8 %collective-permute-start.4 = (f32[36,256]{1,0:T(8,128)S(1)}, f32[36,256]{1,0:T(8,128)S(1)}, u32[]{:S(2)}, u32[]{:S(2)}) collective-permute-start(f32[36,256]{1,0:T(8,128)S(1)} %pad_maximum_fusion), channel_id=1, source_target_pairs={{0,1},{1,2},{2,3},{4,5},{5,6},{6,7},{8,9},{9,10},{10,11},{12,13},{... | collective-permute-start | bytes 110600 | tf_op jit(solution)/shard_map/ppermute | solution.py:416
  43.6 3.6 %collective-permute-start.5 = (f32[36,256]{1,0:T(8,128)S(1)}, f32[36,256]{1,0:T(8,128)S(1)}, u32[]{:S(2)}, u32[]{:S(2)}) collective-permute-start(f32[36,256]{1,0:T(8,128)S(1)} %pad_maximum_fusion), channel_id=1, source_target_pairs={{0,2},{1,3},{4,6},{5,7},{8,10},{9,11},{12,14},{13,15},{16,18},{17,... | collective-permute-start | bytes 110600 | tf_op jit(solution)/shard_map/ppermute | solution.py:416
  47.1 1.3 %collective-permute-start.6 = (f32[36,256]{1,0:T(8,128)S(1)}, f32[36,256]{1,0:T(8,128)S(1)}, u32[]{:S(2)}, u32[]{:S(2)}) collective-permute-start(f32[36,256]{1,0:T(8,128)S(1)} %pad_maximum_fusion), channel_id=1, source_target_pairs={{0,3},{4,7},{8,11},{12,15},{16,19},{20,23},{24,27},{28,31},{32,35}... | collective-permute-start | bytes 110600 | tf_op jit(solution)/shard_map/ppermute | solution.py:416
  48.5 0.6 stack.23.lane_ref
  49.1 1.9 %copy.44.ys_ref = f32[4,24,32,1]{3,2,1,0:T(8,128)} copy(f32[4,24,32,1]{2,1,3,0:T(8,128)S(1)} %collective-permute-done.2) | data formatting | bytes 24576 | tf_op jit(solution)/shard_map/ppermute | solution.py:380
  51.0 1.8 %copy.45.yn_ref = f32[4,24,32,1]{3,2,1,0:T(8,128)} copy(f32[4,24,32,1]{2,1,3,0:T(8,128)S(1)} %collective-permute-done.3) | data formatting | bytes 24576 | tf_op jit(solution)/shard_map/ppermute | solution.py:381
  52.8 0.6 slice.300.sc_ref
  53.4 0.7 copy.46.sys_ref
  54.1 0.7 copy.47.syn_ref
  54.8 0.6 fusion.50
  55.4 15.1 %shard_map.47 = (f32[4,24,32,256]{3,2,1,0:T(8,128)}, f32[8,32,256]{2,1,0:T(8,128)}) custom-call(f32[4,24,32,256]{3,2,1,0:T(8,128)} %st_ref.1, f32[4,24,1,256]{3,2,1,0:T(1,128)} %copy-done.7, f32[4,24,1,256]{3,2,1,0:T(1,128)} %copy-done.6, f32[4,24,32,1]{3,2,1,0:T(8,128)} %copy.44.ys_ref, f32[4,24,32,1]{3,2,1,0:T(8,128)} %copy.45.yn_ref, ...), custom_call_target="tpu_custom_call" | custom-call | tf_op jit(solution)/shard_map/pallas_call | solution.py:352
  70.4 0.1 collective-permute-start.10
  70.5 3.2 %collective-permute-start.8 = (f32[8,32,256]{2,1,0:T(8,128)}, f32[8,32,256]{2,1,0:T(8,128)S(1)}, u32[]{:S(2)}, u32[]{:S(2)}) collective-permute-start(f32[8,32,256]{2,1,0:T(8,128)} %get-tuple-element.39), channel_id=1, source_target_pairs={{0,3},{1,0},{2,1},{3,2},{4,7},{5,4},{6,5},{7,6},{8,11},{9,8},{10,9... | collective-permute-start | bytes 786440 | tf_op jit(solution)/shard_map/ppermute | solution.py:201
  73.7 12.6 %collective-permute-done.10 = f32[8,32,256]{2,1,0:T(8,128)S(1)} collective-permute-done((f32[8,32,256]{2,1,0:T(8,128)}, f32[8,32,256]{2,1,0:T(8,128)S(1)}, u32[]{:S(2)}, u32[]{:S(2)}) %collective-permute-start.10) | collective-permute-done | bytes 262176 | tf_op jit(solution)/shard_map/ppermute | solution.py:201
  86.4 1.1 %select_bitcast_fusion.2 = (f32[1,8,32,256]{3,2,1,0:T(8,128)S(1)}, f32[1,8,32,256]{3,2,1,0:T(8,128)S(1)}, f32[1,8,32,256]{3,2,1,0:T(8,128)S(1)}, f32[1,8,32,256]{3,2,1,0:T(8,128)S(1)}) fusion(f32[8,32,256]{2,1,0:T(8,128)S(1)} %collective-permute-done.8, f32[8,32,256]{2,1,0:T(8,128)S(1)} %collective-permute-done.9, ...), kind=kLoop, calls=%fused_computation.18 | loop fusion | flops 786432 | bytes 2097164 | tf_op jit(solution)/shard_map/stack | solution.py:208
  87.5 1.6 %broadcast_in_dim.54 = f32[4,8,2,32,256]{4,3,2,1,0:T(8,128)S(1)} broadcast(f32[4,8,32,256]{3,2,1,0:T(8,128)} %bitcast.303), dimensions={0,1,3,4} | broadcast | bytes 3145728 | tf_op jit(solution)/shard_map/broadcast_in_dim | solution.py:160
  89.2 0.2 select_select_fusion
  89.4 0.3 select_select_fusion.1
  89.6 1.4 %copy-done.1 = f32[4,24,32,256]{3,2,1,0:T(8,128)S(1)} copy-done((f32[4,24,32,256]{3,2,1,0:T(8,128)S(1)}, f32[4,24,32,256]{3,2,1,0:T(8,128)}, u32[]{:S(2)}) %copy-start.1) | copy-done | bytes 3145752
  91.1 0.5 copy-done.3
  91.5 2.5 %fusion = f32[4,24,32,256]{3,2,1,0:T(8,128)} fusion(f32[4,24,32,256]{3,2,1,0:T(8,128)S(1)} %copy-done.1, f32[2,24,32,256]{3,2,1,0:T(8,128)S(1)} %copy-done.4, f32[4,32,256]{2,1,0:T(8,128)S(1)} %select_select_fusion, f32[2,24,32,256]{3,2,1,0:T(8,128)S(1)} %copy-done.3, f32[4,32,256]{2,1,0:T(8,128)S(1)} %select_select_fusion.1), kind=kLoop, calls=%fused_computation.3 | loop fusion | flops 3145728 | bytes 9699328 | tf_op jit(solution)/shard_map/add | solution.py:436
  (53 shorter events, 0.4 us)
Async XLA Ops:
  6.5 19.1 %copy-start = (s32[128,2048]{1,0:T(8,128)S(1)}, s32[128,2048]{1,0:T(8,128)}, u32[]{:S(2)}) copy-start(s32[128,2048]{1,0:T(8,128)} %param.10) | copy-start | bytes 3145732
  6.5 81.0 %all-gather.3.cloned.1.call-start = ((), (), s32[]{:S(2)}) async-start(), calls=%async_computation | async-start | bytes 1310720 | tf_op jit(solution)/shard_map/all_gather | solution.py:403
  12.3 21.2 %collective-permute-start.2 = (f32[4,24,32,1]{2,1,3,0:T(8,128)S(1)}, f32[4,24,32,1]{2,1,3,0:T(8,128)S(1)}, u32[]{:S(2)}, u32[]{:S(2)}) collective-permute-start(f32[4,24,32,1]{2,1,3,0:T(8,128)S(1)} %copy.48), channel_id=1, source_target_pairs={{0,4},{4,8},{8,12},{12,16},{16,20},{20,24},{24,28},{28,0},{1,5},{5... | collective-permute-start | bytes 36872 | tf_op jit(solution)/shard_map/ppermute | solution.py:380
  16.1 17.4 %collective-permute-start.3 = (f32[4,24,32,1]{2,1,3,0:T(8,128)S(1)}, f32[4,24,32,1]{2,1,3,0:T(8,128)S(1)}, u32[]{:S(2)}, u32[]{:S(2)}) collective-permute-start(f32[4,24,32,1]{2,1,3,0:T(8,128)S(1)} %copy.49), channel_id=1, source_target_pairs={{4,0},{8,4},{12,8},{16,12},{20,16},{24,20},{28,24},{0,28},{5,1},{9... | collective-permute-start | bytes 36872 | tf_op jit(solution)/shard_map/ppermute | solution.py:381
  20.2 19.3 %collective-permute-start.1 = (f32[4,24,1,256]{3,2,1,0:T(1,128)S(1)}, f32[4,24,1,256]{3,2,1,0:T(1,128)S(1)}, u32[]{:S(2)}, u32[]{:S(2)}) collective-permute-start(f32[4,24,1,256]{3,2,1,0:T(1,128)S(1)} %get-tuple-element.47), channel_id=1, source_target_pairs={{32,0},{64,32},{96,64},{0,96},{33,1},{65,33},{97,65},{1,97},{34,2}... | collective-permute-start | bytes 294920 | tf_op jit(solution)/shard_map/ppermute | solution.py:379
  20.7 18.9 %collective-permute-start = (f32[4,24,1,256]{3,2,1,0:T(1,128)S(1)}, f32[4,24,1,256]{3,2,1,0:T(1,128)S(1)}, u32[]{:S(2)}, u32[]{:S(2)}) collective-permute-start(f32[4,24,1,256]{3,2,1,0:T(1,128)S(1)} %get-tuple-element.48), channel_id=1, source_target_pairs={{0,32},{32,64},{64,96},{96,0},{1,33},{33,65},{65,97},{97,1},{2,34}... | collective-permute-start | bytes 294920 | tf_op jit(solution)/shard_map/ppermute | solution.py:378
  21.6 12.1 %collective-permute-start.7 = (f32[2,32,256]{2,1,0:T(8,128)S(1)}, f32[2,32,256]{2,1,0:T(8,128)S(1)}, u32[]{:S(2)}, u32[]{:S(2)}) collective-permute-start(f32[2,32,256]{2,1,0:T(8,128)S(1)} %slice_bitcast_fusion.17), channel_id=1, source_target_pairs={{0,1},{1,2},{2,3},{4,5},{5,6},{6,7},{8,9},{9,10},{10,11},{12,13},{... | collective-permute-start | bytes 196616 | tf_op jit(solution)/shard_map/ppermute | solution.py:373
  27.8 3.6 %copy-start.2 = (f32[2,24,32,256]{3,2,1,0:T(8,128)S(1)}, f32[2,24,32,256]{3,2,1,0:T(8,128)}, u32[]{:S(2)}) copy-start(f32[2,24,32,256]{3,2,1,0:T(8,128)} %param.9) | copy-start | bytes 4718596
  29.5 3.3 %copy-start.5 = (s32[32,256]{1,0:T(8,128)}, s32[32,256]{1,0:T(8,128)S(1)}, u32[]{:S(2)}) copy-start(s32[32,256]{1,0:T(8,128)S(1)} %get-tuple-element.61.dc_ref) | copy-start | bytes 98308
  29.6 9.9 %copy-start.9 = (s32[1,256]{1,0:T(1,128)}, s32[1,256]{1,0:T(1,128)S(1)}, u32[]{:S(2)}) copy-start(s32[1,256]{1,0:T(1,128)S(1)} %get-tuple-element.55.dxe_ref) | copy-start | bytes 3076
  29.6 10.0 %copy-start.10 = (s32[1,256]{1,0:T(1,128)}, s32[1,256]{1,0:T(1,128)S(1)}, u32[]{:S(2)}) copy-start(s32[1,256]{1,0:T(1,128)S(1)} %get-tuple-element.56.dxw_ref) | copy-start | bytes 3076
  31.4 1.4 %copy-start.8 = (f32[2,32,256]{2,1,0:T(8,128)S(1)}, f32[2,32,256]{2,1,0:T(8,128)}, u32[]{:S(2)}) copy-start(f32[2,32,256]{2,1,0:T(8,128)} %param.11) | copy-start | bytes 196612
  39.5 15.9 %copy-start.6 = (f32[4,24,1,256]{3,2,1,0:T(1,128)}, f32[4,24,1,256]{3,2,1,0:T(1,128)S(1)}, u32[]{:S(2)}) copy-start(f32[4,24,1,256]{3,2,1,0:T(1,128)S(1)} %collective-permute-done.1.xe_ref) | copy-start | bytes 294916
  39.6 15.8 %copy-start.7 = (f32[4,24,1,256]{3,2,1,0:T(1,128)}, f32[4,24,1,256]{3,2,1,0:T(1,128)S(1)}, u32[]{:S(2)}) copy-start(f32[4,24,1,256]{3,2,1,0:T(1,128)S(1)} %collective-permute-done.xw_ref) | copy-start | bytes 294916
  39.7 13.1 %collective-permute-start.4 = (f32[36,256]{1,0:T(8,128)S(1)}, f32[36,256]{1,0:T(8,128)S(1)}, u32[]{:S(2)}, u32[]{:S(2)}) collective-permute-start(f32[36,256]{1,0:T(8,128)S(1)} %pad_maximum_fusion), channel_id=1, source_target_pairs={{0,1},{1,2},{2,3},{4,5},{5,6},{6,7},{8,9},{9,10},{10,11},{12,13},{... | collective-permute-start | bytes 110600 | tf_op jit(solution)/shard_map/ppermute | solution.py:416
  43.6 9.2 %collective-permute-start.5 = (f32[36,256]{1,0:T(8,128)S(1)}, f32[36,256]{1,0:T(8,128)S(1)}, u32[]{:S(2)}, u32[]{:S(2)}) collective-permute-start(f32[36,256]{1,0:T(8,128)S(1)} %pad_maximum_fusion), channel_id=1, source_target_pairs={{0,2},{1,3},{4,6},{5,7},{8,10},{9,11},{12,14},{13,15},{16,18},{17,... | collective-permute-start | bytes 110600 | tf_op jit(solution)/shard_map/ppermute | solution.py:416
  47.1 5.6 %collective-permute-start.6 = (f32[36,256]{1,0:T(8,128)S(1)}, f32[36,256]{1,0:T(8,128)S(1)}, u32[]{:S(2)}, u32[]{:S(2)}) collective-permute-start(f32[36,256]{1,0:T(8,128)S(1)} %pad_maximum_fusion), channel_id=1, source_target_pairs={{0,3},{4,7},{8,11},{12,15},{16,19},{20,23},{24,27},{28,31},{32,35}... | collective-permute-start | bytes 110600 | tf_op jit(solution)/shard_map/ppermute | solution.py:416
  70.4 15.9 %collective-permute-start.10 = (f32[8,32,256]{2,1,0:T(8,128)}, f32[8,32,256]{2,1,0:T(8,128)S(1)}, u32[]{:S(2)}, u32[]{:S(2)}) collective-permute-start(f32[8,32,256]{2,1,0:T(8,128)} %get-tuple-element.39), channel_id=1, source_target_pairs={{0,1},{1,2},{2,3},{3,0},{4,5},{5,6},{6,7},{7,4},{8,9},{9,10},{10,1... | collective-permute-start | bytes 786440 | tf_op jit(solution)/shard_map/ppermute | solution.py:201
  70.5 15.9 %collective-permute-start.8 = (f32[8,32,256]{2,1,0:T(8,128)}, f32[8,32,256]{2,1,0:T(8,128)S(1)}, u32[]{:S(2)}, u32[]{:S(2)}) collective-permute-start(f32[8,32,256]{2,1,0:T(8,128)} %get-tuple-element.39), channel_id=1, source_target_pairs={{0,3},{1,0},{2,1},{3,2},{4,7},{5,4},{6,5},{7,6},{8,11},{9,8},{10,9... | collective-permute-start | bytes 786440 | tf_op jit(solution)/shard_map/ppermute | solution.py:201
  73.7 12.6 %collective-permute-start.9 = (f32[8,32,256]{2,1,0:T(8,128)}, f32[8,32,256]{2,1,0:T(8,128)S(1)}, u32[]{:S(2)}, u32[]{:S(2)}) collective-permute-start(f32[8,32,256]{2,1,0:T(8,128)} %get-tuple-element.39), channel_id=1, source_target_pairs={{0,2},{1,3},{2,0},{3,1},{4,6},{5,7},{6,4},{7,5},{8,10},{9,11},{10,... | collective-permute-start | bytes 786440 | tf_op jit(solution)/shard_map/ppermute | solution.py:201
  87.5 2.1 %copy-start.4 = (f32[2,24,32,256]{3,2,1,0:T(8,128)S(1)}, f32[2,24,32,256]{3,2,1,0:T(8,128)}, u32[]{:S(2)}) copy-start(f32[2,24,32,256]{3,2,1,0:T(8,128)} %get-tuple-element.42) | copy-start | bytes 4718596
  89.1 1.9 %copy-start.1 = (f32[4,24,32,256]{3,2,1,0:T(8,128)S(1)}, f32[4,24,32,256]{3,2,1,0:T(8,128)}, u32[]{:S(2)}) copy-start(f32[4,24,32,256]{3,2,1,0:T(8,128)} %get-tuple-element.38) | copy-start | bytes 9437188
  89.1 2.4 %copy-start.3 = (f32[2,24,32,256]{3,2,1,0:T(8,128)S(1)}, f32[2,24,32,256]{3,2,1,0:T(8,128)}, u32[]{:S(2)}) copy-start(f32[2,24,32,256]{3,2,1,0:T(8,128)} %get-tuple-element.41) | copy-start | bytes 4718596
Sparse Core Ops, SparseCore 0:
  39.6 24.3 all-gather.2

commit v5 on v4

--- a/solution.py
+++ b/solution.py
@@ -254,8 +254,8 @@
         wys = (k < d_ys).astype(jnp.float32)
         wyn = (k < d_yn).astype(jnp.float32)
         cen = [st_ref[f, k] for f in range(fields)]
-        hxw = [xw_ref[f, k] for f in range(fields)]
-        hxe = [xe_ref[f, k] for f in range(fields)]
+        hxw = [xw_ref[f, pl.ds(k, 1), :] for f in range(fields)]
+        hxe = [xe_ref[f, pl.ds(k, 1), :] for f in range(fields)]
         hys = [ys_ref[f, k] for f in range(fields)]
         hyn = [yn_ref[f, k] for f in range(fields)]
         run_c, run_xw, run_xe, run_ys, run_yn = run
@@ -375,10 +375,10 @@
     dn_x = [(j, i) for i, j in up_x]
     up_y = [(i, (i + 1) % peers_y) for i in range(peers_y)]
     dn_y = [(j, i) for i, j in up_y]
-    halo_xw = lax.ppermute(state[:, :, col_x - 1:], "gx", up_x)
-    halo_xe = lax.ppermute(state[:, :, :1], "gx", dn_x)
-    halo_ys = lax.ppermute(state[:, :, :, col_y - 1:], "gy", up_y)
-    halo_yn = lax.ppermute(state[:, :, :, :1], "gy", dn_y)
+    halo_xw = lax.ppermute(state[:, :, col_x - 1], "gx", up_x)
+    halo_xe = lax.ppermute(state[:, :, 0], "gx", dn_x)
+    halo_ys = lax.ppermute(state[:, :, :, col_y - 1], "gy", up_y)
+    halo_yn = lax.ppermute(state[:, :, :, 0], "gy", dn_y)
     levels = start_z + jnp.arange(lev_count, dtype=jnp.int32)
     row_index = (start_x - 1 + jnp.arange(col_x + 2, dtype=jnp.int32)) % total_x
     col_index = (start_y - 1 + jnp.arange(col_y + 2, dtype=jnp.int32)) % total_y
@@ -403,13 +403,14 @@
     uv_all = lax.all_gather(uv_ends, "gz")
     lev3 = local[:, None, None]
     tot_c = jnp.sum(density_of(state, (lev3 < d_c[None]).astype(jnp.float32)), axis=0)
-    tot_xw = jnp.sum(density_of(halo_xw, (lev3 < d_xw[None]).astype(jnp.float32)), axis=0)
-    tot_xe = jnp.sum(density_of(halo_xe, (lev3 < d_xe[None]).astype(jnp.float32)), axis=0)
-    tot_ys = jnp.sum(density_of(halo_ys, (lev3 < d_ys[None]).astype(jnp.float32)), axis=0)
-    tot_yn = jnp.sum(density_of(halo_yn, (lev3 < d_yn[None]).astype(jnp.float32)), axis=0)
+    lev2 = local[:, None]
+    tot_xw = jnp.sum(density_of(halo_xw, (lev2 < d_xw[0][None]).astype(jnp.float32)), axis=0)
+    tot_xe = jnp.sum(density_of(halo_xe, (lev2 < d_xe[0][None]).astype(jnp.float32)), axis=0)
+    tot_ys = jnp.sum(density_of(halo_ys, (lev2 < d_ys[:, 0][None]).astype(jnp.float32)), axis=0)
+    tot_yn = jnp.sum(density_of(halo_yn, (lev2 < d_yn[:, 0][None]).astype(jnp.float32)), axis=0)
     side = jnp.zeros((2, col_y), jnp.float32)
-    side = side.at[0, :col_x].set(tot_ys[:, 0]).at[1, :col_x].set(tot_yn[:, 0])
-    pack = jnp.concatenate([tot_c, tot_xw, tot_xe, side], axis=0)
+    side = side.at[0, :col_x].set(tot_ys).at[1, :col_x].set(tot_yn)
+    pack = jnp.concatenate([tot_c, tot_xw[None], tot_xe[None], side], axis=0)
     shallower = jnp.zeros_like(pack)
     for hop in range(1, peers_z):
         pairs_z = [(i, i + hop) for i in range(peers_z - hop)]
@@ -425,15 +426,18 @@
     coriolis = 0.5 + (face_row.astype(jnp.float32) + 0.5) / total_y
     lanes = jnp.stack([wall_n, wall_s, 0.3 * coriolis] + [jnp.zeros_like(wall_n)] * 5)
     wind_top = jnp.where(place_z == 0, wind, 0.0)
-    y, y_ends = fused_solve(state, halo_xw, halo_xe, halo_ys, halo_yn,
+    y, y_ends = fused_solve(state, halo_xw, halo_xe, halo_ys[..., None], halo_yn[..., None],
                             d_c, d_e, d_w, d_n, d_s, d_xw, d_xe, d_ys, d_yn,
                             s_c, s_xw, s_xe, s_ys, s_yn, lanes, wind_top,
                             coupling, inv, ratio)
     y_all = gather_by_permutes(y_ends, "gz", place_z, peers_z)
     x_above, x_below = interface_values(y_all, uv_all, place_z, peers_z)
-    u4 = jnp.repeat(u, 2, axis=0)
-    v4 = jnp.repeat(v, 2, axis=0)
-    return y + x_above[:, None] * u4 + x_below[:, None] * v4
+    pairs = u.shape[0]
+    shape5 = (pairs, fields // pairs) + y.shape[1:]
+    plane5 = (pairs, fields // pairs, 1, col_x, col_y)
+    x = (y.reshape(shape5) + x_above.reshape(plane5) * u[:, None]
+         + x_below.reshape(plane5) * v[:, None])
+    return x.reshape(y.shape)
 
 
 def solution(mesh):

time: 102 us -> 101 us (level)
  starting transfers between devices: 22.2 us -> 23.5 us
  waiting for transfers between devices: 12.7 us -> 11.4 us
    broadcast_in_dim x0 -> x2, local copies, waits for them, and re-layouts: none -> 3.68 us  [the longest x1 1.89 us: per_device(): halo_ys[..., None]]
    ppermute x2 -> x0, local copies, waits for them, and re-layouts: 3.68 us -> none  [the longest x1 1.89 us: per_device(): halo_ys = lax.ppermute(state[:, :, :, col_y - 1:], 'gy', up_y)]
    ppermute x4, starting transfers between devices: 6.32 us -> 7.6 us  [the longest x1 3.19 us: per_device(): halo_ys = lax.ppermute(state[:, :, :, col_y - 1], 'gy', up_y)]
    ppermute x3, waiting for transfers between devices: 12.6 us -> 11.4 us  [gather_by_permutes(): received.append(lax.ppermute(part, axis, shift))]
    unnamed x24 -> x26, local copies, waits for them, and re-layouts: 4.56 us -> 4.58 us
where the time goes in v5:
time: 101 us
  starting transfers between devices  23.5 us (23%)
  local copies, waits for them, and re-layouts  23 us (23%)
  Pallas kernels  20.1 us (20%)
  between operations  13.8 us (14%)
  waiting for transfers between devices  11.4 us (11%)
  other arithmetic  8.86 us (9%)
    pallas_call x1, Pallas kernels, fused_solve(): pl.pallas_call(fused_kernel, in_specs=[vmem] * len(operands), out_specs=[...  15 us
    ppermute x3, waiting for transfers between devices, gather_by_permutes(): received.append(lax.ppermute(part, axis, shift))  11.4 us
    ppermute x3, starting transfers between devices, per_device(): shallower = shallower + lax.ppermute(pack, 'gz', pairs_z)  8.7 us
    pallas_call x1, Pallas kernels, coupling_solve(): pl.pallas_call(coupling_kernel, grid=(cols_x // bx,), in_specs=[cspec, _p...  5.11 us
    unnamed x26, local copies, waits for them, and re-layouts  4.58 us
    ppermute x1, starting transfers between devices, per_device(): mix_above = lax.ppermute(mixing[:, lev_count - 1], 'gz', down_z)  3.93 us
    slice x1, local copies, waits for them, and re-layouts, per_device(): halo_yn = lax.ppermute(state[:, :, :, 0], 'gy', dn_y)  3.7 us
    ppermute x3, starting transfers between devices, gather_by_permutes(): received.append(lax.ppermute(part, axis, shift))  3.28 us
  transfers between devices with their start and end apart: 12, of which 1 were waited for; matrix products, arithmetic and copies ran while one was open for 20% of the time, Pallas kernels for 20%

profile of v5, /device:TPU:0, one launch (start us, length us, event | category | flops | bytes accessed | tf_op | source)
XLA Modules:
  0.0 100.7 jit_solution(573355855981463316)
XLA Ops:
  6.5 3.7 %fusion.48 = (f32[4,24,32,1]{3,2,1,0:T(8,128)S(1)}, f32[4,24,32,1]{3,2,1,0:T(8,128)}) fusion(f32[4,24,32,256]{3,2,1,0:T(8,128)} %st_ref.1), kind=kLoop, calls=%fused_computation.140 | loop fusion | bytes 49152 | tf_op jit(solution)/shard_map/slice | solution.py:381
  10.2 2.0 %copy.49 = f32[4,24,32,1]{2,1,0,3:T(8,128)S(1)} copy(f32[4,24,32,1]{3,2,1,0:T(8,128)} %get-tuple-element.46) | data formatting | bytes 24576
  12.3 3.2 %collective-permute-start.2 = (f32[4,24,32]{2,1,0:T(8,128)S(1)}, f32[4,24,32]{2,1,0:T(8,128)S(1)}, u32[]{:S(2)}, u32[]{:S(2)}) collective-permute-start(f32[4,24,32]{2,1,0:T(8,128)S(1)} %bitcast.311), channel_id=1, source_target_pairs={{0,4},{4,8},{8,12},{12,16},{16,20},{20,24},{24,28},{28,0},{1,5},{5... | collective-permute-start | bytes 36872 | tf_op jit(solution)/shard_map/ppermute | solution.py:380
  15.5 0.6 copy.50
  16.1 2.6 %collective-permute-start.3 = (f32[4,24,32]{2,1,0:T(8,128)S(1)}, f32[4,24,32]{2,1,0:T(8,128)S(1)}, u32[]{:S(2)}, u32[]{:S(2)}) collective-permute-start(f32[4,24,32]{2,1,0:T(8,128)S(1)} %bitcast.310), channel_id=1, source_target_pairs={{4,0},{8,4},{12,8},{16,12},{20,16},{24,20},{28,24},{0,28},{5,1},{9... | collective-permute-start | bytes 36872 | tf_op jit(solution)/shard_map/ppermute | solution.py:381
  18.6 1.5 %fusion.49 = (f32[4,24,1,256]{3,2,1,0:T(1,128)S(1)}, f32[4,24,1,256]{3,2,1,0:T(1,128)S(1)}) fusion(f32[4,24,32,256]{3,2,1,0:T(8,128)} %st_ref.1), kind=kLoop, calls=%fused_computation.141 | loop fusion | bytes 393216 | tf_op jit(solution)/shard_map/slice | solution.py:379
  20.2 0.1 collective-permute-start
  20.3 1.8 %collective-permute-start.1 = (f32[4,24,256]{2,1,0:T(8,128)S(1)}, f32[4,24,256]{2,1,0:T(8,128)S(1)}, u32[]{:S(2)}, u32[]{:S(2)}) collective-permute-start(f32[4,24,256]{2,1,0:T(8,128)S(1)} %bitcast.309), channel_id=1, source_target_pairs={{32,0},{64,32},{96,64},{0,96},{33,1},{65,33},{97,65},{1,97},{34,2}... | collective-permute-start | bytes 294920 | tf_op jit(solution)/shard_map/ppermute | solution.py:379
  22.1 0.8 slice_bitcast_fusion.17
  22.9 3.9 %collective-permute-start.7 = (f32[2,32,256]{2,1,0:T(8,128)S(1)}, f32[2,32,256]{2,1,0:T(8,128)S(1)}, u32[]{:S(2)}, u32[]{:S(2)}) collective-permute-start(f32[2,32,256]{2,1,0:T(8,128)S(1)} %slice_bitcast_fusion.17), channel_id=1, source_target_pairs={{0,1},{1,2},{2,3},{4,5},{5,6},{6,7},{8,9},{9,10},{10,11},{12,13},{... | collective-permute-start | bytes 196616 | tf_op jit(solution)/shard_map/ppermute | solution.py:373
  27.0 0.7 gather_fusion
  27.6 0.1 broadcast_select_fusion
  27.7 0.4 copy.40
  28.1 1.0 %gather_fusion.1 = s32[258,34]{1,0:T(8,128)S(1)} fusion(s32[34,2048]{0,1:T(8,128)S(1)} %copy.40, s32[1024]{0:T(1024)S(1)} %pad_clamp_fusion), kind=kCustom, calls=%fused_computation.1 | custom fusion | bytes 71208 | tf_op jit(solution)/shard_map/jit(_take)/gather | solution.py:385
  29.2 0.1 copy.41
  29.3 0.8 slice_reduce_fusion
  30.1 0.7 fusion.51
  30.8 0.1 fusion.50
  30.9 0.1 fusion.5
  31.0 1.7 %compare_select_fusion = (f32[24,32,256]{2,1,0:T(8,128)S(1)}, f32[32,256]{1,0:T(8,128)S(1)}) fusion(s32[32,256]{1,0:T(8,128)S(1)} %get-tuple-element.61.dc_ref, s32[24]{0:T(128)S(1)} %iota_add_fusion.1, f32[4,24,32,256]{3,2,1,0:T(8,128)} %st_ref.1), kind=kLoop, calls=%fused_computation.15 | loop fusion | flops 2351104 | bytes 2424928 | tf_op jit(solution)/shard_map/mul | solution.py:398
  32.7 0.1 fusion.21
  32.8 1.3 %broadcast_multiply_fusion.c_ref = f32[2,24,32,256]{3,2,1,0:T(8,128)} fusion(f32[2,24,32,256]{3,2,1,0:T(8,128)S(1)} %copy-done.2, f32[24,32,256]{2,1,0:T(8,128)S(1)} %get-tuple-element.66), kind=kLoop, calls=%fused_computation.12 | loop fusion | flops 393216 | bytes 3932160 | tf_op jit(solution)/shard_map/mul | solution.py:398
  34.1 0.6 broadcast_select_fusion.1.wind_ref
  34.8 0.2 scatter.9
  35.0 0.6 multiply_select_fusion.ctop_ref
  35.7 5.1 %shard_map.46 = (f32[2,24,32,256]{3,2,1,0:T(8,128)}, f32[2,24,32,256]{3,2,1,0:T(8,128)}, f32[2,24,32,256]{3,2,1,0:T(8,128)}, f32[2,24,32,256]{3,2,1,0:T(8,128)}, f32[8,32,256]{2,1,0:T(8,128)}) custom-call(f32[2,24,32,256]{3,2,1,0:T(8,128)} %broadcast_multiply_fusion.c_ref, f32[2,32,256]{2,1,0:T(8,128)} %multiply_select_fusion.ctop_ref), custom_call_target="tpu_custom_call" | custom-call | tf_op jit(solution)/shard_map/pallas_call | solution.py:130
  40.9 3.8 %collective-permute-start.4 = (f32[36,256]{1,0:T(8,128)S(1)}, f32[36,256]{1,0:T(8,128)S(1)}, u32[]{:S(2)}, u32[]{:S(2)}) collective-permute-start(f32[36,256]{1,0:T(8,128)S(1)} %pad_maximum_fusion), channel_id=1, source_target_pairs={{0,1},{1,2},{2,3},{4,5},{5,6},{6,7},{8,9},{9,10},{10,11},{12,13},{... | collective-permute-start | bytes 110600 | tf_op jit(solution)/shard_map/ppermute | solution.py:417
  44.8 3.6 %collective-permute-start.5 = (f32[36,256]{1,0:T(8,128)S(1)}, f32[36,256]{1,0:T(8,128)S(1)}, u32[]{:S(2)}, u32[]{:S(2)}) collective-permute-start(f32[36,256]{1,0:T(8,128)S(1)} %pad_maximum_fusion), channel_id=1, source_target_pairs={{0,2},{1,3},{4,6},{5,7},{8,10},{9,11},{12,14},{13,15},{16,18},{17,... | collective-permute-start | bytes 110600 | tf_op jit(solution)/shard_map/ppermute | solution.py:417
  48.4 1.3 %collective-permute-start.6 = (f32[36,256]{1,0:T(8,128)S(1)}, f32[36,256]{1,0:T(8,128)S(1)}, u32[]{:S(2)}, u32[]{:S(2)}) collective-permute-start(f32[36,256]{1,0:T(8,128)S(1)} %pad_maximum_fusion), channel_id=1, source_target_pairs={{0,3},{4,7},{8,11},{12,15},{16,19},{20,23},{24,27},{28,31},{32,35}... | collective-permute-start | bytes 110600 | tf_op jit(solution)/shard_map/ppermute | solution.py:417
  49.7 0.6 stack.23.lane_ref
  50.3 1.9 %copy.43.ys_ref = f32[4,24,32,1]{3,2,1,0:T(8,128)} copy(f32[4,24,32,1]{2,1,0,3:T(8,128)S(1)} %bitcast.306) | data formatting | bytes 24576 | tf_op jit(solution)/shard_map/broadcast_in_dim | solution.py:429
  52.2 1.8 %copy.44.yn_ref = f32[4,24,32,1]{3,2,1,0:T(8,128)} copy(f32[4,24,32,1]{2,1,0,3:T(8,128)S(1)} %bitcast.307) | data formatting | bytes 24576 | tf_op jit(solution)/shard_map/broadcast_in_dim | solution.py:429
  54.0 0.6 slice.288.sc_ref
  54.6 0.7 copy.45.sys_ref
  55.3 0.7 copy.46.syn_ref
  56.0 0.6 fusion.52
  56.6 15.0 %shard_map.47 = (f32[4,24,32,256]{3,2,1,0:T(8,128)}, f32[8,32,256]{2,1,0:T(8,128)}) custom-call(f32[4,24,32,256]{3,2,1,0:T(8,128)} %st_ref.1, f32[4,24,256]{2,1,0:T(8,128)} %copy-done.6, f32[4,24,256]{2,1,0:T(8,128)} %copy-done.7, f32[4,24,32,1]{3,2,1,0:T(8,128)} %copy.43.ys_ref, f32[4,24,32,1]{3,2,1,0:T(8,128)} %copy.44.yn_ref, s32[32,256]{1,0:T(8,128)} %copy-done.5, ...), custom_call_target="tpu_custom_call" | custom-call | tf_op jit(solution)/shard_map/pallas_call | solution.py:352
  71.6 0.1 collective-permute-start.10
  71.6 3.2 %collective-permute-start.8 = (f32[8,32,256]{2,1,0:T(8,128)}, f32[8,32,256]{2,1,0:T(8,128)S(1)}, u32[]{:S(2)}, u32[]{:S(2)}) collective-permute-start(f32[8,32,256]{2,1,0:T(8,128)} %get-tuple-element.39), channel_id=1, source_target_pairs={{0,3},{1,0},{2,1},{3,2},{4,7},{5,4},{6,5},{7,6},{8,11},{9,8},{10,9... | collective-permute-start | bytes 786440 | tf_op jit(solution)/shard_map/ppermute | solution.py:201
  74.9 11.4 %collective-permute-done.10 = f32[8,32,256]{2,1,0:T(8,128)S(1)} collective-permute-done((f32[8,32,256]{2,1,0:T(8,128)}, f32[8,32,256]{2,1,0:T(8,128)S(1)}, u32[]{:S(2)}, u32[]{:S(2)}) %collective-permute-start.10) | collective-permute-done | bytes 262176 | tf_op jit(solution)/shard_map/ppermute | solution.py:201
  86.2 1.1 %select_bitcast_fusion.2 = (f32[1,8,32,256]{3,2,1,0:T(8,128)S(1)}, f32[1,8,32,256]{3,2,1,0:T(8,128)S(1)}, f32[1,8,32,256]{3,2,1,0:T(8,128)S(1)}, f32[1,8,32,256]{3,2,1,0:T(8,128)S(1)}) fusion(f32[8,32,256]{2,1,0:T(8,128)S(1)} %collective-permute-done.8, f32[8,32,256]{2,1,0:T(8,128)S(1)} %collective-permute-done.9, ...), kind=kLoop, calls=%fused_computation.18 | loop fusion | flops 786432 | bytes 2097164 | tf_op jit(solution)/shard_map/stack | solution.py:208
  87.3 0.0 all-gather.3.cloned.1.call-done
  87.4 1.6 %broadcast_in_dim.61 = f32[4,8,2,32,256]{4,3,2,1,0:T(8,128)S(1)} broadcast(f32[4,8,32,256]{3,2,1,0:T(8,128)} %bitcast.305), dimensions={0,1,3,4} | broadcast | bytes 3145728 | tf_op jit(solution)/shard_map/broadcast_in_dim | solution.py:160
  89.0 0.2 select_select_fusion
  89.2 0.3 select_select_fusion.1
  89.5 1.4 %copy-done.1 = f32[4,24,32,256]{3,2,1,0:T(8,128)S(1)} copy-done((f32[4,24,32,256]{3,2,1,0:T(8,128)S(1)}, f32[4,24,32,256]{3,2,1,0:T(8,128)}, u32[]{:S(2)}) %copy-start.1) | copy-done | bytes 3145752
  90.9 0.5 copy-done.3
  91.4 2.5 %fusion = f32[4,24,32,256]{3,2,1,0:T(8,128)} fusion(f32[4,24,32,256]{3,2,1,0:T(8,128)S(1)} %copy-done.1, f32[2,24,32,256]{3,2,1,0:T(8,128)S(1)} %copy-done.4, f32[4,32,256]{2,1,0:T(8,128)S(1)} %select_select_fusion, f32[2,24,32,256]{3,2,1,0:T(8,128)S(1)} %copy-done.3, f32[4,32,256]{2,1,0:T(8,128)S(1)} %select_select_fusion.1), kind=kLoop, calls=%fused_computation.3 | loop fusion | flops 3145728 | bytes 9699328 | tf_op jit(solution)/shard_map/add | solution.py:438
  (55 shorter events, 0.4 us)
Async XLA Ops:
  6.5 20.4 %copy-start = (s32[128,2048]{1,0:T(8,128)S(1)}, s32[128,2048]{1,0:T(8,128)}, u32[]{:S(2)}) copy-start(s32[128,2048]{1,0:T(8,128)} %param.10) | copy-start | bytes 3145732
  6.5 80.8 %all-gather.3.cloned.1.call-start = ((), (), s32[]{:S(2)}) async-start(), calls=%async_computation | async-start | bytes 1310720 | tf_op jit(solution)/shard_map/all_gather | solution.py:403
  12.3 22.5 %collective-permute-start.2 = (f32[4,24,32]{2,1,0:T(8,128)S(1)}, f32[4,24,32]{2,1,0:T(8,128)S(1)}, u32[]{:S(2)}, u32[]{:S(2)}) collective-permute-start(f32[4,24,32]{2,1,0:T(8,128)S(1)} %bitcast.311), channel_id=1, source_target_pairs={{0,4},{4,8},{8,12},{12,16},{16,20},{20,24},{24,28},{28,0},{1,5},{5... | collective-permute-start | bytes 36872 | tf_op jit(solution)/shard_map/ppermute | solution.py:380
  16.1 18.7 %collective-permute-start.3 = (f32[4,24,32]{2,1,0:T(8,128)S(1)}, f32[4,24,32]{2,1,0:T(8,128)S(1)}, u32[]{:S(2)}, u32[]{:S(2)}) collective-permute-start(f32[4,24,32]{2,1,0:T(8,128)S(1)} %bitcast.310), channel_id=1, source_target_pairs={{4,0},{8,4},{12,8},{16,12},{20,16},{24,20},{28,24},{0,28},{5,1},{9... | collective-permute-start | bytes 36872 | tf_op jit(solution)/shard_map/ppermute | solution.py:381
  20.2 20.6 %collective-permute-start = (f32[4,24,256]{2,1,0:T(8,128)S(1)}, f32[4,24,256]{2,1,0:T(8,128)S(1)}, u32[]{:S(2)}, u32[]{:S(2)}) collective-permute-start(f32[4,24,256]{2,1,0:T(8,128)S(1)} %bitcast.308), channel_id=1, source_target_pairs={{0,32},{32,64},{64,96},{96,0},{1,33},{33,65},{65,97},{97,1},{2,34}... | collective-permute-start | bytes 294920 | tf_op jit(solution)/shard_map/ppermute | solution.py:378
  20.3 20.6 %collective-permute-start.1 = (f32[4,24,256]{2,1,0:T(8,128)S(1)}, f32[4,24,256]{2,1,0:T(8,128)S(1)}, u32[]{:S(2)}, u32[]{:S(2)}) collective-permute-start(f32[4,24,256]{2,1,0:T(8,128)S(1)} %bitcast.309), channel_id=1, source_target_pairs={{32,0},{64,32},{96,64},{0,96},{33,1},{65,33},{97,65},{1,97},{34,2}... | collective-permute-start | bytes 294920 | tf_op jit(solution)/shard_map/ppermute | solution.py:379
  22.9 12.1 %collective-permute-start.7 = (f32[2,32,256]{2,1,0:T(8,128)S(1)}, f32[2,32,256]{2,1,0:T(8,128)S(1)}, u32[]{:S(2)}, u32[]{:S(2)}) collective-permute-start(f32[2,32,256]{2,1,0:T(8,128)S(1)} %slice_bitcast_fusion.17), channel_id=1, source_target_pairs={{0,1},{1,2},{2,3},{4,5},{5,6},{6,7},{8,9},{9,10},{10,11},{12,13},{... | collective-permute-start | bytes 196616 | tf_op jit(solution)/shard_map/ppermute | solution.py:373
  29.2 3.6 %copy-start.2 = (f32[2,24,32,256]{3,2,1,0:T(8,128)S(1)}, f32[2,24,32,256]{3,2,1,0:T(8,128)}, u32[]{:S(2)}) copy-start(f32[2,24,32,256]{3,2,1,0:T(8,128)} %param.9) | copy-start | bytes 4718596
  30.8 3.3 %copy-start.5 = (s32[32,256]{1,0:T(8,128)}, s32[32,256]{1,0:T(8,128)S(1)}, u32[]{:S(2)}) copy-start(s32[32,256]{1,0:T(8,128)S(1)} %get-tuple-element.61.dc_ref) | copy-start | bytes 98308
  30.9 9.9 %copy-start.10 = (s32[1,256]{1,0:T(1,128)}, s32[1,256]{1,0:T(1,128)S(1)}, u32[]{:S(2)}) copy-start(s32[1,256]{1,0:T(1,128)S(1)} %get-tuple-element.56.dxw_ref) | copy-start | bytes 3076
  30.9 10.0 %copy-start.9 = (s32[1,256]{1,0:T(1,128)}, s32[1,256]{1,0:T(1,128)S(1)}, u32[]{:S(2)}) copy-start(s32[1,256]{1,0:T(1,128)S(1)} %get-tuple-element.55.dxe_ref) | copy-start | bytes 3076
  32.7 1.4 %copy-start.8 = (f32[2,32,256]{2,1,0:T(8,128)S(1)}, f32[2,32,256]{2,1,0:T(8,128)}, u32[]{:S(2)}) copy-start(f32[2,32,256]{2,1,0:T(8,128)} %param.11) | copy-start | bytes 196612
  40.8 15.8 %copy-start.6 = (f32[4,24,256]{2,1,0:T(8,128)}, f32[4,24,256]{2,1,0:T(8,128)S(1)}, u32[]{:S(2)}) copy-start(f32[4,24,256]{2,1,0:T(8,128)S(1)} %collective-permute-done.xw_ref) | copy-start | bytes 294916
  40.9 15.7 %copy-start.7 = (f32[4,24,256]{2,1,0:T(8,128)}, f32[4,24,256]{2,1,0:T(8,128)S(1)}, u32[]{:S(2)}) copy-start(f32[4,24,256]{2,1,0:T(8,128)S(1)} %collective-permute-done.1.xe_ref) | copy-start | bytes 294916
  40.9 13.1 %collective-permute-start.4 = (f32[36,256]{1,0:T(8,128)S(1)}, f32[36,256]{1,0:T(8,128)S(1)}, u32[]{:S(2)}, u32[]{:S(2)}) collective-permute-start(f32[36,256]{1,0:T(8,128)S(1)} %pad_maximum_fusion), channel_id=1, source_target_pairs={{0,1},{1,2},{2,3},{4,5},{5,6},{6,7},{8,9},{9,10},{10,11},{12,13},{... | collective-permute-start | bytes 110600 | tf_op jit(solution)/shard_map/ppermute | solution.py:417
  44.8 9.2 %collective-permute-start.5 = (f32[36,256]{1,0:T(8,128)S(1)}, f32[36,256]{1,0:T(8,128)S(1)}, u32[]{:S(2)}, u32[]{:S(2)}) collective-permute-start(f32[36,256]{1,0:T(8,128)S(1)} %pad_maximum_fusion), channel_id=1, source_target_pairs={{0,2},{1,3},{4,6},{5,7},{8,10},{9,11},{12,14},{13,15},{16,18},{17,... | collective-permute-start | bytes 110600 | tf_op jit(solution)/shard_map/ppermute | solution.py:417
  48.4 5.6 %collective-permute-start.6 = (f32[36,256]{1,0:T(8,128)S(1)}, f32[36,256]{1,0:T(8,128)S(1)}, u32[]{:S(2)}, u32[]{:S(2)}) collective-permute-start(f32[36,256]{1,0:T(8,128)S(1)} %pad_maximum_fusion), channel_id=1, source_target_pairs={{0,3},{4,7},{8,11},{12,15},{16,19},{20,23},{24,27},{28,31},{32,35}... | collective-permute-start | bytes 110600 | tf_op jit(solution)/shard_map/ppermute | solution.py:417
  71.6 14.6 %collective-permute-start.10 = (f32[8,32,256]{2,1,0:T(8,128)}, f32[8,32,256]{2,1,0:T(8,128)S(1)}, u32[]{:S(2)}, u32[]{:S(2)}) collective-permute-start(f32[8,32,256]{2,1,0:T(8,128)} %get-tuple-element.39), channel_id=1, source_target_pairs={{0,1},{1,2},{2,3},{3,0},{4,5},{5,6},{6,7},{7,4},{8,9},{9,10},{10,1... | collective-permute-start | bytes 786440 | tf_op jit(solution)/shard_map/ppermute | solution.py:201
  71.6 14.6 %collective-permute-start.8 = (f32[8,32,256]{2,1,0:T(8,128)}, f32[8,32,256]{2,1,0:T(8,128)S(1)}, u32[]{:S(2)}, u32[]{:S(2)}) collective-permute-start(f32[8,32,256]{2,1,0:T(8,128)} %get-tuple-element.39), channel_id=1, source_target_pairs={{0,3},{1,0},{2,1},{3,2},{4,7},{5,4},{6,5},{7,6},{8,11},{9,8},{10,9... | collective-permute-start | bytes 786440 | tf_op jit(solution)/shard_map/ppermute | solution.py:201
  74.9 11.4 %collective-permute-start.9 = (f32[8,32,256]{2,1,0:T(8,128)}, f32[8,32,256]{2,1,0:T(8,128)S(1)}, u32[]{:S(2)}, u32[]{:S(2)}) collective-permute-start(f32[8,32,256]{2,1,0:T(8,128)} %get-tuple-element.39), channel_id=1, source_target_pairs={{0,2},{1,3},{2,0},{3,1},{4,6},{5,7},{6,4},{7,5},{8,10},{9,11},{10,... | collective-permute-start | bytes 786440 | tf_op jit(solution)/shard_map/ppermute | solution.py:201
  87.4 2.1 %copy-start.4 = (f32[2,24,32,256]{3,2,1,0:T(8,128)S(1)}, f32[2,24,32,256]{3,2,1,0:T(8,128)}, u32[]{:S(2)}) copy-start(f32[2,24,32,256]{3,2,1,0:T(8,128)} %get-tuple-element.42) | copy-start | bytes 4718596
  89.0 1.9 %copy-start.1 = (f32[4,24,32,256]{3,2,1,0:T(8,128)S(1)}, f32[4,24,32,256]{3,2,1,0:T(8,128)}, u32[]{:S(2)}) copy-start(f32[4,24,32,256]{3,2,1,0:T(8,128)} %get-tuple-element.38) | copy-start | bytes 9437188
  89.0 2.4 %copy-start.3 = (f32[2,24,32,256]{3,2,1,0:T(8,128)S(1)}, f32[2,24,32,256]{3,2,1,0:T(8,128)}, u32[]{:S(2)}) copy-start(f32[2,24,32,256]{3,2,1,0:T(8,128)} %get-tuple-element.41) | copy-start | bytes 4718596
Sparse Core Ops, SparseCore 0:
  40.9 24.1 all-gather.2

commit v6 on v5

--- a/solution.py
+++ b/solution.py
@@ -155,13 +155,14 @@
 
 def interface_values(y_ends, uv_ends, place, peers):
     fields = 4
-    y0 = y_ends[:, 0:fields]
-    y1 = y_ends[:, fields:2 * fields]
-    rest = jnp.repeat(uv_ends, 2, axis=1)
-    u0 = rest[:, 0:4]
-    u1 = rest[:, 4:8]
-    v0 = rest[:, 8:12]
-    v1 = rest[:, 12:16]
+    pairs = uv_ends.shape[1] // 4
+    grouped = (peers, pairs, fields // pairs) + y_ends.shape[2:]
+    y0 = y_ends[:, 0:fields].reshape(grouped)
+    y1 = y_ends[:, fields:2 * fields].reshape(grouped)
+    u0 = uv_ends[:, 0:pairs][:, :, None]
+    u1 = uv_ends[:, pairs:2 * pairs][:, :, None]
+    v0 = uv_ends[:, 2 * pairs:3 * pairs][:, :, None]
+    v1 = uv_ends[:, 3 * pairs:4 * pairs][:, :, None]
     pt, qt, pb, qb = [], [], [], []
     for q in range(peers):
         if q == 0:
@@ -231,17 +232,26 @@
     d_c, d_e, d_w, d_n, d_s = dc_ref[...], de_ref[...], dw_ref[...], dn_ref[...], ds_ref[...]
     d_xw, d_xe, d_ys, d_yn = dxw_ref[...], dxe_ref[...], dys_ref[...], dyn_ref[...]
 
+    tx = xw_ref.shape[2]
+    ty = ys_ref.shape[3]
+
+    def rows(a):
+        return a if tx == nx else jnp.concatenate([a] * (nx // tx), axis=0)
+
+    def lanes(a):
+        return a if ty == ny else jnp.concatenate([a] * (ny // ty), axis=1)
+
     def east(r, h):
-        return jnp.where(row == nx - 1, h, pltpu.roll(r, nx - 1, 0))
+        return jnp.where(row == nx - 1, rows(pltpu.roll(h, tx - 1, 0)), pltpu.roll(r, nx - 1, 0))
 
     def west(r, h):
-        return jnp.where(row == 0, h, pltpu.roll(r, 1, 0))
+        return jnp.where(row == 0, rows(pltpu.roll(h, 1, 0)), pltpu.roll(r, 1, 0))
 
     def north(r, h):
-        return jnp.where(lane == ny - 1, h, pltpu.roll(r, ny - 1, 1))
+        return jnp.where(lane == ny - 1, lanes(pltpu.roll(h, ty - 1, 1)), pltpu.roll(r, ny - 1, 1))
 
     def south(r, h):
-        return jnp.where(lane == 0, h, pltpu.roll(r, 1, 1))
+        return jnp.where(lane == 0, lanes(pltpu.roll(h, 1, 1)), pltpu.roll(r, 1, 1))
 
     def level(k, run, vy_prev):
         wc = (k < d_c).astype(jnp.float32)
@@ -254,8 +264,8 @@
         wys = (k < d_ys).astype(jnp.float32)
         wyn = (k < d_yn).astype(jnp.float32)
         cen = [st_ref[f, k] for f in range(fields)]
-        hxw = [xw_ref[f, pl.ds(k, 1), :] for f in range(fields)]
-        hxe = [xe_ref[f, pl.ds(k, 1), :] for f in range(fields)]
+        hxw = [xw_ref[f, k] for f in range(fields)]
+        hxe = [xe_ref[f, k] for f in range(fields)]
         hys = [ys_ref[f, k] for f in range(fields)]
         hyn = [yn_ref[f, k] for f in range(fields)]
         run_c, run_xw, run_xe, run_ys, run_yn = run
@@ -317,9 +327,9 @@
             vy.append(val)
         return (run_c, run_xw, run_xe, run_ys, run_yn), vy
 
-    run0 = (jnp.zeros((nx, ny), jnp.float32), jnp.zeros((1, ny), jnp.float32),
-            jnp.zeros((1, ny), jnp.float32), jnp.zeros((nx, 1), jnp.float32),
-            jnp.zeros((nx, 1), jnp.float32))
+    run0 = (jnp.zeros((nx, ny), jnp.float32), jnp.zeros((tx, ny), jnp.float32),
+            jnp.zeros((tx, ny), jnp.float32), jnp.zeros((nx, ty), jnp.float32),
+            jnp.zeros((nx, ty), jnp.float32))
     run, vy = level(0, run0, None)
 
     def step(k, carry):
@@ -375,10 +385,12 @@
     dn_x = [(j, i) for i, j in up_x]
     up_y = [(i, (i + 1) % peers_y) for i in range(peers_y)]
     dn_y = [(j, i) for i, j in up_y]
-    halo_xw = lax.ppermute(state[:, :, col_x - 1], "gx", up_x)
-    halo_xe = lax.ppermute(state[:, :, 0], "gx", dn_x)
-    halo_ys = lax.ppermute(state[:, :, :, col_y - 1], "gy", up_y)
-    halo_yn = lax.ppermute(state[:, :, :, 0], "gy", dn_y)
+    tx = min(8, col_x)
+    ty = min(128, col_y)
+    halo_xw = lax.ppermute(state[:, :, col_x - tx:], "gx", up_x)
+    halo_xe = lax.ppermute(state[:, :, :tx], "gx", dn_x)
+    halo_ys = lax.ppermute(state[:, :, :, col_y - ty:], "gy", up_y)
+    halo_yn = lax.ppermute(state[:, :, :, :ty], "gy", dn_y)
     levels = start_z + jnp.arange(lev_count, dtype=jnp.int32)
     row_index = (start_x - 1 + jnp.arange(col_x + 2, dtype=jnp.int32)) % total_x
     col_index = (start_y - 1 + jnp.arange(col_y + 2, dtype=jnp.int32)) % total_y
@@ -404,10 +416,10 @@
     lev3 = local[:, None, None]
     tot_c = jnp.sum(density_of(state, (lev3 < d_c[None]).astype(jnp.float32)), axis=0)
     lev2 = local[:, None]
-    tot_xw = jnp.sum(density_of(halo_xw, (lev2 < d_xw[0][None]).astype(jnp.float32)), axis=0)
-    tot_xe = jnp.sum(density_of(halo_xe, (lev2 < d_xe[0][None]).astype(jnp.float32)), axis=0)
-    tot_ys = jnp.sum(density_of(halo_ys, (lev2 < d_ys[:, 0][None]).astype(jnp.float32)), axis=0)
-    tot_yn = jnp.sum(density_of(halo_yn, (lev2 < d_yn[:, 0][None]).astype(jnp.float32)), axis=0)
+    tot_xw = jnp.sum(density_of(halo_xw[:, :, tx - 1], (lev2 < d_xw[0][None]).astype(jnp.float32)), axis=0)
+    tot_xe = jnp.sum(density_of(halo_xe[:, :, 0], (lev2 < d_xe[0][None]).astype(jnp.float32)), axis=0)
+    tot_ys = jnp.sum(density_of(halo_ys[..., ty - 1], (lev2 < d_ys[:, 0][None]).astype(jnp.float32)), axis=0)
+    tot_yn = jnp.sum(density_of(halo_yn[..., 0], (lev2 < d_yn[:, 0][None]).astype(jnp.float32)), axis=0)
     side = jnp.zeros((2, col_y), jnp.float32)
     side = side.at[0, :col_x].set(tot_ys).at[1, :col_x].set(tot_yn)
     pack = jnp.concatenate([tot_c, tot_xw[None], tot_xe[None], side], axis=0)
@@ -426,15 +438,23 @@
     coriolis = 0.5 + (face_row.astype(jnp.float32) + 0.5) / total_y
     lanes = jnp.stack([wall_n, wall_s, 0.3 * coriolis] + [jnp.zeros_like(wall_n)] * 5)
     wind_top = jnp.where(place_z == 0, wind, 0.0)
-    y, y_ends = fused_solve(state, halo_xw, halo_xe, halo_ys[..., None], halo_yn[..., None],
-                            d_c, d_e, d_w, d_n, d_s, d_xw, d_xe, d_ys, d_yn,
-                            s_c, s_xw, s_xe, s_ys, s_yn, lanes, wind_top,
+    tile_x = (tx, col_y)
+    tile_y = (col_x, ty)
+    y, y_ends = fused_solve(state, halo_xw, halo_xe, halo_ys, halo_yn,
+                            d_c, d_e, d_w, d_n, d_s,
+                            jnp.broadcast_to(d_xw, tile_x), jnp.broadcast_to(d_xe, tile_x),
+                            jnp.broadcast_to(d_ys, tile_y), jnp.broadcast_to(d_yn, tile_y),
+                            s_c, jnp.broadcast_to(s_xw, tile_x), jnp.broadcast_to(s_xe, tile_x),
+                            jnp.broadcast_to(s_ys, tile_y), jnp.broadcast_to(s_yn, tile_y),
+                            lanes, wind_top,
                             coupling, inv, ratio)
     y_all = gather_by_permutes(y_ends, "gz", place_z, peers_z)
     x_above, x_below = interface_values(y_all, uv_all, place_z, peers_z)
     pairs = u.shape[0]
     shape5 = (pairs, fields // pairs) + y.shape[1:]
     plane5 = (pairs, fields // pairs, 1, col_x, col_y)
+    x_above = x_above.reshape(plane5)
+    x_below = x_below.reshape(plane5)
     x = (y.reshape(shape5) + x_above.reshape(plane5) * u[:, None]
          + x_below.reshape(plane5) * v[:, None])
     return x.reshape(y.shape)

time: 101 us -> 164 us (1.62)
  waiting for transfers between devices: 11.4 us -> 64 us
  other arithmetic: 8.86 us -> 15.5 us
  starting transfers between devices: 23.5 us -> 25.9 us
    ppermute x4, waiting for transfers between devices: 0.01 us -> 57.8 us  [the longest x1 29.7 us: per_device(): halo_yn = lax.ppermute(state[:, :, :, :ty], 'gy', dn_y)]
    ppermute x3, waiting for transfers between devices: 11.4 us -> 6.19 us  [gather_by_permutes(): received.append(lax.ppermute(part, axis, shift))]
    mul x0 -> x3, other arithmetic: none -> 2.78 us  [the longest x2 1.89 us: density_of(): 0.7 * fields[1]]
    ppermute x0 -> x1, local copies, waits for them, and re-layouts: none -> 2.28 us  [per_device(): halo_xw = lax.ppermute(state[:, :, col_x - tx:], 'gx', up_x)]
    div x0 -> x2, other arithmetic: none -> 2.04 us  [interface_values(): inv = 1.0 / (1.0 - u0[q] * qb[-1])]
    ppermute x3, starting transfers between devices: 8.7 us -> 10.6 us  [per_device(): shallower = shallower + lax.ppermute(pack, 'gz', pairs_z)]
    unnamed x26 -> x21, local copies, waits for them, and re-layouts: 4.58 us -> 2.8 us
    broadcast_in_dim x3 -> x9, local copies, waits for them, and re-layouts: 5.27 us -> 5.05 us  [the longest x1 0.67 us: per_device(): jnp.broadcast_to(d_ys, tile_y)]
  transfers between devices with their start and end apart: 12 -> 12, of which waited for: 1 -> 5; matrix products, arithmetic and copies ran while one was open for 20% -> 18% of each run, Pallas kernels for 20% -> 13%
where the time goes in v6:
time: 164 us
  waiting for transfers between devices  64 us (39%)
  starting transfers between devices  25.9 us (16%)
  local copies, waits for them, and re-layouts  23.5 us (14%)
  Pallas kernels  20.9 us (13%)
  other arithmetic  15.5 us (9%)
  between operations  13.8 us (8%)
    ppermute x1, waiting for transfers between devices, per_device(): halo_yn = lax.ppermute(state[:, :, :, :ty], 'gy', dn_y)  29.7 us
    ppermute x1, waiting for transfers between devices, per_device(): halo_ys = lax.ppermute(state[:, :, :, col_y - ty:], 'gy', up_y)  28 us
    pallas_call x1, Pallas kernels, fused_solve(): pl.pallas_call(fused_kernel, in_specs=[vmem] * len(operands), out_specs=[...  15.7 us
    ppermute x3, starting transfers between devices, per_device(): shallower = shallower + lax.ppermute(pack, 'gz', pairs_z)  10.6 us
    ppermute x3, waiting for transfers between devices, gather_by_permutes(): received.append(lax.ppermute(part, axis, shift))  6.19 us
    pallas_call x1, Pallas kernels, coupling_solve(): pl.pallas_call(coupling_kernel, grid=(cols_x // bx,), in_specs=[cspec, _p...  5.13 us
    ppermute x3, starting transfers between devices, gather_by_permutes(): received.append(lax.ppermute(part, axis, shift))  3.94 us
    ppermute x1, starting transfers between devices, per_device(): mix_above = lax.ppermute(mixing[:, lev_count - 1], 'gz', down_z)  3.92 us
  transfers between devices with their start and end apart: 12, of which 5 were waited for; matrix products, arithmetic and copies ran while one was open for 18% of the time, Pallas kernels for 13%

profile of v6, /device:TPU:0, one launch (start us, length us, event | category | flops | bytes accessed | tf_op | source)
XLA Modules:
  0.0 163.5 jit_solution(12466345815241361639)
XLA Ops:
  6.5 2.5 %fusion.60 = (f32[4,24,8,256]{3,2,1,0:T(8,128)}, f32[4,24,8,256]{3,2,1,0:T(8,128)S(1)}) fusion(f32[4,24,32,256]{3,2,1,0:T(8,128)} %st_ref.1), kind=kLoop, calls=%fused_computation.156 | loop fusion | bytes 3145728 | tf_op jit(solution)/shard_map/slice | solution.py:391
  9.1 1.1 copy.57
  10.2 1.7 %collective-permute-start.1 = (f32[4,24,8,256]{3,2,1,0:T(8,128)}, f32[4,24,8,256]{3,2,1,0:T(8,128)}, u32[]{:S(2)}, u32[]{:S(2)}) collective-permute-start(f32[4,24,8,256]{3,2,1,0:T(8,128)} %get-tuple-element.57), channel_id=1, source_target_pairs={{32,0},{64,32},{96,64},{0,96},{33,1},{65,33},{97,65},{1,97},{34,2}... | collective-permute-start | bytes 2359304 | tf_op jit(solution)/shard_map/ppermute | solution.py:391
  12.0 2.1 %fusion.59 = (f32[4,24,32,128]{3,2,1,0:T(8,128)}, f32[4,24,32,128]{3,2,1,0:T(8,128)}) fusion(f32[4,24,32,256]{3,2,1,0:T(8,128)S(1)} %copy-done.1), kind=kLoop, calls=%fused_computation.155 | loop fusion | bytes 6291456 | tf_op jit(solution)/shard_map/slice | solution.py:393
  14.1 3.1 %collective-permute-start.2 = (f32[4,24,32,128]{3,2,1,0:T(8,128)}, f32[4,24,32,128]{3,2,1,0:T(8,128)S(1)}, u32[]{:S(2)}, u32[]{:S(2)}) collective-permute-start(f32[4,24,32,128]{3,2,1,0:T(8,128)} %get-tuple-element.56), channel_id=1, source_target_pairs={{0,4},{4,8},{8,12},{12,16},{16,20},{20,24},{24,28},{28,0},{1,5},{5... | collective-permute-start | bytes 4718600 | tf_op jit(solution)/shard_map/ppermute | solution.py:392
  17.2 2.5 %collective-permute-start.3 = (f32[4,24,32,128]{3,2,1,0:T(8,128)}, f32[4,24,32,128]{3,2,1,0:T(8,128)}, u32[]{:S(2)}, u32[]{:S(2)}) collective-permute-start(f32[4,24,32,128]{3,2,1,0:T(8,128)} %get-tuple-element.55), channel_id=1, source_target_pairs={{4,0},{8,4},{12,8},{16,12},{20,16},{24,20},{28,24},{0,28},{5,1},{9... | collective-permute-start | bytes 4718600 | tf_op jit(solution)/shard_map/ppermute | solution.py:393
  19.7 0.8 slice_bitcast_fusion.17
  20.6 3.9 %collective-permute-start.7 = (f32[2,32,256]{2,1,0:T(8,128)S(1)}, f32[2,32,256]{2,1,0:T(8,128)S(1)}, u32[]{:S(2)}, u32[]{:S(2)}) collective-permute-start(f32[2,32,256]{2,1,0:T(8,128)S(1)} %slice_bitcast_fusion.17), channel_id=1, source_target_pairs={{0,1},{1,2},{2,3},{4,5},{5,6},{6,7},{8,9},{9,10},{10,11},{12,13},{... | collective-permute-start | bytes 196616 | tf_op jit(solution)/shard_map/ppermute | solution.py:383
  24.6 0.7 gather_fusion
  25.4 1.3 copy.50
  26.8 2.3 %gather_fusion.1 = s32[258,34]{1,0:T(8,128)S(1)} fusion(s32[34,2048]{0,1:T(8,128)} %copy.50, s32[1024]{0:T(1024)S(1)} %pad_clamp_fusion), kind=kCustom, calls=%fused_computation.1 | custom fusion | bytes 71208 | tf_op jit(solution)/shard_map/jit(_take)/gather | solution.py:397
  29.2 0.7 fusion.63
  30.0 1.8 %compare_select_fusion = (f32[24,32,256]{2,1,0:T(8,128)S(1)}, f32[32,256]{1,0:T(8,128)S(1)}) fusion(s32[32,256]{1,0:T(8,128)S(1)} %get-tuple-element.78.dc_ref, s32[24]{0:T(128)S(1)} %iota_add_fusion.1, f32[4,24,32,256]{3,2,1,0:T(8,128)} %st_ref.1), kind=kLoop, calls=%fused_computation.15 | loop fusion | flops 2351104 | bytes 2424928 | tf_op jit(solution)/shard_map/mul | solution.py:410
  31.8 1.4 broadcast_multiply_fusion.c_ref
  33.3 0.6 broadcast_select_fusion.1.wind_ref
  34.1 0.6 multiply_select_fusion.ctop_ref
  34.8 5.1 %shard_map.46 = (f32[2,24,32,256]{3,2,1,0:T(8,128)}, f32[2,24,32,256]{3,2,1,0:T(8,128)}, f32[2,24,32,256]{3,2,1,0:T(8,128)}, f32[2,24,32,256]{3,2,1,0:T(8,128)}, f32[8,32,256]{2,1,0:T(8,128)}) custom-call(f32[2,24,32,256]{3,2,1,0:T(8,128)} %broadcast_multiply_fusion.c_ref, f32[2,32,256]{2,1,0:T(8,128)} %multiply_select_fusion.ctop_ref), custom_call_target="tpu_custom_call" | custom-call | tf_op jit(solution)/shard_map/pallas_call | solution.py:130
  39.9 1.1 fusion.61
  41.0 0.8 fusion.38
  41.8 28.0 %collective-permute-done.2.ys_ref = f32[4,24,32,128]{3,2,1,0:T(8,128)S(1)} collective-permute-done((f32[4,24,32,128]{3,2,1,0:T(8,128)}, f32[4,24,32,128]{3,2,1,0:T(8,128)S(1)}, u32[]{:S(2)}, u32[]{:S(2)}) %collective-permute-start.2) | collective-permute-done | bytes 1572896 | tf_op jit(solution)/shard_map/ppermute | solution.py:392
  70.4 29.7 %collective-permute-done.3.yn_ref = f32[4,24,32,128]{3,2,1,0:T(8,128)} collective-permute-done((f32[4,24,32,128]{3,2,1,0:T(8,128)}, f32[4,24,32,128]{3,2,1,0:T(8,128)}, u32[]{:S(2)}, u32[]{:S(2)}) %collective-permute-start.3) | collective-permute-done | bytes 1572896 | tf_op jit(solution)/shard_map/ppermute | solution.py:393
  100.1 1.4 fusion.6
  101.7 5.9 %collective-permute-start.6 = (f32[36,256]{1,0:T(8,128)S(1)}, f32[36,256]{1,0:T(8,128)S(1)}, u32[]{:S(2)}, u32[]{:S(2)}) collective-permute-start(f32[36,256]{1,0:T(8,128)S(1)} %pad_maximum_fusion), channel_id=1, source_target_pairs={{0,3},{4,7},{8,11},{12,15},{16,19},{20,23},{24,27},{28,31},{32,35}... | collective-permute-start | bytes 110600 | tf_op jit(solution)/shard_map/ppermute | solution.py:429
  107.7 1.3 collective-permute-start.4
  109.0 3.4 %collective-permute-start.5 = (f32[36,256]{1,0:T(8,128)S(1)}, f32[36,256]{1,0:T(8,128)S(1)}, u32[]{:S(2)}, u32[]{:S(2)}) collective-permute-start(f32[36,256]{1,0:T(8,128)S(1)} %pad_maximum_fusion), channel_id=1, source_target_pairs={{0,2},{1,3},{4,6},{5,7},{8,10},{9,11},{12,14},{13,15},{16,18},{17,... | collective-permute-start | bytes 110600 | tf_op jit(solution)/shard_map/ppermute | solution.py:429
  112.5 0.6 stack.23.lane_ref
  113.1 2.3 %copy.55.xw_ref = f32[4,24,8,256]{3,2,1,0:T(8,128)} copy(f32[4,24,8,256]{3,1,2,0:T(8,128)} %collective-permute-done) | data formatting | bytes 1572864 | tf_op jit(solution)/shard_map/ppermute | solution.py:390
  115.4 0.6 slice.325.sc_ref
  116.6 0.6 broadcast_in_dim.110.dxe_ref
  117.2 0.7 broadcast_in_dim.112.dys_ref
  117.9 0.7 broadcast_in_dim.114.dyn_ref
  118.5 0.6 broadcast_in_dim.118.sxw_ref
  119.1 0.6 broadcast_in_dim.120.sxe_ref
  119.7 0.7 broadcast_in_dim.122.sys_ref
  120.4 0.7 broadcast_in_dim.124.syn_ref
  121.1 15.7 %shard_map.47 = (f32[4,24,32,256]{3,2,1,0:T(8,128)}, f32[8,32,256]{2,1,0:T(8,128)}) custom-call(f32[4,24,32,256]{3,2,1,0:T(8,128)} %st_ref.1, f32[4,24,8,256]{3,2,1,0:T(8,128)} %copy.55.xw_ref, f32[4,24,8,256]{3,2,1,0:T(8,128)} %collective-permute-done.1.xe_ref, f32[4,24,32,128]{3,2,1,0:T(8,128)} %copy-done.2, ...), custom_call_target="tpu_custom_call" | custom-call | tf_op jit(solution)/shard_map/pallas_call | solution.py:362
  137.3 2.2 %collective-permute-start.9 = (f32[8,32,256]{2,1,0:T(8,128)}, f32[8,32,256]{2,1,0:T(8,128)S(1)}, u32[]{:S(2)}, u32[]{:S(2)}) collective-permute-start(f32[8,32,256]{2,1,0:T(8,128)} %get-tuple-element.39), channel_id=1, source_target_pairs={{0,2},{1,3},{2,0},{3,1},{4,6},{5,7},{6,4},{7,5},{8,10},{9,11},{10,... | collective-permute-start | bytes 786440 | tf_op jit(solution)/shard_map/ppermute | solution.py:202
  139.4 1.3 collective-permute-start.10
  140.8 1.0 subtract_divide_fusion.1
  141.8 1.0 subtract_divide_fusion
  142.8 0.9 fusion.30
  143.7 1.1 slice_bitcast_fusion.13
  144.9 1.4 collective-permute-done.8
  146.3 1.9 %collective-permute-done.9 = f32[8,32,256]{2,1,0:T(8,128)S(1)} collective-permute-done((f32[8,32,256]{2,1,0:T(8,128)}, f32[8,32,256]{2,1,0:T(8,128)S(1)}, u32[]{:S(2)}, u32[]{:S(2)}) %collective-permute-start.9) | collective-permute-done | bytes 262176 | tf_op jit(solution)/shard_map/ppermute | solution.py:202
  148.2 2.9 %collective-permute-done.10 = f32[8,32,256]{2,1,0:T(8,128)} collective-permute-done((f32[8,32,256]{2,1,0:T(8,128)}, f32[8,32,256]{2,1,0:T(8,128)}, u32[]{:S(2)}, u32[]{:S(2)}) %collective-permute-start.10) | collective-permute-done | bytes 262176 | tf_op jit(solution)/shard_map/ppermute | solution.py:202
  151.1 1.2 select_bitcast_fusion.2
  152.6 1.6 copy-done.3
  154.2 2.5 %fusion = f32[4,24,32,256]{3,2,1,0:T(8,128)} fusion(f32[4,24,32,256]{3,2,1,0:T(8,128)S(1)} %copy-done.3, f32[2,24,32,256]{3,2,1,0:T(8,128)S(1)} %copy-done.6, f32[4,32,256]{2,1,0:T(8,128)S(1)} %select_select_fusion, f32[2,24,32,256]{3,2,1,0:T(8,128)S(1)} %copy-done.5, f32[4,32,256]{2,1,0:T(8,128)S(1)} %fusion.14), kind=kLoop, calls=%fused_computation.3 | loop fusion | flops 3145728 | bytes 9699328 | tf_op jit(solution)/shard_map/add | solution.py:458
  (60 shorter events, 2.9 us)
Async XLA Ops:
  6.5 18.1 %copy-start = (s32[128,2048]{1,0:T(8,128)S(1)}, s32[128,2048]{1,0:T(8,128)}, u32[]{:S(2)}) copy-start(s32[128,2048]{1,0:T(8,128)} %param.10) | copy-start | bytes 3145732
  6.5 134.2 %all-gather.3.cloned.1.call-start = ((), (), s32[]{:S(2)}) async-start(), calls=%async_computation | async-start | bytes 1310720 | tf_op jit(solution)/shard_map/all_gather | solution.py:415
  6.5 5.4 %copy-start.1 = (f32[4,24,32,256]{3,2,1,0:T(8,128)S(1)}, f32[4,24,32,256]{3,2,1,0:T(8,128)}, u32[]{:S(2)}) copy-start(f32[4,24,32,256]{3,2,1,0:T(8,128)} %st_ref.1) | copy-start | bytes 9437188
  10.2 30.8 %collective-permute-start = (f32[4,24,8,256]{3,1,2,0:T(8,128)}, f32[4,24,8,256]{3,1,2,0:T(8,128)}, u32[]{:S(2)}, u32[]{:S(2)}) collective-permute-start(f32[4,24,8,256]{3,1,2,0:T(8,128)} %copy.57), channel_id=1, source_target_pairs={{0,32},{32,64},{64,96},{96,0},{1,33},{33,65},{65,97},{97,1},{2,34}... | collective-permute-start | bytes 2359304 | tf_op jit(solution)/shard_map/ppermute | solution.py:390
  10.2 29.7 %collective-permute-start.1 = (f32[4,24,8,256]{3,2,1,0:T(8,128)}, f32[4,24,8,256]{3,2,1,0:T(8,128)}, u32[]{:S(2)}, u32[]{:S(2)}) collective-permute-start(f32[4,24,8,256]{3,2,1,0:T(8,128)} %get-tuple-element.57), channel_id=1, source_target_pairs={{32,0},{64,32},{96,64},{0,96},{33,1},{65,33},{97,65},{1,97},{34,2}... | collective-permute-start | bytes 2359304 | tf_op jit(solution)/shard_map/ppermute | solution.py:391
  14.1 55.8 %collective-permute-start.2 = (f32[4,24,32,128]{3,2,1,0:T(8,128)}, f32[4,24,32,128]{3,2,1,0:T(8,128)S(1)}, u32[]{:S(2)}, u32[]{:S(2)}) collective-permute-start(f32[4,24,32,128]{3,2,1,0:T(8,128)} %get-tuple-element.56), channel_id=1, source_target_pairs={{0,4},{4,8},{8,12},{12,16},{16,20},{20,24},{24,28},{28,0},{1,5},{5... | collective-permute-start | bytes 4718600 | tf_op jit(solution)/shard_map/ppermute | solution.py:392
  17.2 82.9 %collective-permute-start.3 = (f32[4,24,32,128]{3,2,1,0:T(8,128)}, f32[4,24,32,128]{3,2,1,0:T(8,128)}, u32[]{:S(2)}, u32[]{:S(2)}) collective-permute-start(f32[4,24,32,128]{3,2,1,0:T(8,128)} %get-tuple-element.55), channel_id=1, source_target_pairs={{4,0},{8,4},{12,8},{16,12},{20,16},{24,20},{28,24},{0,28},{5,1},{9... | collective-permute-start | bytes 4718600 | tf_op jit(solution)/shard_map/ppermute | solution.py:393
  20.6 13.6 %collective-permute-start.7 = (f32[2,32,256]{2,1,0:T(8,128)S(1)}, f32[2,32,256]{2,1,0:T(8,128)S(1)}, u32[]{:S(2)}, u32[]{:S(2)}) collective-permute-start(f32[2,32,256]{2,1,0:T(8,128)S(1)} %slice_bitcast_fusion.17), channel_id=1, source_target_pairs={{0,1},{1,2},{2,3},{4,5},{5,6},{6,7},{8,9},{9,10},{10,11},{12,13},{... | collective-permute-start | bytes 196616 | tf_op jit(solution)/shard_map/ppermute | solution.py:383
  29.9 1.9 %copy-start.7 = (s32[32,256]{1,0:T(8,128)}, s32[32,256]{1,0:T(8,128)S(1)}, u32[]{:S(2)}) copy-start(s32[32,256]{1,0:T(8,128)S(1)} %get-tuple-element.78.dc_ref) | copy-start | bytes 98308
  29.9 1.9 %copy-start.4 = (f32[2,24,32,256]{3,2,1,0:T(8,128)S(1)}, f32[2,24,32,256]{3,2,1,0:T(8,128)}, u32[]{:S(2)}) copy-start(f32[2,24,32,256]{3,2,1,0:T(8,128)} %param.9) | copy-start | bytes 4718596
  31.8 1.5 copy-start.9
  69.8 45.5 %copy-start.2 = (f32[4,24,32,128]{3,2,1,0:T(8,128)}, f32[4,24,32,128]{3,2,1,0:T(8,128)S(1)}, u32[]{:S(2)}) copy-start(f32[4,24,32,128]{3,2,1,0:T(8,128)S(1)} %collective-permute-done.2.ys_ref) | copy-start | bytes 4718596
  101.7 13.6 %collective-permute-start.6 = (f32[36,256]{1,0:T(8,128)S(1)}, f32[36,256]{1,0:T(8,128)S(1)}, u32[]{:S(2)}, u32[]{:S(2)}) collective-permute-start(f32[36,256]{1,0:T(8,128)S(1)} %pad_maximum_fusion), channel_id=1, source_target_pairs={{0,3},{4,7},{8,11},{12,15},{16,19},{20,23},{24,27},{28,31},{32,35}... | collective-permute-start | bytes 110600 | tf_op jit(solution)/shard_map/ppermute | solution.py:429
  107.7 7.7 %collective-permute-start.4 = (f32[36,256]{1,0:T(8,128)S(1)}, f32[36,256]{1,0:T(8,128)S(1)}, u32[]{:S(2)}, u32[]{:S(2)}) collective-permute-start(f32[36,256]{1,0:T(8,128)S(1)} %pad_maximum_fusion), channel_id=1, source_target_pairs={{0,1},{1,2},{2,3},{4,5},{5,6},{6,7},{8,9},{9,10},{10,11},{12,13},{... | collective-permute-start | bytes 110600 | tf_op jit(solution)/shard_map/ppermute | solution.py:429
  109.0 6.4 %collective-permute-start.5 = (f32[36,256]{1,0:T(8,128)S(1)}, f32[36,256]{1,0:T(8,128)S(1)}, u32[]{:S(2)}, u32[]{:S(2)}) collective-permute-start(f32[36,256]{1,0:T(8,128)S(1)} %pad_maximum_fusion), channel_id=1, source_target_pairs={{0,2},{1,3},{4,6},{5,7},{8,10},{9,11},{12,14},{13,15},{16,18},{17,... | collective-permute-start | bytes 110600 | tf_op jit(solution)/shard_map/ppermute | solution.py:429
  136.8 14.2 %copy-start.8 = (f32[8,32,256]{2,1,0:T(8,128)S(1)}, f32[8,32,256]{2,1,0:T(8,128)}, u32[]{:S(2)}) copy-start(f32[8,32,256]{2,1,0:T(8,128)} %get-tuple-element.39) | copy-start | bytes 786436
  136.8 9.5 %collective-permute-start.8 = (f32[8,32,256]{2,1,0:T(8,128)}, f32[8,32,256]{2,1,0:T(8,128)S(1)}, u32[]{:S(2)}, u32[]{:S(2)}) collective-permute-start(f32[8,32,256]{2,1,0:T(8,128)} %get-tuple-element.39), channel_id=1, source_target_pairs={{0,3},{1,0},{2,1},{3,2},{4,7},{5,4},{6,5},{7,6},{8,11},{9,8},{10,9... | collective-permute-start | bytes 786440 | tf_op jit(solution)/shard_map/ppermute | solution.py:202
  137.3 10.9 %collective-permute-start.9 = (f32[8,32,256]{2,1,0:T(8,128)}, f32[8,32,256]{2,1,0:T(8,128)S(1)}, u32[]{:S(2)}, u32[]{:S(2)}) collective-permute-start(f32[8,32,256]{2,1,0:T(8,128)} %get-tuple-element.39), channel_id=1, source_target_pairs={{0,2},{1,3},{2,0},{3,1},{4,6},{5,7},{6,4},{7,5},{8,10},{9,11},{10,... | collective-permute-start | bytes 786440 | tf_op jit(solution)/shard_map/ppermute | solution.py:202
  139.4 11.6 %collective-permute-start.10 = (f32[8,32,256]{2,1,0:T(8,128)}, f32[8,32,256]{2,1,0:T(8,128)}, u32[]{:S(2)}, u32[]{:S(2)}) collective-permute-start(f32[8,32,256]{2,1,0:T(8,128)} %get-tuple-element.39), channel_id=1, source_target_pairs={{0,1},{1,2},{2,3},{3,0},{4,5},{5,6},{6,7},{7,4},{8,9},{9,10},{10,1... | collective-permute-start | bytes 786440 | tf_op jit(solution)/shard_map/ppermute | solution.py:202
  143.7 8.9 %copy-start.6 = (f32[2,24,32,256]{3,2,1,0:T(8,128)S(1)}, f32[2,24,32,256]{3,2,1,0:T(8,128)}, u32[]{:S(2)}) copy-start(f32[2,24,32,256]{3,2,1,0:T(8,128)} %get-tuple-element.42) | copy-start | bytes 4718596
  151.1 1.5 copy-start.5
  152.3 2.0 %copy-start.3 = (f32[4,24,32,256]{3,2,1,0:T(8,128)S(1)}, f32[4,24,32,256]{3,2,1,0:T(8,128)}, u32[]{:S(2)}) copy-start(f32[4,24,32,256]{3,2,1,0:T(8,128)} %get-tuple-element.38) | copy-start | bytes 9437188
Sparse Core Ops, SparseCore 0:
  40.0 24.1 all-gather.2

commit v7 on v5

--- a/solution.py
+++ b/solution.py
@@ -155,13 +155,14 @@
 
 def interface_values(y_ends, uv_ends, place, peers):
     fields = 4
-    y0 = y_ends[:, 0:fields]
-    y1 = y_ends[:, fields:2 * fields]
-    rest = jnp.repeat(uv_ends, 2, axis=1)
-    u0 = rest[:, 0:4]
-    u1 = rest[:, 4:8]
-    v0 = rest[:, 8:12]
-    v1 = rest[:, 12:16]
+    pairs = uv_ends.shape[1] // 4
+    grouped = (peers, pairs, fields // pairs) + y_ends.shape[2:]
+    y0 = y_ends[:, 0:fields].reshape(grouped)
+    y1 = y_ends[:, fields:2 * fields].reshape(grouped)
+    u0 = uv_ends[:, 0:pairs][:, :, None]
+    u1 = uv_ends[:, pairs:2 * pairs][:, :, None]
+    v0 = uv_ends[:, 2 * pairs:3 * pairs][:, :, None]
+    v1 = uv_ends[:, 3 * pairs:4 * pairs][:, :, None]
     pt, qt, pb, qb = [], [], [], []
     for q in range(peers):
         if q == 0:
@@ -435,6 +436,8 @@
     pairs = u.shape[0]
     shape5 = (pairs, fields // pairs) + y.shape[1:]
     plane5 = (pairs, fields // pairs, 1, col_x, col_y)
+    x_above = x_above.reshape(plane5)
+    x_below = x_below.reshape(plane5)
     x = (y.reshape(shape5) + x_above.reshape(plane5) * u[:, None]
          + x_below.reshape(plane5) * v[:, None])
     return x.reshape(y.shape)

time: 101 us -> 115 us (1.14); the launches traced: 101 us -> 113 us
  other arithmetic: 8.86 us -> 18.1 us
  local copies, waits for them, and re-layouts: 23 us -> 27.6 us
  starting transfers between devices: 23.5 us -> 21.5 us
    unnamed x26 -> x28, local copies, waits for them, and re-layouts: 4.58 us -> 7.47 us
    div x0 -> x2, other arithmetic: none -> 2.08 us  [interface_values(): inv = 1.0 / (1.0 - u0[q] * qb[-1])]
    broadcast_in_dim x1 -> x0, local copies, waits for them, and re-layouts: 1.59 us -> none  [interface_values(): rest = jnp.repeat(uv_ends, 2, axis=1)]
    ppermute x3, starting transfers between devices: 8.7 us -> 7.46 us  [per_device(): shallower = shallower + lax.ppermute(pack, 'gz', pairs_z)]
    ppermute x3, starting transfers between devices: 3.28 us -> 2.07 us  [gather_by_permutes(): received.append(lax.ppermute(part, axis, shift))]
  transfers between devices with their start and end apart: 12 -> 12, of which waited for: 1 -> 3; matrix products, arithmetic and copies ran while one was open for 20% -> 30% of each run, Pallas kernels for 20% -> 18%
where the time goes in v7:
time: 115 us; the launch traced here: 113 us
  local copies, waits for them, and re-layouts  27.6 us (24%)
  starting transfers between devices  21.5 us (19%)
  Pallas kernels  20.1 us (17%)
  other arithmetic  18.1 us (16%)
  between operations  13.7 us (12%)
  waiting for transfers between devices  11.8 us (10%)
    pallas_call x1, Pallas kernels, fused_solve(): pl.pallas_call(fused_kernel, in_specs=[vmem] * len(operands), out_specs=[...  15 us
    ppermute x3, waiting for transfers between devices, gather_by_permutes(): received.append(lax.ppermute(part, axis, shift))  11.8 us
    unnamed x28, local copies, waits for them, and re-layouts  7.47 us
    ppermute x3, starting transfers between devices, per_device(): shallower = shallower + lax.ppermute(pack, 'gz', pairs_z)  7.46 us
    pallas_call x1, Pallas kernels, coupling_solve(): pl.pallas_call(coupling_kernel, grid=(cols_x // bx,), in_specs=[cspec, _p...  5.12 us
    ppermute x1, starting transfers between devices, per_device(): mix_above = lax.ppermute(mixing[:, lev_count - 1], 'gz', down_z)  4.55 us
    slice x1, local copies, waits for them, and re-layouts, per_device(): halo_yn = lax.ppermute(state[:, :, :, 0], 'gy', dn_y)  3.61 us
    ppermute x1, starting transfers between devices, per_device(): halo_ys = lax.ppermute(state[:, :, :, col_y - 1], 'gy', up_y)  3.14 us
  transfers between devices with their start and end apart: 12, of which 3 were waited for; matrix products, arithmetic and copies ran while one was open for 30% of the time, Pallas kernels for 18%

profile of v7, /device:TPU:0, one launch (start us, length us, event | category | flops | bytes accessed | tf_op | source)
XLA Modules:
  0.0 112.9 jit_solution(12567461140670895620)
XLA Ops:
  6.5 1.6 %fusion.64 = (f32[4,24,1,256]{3,2,1,0:T(1,128)S(1)}, f32[4,24,1,256]{3,2,1,0:T(1,128)S(1)}) fusion(f32[4,24,32,256]{3,2,1,0:T(8,128)} %st_ref.1), kind=kLoop, calls=%fused_computation.161 | loop fusion | bytes 393216 | tf_op jit(solution)/shard_map/slice | solution.py:380
  8.1 0.6 copy.55
  8.8 0.6 copy.54
  9.4 1.7 %collective-permute-start.1 = (f32[4,24,256]{2,1,0:T(8,128)}, f32[4,24,256]{2,1,0:T(8,128)}, u32[]{:S(2)}, u32[]{:S(2)}) collective-permute-start(f32[4,24,256]{2,1,0:T(8,128)} %bitcast.348), channel_id=1, source_target_pairs={{32,0},{64,32},{96,64},{0,96},{33,1},{65,33},{97,65},{1,97},{34,2}... | collective-permute-start | bytes 294920 | tf_op jit(solution)/shard_map/ppermute | solution.py:380
  11.2 3.6 %fusion.63 = (f32[4,24,32,1]{3,2,1,0:T(8,128)S(1)}, f32[4,24,32,1]{3,2,1,0:T(8,128)}) fusion(f32[4,24,32,256]{3,2,1,0:T(8,128)} %st_ref.1), kind=kLoop, calls=%fused_computation.160 | loop fusion | bytes 49152 | tf_op jit(solution)/shard_map/slice | solution.py:382
  14.8 2.6 %copy.49 = f32[4,24,32,1]{2,1,0,3:T(8,128)} copy(f32[4,24,32,1]{3,2,1,0:T(8,128)} %get-tuple-element.52) | data formatting | bytes 24576
  17.4 3.1 %collective-permute-start.2 = (f32[4,24,32]{2,1,0:T(8,128)}, f32[4,24,32]{2,1,0:T(8,128)}, u32[]{:S(2)}, u32[]{:S(2)}) collective-permute-start(f32[4,24,32]{2,1,0:T(8,128)} %bitcast.2), channel_id=1, source_target_pairs={{0,4},{4,8},{8,12},{12,16},{16,20},{20,24},{24,28},{28,0},{1,5},{5... | collective-permute-start | bytes 36872 | tf_op jit(solution)/shard_map/ppermute | solution.py:381
  20.6 1.2 %copy.50 = f32[4,24,32,1]{2,1,0,3:T(8,128)} copy(f32[4,24,32,1]{3,2,1,0:T(8,128)S(1)} %get-tuple-element.51) | data formatting | bytes 24576
  21.8 2.5 %collective-permute-start.3 = (f32[4,24,32]{2,1,0:T(8,128)}, f32[4,24,32]{2,1,0:T(8,128)}, u32[]{:S(2)}, u32[]{:S(2)}) collective-permute-start(f32[4,24,32]{2,1,0:T(8,128)} %bitcast.4), channel_id=1, source_target_pairs={{4,0},{8,4},{12,8},{16,12},{20,16},{24,20},{28,24},{0,28},{5,1},{9... | collective-permute-start | bytes 36872 | tf_op jit(solution)/shard_map/ppermute | solution.py:382
  24.3 1.5 %slice_bitcast_fusion.17 = f32[2,32,256]{2,1,0:T(8,128)} fusion(f32[2,24,32,256]{3,2,1,0:T(8,128)} %param.9), kind=kLoop, calls=%fused_computation.82 | loop fusion | bytes 131072 | tf_op jit(solution)/shard_map/squeeze | solution.py:374
  25.8 4.6 %collective-permute-start.7 = (f32[2,32,256]{2,1,0:T(8,128)}, f32[2,32,256]{2,1,0:T(8,128)}, u32[]{:S(2)}, u32[]{:S(2)}) collective-permute-start(f32[2,32,256]{2,1,0:T(8,128)} %slice_bitcast_fusion.17), channel_id=1, source_target_pairs={{0,1},{1,2},{2,3},{4,5},{5,6},{6,7},{8,9},{9,10},{10,11},{12,13},{... | collective-permute-start | bytes 196616 | tf_op jit(solution)/shard_map/ppermute | solution.py:374
  30.4 0.7 gather_fusion
  31.6 1.0 gather_fusion.1
  32.8 0.7 fusion.66
  33.6 0.8 slice_reduce_fusion
  34.4 1.0 fusion.5
  35.4 1.7 %compare_select_fusion = (f32[24,32,256]{2,1,0:T(8,128)S(1)}, f32[32,256]{1,0:T(8,128)S(1)}) fusion(s32[32,256]{1,0:T(8,128)S(1)} %get-tuple-element.74.dc_ref, s32[24]{0:T(128)S(1)} %iota_add_fusion.1, f32[4,24,32,256]{3,2,1,0:T(8,128)} %st_ref.1), kind=kLoop, calls=%fused_computation.15 | loop fusion | flops 2351104 | bytes 2424928 | tf_op jit(solution)/shard_map/mul | solution.py:399
  37.1 1.3 %broadcast_multiply_fusion.c_ref = f32[2,24,32,256]{3,2,1,0:T(8,128)} fusion(f32[2,24,32,256]{3,2,1,0:T(8,128)S(1)} %copy-done.2, f32[24,32,256]{2,1,0:T(8,128)S(1)} %get-tuple-element.79), kind=kLoop, calls=%fused_computation.12 | loop fusion | flops 393216 | bytes 3932160 | tf_op jit(solution)/shard_map/mul | solution.py:399
  38.4 0.8 fusion.33
  39.3 0.6 broadcast_select_fusion.1.wind_ref
  39.9 0.7 fusion.46
  40.7 0.7 fusion.49
  41.6 1.5 %multiply_select_fusion.ctop_ref = f32[2,32,256]{2,1,0:T(8,128)} fusion(f32[2,32,256]{2,1,0:T(8,128)} %collective-permute-done.7, f32[32,256]{1,0:T(8,128)S(1)} %fusion.33, pred[]{:T(512)S(6)} %gt.9), kind=kLoop, calls=%fused_computation.81 | loop fusion | flops 32768 | bytes 163841 | tf_op jit(solution)/shard_map/jit(_where)/select_n | solution.py:402
  43.1 5.1 %shard_map.46 = (f32[2,24,32,256]{3,2,1,0:T(8,128)}, f32[2,24,32,256]{3,2,1,0:T(8,128)}, f32[2,24,32,256]{3,2,1,0:T(8,128)}, f32[2,24,32,256]{3,2,1,0:T(8,128)}, f32[8,32,256]{2,1,0:T(8,128)}) custom-call(f32[2,24,32,256]{3,2,1,0:T(8,128)} %broadcast_multiply_fusion.c_ref, f32[2,32,256]{2,1,0:T(8,128)} %multiply_select_fusion.ctop_ref), custom_call_target="tpu_custom_call" | custom-call | tf_op jit(solution)/shard_map/pallas_call | solution.py:130
  48.3 0.8 fusion.39
  49.1 0.8 fusion.36
  49.9 2.8 %collective-permute-start.6 = (f32[36,256]{1,0:T(8,128)S(1)}, f32[36,256]{1,0:T(8,128)S(1)}, u32[]{:S(2)}, u32[]{:S(2)}) collective-permute-start(f32[36,256]{1,0:T(8,128)S(1)} %pad_maximum_fusion), channel_id=1, source_target_pairs={{0,3},{4,7},{8,11},{12,15},{16,19},{20,23},{24,27},{28,31},{32,35}... | collective-permute-start | bytes 110600 | tf_op jit(solution)/shard_map/ppermute | solution.py:418
  52.7 1.3 %collective-permute-start.4 = (f32[36,256]{1,0:T(8,128)S(1)}, f32[36,256]{1,0:T(8,128)S(1)}, u32[]{:S(2)}, u32[]{:S(2)}) collective-permute-start(f32[36,256]{1,0:T(8,128)S(1)} %pad_maximum_fusion), channel_id=1, source_target_pairs={{0,1},{1,2},{2,3},{4,5},{5,6},{6,7},{8,9},{9,10},{10,11},{12,13},{... | collective-permute-start | bytes 110600 | tf_op jit(solution)/shard_map/ppermute | solution.py:418
  54.0 3.4 %collective-permute-start.5 = (f32[36,256]{1,0:T(8,128)S(1)}, f32[36,256]{1,0:T(8,128)S(1)}, u32[]{:S(2)}, u32[]{:S(2)}) collective-permute-start(f32[36,256]{1,0:T(8,128)S(1)} %pad_maximum_fusion), channel_id=1, source_target_pairs={{0,2},{1,3},{4,6},{5,7},{8,10},{9,11},{12,14},{13,15},{16,18},{17,... | collective-permute-start | bytes 110600 | tf_op jit(solution)/shard_map/ppermute | solution.py:418
  57.4 0.6 stack.23.lane_ref
  58.0 2.7 %copy.43.ys_ref = f32[4,24,32,1]{3,2,1,0:T(8,128)} copy(f32[4,24,32,1]{2,1,0,3:T(8,128)} %bitcast.3) | data formatting | bytes 24576 | tf_op jit(solution)/shard_map/broadcast_in_dim | solution.py:430
  60.7 2.6 %copy.44.yn_ref = f32[4,24,32,1]{3,2,1,0:T(8,128)} copy(f32[4,24,32,1]{2,1,0,3:T(8,128)} %bitcast.5) | data formatting | bytes 24576 | tf_op jit(solution)/shard_map/broadcast_in_dim | solution.py:430
  63.9 0.7 copy.45.sys_ref
  64.6 0.7 copy.46.syn_ref
  65.8 15.0 %shard_map.47 = (f32[4,24,32,256]{3,2,1,0:T(8,128)}, f32[8,32,256]{2,1,0:T(8,128)}) custom-call(f32[4,24,32,256]{3,2,1,0:T(8,128)} %st_ref.1, f32[4,24,256]{2,1,0:T(8,128)} %collective-permute-done.xw_ref, f32[4,24,256]{2,1,0:T(8,128)} %collective-permute-done.1.xe_ref, f32[4,24,32,1]{3,2,1,0:T(8,128)} %copy.43.ys_ref, f32[4,24,32,1]{3,2,1,0:T(8,128)} %copy.44.yn_ref, ...), custom_call_target="tpu_custom_call" | custom-call | tf_op jit(solution)/shard_map/pallas_call | solution.py:353
  80.9 1.3 %collective-permute-start.9 = (f32[8,32,256]{2,1,0:T(8,128)}, f32[8,32,256]{2,1,0:T(8,128)S(1)}, u32[]{:S(2)}, u32[]{:S(2)}) collective-permute-start(f32[8,32,256]{2,1,0:T(8,128)} %get-tuple-element.39), channel_id=1, source_target_pairs={{0,2},{1,3},{2,0},{3,1},{4,6},{5,7},{6,4},{7,5},{8,10},{9,11},{10,... | collective-permute-start | bytes 786440 | tf_op jit(solution)/shard_map/ppermute | solution.py:202
  82.2 0.7 collective-permute-start.10
  82.9 7.4 %collective-permute-done.8 = f32[8,32,256]{2,1,0:T(8,128)S(1)} collective-permute-done((f32[8,32,256]{2,1,0:T(8,128)}, f32[8,32,256]{2,1,0:T(8,128)S(1)}, u32[]{:S(2)}, u32[]{:S(2)}) %collective-permute-start.8) | collective-permute-done | bytes 262176 | tf_op jit(solution)/shard_map/ppermute | solution.py:202
  90.2 1.6 %collective-permute-done.9 = f32[8,32,256]{2,1,0:T(8,128)S(1)} collective-permute-done((f32[8,32,256]{2,1,0:T(8,128)}, f32[8,32,256]{2,1,0:T(8,128)S(1)}, u32[]{:S(2)}, u32[]{:S(2)}) %collective-permute-start.9) | collective-permute-done | bytes 262176 | tf_op jit(solution)/shard_map/ppermute | solution.py:202
  91.9 0.7 copy-done.8
  92.6 2.8 %collective-permute-done.10 = f32[8,32,256]{2,1,0:T(8,128)} collective-permute-done((f32[8,32,256]{2,1,0:T(8,128)}, f32[8,32,256]{2,1,0:T(8,128)}, u32[]{:S(2)}, u32[]{:S(2)}) %collective-permute-start.10) | collective-permute-done | bytes 262176 | tf_op jit(solution)/shard_map/ppermute | solution.py:202
  95.3 2.2 %select_bitcast_fusion.2 = (f32[1,8,32,256]{3,2,1,0:T(8,128)S(1)}, f32[1,8,32,256]{3,2,1,0:T(8,128)S(1)}, f32[1,8,32,256]{3,2,1,0:T(8,128)}, f32[1,8,32,256]{3,2,1,0:T(8,128)S(1)}) fusion(f32[8,32,256]{2,1,0:T(8,128)} %copy-done.7, f32[8,32,256]{2,1,0:T(8,128)} %copy-done.8, f32[8,32,256]{2,1,0:T(8,128)} %collective-permute-done.10, ...), kind=kLoop, calls=%fused_computation.18 | loop fusion | flops 786432 | bytes 2097164 | tf_op jit(solution)/shard_map/stack | solution.py:209
  97.5 1.1 subtract_divide_fusion.1
  98.6 1.1 %slice_bitcast_fusion.13 = (f32[2,32,256]{2,1,0:T(8,128)S(1)}, f32[2,32,256]{2,1,0:T(8,128)S(1)}, f32[2,32,256]{2,1,0:T(8,128)S(1)}, f32[2,32,256]{2,1,0:T(8,128...) fusion(f32[4,8,32,256]{3,2,1,0:T(8,128)} %bitcast.351), kind=kLoop, calls=%fused_computation.74 | loop fusion | bytes 786432 | tf_op jit(solution)/shard_map/mul | solution.py:173
  99.8 1.0 subtract_divide_fusion
  100.8 0.9 fusion.28
  102.0 1.6 %copy-done.1 = f32[4,24,32,256]{3,2,1,0:T(8,128)S(1)} copy-done((f32[4,24,32,256]{3,2,1,0:T(8,128)S(1)}, f32[4,24,32,256]{3,2,1,0:T(8,128)}, u32[]{:S(2)}) %copy-start.1) | copy-done | bytes 3145752
  103.6 2.5 %fusion = f32[4,24,32,256]{3,2,1,0:T(8,128)} fusion(f32[4,24,32,256]{3,2,1,0:T(8,128)S(1)} %copy-done.1, f32[2,24,32,256]{3,2,1,0:T(8,128)S(1)} %copy-done.4, f32[4,32,256]{2,1,0:T(8,128)S(1)} %select_select_fusion, f32[2,24,32,256]{3,2,1,0:T(8,128)S(1)} %copy-done.3, f32[4,32,256]{2,1,0:T(8,128)S(1)} %fusion.12), kind=kLoop, calls=%fused_computation.3 | loop fusion | flops 3145728 | bytes 9699328 | tf_op jit(solution)/shard_map/add | solution.py:441
  (60 shorter events, 2.6 us)
Async XLA Ops:
  6.5 23.9 %copy-start = (s32[128,2048]{1,0:T(8,128)S(1)}, s32[128,2048]{1,0:T(8,128)}, u32[]{:S(2)}) copy-start(s32[128,2048]{1,0:T(8,128)} %param.10) | copy-start | bytes 3145732
  6.5 91.0 %all-gather.3.cloned.1.call-start = ((), (), s32[]{:S(2)}) async-start(), calls=%async_computation | async-start | bytes 1310720 | tf_op jit(solution)/shard_map/all_gather | solution.py:404
  8.8 40.2 %collective-permute-start = (f32[4,24,256]{2,1,0:T(8,128)}, f32[4,24,256]{2,1,0:T(8,128)}, u32[]{:S(2)}, u32[]{:S(2)}) collective-permute-start(f32[4,24,256]{2,1,0:T(8,128)} %bitcast.349), channel_id=1, source_target_pairs={{0,32},{32,64},{64,96},{96,0},{1,33},{33,65},{65,97},{97,1},{2,34}... | collective-permute-start | bytes 294920 | tf_op jit(solution)/shard_map/ppermute | solution.py:379
  9.4 38.8 %collective-permute-start.1 = (f32[4,24,256]{2,1,0:T(8,128)}, f32[4,24,256]{2,1,0:T(8,128)}, u32[]{:S(2)}, u32[]{:S(2)}) collective-permute-start(f32[4,24,256]{2,1,0:T(8,128)} %bitcast.348), channel_id=1, source_target_pairs={{32,0},{64,32},{96,64},{0,96},{33,1},{65,33},{97,65},{1,97},{34,2}... | collective-permute-start | bytes 294920 | tf_op jit(solution)/shard_map/ppermute | solution.py:380
  17.4 22.5 %collective-permute-start.2 = (f32[4,24,32]{2,1,0:T(8,128)}, f32[4,24,32]{2,1,0:T(8,128)}, u32[]{:S(2)}, u32[]{:S(2)}) collective-permute-start(f32[4,24,32]{2,1,0:T(8,128)} %bitcast.2), channel_id=1, source_target_pairs={{0,4},{4,8},{8,12},{12,16},{16,20},{20,24},{24,28},{28,0},{1,5},{5... | collective-permute-start | bytes 36872 | tf_op jit(solution)/shard_map/ppermute | solution.py:381
  21.8 18.9 %collective-permute-start.3 = (f32[4,24,32]{2,1,0:T(8,128)}, f32[4,24,32]{2,1,0:T(8,128)}, u32[]{:S(2)}, u32[]{:S(2)}) collective-permute-start(f32[4,24,32]{2,1,0:T(8,128)} %bitcast.4), channel_id=1, source_target_pairs={{4,0},{8,4},{12,8},{16,12},{20,16},{24,20},{28,24},{0,28},{5,1},{9... | collective-permute-start | bytes 36872 | tf_op jit(solution)/shard_map/ppermute | solution.py:382
  25.8 15.8 %collective-permute-start.7 = (f32[2,32,256]{2,1,0:T(8,128)}, f32[2,32,256]{2,1,0:T(8,128)}, u32[]{:S(2)}, u32[]{:S(2)}) collective-permute-start(f32[2,32,256]{2,1,0:T(8,128)} %slice_bitcast_fusion.17), channel_id=1, source_target_pairs={{0,1},{1,2},{2,3},{4,5},{5,6},{6,7},{8,9},{9,10},{10,11},{12,13},{... | collective-permute-start | bytes 196616 | tf_op jit(solution)/shard_map/ppermute | solution.py:374
  33.5 3.5 %copy-start.6 = (s32[32,256]{1,0:T(8,128)}, s32[32,256]{1,0:T(8,128)S(1)}, u32[]{:S(2)}) copy-start(s32[32,256]{1,0:T(8,128)S(1)} %get-tuple-element.74.dc_ref) | copy-start | bytes 98308
  33.6 14.7 %copy-start.10 = (s32[1,256]{1,0:T(1,128)}, s32[1,256]{1,0:T(1,128)S(1)}, u32[]{:S(2)}) copy-start(s32[1,256]{1,0:T(1,128)S(1)} %get-tuple-element.68.dxe_ref) | copy-start | bytes 3076
  33.6 15.5 %copy-start.11 = (s32[1,256]{1,0:T(1,128)}, s32[1,256]{1,0:T(1,128)S(1)}, u32[]{:S(2)}) copy-start(s32[1,256]{1,0:T(1,128)S(1)} %get-tuple-element.69.dxw_ref) | copy-start | bytes 3076
  34.4 2.7 %copy-start.2 = (f32[2,24,32,256]{3,2,1,0:T(8,128)S(1)}, f32[2,24,32,256]{3,2,1,0:T(8,128)}, u32[]{:S(2)}) copy-start(f32[2,24,32,256]{3,2,1,0:T(8,128)} %param.9) | copy-start | bytes 4718596
  37.1 2.2 %copy-start.9 = (f32[2,32,256]{2,1,0:T(8,128)S(1)}, f32[2,32,256]{2,1,0:T(8,128)}, u32[]{:S(2)}) copy-start(f32[2,32,256]{2,1,0:T(8,128)} %param.11) | copy-start | bytes 196612
  49.9 13.4 %collective-permute-start.6 = (f32[36,256]{1,0:T(8,128)S(1)}, f32[36,256]{1,0:T(8,128)S(1)}, u32[]{:S(2)}, u32[]{:S(2)}) collective-permute-start(f32[36,256]{1,0:T(8,128)S(1)} %pad_maximum_fusion), channel_id=1, source_target_pairs={{0,3},{4,7},{8,11},{12,15},{16,19},{20,23},{24,27},{28,31},{32,35}... | collective-permute-start | bytes 110600 | tf_op jit(solution)/shard_map/ppermute | solution.py:418
  52.7 10.6 %collective-permute-start.4 = (f32[36,256]{1,0:T(8,128)S(1)}, f32[36,256]{1,0:T(8,128)S(1)}, u32[]{:S(2)}, u32[]{:S(2)}) collective-permute-start(f32[36,256]{1,0:T(8,128)S(1)} %pad_maximum_fusion), channel_id=1, source_target_pairs={{0,1},{1,2},{2,3},{4,5},{5,6},{6,7},{8,9},{9,10},{10,11},{12,13},{... | collective-permute-start | bytes 110600 | tf_op jit(solution)/shard_map/ppermute | solution.py:418
  54.0 9.3 %collective-permute-start.5 = (f32[36,256]{1,0:T(8,128)S(1)}, f32[36,256]{1,0:T(8,128)S(1)}, u32[]{:S(2)}, u32[]{:S(2)}) collective-permute-start(f32[36,256]{1,0:T(8,128)S(1)} %pad_maximum_fusion), channel_id=1, source_target_pairs={{0,2},{1,3},{4,6},{5,7},{8,10},{9,11},{12,14},{13,15},{16,18},{17,... | collective-permute-start | bytes 110600 | tf_op jit(solution)/shard_map/ppermute | solution.py:418
  80.8 9.4 %collective-permute-start.8 = (f32[8,32,256]{2,1,0:T(8,128)}, f32[8,32,256]{2,1,0:T(8,128)S(1)}, u32[]{:S(2)}, u32[]{:S(2)}) collective-permute-start(f32[8,32,256]{2,1,0:T(8,128)} %get-tuple-element.39), channel_id=1, source_target_pairs={{0,3},{1,0},{2,1},{3,2},{4,7},{5,4},{6,5},{7,6},{8,11},{9,8},{10,9... | collective-permute-start | bytes 786440 | tf_op jit(solution)/shard_map/ppermute | solution.py:202
  80.9 11.0 %collective-permute-start.9 = (f32[8,32,256]{2,1,0:T(8,128)}, f32[8,32,256]{2,1,0:T(8,128)S(1)}, u32[]{:S(2)}, u32[]{:S(2)}) collective-permute-start(f32[8,32,256]{2,1,0:T(8,128)} %get-tuple-element.39), channel_id=1, source_target_pairs={{0,2},{1,3},{2,0},{3,1},{4,6},{5,7},{6,4},{7,5},{8,10},{9,11},{10,... | collective-permute-start | bytes 786440 | tf_op jit(solution)/shard_map/ppermute | solution.py:202
  82.2 13.1 %collective-permute-start.10 = (f32[8,32,256]{2,1,0:T(8,128)}, f32[8,32,256]{2,1,0:T(8,128)}, u32[]{:S(2)}, u32[]{:S(2)}) collective-permute-start(f32[8,32,256]{2,1,0:T(8,128)} %get-tuple-element.39), channel_id=1, source_target_pairs={{0,1},{1,2},{2,3},{3,0},{4,5},{5,6},{6,7},{7,4},{8,9},{9,10},{10,1... | collective-permute-start | bytes 786440 | tf_op jit(solution)/shard_map/ppermute | solution.py:202
  90.2 1.6 %copy-start.7 = (f32[8,32,256]{2,1,0:T(8,128)}, f32[8,32,256]{2,1,0:T(8,128)S(1)}, u32[]{:S(2)}) copy-start(f32[8,32,256]{2,1,0:T(8,128)S(1)} %collective-permute-done.8) | copy-start | bytes 786436
  91.9 0.7 copy-start.8
  95.3 6.6 %copy-start.4 = (f32[2,24,32,256]{3,2,1,0:T(8,128)S(1)}, f32[2,24,32,256]{3,2,1,0:T(8,128)}, u32[]{:S(2)}) copy-start(f32[2,24,32,256]{3,2,1,0:T(8,128)} %get-tuple-element.42) | copy-start | bytes 4718596
  97.5 4.1 %copy-start.5 = (f32[1,8,32,256]{3,2,1,0:T(8,128)S(1)}, f32[1,8,32,256]{3,2,1,0:T(8,128)}, u32[]{:S(2)}) copy-start(f32[1,8,32,256]{3,2,1,0:T(8,128)} %get-tuple-element.64) | copy-start | bytes 786436
  98.6 3.4 %copy-start.3 = (f32[2,24,32,256]{3,2,1,0:T(8,128)S(1)}, f32[2,24,32,256]{3,2,1,0:T(8,128)}, u32[]{:S(2)}) copy-start(f32[2,24,32,256]{3,2,1,0:T(8,128)} %get-tuple-element.41) | copy-start | bytes 4718596
  101.7 1.9 %copy-start.1 = (f32[4,24,32,256]{3,2,1,0:T(8,128)S(1)}, f32[4,24,32,256]{3,2,1,0:T(8,128)}, u32[]{:S(2)}) copy-start(f32[4,24,32,256]{3,2,1,0:T(8,128)} %get-tuple-element.38) | copy-start | bytes 9437188
Sparse Core Ops, SparseCore 0:
  48.4 23.5 all-gather.2

commit v8 on v5

--- a/solution.py
+++ b/solution.py
@@ -221,8 +221,11 @@
                  dxw_ref, dxe_ref, dys_ref, dyn_ref,
                  sc_ref, sxw_ref, sxe_ref, sys_ref, syn_ref,
                  lane_ref, wind_ref, c_ref, inv_ref, ratio_ref,
-                 y_ref, ends_ref):
-    fields, levels, nx, ny = st_ref.shape
+                 y_ref, ends_ref,
+                 run_c_s, run_xw_s, run_xe_s, run_ys_s, run_yn_s, vy_s, cprev_s):
+    fields, chunk, nx, ny = st_ref.shape
+    levels = y_ref.shape[1]
+    step_i = pl.program_id(0)
     row = lax.broadcasted_iota(jnp.int32, (nx, ny), 0)
     lane = lax.broadcasted_iota(jnp.int32, (nx, ny), 1)
     wall_n = lane_ref[0:1]
@@ -231,6 +234,16 @@
     d_c, d_e, d_w, d_n, d_s = dc_ref[...], de_ref[...], dw_ref[...], dn_ref[...], ds_ref[...]
     d_xw, d_xe, d_ys, d_yn = dxw_ref[...], dxe_ref[...], dys_ref[...], dyn_ref[...]
 
+    @pl.when(step_i == 0)
+    def _():
+        run_c_s[...] = jnp.zeros_like(run_c_s)
+        run_xw_s[...] = jnp.zeros_like(run_xw_s)
+        run_xe_s[...] = jnp.zeros_like(run_xe_s)
+        run_ys_s[...] = jnp.zeros_like(run_ys_s)
+        run_yn_s[...] = jnp.zeros_like(run_yn_s)
+        vy_s[...] = jnp.zeros_like(vy_s)
+        cprev_s[...] = jnp.zeros_like(cprev_s)
+
     def east(r, h):
         return jnp.where(row == nx - 1, h, pltpu.roll(r, nx - 1, 0))
 
@@ -243,7 +256,9 @@
     def south(r, h):
         return jnp.where(lane == 0, h, pltpu.roll(r, 1, 1))
 
-    def level(k, run, vy_prev):
+    def level(kk, carry):
+        run, vy_prev, c_prev = carry
+        k = step_i * chunk + kk
         wc = (k < d_c).astype(jnp.float32)
         we = (k < d_e).astype(jnp.float32)
         ww = (k < d_w).astype(jnp.float32)
@@ -253,11 +268,11 @@
         wxe = (k < d_xe).astype(jnp.float32)
         wys = (k < d_ys).astype(jnp.float32)
         wyn = (k < d_yn).astype(jnp.float32)
-        cen = [st_ref[f, k] for f in range(fields)]
+        cen = [st_ref[f, kk] for f in range(fields)]
         hxw = [xw_ref[f, pl.ds(k, 1), :] for f in range(fields)]
         hxe = [xe_ref[f, pl.ds(k, 1), :] for f in range(fields)]
-        hys = [ys_ref[f, k] for f in range(fields)]
-        hyn = [yn_ref[f, k] for f in range(fields)]
+        hys = [ys_ref[f, kk] for f in range(fields)]
+        hyn = [yn_ref[f, kk] for f in range(fields)]
         run_c, run_xw, run_xe, run_ys, run_yn = run
         den_c = _density(cen[0], cen[1], wc)
         den_xw = _density(hxw[0], hxw[1], wxw)
@@ -301,60 +316,67 @@
         grad_y = 0.5 * (face_n * (p_n - p_c) + face_s * (p_c - p_s))
         east_new = moved[2] + cor03 * cen[3] - grad_x
         north_new = moved[3] - cor03 * cen[2] - grad_y
-        forced = [moved[0] * wc, moved[1] * wc, east_new * wc, north_new * wc]
-        if isinstance(k, int) and k == 0:
-            forced[2] = forced[2] + wind_ref[0] * wc
-            forced[3] = forced[3] + wind_ref[1] * wc
+        top = (k == 0).astype(jnp.float32)
+        forced = [moved[0] * wc, moved[1] * wc,
+                  east_new * wc + wind_ref[0] * wc * top,
+                  north_new * wc + wind_ref[1] * wc * top]
         vy = []
         for f in range(fields):
             m = f // 2
-            inv = inv_ref[m, k]
-            if vy_prev is None:
-                val = forced[f] * inv
-            else:
-                val = (forced[f] + c_ref[m, k - 1] * vy_prev[f]) * inv
+            val = (forced[f] + c_prev[m] * vy_prev[f]) * inv_ref[m, kk]
             y_ref[f, k] = val
             vy.append(val)
-        return (run_c, run_xw, run_xe, run_ys, run_yn), vy
-
-    run0 = (jnp.zeros((nx, ny), jnp.float32), jnp.zeros((1, ny), jnp.float32),
-            jnp.zeros((1, ny), jnp.float32), jnp.zeros((nx, 1), jnp.float32),
-            jnp.zeros((nx, 1), jnp.float32))
-    run, vy = level(0, run0, None)
-
-    def step(k, carry):
-        run, vy = carry
-        run, vy = level(k, run, vy)
-        return run, vy
-
-    run, vy = lax.fori_loop(1, levels, step, (run, vy), unroll=2)
-    for f in range(fields):
-        ends_ref[fields + f] = vy[f]
-
-    def back(j, later):
-        k = levels - 2 - j
-        out = []
+        c_here = jnp.stack([c_ref[0, kk], c_ref[1, kk]])
+        return (run_c, run_xw, run_xe, run_ys, run_yn), jnp.stack(vy), c_here
+
+    run = (run_c_s[...], run_xw_s[...], run_xe_s[...], run_ys_s[...], run_yn_s[...])
+    carry = lax.fori_loop(0, chunk, level, (run, vy_s[...], cprev_s[...]), unroll=2)
+    run, vy, c_prev = carry
+    run_c_s[...], run_xw_s[...], run_xe_s[...], run_ys_s[...], run_yn_s[...] = run
+    vy_s[...] = vy
+    cprev_s[...] = c_prev
+
+    @pl.when(step_i == pl.num_programs(0) - 1)
+    def _():
         for f in range(fields):
-            val = y_ref[f, k] + ratio_ref[f // 2, k] * later[f]
-            y_ref[f, k] = val
-            out.append(val)
-        return out
-
-    later = lax.fori_loop(0, levels - 1, back, vy, unroll=2)
-    for f in range(fields):
-        ends_ref[f] = later[f]
+            ends_ref[fields + f] = vy[f]
+
+        def back(j, later):
+            k = levels - 2 - j
+            out = []
+            for f in range(fields):
+                val = y_ref[f, k] + ratio_ref[f // 2, k] * later[f]
+                y_ref[f, k] = val
+                out.append(val)
+            return jnp.stack(out)
+
+        later = lax.fori_loop(0, levels - 1, back, vy, unroll=2)
+        for f in range(fields):
+            ends_ref[f] = later[f]
 
 
 def fused_solve(*operands):
     st = operands[0]
     fields, levels, nx, ny = st.shape
-    vmem = pl.BlockSpec(memory_space=pltpu.VMEM)
+    pairs = operands[21].shape[0]
+    chunk = 8 if levels % 8 == 0 else levels
+    whole = [pl.BlockSpec(op.shape, (lambda i, n=op.ndim: (0,) * n)) for op in operands]
+    by_level = lambda op: pl.BlockSpec((op.shape[0], chunk) + op.shape[2:], lambda i: (0, i, 0, 0))
+    specs = list(whole)
+    for idx in (0, 3, 4, 21, 22):
+        specs[idx] = by_level(operands[idx])
     return pl.pallas_call(
         fused_kernel,
-        in_specs=[vmem] * len(operands),
-        out_specs=[vmem, vmem],
+        grid=(levels // chunk,),
+        in_specs=specs,
+        out_specs=[pl.BlockSpec(st.shape, lambda i: (0, 0, 0, 0)),
+                   pl.BlockSpec((2 * fields, nx, ny), lambda i: (0, 0, 0))],
         out_shape=[jax.ShapeDtypeStruct(st.shape, jnp.float32),
                    jax.ShapeDtypeStruct((2 * fields, nx, ny), jnp.float32)],
+        scratch_shapes=[pltpu.VMEM((nx, ny), jnp.float32), pltpu.VMEM((1, ny), jnp.float32),
+                        pltpu.VMEM((1, ny), jnp.float32), pltpu.VMEM((nx, 1), jnp.float32),
+                        pltpu.VMEM((nx, 1), jnp.float32), pltpu.VMEM((fields, nx, ny), jnp.float32),
+                        pltpu.VMEM((pairs, nx, ny), jnp.float32)],
         compiler_params=pltpu.CompilerParams(vmem_limit_bytes=60 * 1024 * 1024),
     )(*operands)
 

time: 101 us -> 99.9 us (0.989)
  Pallas kernels: 20.1 us -> 18.9 us
    pallas_call x1, Pallas kernels: 15 us -> 13.8 us  [fused_solve(): pl.pallas_call(fused_kernel, grid=(levels // chunk,), in_specs=specs, out...]
  transfers between devices with their start and end apart: 12 -> 12, of which waited for: 1 -> 1; matrix products, arithmetic and copies ran while one was open for 20% -> 20% of each run, Pallas kernels for 20% -> 19%
where the time goes in v8:
time: 99.9 us; the launch traced here: 99.4 us
  starting transfers between devices  23.5 us (24%)
  local copies, waits for them, and re-layouts  23 us (23%)
  Pallas kernels  18.9 us (19%)
  between operations  13.8 us (14%)
  waiting for transfers between devices  11.4 us (11%)
  other arithmetic  8.86 us (9%)
    pallas_call x1, Pallas kernels, fused_solve(): pl.pallas_call(fused_kernel, grid=(levels // chunk,), in_specs=specs, out...  13.8 us
    ppermute x3, waiting for transfers between devices, gather_by_permutes(): received.append(lax.ppermute(part, axis, shift))  11.3 us
    ppermute x3, starting transfers between devices, per_device(): shallower = shallower + lax.ppermute(pack, 'gz', pairs_z)  8.7 us
    pallas_call x1, Pallas kernels, coupling_solve(): pl.pallas_call(coupling_kernel, grid=(cols_x // bx,), in_specs=[cspec, _p...  5.11 us
    unnamed x26, local copies, waits for them, and re-layouts  4.58 us
    ppermute x1, starting transfers between devices, per_device(): mix_above = lax.ppermute(mixing[:, lev_count - 1], 'gz', down_z)  3.93 us
    slice x1, local copies, waits for them, and re-layouts, per_device(): halo_yn = lax.ppermute(state[:, :, :, 0], 'gy', dn_y)  3.7 us
    ppermute x3, starting transfers between devices, gather_by_permutes(): received.append(lax.ppermute(part, axis, shift))  3.3 us
  transfers between devices with their start and end apart: 12, of which 1 were waited for; matrix products, arithmetic and copies ran while one was open for 20% of the time, Pallas kernels for 19%

profile of v8, /device:TPU:0, one launch (start us, length us, event | category | flops | bytes accessed | tf_op | source)
XLA Modules:
  0.0 99.4 jit_solution(3774120519107433319)
XLA Ops:
  6.5 3.7 %fusion.48 = (f32[4,24,32,1]{3,2,1,0:T(8,128)S(1)}, f32[4,24,32,1]{3,2,1,0:T(8,128)}) fusion(f32[4,24,32,256]{3,2,1,0:T(8,128)} %st_ref.1), kind=kLoop, calls=%fused_computation.140 | loop fusion | bytes 49152 | tf_op jit(solution)/shard_map/slice | solution.py:403
  10.2 2.0 %copy.49 = f32[4,24,32,1]{2,1,0,3:T(8,128)S(1)} copy(f32[4,24,32,1]{3,2,1,0:T(8,128)} %get-tuple-element.46) | data formatting | bytes 24576
  12.3 3.2 %collective-permute-start.2 = (f32[4,24,32]{2,1,0:T(8,128)S(1)}, f32[4,24,32]{2,1,0:T(8,128)S(1)}, u32[]{:S(2)}, u32[]{:S(2)}) collective-permute-start(f32[4,24,32]{2,1,0:T(8,128)S(1)} %bitcast.311), channel_id=1, source_target_pairs={{0,4},{4,8},{8,12},{12,16},{16,20},{20,24},{24,28},{28,0},{1,5},{5... | collective-permute-start | bytes 36872 | tf_op jit(solution)/shard_map/ppermute | solution.py:402
  15.5 0.6 copy.50
  16.1 2.6 %collective-permute-start.3 = (f32[4,24,32]{2,1,0:T(8,128)S(1)}, f32[4,24,32]{2,1,0:T(8,128)S(1)}, u32[]{:S(2)}, u32[]{:S(2)}) collective-permute-start(f32[4,24,32]{2,1,0:T(8,128)S(1)} %bitcast.310), channel_id=1, source_target_pairs={{4,0},{8,4},{12,8},{16,12},{20,16},{24,20},{28,24},{0,28},{5,1},{9... | collective-permute-start | bytes 36872 | tf_op jit(solution)/shard_map/ppermute | solution.py:403
  18.6 1.5 %fusion.49 = (f32[4,24,1,256]{3,2,1,0:T(1,128)S(1)}, f32[4,24,1,256]{3,2,1,0:T(1,128)S(1)}) fusion(f32[4,24,32,256]{3,2,1,0:T(8,128)} %st_ref.1), kind=kLoop, calls=%fused_computation.141 | loop fusion | bytes 393216 | tf_op jit(solution)/shard_map/slice | solution.py:401
  20.2 0.1 collective-permute-start
  20.3 1.8 %collective-permute-start.1 = (f32[4,24,256]{2,1,0:T(8,128)S(1)}, f32[4,24,256]{2,1,0:T(8,128)S(1)}, u32[]{:S(2)}, u32[]{:S(2)}) collective-permute-start(f32[4,24,256]{2,1,0:T(8,128)S(1)} %bitcast.309), channel_id=1, source_target_pairs={{32,0},{64,32},{96,64},{0,96},{33,1},{65,33},{97,65},{1,97},{34,2}... | collective-permute-start | bytes 294920 | tf_op jit(solution)/shard_map/ppermute | solution.py:401
  22.1 0.8 slice_bitcast_fusion.17
  22.9 3.9 %collective-permute-start.7 = (f32[2,32,256]{2,1,0:T(8,128)S(1)}, f32[2,32,256]{2,1,0:T(8,128)S(1)}, u32[]{:S(2)}, u32[]{:S(2)}) collective-permute-start(f32[2,32,256]{2,1,0:T(8,128)S(1)} %slice_bitcast_fusion.17), channel_id=1, source_target_pairs={{0,1},{1,2},{2,3},{4,5},{5,6},{6,7},{8,9},{9,10},{10,11},{12,13},{... | collective-permute-start | bytes 196616 | tf_op jit(solution)/shard_map/ppermute | solution.py:395
  27.0 0.7 gather_fusion
  27.6 0.1 broadcast_select_fusion
  27.7 0.4 copy.40
  28.1 1.0 %gather_fusion.1 = s32[258,34]{1,0:T(8,128)S(1)} fusion(s32[34,2048]{0,1:T(8,128)S(1)} %copy.40, s32[1024]{0:T(1024)S(1)} %pad_clamp_fusion), kind=kCustom, calls=%fused_computation.1 | custom fusion | bytes 71208 | tf_op jit(solution)/shard_map/jit(_take)/gather | solution.py:407
  29.2 0.1 copy.41
  29.3 0.8 slice_reduce_fusion
  30.1 0.7 fusion.51
  30.8 0.1 fusion.50
  30.9 0.1 fusion.5
  31.0 1.7 %compare_select_fusion = (f32[24,32,256]{2,1,0:T(8,128)S(1)}, f32[32,256]{1,0:T(8,128)S(1)}) fusion(s32[32,256]{1,0:T(8,128)S(1)} %get-tuple-element.61.dc_ref, s32[24]{0:T(128)S(1)} %iota_add_fusion.1, f32[4,24,32,256]{3,2,1,0:T(8,128)} %st_ref.1), kind=kLoop, calls=%fused_computation.15 | loop fusion | flops 2351104 | bytes 2424928 | tf_op jit(solution)/shard_map/mul | solution.py:420
  32.7 0.1 fusion.21
  32.8 1.3 %broadcast_multiply_fusion.c_ref = f32[2,24,32,256]{3,2,1,0:T(8,128)} fusion(f32[2,24,32,256]{3,2,1,0:T(8,128)S(1)} %copy-done.2, f32[24,32,256]{2,1,0:T(8,128)S(1)} %get-tuple-element.66), kind=kLoop, calls=%fused_computation.12 | loop fusion | flops 393216 | bytes 3932160 | tf_op jit(solution)/shard_map/mul | solution.py:420
  34.1 0.6 broadcast_select_fusion.1.wind_ref
  34.8 0.2 scatter.9
  35.0 0.6 multiply_select_fusion.ctop_ref
  35.7 5.1 %shard_map.46 = (f32[2,24,32,256]{3,2,1,0:T(8,128)}, f32[2,24,32,256]{3,2,1,0:T(8,128)}, f32[2,24,32,256]{3,2,1,0:T(8,128)}, f32[2,24,32,256]{3,2,1,0:T(8,128)}, f32[8,32,256]{2,1,0:T(8,128)}) custom-call(f32[2,24,32,256]{3,2,1,0:T(8,128)} %broadcast_multiply_fusion.c_ref, f32[2,32,256]{2,1,0:T(8,128)} %multiply_select_fusion.ctop_ref), custom_call_target="tpu_custom_call" | custom-call | tf_op jit(solution)/shard_map/pallas_call | solution.py:130
  40.9 3.8 %collective-permute-start.4 = (f32[36,256]{1,0:T(8,128)S(1)}, f32[36,256]{1,0:T(8,128)S(1)}, u32[]{:S(2)}, u32[]{:S(2)}) collective-permute-start(f32[36,256]{1,0:T(8,128)S(1)} %pad_maximum_fusion), channel_id=1, source_target_pairs={{0,1},{1,2},{2,3},{4,5},{5,6},{6,7},{8,9},{9,10},{10,11},{12,13},{... | collective-permute-start | bytes 110600 | tf_op jit(solution)/shard_map/ppermute | solution.py:439
  44.8 3.6 %collective-permute-start.5 = (f32[36,256]{1,0:T(8,128)S(1)}, f32[36,256]{1,0:T(8,128)S(1)}, u32[]{:S(2)}, u32[]{:S(2)}) collective-permute-start(f32[36,256]{1,0:T(8,128)S(1)} %pad_maximum_fusion), channel_id=1, source_target_pairs={{0,2},{1,3},{4,6},{5,7},{8,10},{9,11},{12,14},{13,15},{16,18},{17,... | collective-permute-start | bytes 110600 | tf_op jit(solution)/shard_map/ppermute | solution.py:439
  48.4 1.3 %collective-permute-start.6 = (f32[36,256]{1,0:T(8,128)S(1)}, f32[36,256]{1,0:T(8,128)S(1)}, u32[]{:S(2)}, u32[]{:S(2)}) collective-permute-start(f32[36,256]{1,0:T(8,128)S(1)} %pad_maximum_fusion), channel_id=1, source_target_pairs={{0,3},{4,7},{8,11},{12,15},{16,19},{20,23},{24,27},{28,31},{32,35}... | collective-permute-start | bytes 110600 | tf_op jit(solution)/shard_map/ppermute | solution.py:439
  49.7 0.6 stack.23.lane_ref
  50.3 1.9 %copy.43.ys_ref = f32[4,24,32,1]{3,2,1,0:T(8,128)} copy(f32[4,24,32,1]{2,1,0,3:T(8,128)S(1)} %bitcast.306) | data formatting | bytes 24576 | tf_op jit(solution)/shard_map/broadcast_in_dim | solution.py:451
  52.2 1.8 %copy.44.yn_ref = f32[4,24,32,1]{3,2,1,0:T(8,128)} copy(f32[4,24,32,1]{2,1,0,3:T(8,128)S(1)} %bitcast.307) | data formatting | bytes 24576 | tf_op jit(solution)/shard_map/broadcast_in_dim | solution.py:451
  54.0 0.6 slice.288.sc_ref
  54.6 0.7 copy.45.sys_ref
  55.3 0.7 copy.46.syn_ref
  56.0 0.6 fusion.52
  56.6 13.8 %shard_map.47 = (f32[4,24,32,256]{3,2,1,0:T(8,128)}, f32[8,32,256]{2,1,0:T(8,128)}) custom-call(f32[4,24,32,256]{3,2,1,0:T(8,128)} %st_ref.1, f32[4,24,256]{2,1,0:T(8,128)} %copy-done.6, f32[4,24,256]{2,1,0:T(8,128)} %copy-done.7, f32[4,24,32,1]{3,2,1,0:T(8,128)} %copy.43.ys_ref, f32[4,24,32,1]{3,2,1,0:T(8,128)} %copy.44.yn_ref, s32[32,256]{1,0:T(8,128)} %copy-done.5, ...), custom_call_target="tpu_custom_call" | custom-call | tf_op jit(solution)/shard_map/pallas_call | solution.py:368
  70.4 0.1 collective-permute-start.10
  70.4 3.2 %collective-permute-start.8 = (f32[8,32,256]{2,1,0:T(8,128)}, f32[8,32,256]{2,1,0:T(8,128)S(1)}, u32[]{:S(2)}, u32[]{:S(2)}) collective-permute-start(f32[8,32,256]{2,1,0:T(8,128)} %get-tuple-element.39), channel_id=1, source_target_pairs={{0,3},{1,0},{2,1},{3,2},{4,7},{5,4},{6,5},{7,6},{8,11},{9,8},{10,9... | collective-permute-start | bytes 786440 | tf_op jit(solution)/shard_map/ppermute | solution.py:201
  73.7 11.3 %collective-permute-done.10 = f32[8,32,256]{2,1,0:T(8,128)S(1)} collective-permute-done((f32[8,32,256]{2,1,0:T(8,128)}, f32[8,32,256]{2,1,0:T(8,128)S(1)}, u32[]{:S(2)}, u32[]{:S(2)}) %collective-permute-start.10) | collective-permute-done | bytes 262176 | tf_op jit(solution)/shard_map/ppermute | solution.py:201
  85.0 1.1 %select_bitcast_fusion.2 = (f32[1,8,32,256]{3,2,1,0:T(8,128)S(1)}, f32[1,8,32,256]{3,2,1,0:T(8,128)S(1)}, f32[1,8,32,256]{3,2,1,0:T(8,128)S(1)}, f32[1,8,32,256]{3,2,1,0:T(8,128)S(1)}) fusion(f32[8,32,256]{2,1,0:T(8,128)S(1)} %collective-permute-done.8, f32[8,32,256]{2,1,0:T(8,128)S(1)} %collective-permute-done.9, ...), kind=kLoop, calls=%fused_computation.18 | loop fusion | flops 786432 | bytes 2097164 | tf_op jit(solution)/shard_map/stack | solution.py:208
  86.1 0.0 all-gather.3.cloned.1.call-done
  86.2 1.6 %broadcast_in_dim.61 = f32[4,8,2,32,256]{4,3,2,1,0:T(8,128)S(1)} broadcast(f32[4,8,32,256]{3,2,1,0:T(8,128)} %bitcast.305), dimensions={0,1,3,4} | broadcast | bytes 3145728 | tf_op jit(solution)/shard_map/broadcast_in_dim | solution.py:160
  87.8 0.2 select_select_fusion
  88.0 0.3 select_select_fusion.1
  88.3 1.4 %copy-done.1 = f32[4,24,32,256]{3,2,1,0:T(8,128)S(1)} copy-done((f32[4,24,32,256]{3,2,1,0:T(8,128)S(1)}, f32[4,24,32,256]{3,2,1,0:T(8,128)}, u32[]{:S(2)}) %copy-start.1) | copy-done | bytes 3145752
  89.7 0.5 copy-done.3
  90.1 2.5 %fusion = f32[4,24,32,256]{3,2,1,0:T(8,128)} fusion(f32[4,24,32,256]{3,2,1,0:T(8,128)S(1)} %copy-done.1, f32[2,24,32,256]{3,2,1,0:T(8,128)S(1)} %copy-done.4, f32[4,32,256]{2,1,0:T(8,128)S(1)} %select_select_fusion, f32[2,24,32,256]{3,2,1,0:T(8,128)S(1)} %copy-done.3, f32[4,32,256]{2,1,0:T(8,128)S(1)} %select_select_fusion.1), kind=kLoop, calls=%fused_computation.3 | loop fusion | flops 3145728 | bytes 9699328 | tf_op jit(solution)/shard_map/add | solution.py:460
  (55 shorter events, 0.4 us)
Async XLA Ops:
  6.5 20.4 %copy-start = (s32[128,2048]{1,0:T(8,128)S(1)}, s32[128,2048]{1,0:T(8,128)}, u32[]{:S(2)}) copy-start(s32[128,2048]{1,0:T(8,128)} %param.10) | copy-start | bytes 3145732
  6.5 79.6 %all-gather.3.cloned.1.call-start = ((), (), s32[]{:S(2)}) async-start(), calls=%async_computation | async-start | bytes 1310720 | tf_op jit(solution)/shard_map/all_gather | solution.py:425
  12.3 22.5 %collective-permute-start.2 = (f32[4,24,32]{2,1,0:T(8,128)S(1)}, f32[4,24,32]{2,1,0:T(8,128)S(1)}, u32[]{:S(2)}, u32[]{:S(2)}) collective-permute-start(f32[4,24,32]{2,1,0:T(8,128)S(1)} %bitcast.311), channel_id=1, source_target_pairs={{0,4},{4,8},{8,12},{12,16},{16,20},{20,24},{24,28},{28,0},{1,5},{5... | collective-permute-start | bytes 36872 | tf_op jit(solution)/shard_map/ppermute | solution.py:402
  16.1 18.7 %collective-permute-start.3 = (f32[4,24,32]{2,1,0:T(8,128)S(1)}, f32[4,24,32]{2,1,0:T(8,128)S(1)}, u32[]{:S(2)}, u32[]{:S(2)}) collective-permute-start(f32[4,24,32]{2,1,0:T(8,128)S(1)} %bitcast.310), channel_id=1, source_target_pairs={{4,0},{8,4},{12,8},{16,12},{20,16},{24,20},{28,24},{0,28},{5,1},{9... | collective-permute-start | bytes 36872 | tf_op jit(solution)/shard_map/ppermute | solution.py:403
  20.2 20.6 %collective-permute-start = (f32[4,24,256]{2,1,0:T(8,128)S(1)}, f32[4,24,256]{2,1,0:T(8,128)S(1)}, u32[]{:S(2)}, u32[]{:S(2)}) collective-permute-start(f32[4,24,256]{2,1,0:T(8,128)S(1)} %bitcast.308), channel_id=1, source_target_pairs={{0,32},{32,64},{64,96},{96,0},{1,33},{33,65},{65,97},{97,1},{2,34}... | collective-permute-start | bytes 294920 | tf_op jit(solution)/shard_map/ppermute | solution.py:400
  20.3 20.6 %collective-permute-start.1 = (f32[4,24,256]{2,1,0:T(8,128)S(1)}, f32[4,24,256]{2,1,0:T(8,128)S(1)}, u32[]{:S(2)}, u32[]{:S(2)}) collective-permute-start(f32[4,24,256]{2,1,0:T(8,128)S(1)} %bitcast.309), channel_id=1, source_target_pairs={{32,0},{64,32},{96,64},{0,96},{33,1},{65,33},{97,65},{1,97},{34,2}... | collective-permute-start | bytes 294920 | tf_op jit(solution)/shard_map/ppermute | solution.py:401
  22.9 12.1 %collective-permute-start.7 = (f32[2,32,256]{2,1,0:T(8,128)S(1)}, f32[2,32,256]{2,1,0:T(8,128)S(1)}, u32[]{:S(2)}, u32[]{:S(2)}) collective-permute-start(f32[2,32,256]{2,1,0:T(8,128)S(1)} %slice_bitcast_fusion.17), channel_id=1, source_target_pairs={{0,1},{1,2},{2,3},{4,5},{5,6},{6,7},{8,9},{9,10},{10,11},{12,13},{... | collective-permute-start | bytes 196616 | tf_op jit(solution)/shard_map/ppermute | solution.py:395
  29.2 3.6 %copy-start.2 = (f32[2,24,32,256]{3,2,1,0:T(8,128)S(1)}, f32[2,24,32,256]{3,2,1,0:T(8,128)}, u32[]{:S(2)}) copy-start(f32[2,24,32,256]{3,2,1,0:T(8,128)} %param.9) | copy-start | bytes 4718596
  30.8 3.3 %copy-start.5 = (s32[32,256]{1,0:T(8,128)}, s32[32,256]{1,0:T(8,128)S(1)}, u32[]{:S(2)}) copy-start(s32[32,256]{1,0:T(8,128)S(1)} %get-tuple-element.61.dc_ref) | copy-start | bytes 98308
  30.9 9.9 %copy-start.10 = (s32[1,256]{1,0:T(1,128)}, s32[1,256]{1,0:T(1,128)S(1)}, u32[]{:S(2)}) copy-start(s32[1,256]{1,0:T(1,128)S(1)} %get-tuple-element.56.dxw_ref) | copy-start | bytes 3076
  30.9 10.0 %copy-start.9 = (s32[1,256]{1,0:T(1,128)}, s32[1,256]{1,0:T(1,128)S(1)}, u32[]{:S(2)}) copy-start(s32[1,256]{1,0:T(1,128)S(1)} %get-tuple-element.55.dxe_ref) | copy-start | bytes 3076
  32.7 1.4 %copy-start.8 = (f32[2,32,256]{2,1,0:T(8,128)S(1)}, f32[2,32,256]{2,1,0:T(8,128)}, u32[]{:S(2)}) copy-start(f32[2,32,256]{2,1,0:T(8,128)} %param.11) | copy-start | bytes 196612
  40.8 15.8 %copy-start.6 = (f32[4,24,256]{2,1,0:T(8,128)}, f32[4,24,256]{2,1,0:T(8,128)S(1)}, u32[]{:S(2)}) copy-start(f32[4,24,256]{2,1,0:T(8,128)S(1)} %collective-permute-done.xw_ref) | copy-start | bytes 294916
  40.9 15.7 %copy-start.7 = (f32[4,24,256]{2,1,0:T(8,128)}, f32[4,24,256]{2,1,0:T(8,128)S(1)}, u32[]{:S(2)}) copy-start(f32[4,24,256]{2,1,0:T(8,128)S(1)} %collective-permute-done.1.xe_ref) | copy-start | bytes 294916
  40.9 13.1 %collective-permute-start.4 = (f32[36,256]{1,0:T(8,128)S(1)}, f32[36,256]{1,0:T(8,128)S(1)}, u32[]{:S(2)}, u32[]{:S(2)}) collective-permute-start(f32[36,256]{1,0:T(8,128)S(1)} %pad_maximum_fusion), channel_id=1, source_target_pairs={{0,1},{1,2},{2,3},{4,5},{5,6},{6,7},{8,9},{9,10},{10,11},{12,13},{... | collective-permute-start | bytes 110600 | tf_op jit(solution)/shard_map/ppermute | solution.py:439
  44.8 9.2 %collective-permute-start.5 = (f32[36,256]{1,0:T(8,128)S(1)}, f32[36,256]{1,0:T(8,128)S(1)}, u32[]{:S(2)}, u32[]{:S(2)}) collective-permute-start(f32[36,256]{1,0:T(8,128)S(1)} %pad_maximum_fusion), channel_id=1, source_target_pairs={{0,2},{1,3},{4,6},{5,7},{8,10},{9,11},{12,14},{13,15},{16,18},{17,... | collective-permute-start | bytes 110600 | tf_op jit(solution)/shard_map/ppermute | solution.py:439
  48.4 5.6 %collective-permute-start.6 = (f32[36,256]{1,0:T(8,128)S(1)}, f32[36,256]{1,0:T(8,128)S(1)}, u32[]{:S(2)}, u32[]{:S(2)}) collective-permute-start(f32[36,256]{1,0:T(8,128)S(1)} %pad_maximum_fusion), channel_id=1, source_target_pairs={{0,3},{4,7},{8,11},{12,15},{16,19},{20,23},{24,27},{28,31},{32,35}... | collective-permute-start | bytes 110600 | tf_op jit(solution)/shard_map/ppermute | solution.py:439
  70.4 14.6 %collective-permute-start.10 = (f32[8,32,256]{2,1,0:T(8,128)}, f32[8,32,256]{2,1,0:T(8,128)S(1)}, u32[]{:S(2)}, u32[]{:S(2)}) collective-permute-start(f32[8,32,256]{2,1,0:T(8,128)} %get-tuple-element.39), channel_id=1, source_target_pairs={{0,1},{1,2},{2,3},{3,0},{4,5},{5,6},{6,7},{7,4},{8,9},{9,10},{10,1... | collective-permute-start | bytes 786440 | tf_op jit(solution)/shard_map/ppermute | solution.py:201
  70.4 14.6 %collective-permute-start.8 = (f32[8,32,256]{2,1,0:T(8,128)}, f32[8,32,256]{2,1,0:T(8,128)S(1)}, u32[]{:S(2)}, u32[]{:S(2)}) collective-permute-start(f32[8,32,256]{2,1,0:T(8,128)} %get-tuple-element.39), channel_id=1, source_target_pairs={{0,3},{1,0},{2,1},{3,2},{4,7},{5,4},{6,5},{7,6},{8,11},{9,8},{10,9... | collective-permute-start | bytes 786440 | tf_op jit(solution)/shard_map/ppermute | solution.py:201
  73.7 11.3 %collective-permute-start.9 = (f32[8,32,256]{2,1,0:T(8,128)}, f32[8,32,256]{2,1,0:T(8,128)S(1)}, u32[]{:S(2)}, u32[]{:S(2)}) collective-permute-start(f32[8,32,256]{2,1,0:T(8,128)} %get-tuple-element.39), channel_id=1, source_target_pairs={{0,2},{1,3},{2,0},{3,1},{4,6},{5,7},{6,4},{7,5},{8,10},{9,11},{10,... | collective-permute-start | bytes 786440 | tf_op jit(solution)/shard_map/ppermute | solution.py:201
  86.1 2.1 %copy-start.4 = (f32[2,24,32,256]{3,2,1,0:T(8,128)S(1)}, f32[2,24,32,256]{3,2,1,0:T(8,128)}, u32[]{:S(2)}) copy-start(f32[2,24,32,256]{3,2,1,0:T(8,128)} %get-tuple-element.42) | copy-start | bytes 4718596
  87.8 1.9 %copy-start.1 = (f32[4,24,32,256]{3,2,1,0:T(8,128)S(1)}, f32[4,24,32,256]{3,2,1,0:T(8,128)}, u32[]{:S(2)}) copy-start(f32[4,24,32,256]{3,2,1,0:T(8,128)} %get-tuple-element.38) | copy-start | bytes 9437188
  87.8 2.4 %copy-start.3 = (f32[2,24,32,256]{3,2,1,0:T(8,128)S(1)}, f32[2,24,32,256]{3,2,1,0:T(8,128)}, u32[]{:S(2)}) copy-start(f32[2,24,32,256]{3,2,1,0:T(8,128)} %get-tuple-element.41) | copy-start | bytes 4718596
Sparse Core Ops, SparseCore 0:
  40.9 24.1 all-gather.2

commit v9 on v8

--- a/solution.py
+++ b/solution.py
@@ -79,8 +79,10 @@
     u_later = vu_prev
     v_later = ratio_prev
     pairs = c_ref.shape[0]
-    ends_ref[pairs:2 * pairs] = u_later
-    ends_ref[3 * pairs:4 * pairs] = v_later
+    per = ends_ref.shape[0] // (4 * pairs)
+    for f in range(pairs * per):
+        ends_ref[pairs * per + f] = u_later[f // per]
+        ends_ref[3 * pairs * per + f] = v_later[f // per]
     v_ref[:, levels - 1] = v_later
     for k in range(levels - 2, -1, -1):
         ratio = ratio_ref[:, k]
@@ -88,8 +90,9 @@
         v_later = ratio * v_later
         u_ref[:, k] = u_later
         v_ref[:, k] = v_later
-    ends_ref[0:pairs] = u_later
-    ends_ref[2 * pairs:3 * pairs] = v_later
+    for f in range(pairs * per):
+        ends_ref[f] = u_later[f // per]
+        ends_ref[2 * pairs * per + f] = v_later[f // per]
 
 
 def field_kernel(f_ref, c_ref, ctop_ref, ratio_ref, inv_ref, y_ref, ends_ref):
@@ -122,7 +125,7 @@
     return pl.BlockSpec((lead, bx, cols_y), lambda i: (0, i, 0))
 
 
-def coupling_solve(coupling, ctop):
+def coupling_solve(coupling, ctop, fields):
     pairs, levels, cols_x, cols_y = coupling.shape
     bx = 8 if cols_x % 8 == 0 else cols_x
     cspec = _specs(pairs, levels, bx, cols_y)
@@ -131,9 +134,9 @@
         coupling_kernel,
         grid=(cols_x // bx,),
         in_specs=[cspec, _plane_spec(pairs, bx, cols_y)],
-        out_specs=[cspec, cspec, cspec, cspec, _plane_spec(4 * pairs, bx, cols_y)],
+        out_specs=[cspec, cspec, cspec, cspec, _plane_spec(4 * fields, bx, cols_y)],
         out_shape=[full, full, full, full,
-                   jax.ShapeDtypeStruct((4 * pairs, cols_x, cols_y), jnp.float32)],
+                   jax.ShapeDtypeStruct((4 * fields, cols_x, cols_y), jnp.float32)],
     )(coupling, ctop)
 
 
@@ -157,7 +160,7 @@
     fields = 4
     y0 = y_ends[:, 0:fields]
     y1 = y_ends[:, fields:2 * fields]
-    rest = jnp.repeat(uv_ends, 2, axis=1)
+    rest = uv_ends
     u0 = rest[:, 0:4]
     u1 = rest[:, 4:8]
     v0 = rest[:, 8:12]
@@ -421,7 +424,7 @@
     wet_up = (-1 < d_c).astype(jnp.float32)
     ctop = mix_above * (wet_up * wet_here[0])[None]
     ctop = jnp.where(place_z > 0, ctop, 0.0)
-    ratio, inv, u, v, uv_ends = coupling_solve(coupling, ctop)
+    ratio, inv, u, v, uv_ends = coupling_solve(coupling, ctop, fields)
     uv_all = lax.all_gather(uv_ends, "gz")
     lev3 = local[:, None, None]
     tot_c = jnp.sum(density_of(state, (lev3 < d_c[None]).astype(jnp.float32)), axis=0)

time: 99.9 us -> 105 us (1.051)
  other arithmetic: 8.86 us -> 13.4 us
  local copies, waits for them, and re-layouts: 23 us -> 21.1 us
  waiting for transfers between devices: 11.4 us -> 12.7 us
    add x1, other arithmetic: 2.46 us -> 4.38 us  [per_device(): y.reshape(shape5) + x_above.reshape(plane5) * u[:, None]]
    broadcast_in_dim x1 -> x0, local copies, waits for them, and re-layouts: 1.59 us -> none  [interface_values(): rest = jnp.repeat(uv_ends, 2, axis=1)]
    select_n x1, other arithmetic: 0.22 us -> 1.8 us  [interface_values(): below = jnp.where(place == q, tops[q + 1], below)]
    another operation x1, other arithmetic: 1.11 us -> 2.18 us  [gather_by_permutes(): return jnp.stack(rows)]
    unnamed x26 -> x32, local copies, waits for them, and re-layouts: 4.58 us -> 4.1 us
  transfers between devices with their start and end apart: 12 -> 12, of which waited for: 1 -> 4; matrix products, arithmetic and copies ran while one was open for 20% -> 24% of each run, Pallas kernels for 19% -> 13%
where the time goes in v9:
time: 105 us; the launch traced here: 104 us
  starting transfers between devices  23.7 us (23%)
  local copies, waits for them, and re-layouts  21.1 us (20%)
  Pallas kernels  18.9 us (18%)
  between operations  13.7 us (13%)
  other arithmetic  13.4 us (13%)
  waiting for transfers between devices  12.7 us (12%)
    pallas_call x1, Pallas kernels, fused_solve(): pl.pallas_call(fused_kernel, grid=(levels // chunk,), in_specs=specs, out...  13.7 us
    ppermute x3, waiting for transfers between devices, gather_by_permutes(): received.append(lax.ppermute(part, axis, shift))  12.2 us
    ppermute x3, starting transfers between devices, per_device(): shallower = shallower + lax.ppermute(pack, 'gz', pairs_z)  8.72 us
    pallas_call x1, Pallas kernels, coupling_solve(): pl.pallas_call(coupling_kernel, grid=(cols_x // bx,), in_specs=[cspec, _p...  5.18 us
    add x1, other arithmetic, per_device(): y.reshape(shape5) + x_above.reshape(plane5) * u[:, None]  4.38 us
    unnamed x32, local copies, waits for them, and re-layouts  4.1 us
    ppermute x1, starting transfers between devices, per_device(): mix_above = lax.ppermute(mixing[:, lev_count - 1], 'gz', down_z)  3.92 us
    slice x1, local copies, waits for them, and re-layouts, per_device(): halo_yn = lax.ppermute(state[:, :, :, 0], 'gy', dn_y)  3.59 us
  transfers between devices with their start and end apart: 12, of which 4 were waited for; matrix products, arithmetic and copies ran while one was open for 24% of the time, Pallas kernels for 13%

profile of v9, /device:TPU:0, one launch (start us, length us, event | category | flops | bytes accessed | tf_op | source)
XLA Modules:
  0.0 103.5 jit_solution(269864247399145075)
XLA Ops:
  6.5 0.9 slice_bitcast_fusion.17
  7.5 3.9 %collective-permute-start.7 = (f32[2,32,256]{2,1,0:T(8,128)S(1)}, f32[2,32,256]{2,1,0:T(8,128)S(1)}, u32[]{:S(2)}, u32[]{:S(2)}) collective-permute-start(f32[2,32,256]{2,1,0:T(8,128)S(1)} %slice_bitcast_fusion.17), channel_id=1, source_target_pairs={{0,1},{1,2},{2,3},{4,5},{5,6},{6,7},{8,9},{9,10},{10,11},{12,13},{... | collective-permute-start | bytes 196616 | tf_op jit(solution)/shard_map/ppermute | solution.py:398
  11.5 0.7 gather_fusion
  12.2 0.1 broadcast_select_fusion
  12.3 0.4 copy.40
  12.7 1.0 %gather_fusion.1 = s32[258,34]{1,0:T(8,128)S(1)} fusion(s32[34,2048]{0,1:T(8,128)S(1)} %copy.40, s32[1024]{0:T(1024)S(1)} %pad_clamp_fusion), kind=kCustom, calls=%fused_computation.1 | custom fusion | bytes 71208 | tf_op jit(solution)/shard_map/jit(_take)/gather | solution.py:410
  13.7 0.1 copy.41
  13.9 0.7 fusion.51
  14.6 0.1 fusion.5
  14.7 1.7 %compare_select_fusion = (f32[24,32,256]{2,1,0:T(8,128)S(1)}, f32[32,256]{1,0:T(8,128)S(1)}) fusion(s32[32,256]{1,0:T(8,128)S(1)} %get-tuple-element.61.dc_ref, s32[24]{0:T(128)S(1)} %iota_add_fusion.1, f32[4,24,32,256]{3,2,1,0:T(8,128)} %st_ref.1), kind=kLoop, calls=%fused_computation.15 | loop fusion | flops 2351104 | bytes 2424928 | tf_op jit(solution)/shard_map/mul | solution.py:423
  16.4 1.4 %broadcast_multiply_fusion.c_ref = f32[2,24,32,256]{3,2,1,0:T(8,128)} fusion(f32[2,24,32,256]{3,2,1,0:T(8,128)S(1)} %copy-done.2, f32[24,32,256]{2,1,0:T(8,128)S(1)} %get-tuple-element.66), kind=kLoop, calls=%fused_computation.12 | loop fusion | flops 393216 | bytes 3932160 | tf_op jit(solution)/shard_map/mul | solution.py:423
  17.8 0.1 fusion.21
  17.9 0.6 multiply_select_fusion.ctop_ref
  18.5 5.2 %shard_map.46 = (f32[2,24,32,256]{3,2,1,0:T(8,128)}, f32[2,24,32,256]{3,2,1,0:T(8,128)}, f32[2,24,32,256]{3,2,1,0:T(8,128)}, f32[2,24,32,256]{3,2,1,0:T(8,128)}, f32[16,32,256]{2,1,0:T(8,128)}) custom-call(f32[2,24,32,256]{3,2,1,0:T(8,128)} %broadcast_multiply_fusion.c_ref, f32[2,32,256]{2,1,0:T(8,128)} %multiply_select_fusion.ctop_ref), custom_call_target="tpu_custom_call" | custom-call | tf_op jit(solution)/shard_map/pallas_call | solution.py:133
  23.7 3.6 %fusion.48 = (f32[4,24,32,1]{3,2,1,0:T(8,128)S(1)}, f32[4,24,32,1]{3,2,1,0:T(8,128)}) fusion(f32[4,24,32,256]{3,2,1,0:T(8,128)} %st_ref.1), kind=kLoop, calls=%fused_computation.140 | loop fusion | bytes 49152 | tf_op jit(solution)/shard_map/slice | solution.py:406
  27.3 2.1 %copy.49 = f32[4,24,32,1]{2,1,0,3:T(8,128)S(1)} copy(f32[4,24,32,1]{3,2,1,0:T(8,128)} %get-tuple-element.46) | data formatting | bytes 24576
  29.4 3.1 %collective-permute-start.2 = (f32[4,24,32]{2,1,0:T(8,128)S(1)}, f32[4,24,32]{2,1,0:T(8,128)S(1)}, u32[]{:S(2)}, u32[]{:S(2)}) collective-permute-start(f32[4,24,32]{2,1,0:T(8,128)S(1)} %bitcast.309), channel_id=1, source_target_pairs={{0,4},{4,8},{8,12},{12,16},{16,20},{20,24},{24,28},{28,0},{1,5},{5... | collective-permute-start | bytes 36872 | tf_op jit(solution)/shard_map/ppermute | solution.py:405
  32.4 0.6 copy.50
  33.1 2.7 %collective-permute-start.3 = (f32[4,24,32]{2,1,0:T(8,128)S(1)}, f32[4,24,32]{2,1,0:T(8,128)S(1)}, u32[]{:S(2)}, u32[]{:S(2)}) collective-permute-start(f32[4,24,32]{2,1,0:T(8,128)S(1)} %bitcast.308), channel_id=1, source_target_pairs={{4,0},{8,4},{12,8},{16,12},{20,16},{24,20},{28,24},{0,28},{5,1},{9... | collective-permute-start | bytes 36872 | tf_op jit(solution)/shard_map/ppermute | solution.py:406
  35.7 1.6 %fusion.49 = (f32[4,24,1,256]{3,2,1,0:T(1,128)S(1)}, f32[4,24,1,256]{3,2,1,0:T(1,128)S(1)}) fusion(f32[4,24,32,256]{3,2,1,0:T(8,128)} %st_ref.1), kind=kLoop, calls=%fused_computation.141 | loop fusion | bytes 393216 | tf_op jit(solution)/shard_map/slice | solution.py:404
  37.5 1.8 %collective-permute-start.1 = (f32[4,24,256]{2,1,0:T(8,128)S(1)}, f32[4,24,256]{2,1,0:T(8,128)S(1)}, u32[]{:S(2)}, u32[]{:S(2)}) collective-permute-start(f32[4,24,256]{2,1,0:T(8,128)S(1)} %bitcast.307), channel_id=1, source_target_pairs={{32,0},{64,32},{96,64},{0,96},{33,1},{65,33},{97,65},{1,97},{34,2}... | collective-permute-start | bytes 294920 | tf_op jit(solution)/shard_map/ppermute | solution.py:404
  39.3 0.8 slice_reduce_fusion
  40.1 0.6 broadcast_select_fusion.1.wind_ref
  40.8 0.2 scatter.9
  41.0 0.5 collective-permute-done.xw_ref
  41.6 3.9 %collective-permute-start.4 = (f32[36,256]{1,0:T(8,128)S(1)}, f32[36,256]{1,0:T(8,128)S(1)}, u32[]{:S(2)}, u32[]{:S(2)}) collective-permute-start(f32[36,256]{1,0:T(8,128)S(1)} %pad_maximum_fusion), channel_id=1, source_target_pairs={{0,1},{1,2},{2,3},{4,5},{5,6},{6,7},{8,9},{9,10},{10,11},{12,13},{... | collective-permute-start | bytes 110600 | tf_op jit(solution)/shard_map/ppermute | solution.py:442
  45.4 3.6 %collective-permute-start.5 = (f32[36,256]{1,0:T(8,128)S(1)}, f32[36,256]{1,0:T(8,128)S(1)}, u32[]{:S(2)}, u32[]{:S(2)}) collective-permute-start(f32[36,256]{1,0:T(8,128)S(1)} %pad_maximum_fusion), channel_id=1, source_target_pairs={{0,2},{1,3},{4,6},{5,7},{8,10},{9,11},{12,14},{13,15},{16,18},{17,... | collective-permute-start | bytes 110600 | tf_op jit(solution)/shard_map/ppermute | solution.py:442
  49.0 1.3 %collective-permute-start.6 = (f32[36,256]{1,0:T(8,128)S(1)}, f32[36,256]{1,0:T(8,128)S(1)}, u32[]{:S(2)}, u32[]{:S(2)}) collective-permute-start(f32[36,256]{1,0:T(8,128)S(1)} %pad_maximum_fusion), channel_id=1, source_target_pairs={{0,3},{4,7},{8,11},{12,15},{16,19},{20,23},{24,27},{28,31},{32,35}... | collective-permute-start | bytes 110600 | tf_op jit(solution)/shard_map/ppermute | solution.py:442
  50.3 0.6 stack.23.lane_ref
  51.0 1.8 %copy.43.ys_ref = f32[4,24,32,1]{3,2,1,0:T(8,128)} copy(f32[4,24,32,1]{2,1,0,3:T(8,128)S(1)} %bitcast.304) | data formatting | bytes 24576 | tf_op jit(solution)/shard_map/broadcast_in_dim | solution.py:454
  52.7 1.9 %copy.44.yn_ref = f32[4,24,32,1]{3,2,1,0:T(8,128)} copy(f32[4,24,32,1]{2,1,0,3:T(8,128)S(1)} %bitcast.305) | data formatting | bytes 24576 | tf_op jit(solution)/shard_map/broadcast_in_dim | solution.py:454
  54.7 0.6 slice.288.sc_ref
  55.3 0.7 copy.45.sys_ref
  56.0 0.7 copy.46.syn_ref
  56.7 0.6 fusion.52
  57.3 13.7 %shard_map.47 = (f32[4,24,32,256]{3,2,1,0:T(8,128)}, f32[8,32,256]{2,1,0:T(8,128)}) custom-call(f32[4,24,32,256]{3,2,1,0:T(8,128)} %st_ref.1, f32[4,24,256]{2,1,0:T(8,128)} %copy-done.9, f32[4,24,256]{2,1,0:T(8,128)} %copy-done.10, f32[4,24,32,1]{3,2,1,0:T(8,128)} %copy.43.ys_ref, f32[4,24,32,1]{3,2,1,0:T(8,128)} %copy.44.yn_ref, s32[32,256]{1,0:T(8,128)} %copy-done.6, ...), custom_call_target="tpu_custom_call" | custom-call | tf_op jit(solution)/shard_map/pallas_call | solution.py:371
  71.1 3.2 %collective-permute-start.8 = (f32[8,32,256]{2,1,0:T(8,128)}, f32[8,32,256]{2,1,0:T(8,128)S(1)}, u32[]{:S(2)}, u32[]{:S(2)}) collective-permute-start(f32[8,32,256]{2,1,0:T(8,128)} %get-tuple-element.39), channel_id=1, source_target_pairs={{0,3},{1,0},{2,1},{3,2},{4,7},{5,4},{6,5},{7,6},{8,11},{9,8},{10,9... | collective-permute-start | bytes 786440 | tf_op jit(solution)/shard_map/ppermute | solution.py:204
  74.3 0.2 collective-permute-start.9
  74.5 6.4 %collective-permute-done.10 = f32[8,32,256]{2,1,0:T(8,128)S(1)} collective-permute-done((f32[8,32,256]{2,1,0:T(8,128)}, f32[8,32,256]{2,1,0:T(8,128)S(1)}, u32[]{:S(2)}, u32[]{:S(2)}) %collective-permute-start.10) | collective-permute-done | bytes 262176 | tf_op jit(solution)/shard_map/ppermute | solution.py:204
  80.9 5.4 %collective-permute-done.8 = f32[8,32,256]{2,1,0:T(8,128)S(1)} collective-permute-done((f32[8,32,256]{2,1,0:T(8,128)}, f32[8,32,256]{2,1,0:T(8,128)S(1)}, u32[]{:S(2)}, u32[]{:S(2)}) %collective-permute-start.8) | collective-permute-done | bytes 262176 | tf_op jit(solution)/shard_map/ppermute | solution.py:204
  86.3 0.7 copy-done.8
  87.0 0.4 collective-permute-done.9
  87.4 2.2 %select_bitcast_fusion.2 = (f32[1,8,32,256]{3,2,1,0:T(8,128)S(1)}, f32[1,8,32,256]{3,2,1,0:T(8,128)S(1)}, f32[1,8,32,256]{3,2,1,0:T(8,128)}, f32[1,8,32,256]{3,2,1,0:T(8,128)S(1)}) fusion(f32[8,32,256]{2,1,0:T(8,128)} %copy-done.8, f32[8,32,256]{2,1,0:T(8,128)} %collective-permute-done.9, f32[8,32,256]{2,1,0:T(8,128)} %copy-done.7, ...), kind=kLoop, calls=%fused_computation.18 | loop fusion | flops 786432 | bytes 2097164 | tf_op jit(solution)/shard_map/stack | solution.py:211
  89.6 1.8 %select_select_fusion = f32[4,32,256]{2,1,0:T(8,128)S(1)} fusion(pred[]{:T(512)S(6)} %eq.68, pred[]{:T(512)S(6)} %eq.83, pred[]{:T(512)S(6)} %eq.82, f32[4,16,32,256]{3,2,1,0:T(8,128)} %bitcast.302, f32[1,8,32,256]{3,2,1,0:T(8,128)S(1)} %get-tuple-element.52, f32[1,8,32,256]{3,2,1,0:T(8,128)S(1)} %get-tuple-element.50, ...), kind=kLoop, calls=%fused_computation.53 | loop fusion | flops 1441792 | bytes 2359299 | tf_op jit(solution)/shard_map/jit(_where)/select_n | solution.py:196
  91.4 0.3 copy-done.1
  91.8 0.2 select_select_fusion.1
  92.0 0.3 copy-done.3
  92.3 4.4 %fusion = f32[4,24,32,256]{3,2,1,0:T(8,128)} fusion(f32[4,24,32,256]{3,2,1,0:T(8,128)} %get-tuple-element.38, f32[2,24,32,256]{3,2,1,0:T(8,128)S(1)} %copy-done.4, f32[4,32,256]{2,1,0:T(8,128)S(1)} %select_select_fusion, f32[2,24,32,256]{3,2,1,0:T(8,128)S(1)} %copy-done.3, f32[4,32,256]{2,1,0:T(8,128)S(1)} %select_select_fusion.1), kind=kLoop, calls=%fused_computation.3 | loop fusion | flops 3145728 | bytes 9699328 | tf_op jit(solution)/shard_map/add | solution.py:463
  (60 shorter events, 0.6 us)
Async XLA Ops:
  6.5 5.0 %copy-start = (s32[128,2048]{1,0:T(8,128)S(1)}, s32[128,2048]{1,0:T(8,128)}, u32[]{:S(2)}) copy-start(s32[128,2048]{1,0:T(8,128)} %param.10) | copy-start | bytes 3145732
  6.5 83.1 %all-gather.3.cloned.1.call-start = ((), (), s32[]{:S(2)}) async-start(), calls=%async_computation | async-start | bytes 2621440 | tf_op jit(solution)/shard_map/all_gather | solution.py:428
  7.5 10.4 %collective-permute-start.7 = (f32[2,32,256]{2,1,0:T(8,128)S(1)}, f32[2,32,256]{2,1,0:T(8,128)S(1)}, u32[]{:S(2)}, u32[]{:S(2)}) collective-permute-start(f32[2,32,256]{2,1,0:T(8,128)S(1)} %slice_bitcast_fusion.17), channel_id=1, source_target_pairs={{0,1},{1,2},{2,3},{4,5},{5,6},{6,7},{8,9},{9,10},{10,11},{12,13},{... | collective-permute-start | bytes 196616 | tf_op jit(solution)/shard_map/ppermute | solution.py:398
  13.7 2.7 %copy-start.2 = (f32[2,24,32,256]{3,2,1,0:T(8,128)S(1)}, f32[2,24,32,256]{3,2,1,0:T(8,128)}, u32[]{:S(2)}) copy-start(f32[2,24,32,256]{3,2,1,0:T(8,128)} %param.9) | copy-start | bytes 4718596
  14.6 3.1 %copy-start.6 = (s32[32,256]{1,0:T(8,128)}, s32[32,256]{1,0:T(8,128)S(1)}, u32[]{:S(2)}) copy-start(s32[32,256]{1,0:T(8,128)S(1)} %get-tuple-element.61.dc_ref) | copy-start | bytes 98308
  27.3 12.8 %copy-start.11 = (f32[2,32,256]{2,1,0:T(8,128)S(1)}, f32[2,32,256]{2,1,0:T(8,128)}, u32[]{:S(2)}) copy-start(f32[2,32,256]{2,1,0:T(8,128)} %param.11) | copy-start | bytes 196612
  29.4 11.4 %collective-permute-start.2 = (f32[4,24,32]{2,1,0:T(8,128)S(1)}, f32[4,24,32]{2,1,0:T(8,128)S(1)}, u32[]{:S(2)}, u32[]{:S(2)}) collective-permute-start(f32[4,24,32]{2,1,0:T(8,128)S(1)} %bitcast.309), channel_id=1, source_target_pairs={{0,4},{4,8},{8,12},{12,16},{16,20},{20,24},{24,28},{28,0},{1,5},{5... | collective-permute-start | bytes 36872 | tf_op jit(solution)/shard_map/ppermute | solution.py:405
  33.1 7.7 %collective-permute-start.3 = (f32[4,24,32]{2,1,0:T(8,128)S(1)}, f32[4,24,32]{2,1,0:T(8,128)S(1)}, u32[]{:S(2)}, u32[]{:S(2)}) collective-permute-start(f32[4,24,32]{2,1,0:T(8,128)S(1)} %bitcast.308), channel_id=1, source_target_pairs={{4,0},{8,4},{12,8},{16,12},{20,16},{24,20},{28,24},{0,28},{5,1},{9... | collective-permute-start | bytes 36872 | tf_op jit(solution)/shard_map/ppermute | solution.py:406
  37.4 4.1 %collective-permute-start = (f32[4,24,256]{2,1,0:T(8,128)S(1)}, f32[4,24,256]{2,1,0:T(8,128)S(1)}, u32[]{:S(2)}, u32[]{:S(2)}) collective-permute-start(f32[4,24,256]{2,1,0:T(8,128)S(1)} %bitcast.306), channel_id=1, source_target_pairs={{0,32},{32,64},{64,96},{96,0},{1,33},{33,65},{65,97},{97,1},{2,34}... | collective-permute-start | bytes 294920 | tf_op jit(solution)/shard_map/ppermute | solution.py:403
  37.5 4.1 %collective-permute-start.1 = (f32[4,24,256]{2,1,0:T(8,128)S(1)}, f32[4,24,256]{2,1,0:T(8,128)S(1)}, u32[]{:S(2)}, u32[]{:S(2)}) collective-permute-start(f32[4,24,256]{2,1,0:T(8,128)S(1)} %bitcast.307), channel_id=1, source_target_pairs={{32,0},{64,32},{96,64},{0,96},{33,1},{65,33},{97,65},{1,97},{34,2}... | collective-permute-start | bytes 294920 | tf_op jit(solution)/shard_map/ppermute | solution.py:404
  39.3 17.9 %copy-start.12 = (s32[1,256]{1,0:T(1,128)}, s32[1,256]{1,0:T(1,128)S(1)}, u32[]{:S(2)}) copy-start(s32[1,256]{1,0:T(1,128)S(1)} %get-tuple-element.55.dxe_ref) | copy-start | bytes 3076
  39.3 17.9 %copy-start.13 = (s32[1,256]{1,0:T(1,128)}, s32[1,256]{1,0:T(1,128)S(1)}, u32[]{:S(2)}) copy-start(s32[1,256]{1,0:T(1,128)S(1)} %get-tuple-element.56.dxw_ref) | copy-start | bytes 3076
  41.5 15.8 %copy-start.9 = (f32[4,24,256]{2,1,0:T(8,128)}, f32[4,24,256]{2,1,0:T(8,128)S(1)}, u32[]{:S(2)}) copy-start(f32[4,24,256]{2,1,0:T(8,128)S(1)} %collective-permute-done.xw_ref) | copy-start | bytes 294916
  41.5 15.8 %copy-start.10 = (f32[4,24,256]{2,1,0:T(8,128)}, f32[4,24,256]{2,1,0:T(8,128)S(1)}, u32[]{:S(2)}) copy-start(f32[4,24,256]{2,1,0:T(8,128)S(1)} %collective-permute-done.1.xe_ref) | copy-start | bytes 294916
  41.6 13.1 %collective-permute-start.4 = (f32[36,256]{1,0:T(8,128)S(1)}, f32[36,256]{1,0:T(8,128)S(1)}, u32[]{:S(2)}, u32[]{:S(2)}) collective-permute-start(f32[36,256]{1,0:T(8,128)S(1)} %pad_maximum_fusion), channel_id=1, source_target_pairs={{0,1},{1,2},{2,3},{4,5},{5,6},{6,7},{8,9},{9,10},{10,11},{12,13},{... | collective-permute-start | bytes 110600 | tf_op jit(solution)/shard_map/ppermute | solution.py:442
  45.4 9.2 %collective-permute-start.5 = (f32[36,256]{1,0:T(8,128)S(1)}, f32[36,256]{1,0:T(8,128)S(1)}, u32[]{:S(2)}, u32[]{:S(2)}) collective-permute-start(f32[36,256]{1,0:T(8,128)S(1)} %pad_maximum_fusion), channel_id=1, source_target_pairs={{0,2},{1,3},{4,6},{5,7},{8,10},{9,11},{12,14},{13,15},{16,18},{17,... | collective-permute-start | bytes 110600 | tf_op jit(solution)/shard_map/ppermute | solution.py:442
  49.0 5.6 %collective-permute-start.6 = (f32[36,256]{1,0:T(8,128)S(1)}, f32[36,256]{1,0:T(8,128)S(1)}, u32[]{:S(2)}, u32[]{:S(2)}) collective-permute-start(f32[36,256]{1,0:T(8,128)S(1)} %pad_maximum_fusion), channel_id=1, source_target_pairs={{0,3},{4,7},{8,11},{12,15},{16,19},{20,23},{24,27},{28,31},{32,35}... | collective-permute-start | bytes 110600 | tf_op jit(solution)/shard_map/ppermute | solution.py:442
  71.0 9.9 %collective-permute-start.10 = (f32[8,32,256]{2,1,0:T(8,128)}, f32[8,32,256]{2,1,0:T(8,128)S(1)}, u32[]{:S(2)}, u32[]{:S(2)}) collective-permute-start(f32[8,32,256]{2,1,0:T(8,128)} %get-tuple-element.39), channel_id=1, source_target_pairs={{0,1},{1,2},{2,3},{3,0},{4,5},{5,6},{6,7},{7,4},{8,9},{9,10},{10,1... | collective-permute-start | bytes 786440 | tf_op jit(solution)/shard_map/ppermute | solution.py:204
  71.1 15.2 %collective-permute-start.8 = (f32[8,32,256]{2,1,0:T(8,128)}, f32[8,32,256]{2,1,0:T(8,128)S(1)}, u32[]{:S(2)}, u32[]{:S(2)}) collective-permute-start(f32[8,32,256]{2,1,0:T(8,128)} %get-tuple-element.39), channel_id=1, source_target_pairs={{0,3},{1,0},{2,1},{3,2},{4,7},{5,4},{6,5},{7,6},{8,11},{9,8},{10,9... | collective-permute-start | bytes 786440 | tf_op jit(solution)/shard_map/ppermute | solution.py:204
  74.3 13.1 %collective-permute-start.9 = (f32[8,32,256]{2,1,0:T(8,128)}, f32[8,32,256]{2,1,0:T(8,128)}, u32[]{:S(2)}, u32[]{:S(2)}) collective-permute-start(f32[8,32,256]{2,1,0:T(8,128)} %get-tuple-element.39), channel_id=1, source_target_pairs={{0,2},{1,3},{2,0},{3,1},{4,6},{5,7},{6,4},{7,5},{8,10},{9,11},{10,... | collective-permute-start | bytes 786440 | tf_op jit(solution)/shard_map/ppermute | solution.py:204
  80.9 5.4 %copy-start.7 = (f32[8,32,256]{2,1,0:T(8,128)}, f32[8,32,256]{2,1,0:T(8,128)S(1)}, u32[]{:S(2)}) copy-start(f32[8,32,256]{2,1,0:T(8,128)S(1)} %collective-permute-done.10) | copy-start | bytes 786436
  86.3 0.7 copy-start.8
  87.4 4.6 %copy-start.4 = (f32[2,24,32,256]{3,2,1,0:T(8,128)S(1)}, f32[2,24,32,256]{3,2,1,0:T(8,128)}, u32[]{:S(2)}) copy-start(f32[2,24,32,256]{3,2,1,0:T(8,128)} %get-tuple-element.42) | copy-start | bytes 4718596
  89.6 2.2 %copy-start.1 = (f32[64,32,256]{2,1,0:T(8,128)S(1)}, f32[64,32,256]{2,1,0:T(8,128)}, u32[]{:S(2)}) copy-start(f32[64,32,256]{2,1,0:T(8,128)} %all-gather.3.cloned.1.call-done) | copy-start | bytes 6291460
  89.6 2.2 %copy-start.5 = (f32[1,8,32,256]{3,2,1,0:T(8,128)S(1)}, f32[1,8,32,256]{3,2,1,0:T(8,128)}, u32[]{:S(2)}) copy-start(f32[1,8,32,256]{3,2,1,0:T(8,128)} %get-tuple-element.51) | copy-start | bytes 786436
  89.6 2.7 %copy-start.3 = (f32[2,24,32,256]{3,2,1,0:T(8,128)S(1)}, f32[2,24,32,256]{3,2,1,0:T(8,128)}, u32[]{:S(2)}) copy-start(f32[2,24,32,256]{3,2,1,0:T(8,128)} %get-tuple-element.41) | copy-start | bytes 4718596
Sparse Core Ops, SparseCore 0:
  23.8 32.9 all-gather.2

commit v10 on v8

--- a/solution.py
+++ b/solution.py
@@ -330,7 +330,7 @@
         return (run_c, run_xw, run_xe, run_ys, run_yn), jnp.stack(vy), c_here
 
     run = (run_c_s[...], run_xw_s[...], run_xe_s[...], run_ys_s[...], run_yn_s[...])
-    carry = lax.fori_loop(0, chunk, level, (run, vy_s[...], cprev_s[...]), unroll=2)
+    carry = lax.fori_loop(0, chunk, level, (run, vy_s[...], cprev_s[...]), unroll=4)
     run, vy, c_prev = carry
     run_c_s[...], run_xw_s[...], run_xe_s[...], run_ys_s[...], run_yn_s[...] = run
     vy_s[...] = vy

time: 99.9 us -> 99.6 us (level)
  no operation moved by 1% of the time
where the time goes in v10:
time: 99.6 us; the launch traced here: 99.1 us
  starting transfers between devices  23.5 us (24%)
  local copies, waits for them, and re-layouts  23 us (23%)
  Pallas kernels  18.6 us (19%)
  between operations  13.8 us (14%)
  waiting for transfers between devices  11.4 us (11%)
  other arithmetic  8.86 us (9%)
    pallas_call x1, Pallas kernels, fused_solve(): pl.pallas_call(fused_kernel, grid=(levels // chunk,), in_specs=specs, out...  13.5 us
    ppermute x3, waiting for transfers between devices, gather_by_permutes(): received.append(lax.ppermute(part, axis, shift))  11.3 us
    ppermute x3, starting transfers between devices, per_device(): shallower = shallower + lax.ppermute(pack, 'gz', pairs_z)  8.7 us
    pallas_call x1, Pallas kernels, coupling_solve(): pl.pallas_call(coupling_kernel, grid=(cols_x // bx,), in_specs=[cspec, _p...  5.11 us
    unnamed x26, local copies, waits for them, and re-layouts  4.58 us
    ppermute x1, starting transfers between devices, per_device(): mix_above = lax.ppermute(mixing[:, lev_count - 1], 'gz', down_z)  3.93 us
    slice x1, local copies, waits for them, and re-layouts, per_device(): halo_yn = lax.ppermute(state[:, :, :, 0], 'gy', dn_y)  3.7 us
    ppermute x3, starting transfers between devices, gather_by_permutes(): received.append(lax.ppermute(part, axis, shift))  3.3 us
  transfers between devices with their start and end apart: 12, of which 1 were waited for; matrix products, arithmetic and copies ran while one was open for 20% of the time, Pallas kernels for 19%

profile of v10, /device:TPU:0, one launch (start us, length us, event | category | flops | bytes accessed | tf_op | source)
XLA Modules:
  0.0 99.1 jit_solution(3404521127653773186)
XLA Ops:
  6.5 3.7 %fusion.48 = (f32[4,24,32,1]{3,2,1,0:T(8,128)S(1)}, f32[4,24,32,1]{3,2,1,0:T(8,128)}) fusion(f32[4,24,32,256]{3,2,1,0:T(8,128)} %st_ref.1), kind=kLoop, calls=%fused_computation.140 | loop fusion | bytes 49152 | tf_op jit(solution)/shard_map/slice | solution.py:403
  10.2 2.0 %copy.49 = f32[4,24,32,1]{2,1,0,3:T(8,128)S(1)} copy(f32[4,24,32,1]{3,2,1,0:T(8,128)} %get-tuple-element.46) | data formatting | bytes 24576
  12.3 3.2 %collective-permute-start.2 = (f32[4,24,32]{2,1,0:T(8,128)S(1)}, f32[4,24,32]{2,1,0:T(8,128)S(1)}, u32[]{:S(2)}, u32[]{:S(2)}) collective-permute-start(f32[4,24,32]{2,1,0:T(8,128)S(1)} %bitcast.311), channel_id=1, source_target_pairs={{0,4},{4,8},{8,12},{12,16},{16,20},{20,24},{24,28},{28,0},{1,5},{5... | collective-permute-start | bytes 36872 | tf_op jit(solution)/shard_map/ppermute | solution.py:402
  15.5 0.6 copy.50
  16.1 2.6 %collective-permute-start.3 = (f32[4,24,32]{2,1,0:T(8,128)S(1)}, f32[4,24,32]{2,1,0:T(8,128)S(1)}, u32[]{:S(2)}, u32[]{:S(2)}) collective-permute-start(f32[4,24,32]{2,1,0:T(8,128)S(1)} %bitcast.310), channel_id=1, source_target_pairs={{4,0},{8,4},{12,8},{16,12},{20,16},{24,20},{28,24},{0,28},{5,1},{9... | collective-permute-start | bytes 36872 | tf_op jit(solution)/shard_map/ppermute | solution.py:403
  18.6 1.5 %fusion.49 = (f32[4,24,1,256]{3,2,1,0:T(1,128)S(1)}, f32[4,24,1,256]{3,2,1,0:T(1,128)S(1)}) fusion(f32[4,24,32,256]{3,2,1,0:T(8,128)} %st_ref.1), kind=kLoop, calls=%fused_computation.141 | loop fusion | bytes 393216 | tf_op jit(solution)/shard_map/slice | solution.py:401
  20.2 0.1 collective-permute-start
  20.3 1.8 %collective-permute-start.1 = (f32[4,24,256]{2,1,0:T(8,128)S(1)}, f32[4,24,256]{2,1,0:T(8,128)S(1)}, u32[]{:S(2)}, u32[]{:S(2)}) collective-permute-start(f32[4,24,256]{2,1,0:T(8,128)S(1)} %bitcast.309), channel_id=1, source_target_pairs={{32,0},{64,32},{96,64},{0,96},{33,1},{65,33},{97,65},{1,97},{34,2}... | collective-permute-start | bytes 294920 | tf_op jit(solution)/shard_map/ppermute | solution.py:401
  22.1 0.8 slice_bitcast_fusion.17
  22.9 3.9 %collective-permute-start.7 = (f32[2,32,256]{2,1,0:T(8,128)S(1)}, f32[2,32,256]{2,1,0:T(8,128)S(1)}, u32[]{:S(2)}, u32[]{:S(2)}) collective-permute-start(f32[2,32,256]{2,1,0:T(8,128)S(1)} %slice_bitcast_fusion.17), channel_id=1, source_target_pairs={{0,1},{1,2},{2,3},{4,5},{5,6},{6,7},{8,9},{9,10},{10,11},{12,13},{... | collective-permute-start | bytes 196616 | tf_op jit(solution)/shard_map/ppermute | solution.py:395
  27.0 0.7 gather_fusion
  27.6 0.1 broadcast_select_fusion
  27.7 0.4 copy.40
  28.1 1.0 %gather_fusion.1 = s32[258,34]{1,0:T(8,128)S(1)} fusion(s32[34,2048]{0,1:T(8,128)S(1)} %copy.40, s32[1024]{0:T(1024)S(1)} %pad_clamp_fusion), kind=kCustom, calls=%fused_computation.1 | custom fusion | bytes 71208 | tf_op jit(solution)/shard_map/jit(_take)/gather | solution.py:407
  29.2 0.1 copy.41
  29.3 0.8 slice_reduce_fusion
  30.1 0.7 fusion.51
  30.8 0.1 fusion.50
  30.9 0.1 fusion.5
  31.0 1.7 %compare_select_fusion = (f32[24,32,256]{2,1,0:T(8,128)S(1)}, f32[32,256]{1,0:T(8,128)S(1)}) fusion(s32[32,256]{1,0:T(8,128)S(1)} %get-tuple-element.61.dc_ref, s32[24]{0:T(128)S(1)} %iota_add_fusion.1, f32[4,24,32,256]{3,2,1,0:T(8,128)} %st_ref.1), kind=kLoop, calls=%fused_computation.15 | loop fusion | flops 2351104 | bytes 2424928 | tf_op jit(solution)/shard_map/mul | solution.py:420
  32.7 0.1 fusion.21
  32.8 1.3 %broadcast_multiply_fusion.c_ref = f32[2,24,32,256]{3,2,1,0:T(8,128)} fusion(f32[2,24,32,256]{3,2,1,0:T(8,128)S(1)} %copy-done.2, f32[24,32,256]{2,1,0:T(8,128)S(1)} %get-tuple-element.66), kind=kLoop, calls=%fused_computation.12 | loop fusion | flops 393216 | bytes 3932160 | tf_op jit(solution)/shard_map/mul | solution.py:420
  34.1 0.6 broadcast_select_fusion.1.wind_ref
  34.8 0.2 scatter.9
  35.0 0.6 multiply_select_fusion.ctop_ref
  35.7 5.1 %shard_map.46 = (f32[2,24,32,256]{3,2,1,0:T(8,128)}, f32[2,24,32,256]{3,2,1,0:T(8,128)}, f32[2,24,32,256]{3,2,1,0:T(8,128)}, f32[2,24,32,256]{3,2,1,0:T(8,128)}, f32[8,32,256]{2,1,0:T(8,128)}) custom-call(f32[2,24,32,256]{3,2,1,0:T(8,128)} %broadcast_multiply_fusion.c_ref, f32[2,32,256]{2,1,0:T(8,128)} %multiply_select_fusion.ctop_ref), custom_call_target="tpu_custom_call" | custom-call | tf_op jit(solution)/shard_map/pallas_call | solution.py:130
  40.9 3.8 %collective-permute-start.4 = (f32[36,256]{1,0:T(8,128)S(1)}, f32[36,256]{1,0:T(8,128)S(1)}, u32[]{:S(2)}, u32[]{:S(2)}) collective-permute-start(f32[36,256]{1,0:T(8,128)S(1)} %pad_maximum_fusion), channel_id=1, source_target_pairs={{0,1},{1,2},{2,3},{4,5},{5,6},{6,7},{8,9},{9,10},{10,11},{12,13},{... | collective-permute-start | bytes 110600 | tf_op jit(solution)/shard_map/ppermute | solution.py:439
  44.8 3.6 %collective-permute-start.5 = (f32[36,256]{1,0:T(8,128)S(1)}, f32[36,256]{1,0:T(8,128)S(1)}, u32[]{:S(2)}, u32[]{:S(2)}) collective-permute-start(f32[36,256]{1,0:T(8,128)S(1)} %pad_maximum_fusion), channel_id=1, source_target_pairs={{0,2},{1,3},{4,6},{5,7},{8,10},{9,11},{12,14},{13,15},{16,18},{17,... | collective-permute-start | bytes 110600 | tf_op jit(solution)/shard_map/ppermute | solution.py:439
  48.4 1.3 %collective-permute-start.6 = (f32[36,256]{1,0:T(8,128)S(1)}, f32[36,256]{1,0:T(8,128)S(1)}, u32[]{:S(2)}, u32[]{:S(2)}) collective-permute-start(f32[36,256]{1,0:T(8,128)S(1)} %pad_maximum_fusion), channel_id=1, source_target_pairs={{0,3},{4,7},{8,11},{12,15},{16,19},{20,23},{24,27},{28,31},{32,35}... | collective-permute-start | bytes 110600 | tf_op jit(solution)/shard_map/ppermute | solution.py:439
  49.7 0.6 stack.23.lane_ref
  50.3 1.9 %copy.43.ys_ref = f32[4,24,32,1]{3,2,1,0:T(8,128)} copy(f32[4,24,32,1]{2,1,0,3:T(8,128)S(1)} %bitcast.306) | data formatting | bytes 24576 | tf_op jit(solution)/shard_map/broadcast_in_dim | solution.py:451
  52.2 1.8 %copy.44.yn_ref = f32[4,24,32,1]{3,2,1,0:T(8,128)} copy(f32[4,24,32,1]{2,1,0,3:T(8,128)S(1)} %bitcast.307) | data formatting | bytes 24576 | tf_op jit(solution)/shard_map/broadcast_in_dim | solution.py:451
  54.0 0.6 slice.288.sc_ref
  54.6 0.7 copy.45.sys_ref
  55.3 0.7 copy.46.syn_ref
  56.0 0.6 fusion.52
  56.6 13.5 %shard_map.47 = (f32[4,24,32,256]{3,2,1,0:T(8,128)}, f32[8,32,256]{2,1,0:T(8,128)}) custom-call(f32[4,24,32,256]{3,2,1,0:T(8,128)} %st_ref.1, f32[4,24,256]{2,1,0:T(8,128)} %copy-done.6, f32[4,24,256]{2,1,0:T(8,128)} %copy-done.7, f32[4,24,32,1]{3,2,1,0:T(8,128)} %copy.43.ys_ref, f32[4,24,32,1]{3,2,1,0:T(8,128)} %copy.44.yn_ref, s32[32,256]{1,0:T(8,128)} %copy-done.5, ...), custom_call_target="tpu_custom_call" | custom-call | tf_op jit(solution)/shard_map/pallas_call | solution.py:368
  70.1 0.1 collective-permute-start.10
  70.1 3.2 %collective-permute-start.8 = (f32[8,32,256]{2,1,0:T(8,128)}, f32[8,32,256]{2,1,0:T(8,128)S(1)}, u32[]{:S(2)}, u32[]{:S(2)}) collective-permute-start(f32[8,32,256]{2,1,0:T(8,128)} %get-tuple-element.39), channel_id=1, source_target_pairs={{0,3},{1,0},{2,1},{3,2},{4,7},{5,4},{6,5},{7,6},{8,11},{9,8},{10,9... | collective-permute-start | bytes 786440 | tf_op jit(solution)/shard_map/ppermute | solution.py:201
  73.4 11.3 %collective-permute-done.10 = f32[8,32,256]{2,1,0:T(8,128)S(1)} collective-permute-done((f32[8,32,256]{2,1,0:T(8,128)}, f32[8,32,256]{2,1,0:T(8,128)S(1)}, u32[]{:S(2)}, u32[]{:S(2)}) %collective-permute-start.10) | collective-permute-done | bytes 262176 | tf_op jit(solution)/shard_map/ppermute | solution.py:201
  84.7 1.1 %select_bitcast_fusion.2 = (f32[1,8,32,256]{3,2,1,0:T(8,128)S(1)}, f32[1,8,32,256]{3,2,1,0:T(8,128)S(1)}, f32[1,8,32,256]{3,2,1,0:T(8,128)S(1)}, f32[1,8,32,256]{3,2,1,0:T(8,128)S(1)}) fusion(f32[8,32,256]{2,1,0:T(8,128)S(1)} %collective-permute-done.8, f32[8,32,256]{2,1,0:T(8,128)S(1)} %collective-permute-done.9, ...), kind=kLoop, calls=%fused_computation.18 | loop fusion | flops 786432 | bytes 2097164 | tf_op jit(solution)/shard_map/stack | solution.py:208
  85.8 0.0 all-gather.3.cloned.1.call-done
  85.9 1.6 %broadcast_in_dim.61 = f32[4,8,2,32,256]{4,3,2,1,0:T(8,128)S(1)} broadcast(f32[4,8,32,256]{3,2,1,0:T(8,128)} %bitcast.305), dimensions={0,1,3,4} | broadcast | bytes 3145728 | tf_op jit(solution)/shard_map/broadcast_in_dim | solution.py:160
  87.5 0.2 select_select_fusion
  87.7 0.3 select_select_fusion.1
  88.0 1.4 %copy-done.1 = f32[4,24,32,256]{3,2,1,0:T(8,128)S(1)} copy-done((f32[4,24,32,256]{3,2,1,0:T(8,128)S(1)}, f32[4,24,32,256]{3,2,1,0:T(8,128)}, u32[]{:S(2)}) %copy-start.1) | copy-done | bytes 3145752
  89.4 0.5 copy-done.3
  89.8 2.5 %fusion = f32[4,24,32,256]{3,2,1,0:T(8,128)} fusion(f32[4,24,32,256]{3,2,1,0:T(8,128)S(1)} %copy-done.1, f32[2,24,32,256]{3,2,1,0:T(8,128)S(1)} %copy-done.4, f32[4,32,256]{2,1,0:T(8,128)S(1)} %select_select_fusion, f32[2,24,32,256]{3,2,1,0:T(8,128)S(1)} %copy-done.3, f32[4,32,256]{2,1,0:T(8,128)S(1)} %select_select_fusion.1), kind=kLoop, calls=%fused_computation.3 | loop fusion | flops 3145728 | bytes 9699328 | tf_op jit(solution)/shard_map/add | solution.py:460
  (55 shorter events, 0.4 us)
Async XLA Ops:
  6.5 20.4 %copy-start = (s32[128,2048]{1,0:T(8,128)S(1)}, s32[128,2048]{1,0:T(8,128)}, u32[]{:S(2)}) copy-start(s32[128,2048]{1,0:T(8,128)} %param.10) | copy-start | bytes 3145732
  6.5 79.3 %all-gather.3.cloned.1.call-start = ((), (), s32[]{:S(2)}) async-start(), calls=%async_computation | async-start | bytes 1310720 | tf_op jit(solution)/shard_map/all_gather | solution.py:425
  12.3 22.5 %collective-permute-start.2 = (f32[4,24,32]{2,1,0:T(8,128)S(1)}, f32[4,24,32]{2,1,0:T(8,128)S(1)}, u32[]{:S(2)}, u32[]{:S(2)}) collective-permute-start(f32[4,24,32]{2,1,0:T(8,128)S(1)} %bitcast.311), channel_id=1, source_target_pairs={{0,4},{4,8},{8,12},{12,16},{16,20},{20,24},{24,28},{28,0},{1,5},{5... | collective-permute-start | bytes 36872 | tf_op jit(solution)/shard_map/ppermute | solution.py:402
  16.1 18.7 %collective-permute-start.3 = (f32[4,24,32]{2,1,0:T(8,128)S(1)}, f32[4,24,32]{2,1,0:T(8,128)S(1)}, u32[]{:S(2)}, u32[]{:S(2)}) collective-permute-start(f32[4,24,32]{2,1,0:T(8,128)S(1)} %bitcast.310), channel_id=1, source_target_pairs={{4,0},{8,4},{12,8},{16,12},{20,16},{24,20},{28,24},{0,28},{5,1},{9... | collective-permute-start | bytes 36872 | tf_op jit(solution)/shard_map/ppermute | solution.py:403
  20.2 20.6 %collective-permute-start = (f32[4,24,256]{2,1,0:T(8,128)S(1)}, f32[4,24,256]{2,1,0:T(8,128)S(1)}, u32[]{:S(2)}, u32[]{:S(2)}) collective-permute-start(f32[4,24,256]{2,1,0:T(8,128)S(1)} %bitcast.308), channel_id=1, source_target_pairs={{0,32},{32,64},{64,96},{96,0},{1,33},{33,65},{65,97},{97,1},{2,34}... | collective-permute-start | bytes 294920 | tf_op jit(solution)/shard_map/ppermute | solution.py:400
  20.3 20.6 %collective-permute-start.1 = (f32[4,24,256]{2,1,0:T(8,128)S(1)}, f32[4,24,256]{2,1,0:T(8,128)S(1)}, u32[]{:S(2)}, u32[]{:S(2)}) collective-permute-start(f32[4,24,256]{2,1,0:T(8,128)S(1)} %bitcast.309), channel_id=1, source_target_pairs={{32,0},{64,32},{96,64},{0,96},{33,1},{65,33},{97,65},{1,97},{34,2}... | collective-permute-start | bytes 294920 | tf_op jit(solution)/shard_map/ppermute | solution.py:401
  22.9 12.1 %collective-permute-start.7 = (f32[2,32,256]{2,1,0:T(8,128)S(1)}, f32[2,32,256]{2,1,0:T(8,128)S(1)}, u32[]{:S(2)}, u32[]{:S(2)}) collective-permute-start(f32[2,32,256]{2,1,0:T(8,128)S(1)} %slice_bitcast_fusion.17), channel_id=1, source_target_pairs={{0,1},{1,2},{2,3},{4,5},{5,6},{6,7},{8,9},{9,10},{10,11},{12,13},{... | collective-permute-start | bytes 196616 | tf_op jit(solution)/shard_map/ppermute | solution.py:395
  29.2 3.6 %copy-start.2 = (f32[2,24,32,256]{3,2,1,0:T(8,128)S(1)}, f32[2,24,32,256]{3,2,1,0:T(8,128)}, u32[]{:S(2)}) copy-start(f32[2,24,32,256]{3,2,1,0:T(8,128)} %param.9) | copy-start | bytes 4718596
  30.8 3.3 %copy-start.5 = (s32[32,256]{1,0:T(8,128)}, s32[32,256]{1,0:T(8,128)S(1)}, u32[]{:S(2)}) copy-start(s32[32,256]{1,0:T(8,128)S(1)} %get-tuple-element.61.dc_ref) | copy-start | bytes 98308
  30.9 9.9 %copy-start.10 = (s32[1,256]{1,0:T(1,128)}, s32[1,256]{1,0:T(1,128)S(1)}, u32[]{:S(2)}) copy-start(s32[1,256]{1,0:T(1,128)S(1)} %get-tuple-element.56.dxw_ref) | copy-start | bytes 3076
  30.9 10.0 %copy-start.9 = (s32[1,256]{1,0:T(1,128)}, s32[1,256]{1,0:T(1,128)S(1)}, u32[]{:S(2)}) copy-start(s32[1,256]{1,0:T(1,128)S(1)} %get-tuple-element.55.dxe_ref) | copy-start | bytes 3076
  32.7 1.4 %copy-start.8 = (f32[2,32,256]{2,1,0:T(8,128)S(1)}, f32[2,32,256]{2,1,0:T(8,128)}, u32[]{:S(2)}) copy-start(f32[2,32,256]{2,1,0:T(8,128)} %param.11) | copy-start | bytes 196612
  40.8 15.8 %copy-start.6 = (f32[4,24,256]{2,1,0:T(8,128)}, f32[4,24,256]{2,1,0:T(8,128)S(1)}, u32[]{:S(2)}) copy-start(f32[4,24,256]{2,1,0:T(8,128)S(1)} %collective-permute-done.xw_ref) | copy-start | bytes 294916
  40.9 15.7 %copy-start.7 = (f32[4,24,256]{2,1,0:T(8,128)}, f32[4,24,256]{2,1,0:T(8,128)S(1)}, u32[]{:S(2)}) copy-start(f32[4,24,256]{2,1,0:T(8,128)S(1)} %collective-permute-done.1.xe_ref) | copy-start | bytes 294916
  40.9 13.1 %collective-permute-start.4 = (f32[36,256]{1,0:T(8,128)S(1)}, f32[36,256]{1,0:T(8,128)S(1)}, u32[]{:S(2)}, u32[]{:S(2)}) collective-permute-start(f32[36,256]{1,0:T(8,128)S(1)} %pad_maximum_fusion), channel_id=1, source_target_pairs={{0,1},{1,2},{2,3},{4,5},{5,6},{6,7},{8,9},{9,10},{10,11},{12,13},{... | collective-permute-start | bytes 110600 | tf_op jit(solution)/shard_map/ppermute | solution.py:439
  44.8 9.2 %collective-permute-start.5 = (f32[36,256]{1,0:T(8,128)S(1)}, f32[36,256]{1,0:T(8,128)S(1)}, u32[]{:S(2)}, u32[]{:S(2)}) collective-permute-start(f32[36,256]{1,0:T(8,128)S(1)} %pad_maximum_fusion), channel_id=1, source_target_pairs={{0,2},{1,3},{4,6},{5,7},{8,10},{9,11},{12,14},{13,15},{16,18},{17,... | collective-permute-start | bytes 110600 | tf_op jit(solution)/shard_map/ppermute | solution.py:439
  48.4 5.6 %collective-permute-start.6 = (f32[36,256]{1,0:T(8,128)S(1)}, f32[36,256]{1,0:T(8,128)S(1)}, u32[]{:S(2)}, u32[]{:S(2)}) collective-permute-start(f32[36,256]{1,0:T(8,128)S(1)} %pad_maximum_fusion), channel_id=1, source_target_pairs={{0,3},{4,7},{8,11},{12,15},{16,19},{20,23},{24,27},{28,31},{32,35}... | collective-permute-start | bytes 110600 | tf_op jit(solution)/shard_map/ppermute | solution.py:439
  70.1 14.6 %collective-permute-start.10 = (f32[8,32,256]{2,1,0:T(8,128)}, f32[8,32,256]{2,1,0:T(8,128)S(1)}, u32[]{:S(2)}, u32[]{:S(2)}) collective-permute-start(f32[8,32,256]{2,1,0:T(8,128)} %get-tuple-element.39), channel_id=1, source_target_pairs={{0,1},{1,2},{2,3},{3,0},{4,5},{5,6},{6,7},{7,4},{8,9},{9,10},{10,1... | collective-permute-start | bytes 786440 | tf_op jit(solution)/shard_map/ppermute | solution.py:201
  70.1 14.6 %collective-permute-start.8 = (f32[8,32,256]{2,1,0:T(8,128)}, f32[8,32,256]{2,1,0:T(8,128)S(1)}, u32[]{:S(2)}, u32[]{:S(2)}) collective-permute-start(f32[8,32,256]{2,1,0:T(8,128)} %get-tuple-element.39), channel_id=1, source_target_pairs={{0,3},{1,0},{2,1},{3,2},{4,7},{5,4},{6,5},{7,6},{8,11},{9,8},{10,9... | collective-permute-start | bytes 786440 | tf_op jit(solution)/shard_map/ppermute | solution.py:201
  73.4 11.3 %collective-permute-start.9 = (f32[8,32,256]{2,1,0:T(8,128)}, f32[8,32,256]{2,1,0:T(8,128)S(1)}, u32[]{:S(2)}, u32[]{:S(2)}) collective-permute-start(f32[8,32,256]{2,1,0:T(8,128)} %get-tuple-element.39), channel_id=1, source_target_pairs={{0,2},{1,3},{2,0},{3,1},{4,6},{5,7},{6,4},{7,5},{8,10},{9,11},{10,... | collective-permute-start | bytes 786440 | tf_op jit(solution)/shard_map/ppermute | solution.py:201
  85.8 2.1 %copy-start.4 = (f32[2,24,32,256]{3,2,1,0:T(8,128)S(1)}, f32[2,24,32,256]{3,2,1,0:T(8,128)}, u32[]{:S(2)}) copy-start(f32[2,24,32,256]{3,2,1,0:T(8,128)} %get-tuple-element.42) | copy-start | bytes 4718596
  87.5 1.9 %copy-start.1 = (f32[4,24,32,256]{3,2,1,0:T(8,128)S(1)}, f32[4,24,32,256]{3,2,1,0:T(8,128)}, u32[]{:S(2)}) copy-start(f32[4,24,32,256]{3,2,1,0:T(8,128)} %get-tuple-element.38) | copy-start | bytes 9437188
  87.5 2.4 %copy-start.3 = (f32[2,24,32,256]{3,2,1,0:T(8,128)S(1)}, f32[2,24,32,256]{3,2,1,0:T(8,128)}, u32[]{:S(2)}) copy-start(f32[2,24,32,256]{3,2,1,0:T(8,128)} %get-tuple-element.41) | copy-start | bytes 4718596
Sparse Core Ops, SparseCore 0:
  40.9 24.1 all-gather.2

commit v11 on v10

--- a/solution.py
+++ b/solution.py
@@ -124,7 +124,7 @@
 
 def coupling_solve(coupling, ctop):
     pairs, levels, cols_x, cols_y = coupling.shape
-    bx = 8 if cols_x % 8 == 0 else cols_x
+    bx = 16 if cols_x % 16 == 0 else cols_x
     cspec = _specs(pairs, levels, bx, cols_y)
     full = jax.ShapeDtypeStruct(coupling.shape, jnp.float32)
     return pl.pallas_call(

time: 99.6 us -> 98.7 us (level)
  transfers between devices with their start and end apart: 12 -> 12, of which waited for: 1 -> 1; matrix products, arithmetic and copies ran while one was open for 20% -> 20% of each run, Pallas kernels for 19% -> 18%
where the time goes in v11:
time: 98.7 us; the launch traced here: 98.3 us
  starting transfers between devices  23.5 us (24%)
  local copies, waits for them, and re-layouts  23 us (23%)
  Pallas kernels  17.7 us (18%)
  between operations  13.8 us (14%)
  waiting for transfers between devices  11.4 us (12%)
  other arithmetic  8.86 us (9%)
    pallas_call x1, Pallas kernels, fused_solve(): pl.pallas_call(fused_kernel, grid=(levels // chunk,), in_specs=specs, out...  13.5 us
    ppermute x3, waiting for transfers between devices, gather_by_permutes(): received.append(lax.ppermute(part, axis, shift))  11.3 us
    ppermute x3, starting transfers between devices, per_device(): shallower = shallower + lax.ppermute(pack, 'gz', pairs_z)  8.7 us
    unnamed x26, local copies, waits for them, and re-layouts  4.58 us
    pallas_call x1, Pallas kernels, coupling_solve(): pl.pallas_call(coupling_kernel, grid=(cols_x // bx,), in_specs=[cspec, _p...  4.26 us
    ppermute x1, starting transfers between devices, per_device(): mix_above = lax.ppermute(mixing[:, lev_count - 1], 'gz', down_z)  3.93 us
    slice x1, local copies, waits for them, and re-layouts, per_device(): halo_yn = lax.ppermute(state[:, :, :, 0], 'gy', dn_y)  3.7 us
    ppermute x3, starting transfers between devices, gather_by_permutes(): received.append(lax.ppermute(part, axis, shift))  3.3 us
  transfers between devices with their start and end apart: 12, of which 1 were waited for; matrix products, arithmetic and copies ran while one was open for 20% of the time, Pallas kernels for 18%

profile of v11, /device:TPU:0, one launch (start us, length us, event | category | flops | bytes accessed | tf_op | source)
XLA Modules:
  0.0 98.3 jit_solution(3305876145069947395)
XLA Ops:
  6.5 3.7 %fusion.48 = (f32[4,24,32,1]{3,2,1,0:T(8,128)S(1)}, f32[4,24,32,1]{3,2,1,0:T(8,128)}) fusion(f32[4,24,32,256]{3,2,1,0:T(8,128)} %st_ref.1), kind=kLoop, calls=%fused_computation.140 | loop fusion | bytes 49152 | tf_op jit(solution)/shard_map/slice | solution.py:403
  10.2 2.0 %copy.49 = f32[4,24,32,1]{2,1,0,3:T(8,128)S(1)} copy(f32[4,24,32,1]{3,2,1,0:T(8,128)} %get-tuple-element.46) | data formatting | bytes 24576
  12.3 3.2 %collective-permute-start.2 = (f32[4,24,32]{2,1,0:T(8,128)S(1)}, f32[4,24,32]{2,1,0:T(8,128)S(1)}, u32[]{:S(2)}, u32[]{:S(2)}) collective-permute-start(f32[4,24,32]{2,1,0:T(8,128)S(1)} %bitcast.311), channel_id=1, source_target_pairs={{0,4},{4,8},{8,12},{12,16},{16,20},{20,24},{24,28},{28,0},{1,5},{5... | collective-permute-start | bytes 36872 | tf_op jit(solution)/shard_map/ppermute | solution.py:402
  15.5 0.6 copy.50
  16.1 2.6 %collective-permute-start.3 = (f32[4,24,32]{2,1,0:T(8,128)S(1)}, f32[4,24,32]{2,1,0:T(8,128)S(1)}, u32[]{:S(2)}, u32[]{:S(2)}) collective-permute-start(f32[4,24,32]{2,1,0:T(8,128)S(1)} %bitcast.310), channel_id=1, source_target_pairs={{4,0},{8,4},{12,8},{16,12},{20,16},{24,20},{28,24},{0,28},{5,1},{9... | collective-permute-start | bytes 36872 | tf_op jit(solution)/shard_map/ppermute | solution.py:403
  18.6 1.5 %fusion.49 = (f32[4,24,1,256]{3,2,1,0:T(1,128)S(1)}, f32[4,24,1,256]{3,2,1,0:T(1,128)S(1)}) fusion(f32[4,24,32,256]{3,2,1,0:T(8,128)} %st_ref.1), kind=kLoop, calls=%fused_computation.141 | loop fusion | bytes 393216 | tf_op jit(solution)/shard_map/slice | solution.py:401
  20.2 0.1 collective-permute-start
  20.3 1.8 %collective-permute-start.1 = (f32[4,24,256]{2,1,0:T(8,128)S(1)}, f32[4,24,256]{2,1,0:T(8,128)S(1)}, u32[]{:S(2)}, u32[]{:S(2)}) collective-permute-start(f32[4,24,256]{2,1,0:T(8,128)S(1)} %bitcast.309), channel_id=1, source_target_pairs={{32,0},{64,32},{96,64},{0,96},{33,1},{65,33},{97,65},{1,97},{34,2}... | collective-permute-start | bytes 294920 | tf_op jit(solution)/shard_map/ppermute | solution.py:401
  22.1 0.8 slice_bitcast_fusion.17
  22.9 3.9 %collective-permute-start.7 = (f32[2,32,256]{2,1,0:T(8,128)S(1)}, f32[2,32,256]{2,1,0:T(8,128)S(1)}, u32[]{:S(2)}, u32[]{:S(2)}) collective-permute-start(f32[2,32,256]{2,1,0:T(8,128)S(1)} %slice_bitcast_fusion.17), channel_id=1, source_target_pairs={{0,1},{1,2},{2,3},{4,5},{5,6},{6,7},{8,9},{9,10},{10,11},{12,13},{... | collective-permute-start | bytes 196616 | tf_op jit(solution)/shard_map/ppermute | solution.py:395
  27.0 0.7 gather_fusion
  27.6 0.1 broadcast_select_fusion
  27.7 0.4 copy.40
  28.1 1.0 %gather_fusion.1 = s32[258,34]{1,0:T(8,128)S(1)} fusion(s32[34,2048]{0,1:T(8,128)S(1)} %copy.40, s32[1024]{0:T(1024)S(1)} %pad_clamp_fusion), kind=kCustom, calls=%fused_computation.1 | custom fusion | bytes 71208 | tf_op jit(solution)/shard_map/jit(_take)/gather | solution.py:407
  29.2 0.1 copy.41
  29.3 0.8 slice_reduce_fusion
  30.1 0.7 fusion.51
  30.8 0.1 fusion.50
  30.9 0.1 fusion.5
  31.0 1.7 %compare_select_fusion = (f32[24,32,256]{2,1,0:T(8,128)S(1)}, f32[32,256]{1,0:T(8,128)S(1)}) fusion(s32[32,256]{1,0:T(8,128)S(1)} %get-tuple-element.61.dc_ref, s32[24]{0:T(128)S(1)} %iota_add_fusion.1, f32[4,24,32,256]{3,2,1,0:T(8,128)} %st_ref.1), kind=kLoop, calls=%fused_computation.15 | loop fusion | flops 2351104 | bytes 2424928 | tf_op jit(solution)/shard_map/mul | solution.py:420
  32.7 0.1 fusion.21
  32.8 1.3 %broadcast_multiply_fusion.c_ref = f32[2,24,32,256]{3,2,1,0:T(8,128)} fusion(f32[2,24,32,256]{3,2,1,0:T(8,128)S(1)} %copy-done.2, f32[24,32,256]{2,1,0:T(8,128)S(1)} %get-tuple-element.66), kind=kLoop, calls=%fused_computation.12 | loop fusion | flops 393216 | bytes 3932160 | tf_op jit(solution)/shard_map/mul | solution.py:420
  34.1 0.6 broadcast_select_fusion.1.wind_ref
  34.8 0.2 scatter.9
  35.0 0.6 multiply_select_fusion.ctop_ref
  35.7 4.3 %shard_map.46 = (f32[2,24,32,256]{3,2,1,0:T(8,128)}, f32[2,24,32,256]{3,2,1,0:T(8,128)}, f32[2,24,32,256]{3,2,1,0:T(8,128)}, f32[2,24,32,256]{3,2,1,0:T(8,128)}, f32[8,32,256]{2,1,0:T(8,128)}) custom-call(f32[2,24,32,256]{3,2,1,0:T(8,128)} %broadcast_multiply_fusion.c_ref, f32[2,32,256]{2,1,0:T(8,128)} %multiply_select_fusion.ctop_ref), custom_call_target="tpu_custom_call" | custom-call | tf_op jit(solution)/shard_map/pallas_call | solution.py:130
  40.1 3.8 %collective-permute-start.4 = (f32[36,256]{1,0:T(8,128)S(1)}, f32[36,256]{1,0:T(8,128)S(1)}, u32[]{:S(2)}, u32[]{:S(2)}) collective-permute-start(f32[36,256]{1,0:T(8,128)S(1)} %pad_maximum_fusion), channel_id=1, source_target_pairs={{0,1},{1,2},{2,3},{4,5},{5,6},{6,7},{8,9},{9,10},{10,11},{12,13},{... | collective-permute-start | bytes 110600 | tf_op jit(solution)/shard_map/ppermute | solution.py:439
  43.9 3.6 %collective-permute-start.5 = (f32[36,256]{1,0:T(8,128)S(1)}, f32[36,256]{1,0:T(8,128)S(1)}, u32[]{:S(2)}, u32[]{:S(2)}) collective-permute-start(f32[36,256]{1,0:T(8,128)S(1)} %pad_maximum_fusion), channel_id=1, source_target_pairs={{0,2},{1,3},{4,6},{5,7},{8,10},{9,11},{12,14},{13,15},{16,18},{17,... | collective-permute-start | bytes 110600 | tf_op jit(solution)/shard_map/ppermute | solution.py:439
  47.5 1.3 %collective-permute-start.6 = (f32[36,256]{1,0:T(8,128)S(1)}, f32[36,256]{1,0:T(8,128)S(1)}, u32[]{:S(2)}, u32[]{:S(2)}) collective-permute-start(f32[36,256]{1,0:T(8,128)S(1)} %pad_maximum_fusion), channel_id=1, source_target_pairs={{0,3},{4,7},{8,11},{12,15},{16,19},{20,23},{24,27},{28,31},{32,35}... | collective-permute-start | bytes 110600 | tf_op jit(solution)/shard_map/ppermute | solution.py:439
  48.8 0.6 stack.23.lane_ref
  49.5 1.9 %copy.43.ys_ref = f32[4,24,32,1]{3,2,1,0:T(8,128)} copy(f32[4,24,32,1]{2,1,0,3:T(8,128)S(1)} %bitcast.306) | data formatting | bytes 24576 | tf_op jit(solution)/shard_map/broadcast_in_dim | solution.py:451
  51.3 1.8 %copy.44.yn_ref = f32[4,24,32,1]{3,2,1,0:T(8,128)} copy(f32[4,24,32,1]{2,1,0,3:T(8,128)S(1)} %bitcast.307) | data formatting | bytes 24576 | tf_op jit(solution)/shard_map/broadcast_in_dim | solution.py:451
  53.2 0.6 slice.288.sc_ref
  53.8 0.7 copy.45.sys_ref
  54.5 0.7 copy.46.syn_ref
  55.1 0.6 fusion.52
  55.7 13.5 %shard_map.47 = (f32[4,24,32,256]{3,2,1,0:T(8,128)}, f32[8,32,256]{2,1,0:T(8,128)}) custom-call(f32[4,24,32,256]{3,2,1,0:T(8,128)} %st_ref.1, f32[4,24,256]{2,1,0:T(8,128)} %copy-done.6, f32[4,24,256]{2,1,0:T(8,128)} %copy-done.7, f32[4,24,32,1]{3,2,1,0:T(8,128)} %copy.43.ys_ref, f32[4,24,32,1]{3,2,1,0:T(8,128)} %copy.44.yn_ref, s32[32,256]{1,0:T(8,128)} %copy-done.5, ...), custom_call_target="tpu_custom_call" | custom-call | tf_op jit(solution)/shard_map/pallas_call | solution.py:368
  69.2 0.1 collective-permute-start.10
  69.3 3.2 %collective-permute-start.8 = (f32[8,32,256]{2,1,0:T(8,128)}, f32[8,32,256]{2,1,0:T(8,128)S(1)}, u32[]{:S(2)}, u32[]{:S(2)}) collective-permute-start(f32[8,32,256]{2,1,0:T(8,128)} %get-tuple-element.39), channel_id=1, source_target_pairs={{0,3},{1,0},{2,1},{3,2},{4,7},{5,4},{6,5},{7,6},{8,11},{9,8},{10,9... | collective-permute-start | bytes 786440 | tf_op jit(solution)/shard_map/ppermute | solution.py:201
  72.5 11.3 %collective-permute-done.10 = f32[8,32,256]{2,1,0:T(8,128)S(1)} collective-permute-done((f32[8,32,256]{2,1,0:T(8,128)}, f32[8,32,256]{2,1,0:T(8,128)S(1)}, u32[]{:S(2)}, u32[]{:S(2)}) %collective-permute-start.10) | collective-permute-done | bytes 262176 | tf_op jit(solution)/shard_map/ppermute | solution.py:201
  83.9 1.1 %select_bitcast_fusion.2 = (f32[1,8,32,256]{3,2,1,0:T(8,128)S(1)}, f32[1,8,32,256]{3,2,1,0:T(8,128)S(1)}, f32[1,8,32,256]{3,2,1,0:T(8,128)S(1)}, f32[1,8,32,256]{3,2,1,0:T(8,128)S(1)}) fusion(f32[8,32,256]{2,1,0:T(8,128)S(1)} %collective-permute-done.8, f32[8,32,256]{2,1,0:T(8,128)S(1)} %collective-permute-done.9, ...), kind=kLoop, calls=%fused_computation.18 | loop fusion | flops 786432 | bytes 2097164 | tf_op jit(solution)/shard_map/stack | solution.py:208
  85.0 0.0 all-gather.3.cloned.1.call-done
  85.0 1.6 %broadcast_in_dim.61 = f32[4,8,2,32,256]{4,3,2,1,0:T(8,128)S(1)} broadcast(f32[4,8,32,256]{3,2,1,0:T(8,128)} %bitcast.305), dimensions={0,1,3,4} | broadcast | bytes 3145728 | tf_op jit(solution)/shard_map/broadcast_in_dim | solution.py:160
  86.6 0.2 select_select_fusion
  86.9 0.3 select_select_fusion.1
  87.1 1.4 %copy-done.1 = f32[4,24,32,256]{3,2,1,0:T(8,128)S(1)} copy-done((f32[4,24,32,256]{3,2,1,0:T(8,128)S(1)}, f32[4,24,32,256]{3,2,1,0:T(8,128)}, u32[]{:S(2)}) %copy-start.1) | copy-done | bytes 3145752
  88.5 0.5 copy-done.3
  89.0 2.5 %fusion = f32[4,24,32,256]{3,2,1,0:T(8,128)} fusion(f32[4,24,32,256]{3,2,1,0:T(8,128)S(1)} %copy-done.1, f32[2,24,32,256]{3,2,1,0:T(8,128)S(1)} %copy-done.4, f32[4,32,256]{2,1,0:T(8,128)S(1)} %select_select_fusion, f32[2,24,32,256]{3,2,1,0:T(8,128)S(1)} %copy-done.3, f32[4,32,256]{2,1,0:T(8,128)S(1)} %select_select_fusion.1), kind=kLoop, calls=%fused_computation.3 | loop fusion | flops 3145728 | bytes 9699328 | tf_op jit(solution)/shard_map/add | solution.py:460
  (55 shorter events, 0.4 us)
Async XLA Ops:
  6.5 20.4 %copy-start = (s32[128,2048]{1,0:T(8,128)S(1)}, s32[128,2048]{1,0:T(8,128)}, u32[]{:S(2)}) copy-start(s32[128,2048]{1,0:T(8,128)} %param.10) | copy-start | bytes 3145732
  6.5 78.5 %all-gather.3.cloned.1.call-start = ((), (), s32[]{:S(2)}) async-start(), calls=%async_computation | async-start | bytes 1310720 | tf_op jit(solution)/shard_map/all_gather | solution.py:425
  12.3 22.5 %collective-permute-start.2 = (f32[4,24,32]{2,1,0:T(8,128)S(1)}, f32[4,24,32]{2,1,0:T(8,128)S(1)}, u32[]{:S(2)}, u32[]{:S(2)}) collective-permute-start(f32[4,24,32]{2,1,0:T(8,128)S(1)} %bitcast.311), channel_id=1, source_target_pairs={{0,4},{4,8},{8,12},{12,16},{16,20},{20,24},{24,28},{28,0},{1,5},{5... | collective-permute-start | bytes 36872 | tf_op jit(solution)/shard_map/ppermute | solution.py:402
  16.1 18.7 %collective-permute-start.3 = (f32[4,24,32]{2,1,0:T(8,128)S(1)}, f32[4,24,32]{2,1,0:T(8,128)S(1)}, u32[]{:S(2)}, u32[]{:S(2)}) collective-permute-start(f32[4,24,32]{2,1,0:T(8,128)S(1)} %bitcast.310), channel_id=1, source_target_pairs={{4,0},{8,4},{12,8},{16,12},{20,16},{24,20},{28,24},{0,28},{5,1},{9... | collective-permute-start | bytes 36872 | tf_op jit(solution)/shard_map/ppermute | solution.py:403
  20.2 19.8 %collective-permute-start = (f32[4,24,256]{2,1,0:T(8,128)S(1)}, f32[4,24,256]{2,1,0:T(8,128)S(1)}, u32[]{:S(2)}, u32[]{:S(2)}) collective-permute-start(f32[4,24,256]{2,1,0:T(8,128)S(1)} %bitcast.308), channel_id=1, source_target_pairs={{0,32},{32,64},{64,96},{96,0},{1,33},{33,65},{65,97},{97,1},{2,34}... | collective-permute-start | bytes 294920 | tf_op jit(solution)/shard_map/ppermute | solution.py:400
  20.3 19.7 %collective-permute-start.1 = (f32[4,24,256]{2,1,0:T(8,128)S(1)}, f32[4,24,256]{2,1,0:T(8,128)S(1)}, u32[]{:S(2)}, u32[]{:S(2)}) collective-permute-start(f32[4,24,256]{2,1,0:T(8,128)S(1)} %bitcast.309), channel_id=1, source_target_pairs={{32,0},{64,32},{96,64},{0,96},{33,1},{65,33},{97,65},{1,97},{34,2}... | collective-permute-start | bytes 294920 | tf_op jit(solution)/shard_map/ppermute | solution.py:401
  22.9 12.1 %collective-permute-start.7 = (f32[2,32,256]{2,1,0:T(8,128)S(1)}, f32[2,32,256]{2,1,0:T(8,128)S(1)}, u32[]{:S(2)}, u32[]{:S(2)}) collective-permute-start(f32[2,32,256]{2,1,0:T(8,128)S(1)} %slice_bitcast_fusion.17), channel_id=1, source_target_pairs={{0,1},{1,2},{2,3},{4,5},{5,6},{6,7},{8,9},{9,10},{10,11},{12,13},{... | collective-permute-start | bytes 196616 | tf_op jit(solution)/shard_map/ppermute | solution.py:395
  29.2 3.6 %copy-start.2 = (f32[2,24,32,256]{3,2,1,0:T(8,128)S(1)}, f32[2,24,32,256]{3,2,1,0:T(8,128)}, u32[]{:S(2)}) copy-start(f32[2,24,32,256]{3,2,1,0:T(8,128)} %param.9) | copy-start | bytes 4718596
  30.8 3.3 %copy-start.5 = (s32[32,256]{1,0:T(8,128)}, s32[32,256]{1,0:T(8,128)S(1)}, u32[]{:S(2)}) copy-start(s32[32,256]{1,0:T(8,128)S(1)} %get-tuple-element.61.dc_ref) | copy-start | bytes 98308
  30.9 9.1 %copy-start.10 = (s32[1,256]{1,0:T(1,128)}, s32[1,256]{1,0:T(1,128)S(1)}, u32[]{:S(2)}) copy-start(s32[1,256]{1,0:T(1,128)S(1)} %get-tuple-element.56.dxw_ref) | copy-start | bytes 3076
  30.9 9.1 %copy-start.9 = (s32[1,256]{1,0:T(1,128)}, s32[1,256]{1,0:T(1,128)S(1)}, u32[]{:S(2)}) copy-start(s32[1,256]{1,0:T(1,128)S(1)} %get-tuple-element.55.dxe_ref) | copy-start | bytes 3076
  32.7 1.4 %copy-start.8 = (f32[2,32,256]{2,1,0:T(8,128)S(1)}, f32[2,32,256]{2,1,0:T(8,128)}, u32[]{:S(2)}) copy-start(f32[2,32,256]{2,1,0:T(8,128)} %param.11) | copy-start | bytes 196612
  40.0 15.8 %copy-start.6 = (f32[4,24,256]{2,1,0:T(8,128)}, f32[4,24,256]{2,1,0:T(8,128)S(1)}, u32[]{:S(2)}) copy-start(f32[4,24,256]{2,1,0:T(8,128)S(1)} %collective-permute-done.xw_ref) | copy-start | bytes 294916
  40.0 15.7 %copy-start.7 = (f32[4,24,256]{2,1,0:T(8,128)}, f32[4,24,256]{2,1,0:T(8,128)S(1)}, u32[]{:S(2)}) copy-start(f32[4,24,256]{2,1,0:T(8,128)S(1)} %collective-permute-done.1.xe_ref) | copy-start | bytes 294916
  40.1 13.1 %collective-permute-start.4 = (f32[36,256]{1,0:T(8,128)S(1)}, f32[36,256]{1,0:T(8,128)S(1)}, u32[]{:S(2)}, u32[]{:S(2)}) collective-permute-start(f32[36,256]{1,0:T(8,128)S(1)} %pad_maximum_fusion), channel_id=1, source_target_pairs={{0,1},{1,2},{2,3},{4,5},{5,6},{6,7},{8,9},{9,10},{10,11},{12,13},{... | collective-permute-start | bytes 110600 | tf_op jit(solution)/shard_map/ppermute | solution.py:439
  43.9 9.2 %collective-permute-start.5 = (f32[36,256]{1,0:T(8,128)S(1)}, f32[36,256]{1,0:T(8,128)S(1)}, u32[]{:S(2)}, u32[]{:S(2)}) collective-permute-start(f32[36,256]{1,0:T(8,128)S(1)} %pad_maximum_fusion), channel_id=1, source_target_pairs={{0,2},{1,3},{4,6},{5,7},{8,10},{9,11},{12,14},{13,15},{16,18},{17,... | collective-permute-start | bytes 110600 | tf_op jit(solution)/shard_map/ppermute | solution.py:439
  47.5 5.6 %collective-permute-start.6 = (f32[36,256]{1,0:T(8,128)S(1)}, f32[36,256]{1,0:T(8,128)S(1)}, u32[]{:S(2)}, u32[]{:S(2)}) collective-permute-start(f32[36,256]{1,0:T(8,128)S(1)} %pad_maximum_fusion), channel_id=1, source_target_pairs={{0,3},{4,7},{8,11},{12,15},{16,19},{20,23},{24,27},{28,31},{32,35}... | collective-permute-start | bytes 110600 | tf_op jit(solution)/shard_map/ppermute | solution.py:439
  69.2 14.6 %collective-permute-start.10 = (f32[8,32,256]{2,1,0:T(8,128)}, f32[8,32,256]{2,1,0:T(8,128)S(1)}, u32[]{:S(2)}, u32[]{:S(2)}) collective-permute-start(f32[8,32,256]{2,1,0:T(8,128)} %get-tuple-element.39), channel_id=1, source_target_pairs={{0,1},{1,2},{2,3},{3,0},{4,5},{5,6},{6,7},{7,4},{8,9},{9,10},{10,1... | collective-permute-start | bytes 786440 | tf_op jit(solution)/shard_map/ppermute | solution.py:201
  69.3 14.6 %collective-permute-start.8 = (f32[8,32,256]{2,1,0:T(8,128)}, f32[8,32,256]{2,1,0:T(8,128)S(1)}, u32[]{:S(2)}, u32[]{:S(2)}) collective-permute-start(f32[8,32,256]{2,1,0:T(8,128)} %get-tuple-element.39), channel_id=1, source_target_pairs={{0,3},{1,0},{2,1},{3,2},{4,7},{5,4},{6,5},{7,6},{8,11},{9,8},{10,9... | collective-permute-start | bytes 786440 | tf_op jit(solution)/shard_map/ppermute | solution.py:201
  72.5 11.3 %collective-permute-start.9 = (f32[8,32,256]{2,1,0:T(8,128)}, f32[8,32,256]{2,1,0:T(8,128)S(1)}, u32[]{:S(2)}, u32[]{:S(2)}) collective-permute-start(f32[8,32,256]{2,1,0:T(8,128)} %get-tuple-element.39), channel_id=1, source_target_pairs={{0,2},{1,3},{2,0},{3,1},{4,6},{5,7},{6,4},{7,5},{8,10},{9,11},{10,... | collective-permute-start | bytes 786440 | tf_op jit(solution)/shard_map/ppermute | solution.py:201
  85.0 2.1 %copy-start.4 = (f32[2,24,32,256]{3,2,1,0:T(8,128)S(1)}, f32[2,24,32,256]{3,2,1,0:T(8,128)}, u32[]{:S(2)}) copy-start(f32[2,24,32,256]{3,2,1,0:T(8,128)} %get-tuple-element.42) | copy-start | bytes 4718596
  86.6 1.9 %copy-start.1 = (f32[4,24,32,256]{3,2,1,0:T(8,128)S(1)}, f32[4,24,32,256]{3,2,1,0:T(8,128)}, u32[]{:S(2)}) copy-start(f32[4,24,32,256]{3,2,1,0:T(8,128)} %get-tuple-element.38) | copy-start | bytes 9437188
  86.6 2.4 %copy-start.3 = (f32[2,24,32,256]{3,2,1,0:T(8,128)S(1)}, f32[2,24,32,256]{3,2,1,0:T(8,128)}, u32[]{:S(2)}) copy-start(f32[2,24,32,256]{3,2,1,0:T(8,128)} %get-tuple-element.41) | copy-start | bytes 4718596
Sparse Core Ops, SparseCore 0:
  40.1 24.1 all-gather.2

commit v12 on v11

--- a/solution.py
+++ b/solution.py
@@ -330,7 +330,7 @@
         return (run_c, run_xw, run_xe, run_ys, run_yn), jnp.stack(vy), c_here
 
     run = (run_c_s[...], run_xw_s[...], run_xe_s[...], run_ys_s[...], run_yn_s[...])
-    carry = lax.fori_loop(0, chunk, level, (run, vy_s[...], cprev_s[...]), unroll=4)
+    carry = lax.fori_loop(0, chunk, level, (run, vy_s[...], cprev_s[...]), unroll=chunk)
     run, vy, c_prev = carry
     run_c_s[...], run_xw_s[...], run_xe_s[...], run_ys_s[...], run_yn_s[...] = run
     vy_s[...] = vy

time: 98.7 us -> 98.3 us (level)
  no operation moved by 1% of the time
where the time goes in v12:
time: 98.3 us; the launch traced here: 97.9 us
  starting transfers between devices  23.5 us (24%)
  local copies, waits for them, and re-layouts  23 us (23%)
  Pallas kernels  17.3 us (18%)
  between operations  13.8 us (14%)
  waiting for transfers between devices  11.4 us (12%)
  other arithmetic  8.86 us (9%)
    pallas_call x1, Pallas kernels, fused_solve(): pl.pallas_call(fused_kernel, grid=(levels // chunk,), in_specs=specs, out...  13 us
    ppermute x3, waiting for transfers between devices, gather_by_permutes(): received.append(lax.ppermute(part, axis, shift))  11.3 us
    ppermute x3, starting transfers between devices, per_device(): shallower = shallower + lax.ppermute(pack, 'gz', pairs_z)  8.7 us
    unnamed x26, local copies, waits for them, and re-layouts  4.58 us
    pallas_call x1, Pallas kernels, coupling_solve(): pl.pallas_call(coupling_kernel, grid=(cols_x // bx,), in_specs=[cspec, _p...  4.26 us
    ppermute x1, starting transfers between devices, per_device(): mix_above = lax.ppermute(mixing[:, lev_count - 1], 'gz', down_z)  3.93 us
    slice x1, local copies, waits for them, and re-layouts, per_device(): halo_yn = lax.ppermute(state[:, :, :, 0], 'gy', dn_y)  3.7 us
    ppermute x3, starting transfers between devices, gather_by_permutes(): received.append(lax.ppermute(part, axis, shift))  3.3 us
  transfers between devices with their start and end apart: 12, of which 1 were waited for; matrix products, arithmetic and copies ran while one was open for 20% of the time, Pallas kernels for 18%

profile of v12, /device:TPU:0, one launch (start us, length us, event | category | flops | bytes accessed | tf_op | source)
XLA Modules:
  0.0 97.9 jit_solution(14215557576571541076)
XLA Ops:
  6.5 3.7 %fusion.48 = (f32[4,24,32,1]{3,2,1,0:T(8,128)S(1)}, f32[4,24,32,1]{3,2,1,0:T(8,128)}) fusion(f32[4,24,32,256]{3,2,1,0:T(8,128)} %st_ref.1), kind=kLoop, calls=%fused_computation.140 | loop fusion | bytes 49152 | tf_op jit(solution)/shard_map/slice | solution.py:403
  10.2 2.0 %copy.49 = f32[4,24,32,1]{2,1,0,3:T(8,128)S(1)} copy(f32[4,24,32,1]{3,2,1,0:T(8,128)} %get-tuple-element.46) | data formatting | bytes 24576
  12.3 3.2 %collective-permute-start.2 = (f32[4,24,32]{2,1,0:T(8,128)S(1)}, f32[4,24,32]{2,1,0:T(8,128)S(1)}, u32[]{:S(2)}, u32[]{:S(2)}) collective-permute-start(f32[4,24,32]{2,1,0:T(8,128)S(1)} %bitcast.311), channel_id=1, source_target_pairs={{0,4},{4,8},{8,12},{12,16},{16,20},{20,24},{24,28},{28,0},{1,5},{5... | collective-permute-start | bytes 36872 | tf_op jit(solution)/shard_map/ppermute | solution.py:402
  15.5 0.6 copy.50
  16.1 2.6 %collective-permute-start.3 = (f32[4,24,32]{2,1,0:T(8,128)S(1)}, f32[4,24,32]{2,1,0:T(8,128)S(1)}, u32[]{:S(2)}, u32[]{:S(2)}) collective-permute-start(f32[4,24,32]{2,1,0:T(8,128)S(1)} %bitcast.310), channel_id=1, source_target_pairs={{4,0},{8,4},{12,8},{16,12},{20,16},{24,20},{28,24},{0,28},{5,1},{9... | collective-permute-start | bytes 36872 | tf_op jit(solution)/shard_map/ppermute | solution.py:403
  18.6 1.5 %fusion.49 = (f32[4,24,1,256]{3,2,1,0:T(1,128)S(1)}, f32[4,24,1,256]{3,2,1,0:T(1,128)S(1)}) fusion(f32[4,24,32,256]{3,2,1,0:T(8,128)} %st_ref.1), kind=kLoop, calls=%fused_computation.141 | loop fusion | bytes 393216 | tf_op jit(solution)/shard_map/slice | solution.py:401
  20.2 0.1 collective-permute-start
  20.3 1.8 %collective-permute-start.1 = (f32[4,24,256]{2,1,0:T(8,128)S(1)}, f32[4,24,256]{2,1,0:T(8,128)S(1)}, u32[]{:S(2)}, u32[]{:S(2)}) collective-permute-start(f32[4,24,256]{2,1,0:T(8,128)S(1)} %bitcast.309), channel_id=1, source_target_pairs={{32,0},{64,32},{96,64},{0,96},{33,1},{65,33},{97,65},{1,97},{34,2}... | collective-permute-start | bytes 294920 | tf_op jit(solution)/shard_map/ppermute | solution.py:401
  22.1 0.8 slice_bitcast_fusion.17
  22.9 3.9 %collective-permute-start.7 = (f32[2,32,256]{2,1,0:T(8,128)S(1)}, f32[2,32,256]{2,1,0:T(8,128)S(1)}, u32[]{:S(2)}, u32[]{:S(2)}) collective-permute-start(f32[2,32,256]{2,1,0:T(8,128)S(1)} %slice_bitcast_fusion.17), channel_id=1, source_target_pairs={{0,1},{1,2},{2,3},{4,5},{5,6},{6,7},{8,9},{9,10},{10,11},{12,13},{... | collective-permute-start | bytes 196616 | tf_op jit(solution)/shard_map/ppermute | solution.py:395
  27.0 0.7 gather_fusion
  27.6 0.1 broadcast_select_fusion
  27.7 0.4 copy.40
  28.1 1.0 %gather_fusion.1 = s32[258,34]{1,0:T(8,128)S(1)} fusion(s32[34,2048]{0,1:T(8,128)S(1)} %copy.40, s32[1024]{0:T(1024)S(1)} %pad_clamp_fusion), kind=kCustom, calls=%fused_computation.1 | custom fusion | bytes 71208 | tf_op jit(solution)/shard_map/jit(_take)/gather | solution.py:407
  29.2 0.1 copy.41
  29.3 0.8 slice_reduce_fusion
  30.1 0.7 fusion.51
  30.8 0.1 fusion.50
  30.9 0.1 fusion.5
  31.0 1.7 %compare_select_fusion = (f32[24,32,256]{2,1,0:T(8,128)S(1)}, f32[32,256]{1,0:T(8,128)S(1)}) fusion(s32[32,256]{1,0:T(8,128)S(1)} %get-tuple-element.61.dc_ref, s32[24]{0:T(128)S(1)} %iota_add_fusion.1, f32[4,24,32,256]{3,2,1,0:T(8,128)} %st_ref.1), kind=kLoop, calls=%fused_computation.15 | loop fusion | flops 2351104 | bytes 2424928 | tf_op jit(solution)/shard_map/mul | solution.py:420
  32.7 0.1 fusion.21
  32.8 1.3 %broadcast_multiply_fusion.c_ref = f32[2,24,32,256]{3,2,1,0:T(8,128)} fusion(f32[2,24,32,256]{3,2,1,0:T(8,128)S(1)} %copy-done.2, f32[24,32,256]{2,1,0:T(8,128)S(1)} %get-tuple-element.66), kind=kLoop, calls=%fused_computation.12 | loop fusion | flops 393216 | bytes 3932160 | tf_op jit(solution)/shard_map/mul | solution.py:420
  34.1 0.6 broadcast_select_fusion.1.wind_ref
  34.8 0.2 scatter.9
  35.0 0.6 multiply_select_fusion.ctop_ref
  35.7 4.3 %shard_map.46 = (f32[2,24,32,256]{3,2,1,0:T(8,128)}, f32[2,24,32,256]{3,2,1,0:T(8,128)}, f32[2,24,32,256]{3,2,1,0:T(8,128)}, f32[2,24,32,256]{3,2,1,0:T(8,128)}, f32[8,32,256]{2,1,0:T(8,128)}) custom-call(f32[2,24,32,256]{3,2,1,0:T(8,128)} %broadcast_multiply_fusion.c_ref, f32[2,32,256]{2,1,0:T(8,128)} %multiply_select_fusion.ctop_ref), custom_call_target="tpu_custom_call" | custom-call | tf_op jit(solution)/shard_map/pallas_call | solution.py:130
  40.1 3.8 %collective-permute-start.4 = (f32[36,256]{1,0:T(8,128)S(1)}, f32[36,256]{1,0:T(8,128)S(1)}, u32[]{:S(2)}, u32[]{:S(2)}) collective-permute-start(f32[36,256]{1,0:T(8,128)S(1)} %pad_maximum_fusion), channel_id=1, source_target_pairs={{0,1},{1,2},{2,3},{4,5},{5,6},{6,7},{8,9},{9,10},{10,11},{12,13},{... | collective-permute-start | bytes 110600 | tf_op jit(solution)/shard_map/ppermute | solution.py:439
  43.9 3.6 %collective-permute-start.5 = (f32[36,256]{1,0:T(8,128)S(1)}, f32[36,256]{1,0:T(8,128)S(1)}, u32[]{:S(2)}, u32[]{:S(2)}) collective-permute-start(f32[36,256]{1,0:T(8,128)S(1)} %pad_maximum_fusion), channel_id=1, source_target_pairs={{0,2},{1,3},{4,6},{5,7},{8,10},{9,11},{12,14},{13,15},{16,18},{17,... | collective-permute-start | bytes 110600 | tf_op jit(solution)/shard_map/ppermute | solution.py:439
  47.5 1.3 %collective-permute-start.6 = (f32[36,256]{1,0:T(8,128)S(1)}, f32[36,256]{1,0:T(8,128)S(1)}, u32[]{:S(2)}, u32[]{:S(2)}) collective-permute-start(f32[36,256]{1,0:T(8,128)S(1)} %pad_maximum_fusion), channel_id=1, source_target_pairs={{0,3},{4,7},{8,11},{12,15},{16,19},{20,23},{24,27},{28,31},{32,35}... | collective-permute-start | bytes 110600 | tf_op jit(solution)/shard_map/ppermute | solution.py:439
  48.8 0.6 stack.23.lane_ref
  49.5 1.9 %copy.43.ys_ref = f32[4,24,32,1]{3,2,1,0:T(8,128)} copy(f32[4,24,32,1]{2,1,0,3:T(8,128)S(1)} %bitcast.306) | data formatting | bytes 24576 | tf_op jit(solution)/shard_map/broadcast_in_dim | solution.py:451
  51.3 1.8 %copy.44.yn_ref = f32[4,24,32,1]{3,2,1,0:T(8,128)} copy(f32[4,24,32,1]{2,1,0,3:T(8,128)S(1)} %bitcast.307) | data formatting | bytes 24576 | tf_op jit(solution)/shard_map/broadcast_in_dim | solution.py:451
  53.2 0.6 slice.288.sc_ref
  53.8 0.7 copy.45.sys_ref
  54.5 0.7 copy.46.syn_ref
  55.1 0.6 fusion.52
  55.7 13.0 %shard_map.47 = (f32[4,24,32,256]{3,2,1,0:T(8,128)}, f32[8,32,256]{2,1,0:T(8,128)}) custom-call(f32[4,24,32,256]{3,2,1,0:T(8,128)} %st_ref.1, f32[4,24,256]{2,1,0:T(8,128)} %copy-done.6, f32[4,24,256]{2,1,0:T(8,128)} %copy-done.7, f32[4,24,32,1]{3,2,1,0:T(8,128)} %copy.43.ys_ref, f32[4,24,32,1]{3,2,1,0:T(8,128)} %copy.44.yn_ref, s32[32,256]{1,0:T(8,128)} %copy-done.5, ...), custom_call_target="tpu_custom_call" | custom-call | tf_op jit(solution)/shard_map/pallas_call | solution.py:368
  68.8 0.1 collective-permute-start.10
  68.9 3.2 %collective-permute-start.8 = (f32[8,32,256]{2,1,0:T(8,128)}, f32[8,32,256]{2,1,0:T(8,128)S(1)}, u32[]{:S(2)}, u32[]{:S(2)}) collective-permute-start(f32[8,32,256]{2,1,0:T(8,128)} %get-tuple-element.39), channel_id=1, source_target_pairs={{0,3},{1,0},{2,1},{3,2},{4,7},{5,4},{6,5},{7,6},{8,11},{9,8},{10,9... | collective-permute-start | bytes 786440 | tf_op jit(solution)/shard_map/ppermute | solution.py:201
  72.1 11.3 %collective-permute-done.10 = f32[8,32,256]{2,1,0:T(8,128)S(1)} collective-permute-done((f32[8,32,256]{2,1,0:T(8,128)}, f32[8,32,256]{2,1,0:T(8,128)S(1)}, u32[]{:S(2)}, u32[]{:S(2)}) %collective-permute-start.10) | collective-permute-done | bytes 262176 | tf_op jit(solution)/shard_map/ppermute | solution.py:201
  83.4 1.1 %select_bitcast_fusion.2 = (f32[1,8,32,256]{3,2,1,0:T(8,128)S(1)}, f32[1,8,32,256]{3,2,1,0:T(8,128)S(1)}, f32[1,8,32,256]{3,2,1,0:T(8,128)S(1)}, f32[1,8,32,256]{3,2,1,0:T(8,128)S(1)}) fusion(f32[8,32,256]{2,1,0:T(8,128)S(1)} %collective-permute-done.8, f32[8,32,256]{2,1,0:T(8,128)S(1)} %collective-permute-done.9, ...), kind=kLoop, calls=%fused_computation.18 | loop fusion | flops 786432 | bytes 2097164 | tf_op jit(solution)/shard_map/stack | solution.py:208
  84.5 0.0 all-gather.3.cloned.1.call-done
  84.6 1.6 %broadcast_in_dim.61 = f32[4,8,2,32,256]{4,3,2,1,0:T(8,128)S(1)} broadcast(f32[4,8,32,256]{3,2,1,0:T(8,128)} %bitcast.305), dimensions={0,1,3,4} | broadcast | bytes 3145728 | tf_op jit(solution)/shard_map/broadcast_in_dim | solution.py:160
  86.2 0.2 select_select_fusion
  86.4 0.3 select_select_fusion.1
  86.7 1.4 %copy-done.1 = f32[4,24,32,256]{3,2,1,0:T(8,128)S(1)} copy-done((f32[4,24,32,256]{3,2,1,0:T(8,128)S(1)}, f32[4,24,32,256]{3,2,1,0:T(8,128)}, u32[]{:S(2)}) %copy-start.1) | copy-done | bytes 3145752
  88.1 0.5 copy-done.3
  88.6 2.5 %fusion = f32[4,24,32,256]{3,2,1,0:T(8,128)} fusion(f32[4,24,32,256]{3,2,1,0:T(8,128)S(1)} %copy-done.1, f32[2,24,32,256]{3,2,1,0:T(8,128)S(1)} %copy-done.4, f32[4,32,256]{2,1,0:T(8,128)S(1)} %select_select_fusion, f32[2,24,32,256]{3,2,1,0:T(8,128)S(1)} %copy-done.3, f32[4,32,256]{2,1,0:T(8,128)S(1)} %select_select_fusion.1), kind=kLoop, calls=%fused_computation.3 | loop fusion | flops 3145728 | bytes 9699328 | tf_op jit(solution)/shard_map/add | solution.py:460
  (55 shorter events, 0.4 us)
Async XLA Ops:
  6.5 20.4 %copy-start = (s32[128,2048]{1,0:T(8,128)S(1)}, s32[128,2048]{1,0:T(8,128)}, u32[]{:S(2)}) copy-start(s32[128,2048]{1,0:T(8,128)} %param.10) | copy-start | bytes 3145732
  6.5 78.0 %all-gather.3.cloned.1.call-start = ((), (), s32[]{:S(2)}) async-start(), calls=%async_computation | async-start | bytes 1310720 | tf_op jit(solution)/shard_map/all_gather | solution.py:425
  12.3 22.5 %collective-permute-start.2 = (f32[4,24,32]{2,1,0:T(8,128)S(1)}, f32[4,24,32]{2,1,0:T(8,128)S(1)}, u32[]{:S(2)}, u32[]{:S(2)}) collective-permute-start(f32[4,24,32]{2,1,0:T(8,128)S(1)} %bitcast.311), channel_id=1, source_target_pairs={{0,4},{4,8},{8,12},{12,16},{16,20},{20,24},{24,28},{28,0},{1,5},{5... | collective-permute-start | bytes 36872 | tf_op jit(solution)/shard_map/ppermute | solution.py:402
  16.1 18.7 %collective-permute-start.3 = (f32[4,24,32]{2,1,0:T(8,128)S(1)}, f32[4,24,32]{2,1,0:T(8,128)S(1)}, u32[]{:S(2)}, u32[]{:S(2)}) collective-permute-start(f32[4,24,32]{2,1,0:T(8,128)S(1)} %bitcast.310), channel_id=1, source_target_pairs={{4,0},{8,4},{12,8},{16,12},{20,16},{24,20},{28,24},{0,28},{5,1},{9... | collective-permute-start | bytes 36872 | tf_op jit(solution)/shard_map/ppermute | solution.py:403
  20.2 19.8 %collective-permute-start = (f32[4,24,256]{2,1,0:T(8,128)S(1)}, f32[4,24,256]{2,1,0:T(8,128)S(1)}, u32[]{:S(2)}, u32[]{:S(2)}) collective-permute-start(f32[4,24,256]{2,1,0:T(8,128)S(1)} %bitcast.308), channel_id=1, source_target_pairs={{0,32},{32,64},{64,96},{96,0},{1,33},{33,65},{65,97},{97,1},{2,34}... | collective-permute-start | bytes 294920 | tf_op jit(solution)/shard_map/ppermute | solution.py:400
  20.3 19.7 %collective-permute-start.1 = (f32[4,24,256]{2,1,0:T(8,128)S(1)}, f32[4,24,256]{2,1,0:T(8,128)S(1)}, u32[]{:S(2)}, u32[]{:S(2)}) collective-permute-start(f32[4,24,256]{2,1,0:T(8,128)S(1)} %bitcast.309), channel_id=1, source_target_pairs={{32,0},{64,32},{96,64},{0,96},{33,1},{65,33},{97,65},{1,97},{34,2}... | collective-permute-start | bytes 294920 | tf_op jit(solution)/shard_map/ppermute | solution.py:401
  22.9 12.1 %collective-permute-start.7 = (f32[2,32,256]{2,1,0:T(8,128)S(1)}, f32[2,32,256]{2,1,0:T(8,128)S(1)}, u32[]{:S(2)}, u32[]{:S(2)}) collective-permute-start(f32[2,32,256]{2,1,0:T(8,128)S(1)} %slice_bitcast_fusion.17), channel_id=1, source_target_pairs={{0,1},{1,2},{2,3},{4,5},{5,6},{6,7},{8,9},{9,10},{10,11},{12,13},{... | collective-permute-start | bytes 196616 | tf_op jit(solution)/shard_map/ppermute | solution.py:395
  29.2 3.6 %copy-start.2 = (f32[2,24,32,256]{3,2,1,0:T(8,128)S(1)}, f32[2,24,32,256]{3,2,1,0:T(8,128)}, u32[]{:S(2)}) copy-start(f32[2,24,32,256]{3,2,1,0:T(8,128)} %param.9) | copy-start | bytes 4718596
  30.8 3.3 %copy-start.5 = (s32[32,256]{1,0:T(8,128)}, s32[32,256]{1,0:T(8,128)S(1)}, u32[]{:S(2)}) copy-start(s32[32,256]{1,0:T(8,128)S(1)} %get-tuple-element.61.dc_ref) | copy-start | bytes 98308
  30.9 9.1 %copy-start.10 = (s32[1,256]{1,0:T(1,128)}, s32[1,256]{1,0:T(1,128)S(1)}, u32[]{:S(2)}) copy-start(s32[1,256]{1,0:T(1,128)S(1)} %get-tuple-element.56.dxw_ref) | copy-start | bytes 3076
  30.9 9.1 %copy-start.9 = (s32[1,256]{1,0:T(1,128)}, s32[1,256]{1,0:T(1,128)S(1)}, u32[]{:S(2)}) copy-start(s32[1,256]{1,0:T(1,128)S(1)} %get-tuple-element.55.dxe_ref) | copy-start | bytes 3076
  32.7 1.4 %copy-start.8 = (f32[2,32,256]{2,1,0:T(8,128)S(1)}, f32[2,32,256]{2,1,0:T(8,128)}, u32[]{:S(2)}) copy-start(f32[2,32,256]{2,1,0:T(8,128)} %param.11) | copy-start | bytes 196612
  40.0 15.8 %copy-start.6 = (f32[4,24,256]{2,1,0:T(8,128)}, f32[4,24,256]{2,1,0:T(8,128)S(1)}, u32[]{:S(2)}) copy-start(f32[4,24,256]{2,1,0:T(8,128)S(1)} %collective-permute-done.xw_ref) | copy-start | bytes 294916
  40.0 15.7 %copy-start.7 = (f32[4,24,256]{2,1,0:T(8,128)}, f32[4,24,256]{2,1,0:T(8,128)S(1)}, u32[]{:S(2)}) copy-start(f32[4,24,256]{2,1,0:T(8,128)S(1)} %collective-permute-done.1.xe_ref) | copy-start | bytes 294916
  40.1 13.1 %collective-permute-start.4 = (f32[36,256]{1,0:T(8,128)S(1)}, f32[36,256]{1,0:T(8,128)S(1)}, u32[]{:S(2)}, u32[]{:S(2)}) collective-permute-start(f32[36,256]{1,0:T(8,128)S(1)} %pad_maximum_fusion), channel_id=1, source_target_pairs={{0,1},{1,2},{2,3},{4,5},{5,6},{6,7},{8,9},{9,10},{10,11},{12,13},{... | collective-permute-start | bytes 110600 | tf_op jit(solution)/shard_map/ppermute | solution.py:439
  43.9 9.2 %collective-permute-start.5 = (f32[36,256]{1,0:T(8,128)S(1)}, f32[36,256]{1,0:T(8,128)S(1)}, u32[]{:S(2)}, u32[]{:S(2)}) collective-permute-start(f32[36,256]{1,0:T(8,128)S(1)} %pad_maximum_fusion), channel_id=1, source_target_pairs={{0,2},{1,3},{4,6},{5,7},{8,10},{9,11},{12,14},{13,15},{16,18},{17,... | collective-permute-start | bytes 110600 | tf_op jit(solution)/shard_map/ppermute | solution.py:439
  47.5 5.6 %collective-permute-start.6 = (f32[36,256]{1,0:T(8,128)S(1)}, f32[36,256]{1,0:T(8,128)S(1)}, u32[]{:S(2)}, u32[]{:S(2)}) collective-permute-start(f32[36,256]{1,0:T(8,128)S(1)} %pad_maximum_fusion), channel_id=1, source_target_pairs={{0,3},{4,7},{8,11},{12,15},{16,19},{20,23},{24,27},{28,31},{32,35}... | collective-permute-start | bytes 110600 | tf_op jit(solution)/shard_map/ppermute | solution.py:439
  68.8 14.6 %collective-permute-start.10 = (f32[8,32,256]{2,1,0:T(8,128)}, f32[8,32,256]{2,1,0:T(8,128)S(1)}, u32[]{:S(2)}, u32[]{:S(2)}) collective-permute-start(f32[8,32,256]{2,1,0:T(8,128)} %get-tuple-element.39), channel_id=1, source_target_pairs={{0,1},{1,2},{2,3},{3,0},{4,5},{5,6},{6,7},{7,4},{8,9},{9,10},{10,1... | collective-permute-start | bytes 786440 | tf_op jit(solution)/shard_map/ppermute | solution.py:201
  68.9 14.6 %collective-permute-start.8 = (f32[8,32,256]{2,1,0:T(8,128)}, f32[8,32,256]{2,1,0:T(8,128)S(1)}, u32[]{:S(2)}, u32[]{:S(2)}) collective-permute-start(f32[8,32,256]{2,1,0:T(8,128)} %get-tuple-element.39), channel_id=1, source_target_pairs={{0,3},{1,0},{2,1},{3,2},{4,7},{5,4},{6,5},{7,6},{8,11},{9,8},{10,9... | collective-permute-start | bytes 786440 | tf_op jit(solution)/shard_map/ppermute | solution.py:201
  72.1 11.3 %collective-permute-start.9 = (f32[8,32,256]{2,1,0:T(8,128)}, f32[8,32,256]{2,1,0:T(8,128)S(1)}, u32[]{:S(2)}, u32[]{:S(2)}) collective-permute-start(f32[8,32,256]{2,1,0:T(8,128)} %get-tuple-element.39), channel_id=1, source_target_pairs={{0,2},{1,3},{2,0},{3,1},{4,6},{5,7},{6,4},{7,5},{8,10},{9,11},{10,... | collective-permute-start | bytes 786440 | tf_op jit(solution)/shard_map/ppermute | solution.py:201
  84.6 2.1 %copy-start.4 = (f32[2,24,32,256]{3,2,1,0:T(8,128)S(1)}, f32[2,24,32,256]{3,2,1,0:T(8,128)}, u32[]{:S(2)}) copy-start(f32[2,24,32,256]{3,2,1,0:T(8,128)} %get-tuple-element.42) | copy-start | bytes 4718596
  86.2 1.9 %copy-start.1 = (f32[4,24,32,256]{3,2,1,0:T(8,128)S(1)}, f32[4,24,32,256]{3,2,1,0:T(8,128)}, u32[]{:S(2)}) copy-start(f32[4,24,32,256]{3,2,1,0:T(8,128)} %get-tuple-element.38) | copy-start | bytes 9437188
  86.2 2.4 %copy-start.3 = (f32[2,24,32,256]{3,2,1,0:T(8,128)S(1)}, f32[2,24,32,256]{3,2,1,0:T(8,128)}, u32[]{:S(2)}) copy-start(f32[2,24,32,256]{3,2,1,0:T(8,128)} %get-tuple-element.41) | copy-start | bytes 4718596
Sparse Core Ops, SparseCore 0:
  40.1 24.1 all-gather.2

commit v13 on v12

--- a/solution.py
+++ b/solution.py
@@ -350,7 +350,7 @@
                 out.append(val)
             return jnp.stack(out)
 
-        later = lax.fori_loop(0, levels - 1, back, vy, unroll=2)
+        later = lax.fori_loop(0, levels - 1, back, vy, unroll=levels - 1)
         for f in range(fields):
             ends_ref[f] = later[f]
 

time: 98.3 us -> 98.1 us (level)
  no operation moved by 1% of the time
where the time goes in v13:
time: 98.1 us; the launch traced here: 97.7 us
  starting transfers between devices  23.5 us (24%)
  local copies, waits for them, and re-layouts  23 us (23%)
  Pallas kernels  17.2 us (18%)
  between operations  13.8 us (14%)
  waiting for transfers between devices  11.4 us (12%)
  other arithmetic  8.86 us (9%)
    pallas_call x1, Pallas kernels, fused_solve(): pl.pallas_call(fused_kernel, grid=(levels // chunk,), in_specs=specs, out...  12.9 us
    ppermute x3, waiting for transfers between devices, gather_by_permutes(): received.append(lax.ppermute(part, axis, shift))  11.3 us
    ppermute x3, starting transfers between devices, per_device(): shallower = shallower + lax.ppermute(pack, 'gz', pairs_z)  8.7 us
    unnamed x26, local copies, waits for them, and re-layouts  4.58 us
    pallas_call x1, Pallas kernels, coupling_solve(): pl.pallas_call(coupling_kernel, grid=(cols_x // bx,), in_specs=[cspec, _p...  4.26 us
    ppermute x1, starting transfers between devices, per_device(): mix_above = lax.ppermute(mixing[:, lev_count - 1], 'gz', down_z)  3.93 us
    slice x1, local copies, waits for them, and re-layouts, per_device(): halo_yn = lax.ppermute(state[:, :, :, 0], 'gy', dn_y)  3.7 us
    ppermute x3, starting transfers between devices, gather_by_permutes(): received.append(lax.ppermute(part, axis, shift))  3.3 us
  transfers between devices with their start and end apart: 12, of which 1 were waited for; matrix products, arithmetic and copies ran while one was open for 20% of the time, Pallas kernels for 18%

profile of v13, /device:TPU:0, one launch (start us, length us, event | category | flops | bytes accessed | tf_op | source)
XLA Modules:
  0.0 97.7 jit_solution(6846360840404474561)
XLA Ops:
  6.5 3.7 %fusion.48 = (f32[4,24,32,1]{3,2,1,0:T(8,128)S(1)}, f32[4,24,32,1]{3,2,1,0:T(8,128)}) fusion(f32[4,24,32,256]{3,2,1,0:T(8,128)} %st_ref.1), kind=kLoop, calls=%fused_computation.140 | loop fusion | bytes 49152 | tf_op jit(solution)/shard_map/slice | solution.py:403
  10.2 2.0 %copy.49 = f32[4,24,32,1]{2,1,0,3:T(8,128)S(1)} copy(f32[4,24,32,1]{3,2,1,0:T(8,128)} %get-tuple-element.46) | data formatting | bytes 24576
  12.3 3.2 %collective-permute-start.2 = (f32[4,24,32]{2,1,0:T(8,128)S(1)}, f32[4,24,32]{2,1,0:T(8,128)S(1)}, u32[]{:S(2)}, u32[]{:S(2)}) collective-permute-start(f32[4,24,32]{2,1,0:T(8,128)S(1)} %bitcast.311), channel_id=1, source_target_pairs={{0,4},{4,8},{8,12},{12,16},{16,20},{20,24},{24,28},{28,0},{1,5},{5... | collective-permute-start | bytes 36872 | tf_op jit(solution)/shard_map/ppermute | solution.py:402
  15.5 0.6 copy.50
  16.1 2.6 %collective-permute-start.3 = (f32[4,24,32]{2,1,0:T(8,128)S(1)}, f32[4,24,32]{2,1,0:T(8,128)S(1)}, u32[]{:S(2)}, u32[]{:S(2)}) collective-permute-start(f32[4,24,32]{2,1,0:T(8,128)S(1)} %bitcast.310), channel_id=1, source_target_pairs={{4,0},{8,4},{12,8},{16,12},{20,16},{24,20},{28,24},{0,28},{5,1},{9... | collective-permute-start | bytes 36872 | tf_op jit(solution)/shard_map/ppermute | solution.py:403
  18.6 1.5 %fusion.49 = (f32[4,24,1,256]{3,2,1,0:T(1,128)S(1)}, f32[4,24,1,256]{3,2,1,0:T(1,128)S(1)}) fusion(f32[4,24,32,256]{3,2,1,0:T(8,128)} %st_ref.1), kind=kLoop, calls=%fused_computation.141 | loop fusion | bytes 393216 | tf_op jit(solution)/shard_map/slice | solution.py:401
  20.2 0.1 collective-permute-start
  20.3 1.8 %collective-permute-start.1 = (f32[4,24,256]{2,1,0:T(8,128)S(1)}, f32[4,24,256]{2,1,0:T(8,128)S(1)}, u32[]{:S(2)}, u32[]{:S(2)}) collective-permute-start(f32[4,24,256]{2,1,0:T(8,128)S(1)} %bitcast.309), channel_id=1, source_target_pairs={{32,0},{64,32},{96,64},{0,96},{33,1},{65,33},{97,65},{1,97},{34,2}... | collective-permute-start | bytes 294920 | tf_op jit(solution)/shard_map/ppermute | solution.py:401
  22.1 0.8 slice_bitcast_fusion.17
  22.9 3.9 %collective-permute-start.7 = (f32[2,32,256]{2,1,0:T(8,128)S(1)}, f32[2,32,256]{2,1,0:T(8,128)S(1)}, u32[]{:S(2)}, u32[]{:S(2)}) collective-permute-start(f32[2,32,256]{2,1,0:T(8,128)S(1)} %slice_bitcast_fusion.17), channel_id=1, source_target_pairs={{0,1},{1,2},{2,3},{4,5},{5,6},{6,7},{8,9},{9,10},{10,11},{12,13},{... | collective-permute-start | bytes 196616 | tf_op jit(solution)/shard_map/ppermute | solution.py:395
  27.0 0.7 gather_fusion
  27.6 0.1 broadcast_select_fusion
  27.7 0.4 copy.40
  28.1 1.0 %gather_fusion.1 = s32[258,34]{1,0:T(8,128)S(1)} fusion(s32[34,2048]{0,1:T(8,128)S(1)} %copy.40, s32[1024]{0:T(1024)S(1)} %pad_clamp_fusion), kind=kCustom, calls=%fused_computation.1 | custom fusion | bytes 71208 | tf_op jit(solution)/shard_map/jit(_take)/gather | solution.py:407
  29.2 0.1 copy.41
  29.3 0.8 slice_reduce_fusion
  30.1 0.7 fusion.51
  30.8 0.1 fusion.50
  30.9 0.1 fusion.5
  31.0 1.7 %compare_select_fusion = (f32[24,32,256]{2,1,0:T(8,128)S(1)}, f32[32,256]{1,0:T(8,128)S(1)}) fusion(s32[32,256]{1,0:T(8,128)S(1)} %get-tuple-element.61.dc_ref, s32[24]{0:T(128)S(1)} %iota_add_fusion.1, f32[4,24,32,256]{3,2,1,0:T(8,128)} %st_ref.1), kind=kLoop, calls=%fused_computation.15 | loop fusion | flops 2351104 | bytes 2424928 | tf_op jit(solution)/shard_map/mul | solution.py:420
  32.7 0.1 fusion.21
  32.8 1.3 %broadcast_multiply_fusion.c_ref = f32[2,24,32,256]{3,2,1,0:T(8,128)} fusion(f32[2,24,32,256]{3,2,1,0:T(8,128)S(1)} %copy-done.2, f32[24,32,256]{2,1,0:T(8,128)S(1)} %get-tuple-element.66), kind=kLoop, calls=%fused_computation.12 | loop fusion | flops 393216 | bytes 3932160 | tf_op jit(solution)/shard_map/mul | solution.py:420
  34.1 0.6 broadcast_select_fusion.1.wind_ref
  34.8 0.2 scatter.9
  35.0 0.6 multiply_select_fusion.ctop_ref
  35.7 4.3 %shard_map.46 = (f32[2,24,32,256]{3,2,1,0:T(8,128)}, f32[2,24,32,256]{3,2,1,0:T(8,128)}, f32[2,24,32,256]{3,2,1,0:T(8,128)}, f32[2,24,32,256]{3,2,1,0:T(8,128)}, f32[8,32,256]{2,1,0:T(8,128)}) custom-call(f32[2,24,32,256]{3,2,1,0:T(8,128)} %broadcast_multiply_fusion.c_ref, f32[2,32,256]{2,1,0:T(8,128)} %multiply_select_fusion.ctop_ref), custom_call_target="tpu_custom_call" | custom-call | tf_op jit(solution)/shard_map/pallas_call | solution.py:130
  40.1 3.8 %collective-permute-start.4 = (f32[36,256]{1,0:T(8,128)S(1)}, f32[36,256]{1,0:T(8,128)S(1)}, u32[]{:S(2)}, u32[]{:S(2)}) collective-permute-start(f32[36,256]{1,0:T(8,128)S(1)} %pad_maximum_fusion), channel_id=1, source_target_pairs={{0,1},{1,2},{2,3},{4,5},{5,6},{6,7},{8,9},{9,10},{10,11},{12,13},{... | collective-permute-start | bytes 110600 | tf_op jit(solution)/shard_map/ppermute | solution.py:439
  43.9 3.6 %collective-permute-start.5 = (f32[36,256]{1,0:T(8,128)S(1)}, f32[36,256]{1,0:T(8,128)S(1)}, u32[]{:S(2)}, u32[]{:S(2)}) collective-permute-start(f32[36,256]{1,0:T(8,128)S(1)} %pad_maximum_fusion), channel_id=1, source_target_pairs={{0,2},{1,3},{4,6},{5,7},{8,10},{9,11},{12,14},{13,15},{16,18},{17,... | collective-permute-start | bytes 110600 | tf_op jit(solution)/shard_map/ppermute | solution.py:439
  47.5 1.3 %collective-permute-start.6 = (f32[36,256]{1,0:T(8,128)S(1)}, f32[36,256]{1,0:T(8,128)S(1)}, u32[]{:S(2)}, u32[]{:S(2)}) collective-permute-start(f32[36,256]{1,0:T(8,128)S(1)} %pad_maximum_fusion), channel_id=1, source_target_pairs={{0,3},{4,7},{8,11},{12,15},{16,19},{20,23},{24,27},{28,31},{32,35}... | collective-permute-start | bytes 110600 | tf_op jit(solution)/shard_map/ppermute | solution.py:439
  48.8 0.6 stack.23.lane_ref
  49.5 1.9 %copy.43.ys_ref = f32[4,24,32,1]{3,2,1,0:T(8,128)} copy(f32[4,24,32,1]{2,1,0,3:T(8,128)S(1)} %bitcast.306) | data formatting | bytes 24576 | tf_op jit(solution)/shard_map/broadcast_in_dim | solution.py:451
  51.3 1.8 %copy.44.yn_ref = f32[4,24,32,1]{3,2,1,0:T(8,128)} copy(f32[4,24,32,1]{2,1,0,3:T(8,128)S(1)} %bitcast.307) | data formatting | bytes 24576 | tf_op jit(solution)/shard_map/broadcast_in_dim | solution.py:451
  53.2 0.6 slice.288.sc_ref
  53.8 0.7 copy.45.sys_ref
  54.5 0.7 copy.46.syn_ref
  55.1 0.6 fusion.52
  55.7 12.9 %shard_map.47 = (f32[4,24,32,256]{3,2,1,0:T(8,128)}, f32[8,32,256]{2,1,0:T(8,128)}) custom-call(f32[4,24,32,256]{3,2,1,0:T(8,128)} %st_ref.1, f32[4,24,256]{2,1,0:T(8,128)} %copy-done.6, f32[4,24,256]{2,1,0:T(8,128)} %copy-done.7, f32[4,24,32,1]{3,2,1,0:T(8,128)} %copy.43.ys_ref, f32[4,24,32,1]{3,2,1,0:T(8,128)} %copy.44.yn_ref, s32[32,256]{1,0:T(8,128)} %copy-done.5, ...), custom_call_target="tpu_custom_call" | custom-call | tf_op jit(solution)/shard_map/pallas_call | solution.py:368
  68.6 0.1 collective-permute-start.10
  68.7 3.2 %collective-permute-start.8 = (f32[8,32,256]{2,1,0:T(8,128)}, f32[8,32,256]{2,1,0:T(8,128)S(1)}, u32[]{:S(2)}, u32[]{:S(2)}) collective-permute-start(f32[8,32,256]{2,1,0:T(8,128)} %get-tuple-element.39), channel_id=1, source_target_pairs={{0,3},{1,0},{2,1},{3,2},{4,7},{5,4},{6,5},{7,6},{8,11},{9,8},{10,9... | collective-permute-start | bytes 786440 | tf_op jit(solution)/shard_map/ppermute | solution.py:201
  71.9 11.3 %collective-permute-done.10 = f32[8,32,256]{2,1,0:T(8,128)S(1)} collective-permute-done((f32[8,32,256]{2,1,0:T(8,128)}, f32[8,32,256]{2,1,0:T(8,128)S(1)}, u32[]{:S(2)}, u32[]{:S(2)}) %collective-permute-start.10) | collective-permute-done | bytes 262176 | tf_op jit(solution)/shard_map/ppermute | solution.py:201
  83.3 1.1 %select_bitcast_fusion.2 = (f32[1,8,32,256]{3,2,1,0:T(8,128)S(1)}, f32[1,8,32,256]{3,2,1,0:T(8,128)S(1)}, f32[1,8,32,256]{3,2,1,0:T(8,128)S(1)}, f32[1,8,32,256]{3,2,1,0:T(8,128)S(1)}) fusion(f32[8,32,256]{2,1,0:T(8,128)S(1)} %collective-permute-done.8, f32[8,32,256]{2,1,0:T(8,128)S(1)} %collective-permute-done.9, ...), kind=kLoop, calls=%fused_computation.18 | loop fusion | flops 786432 | bytes 2097164 | tf_op jit(solution)/shard_map/stack | solution.py:208
  84.4 0.0 all-gather.3.cloned.1.call-done
  84.4 1.6 %broadcast_in_dim.61 = f32[4,8,2,32,256]{4,3,2,1,0:T(8,128)S(1)} broadcast(f32[4,8,32,256]{3,2,1,0:T(8,128)} %bitcast.305), dimensions={0,1,3,4} | broadcast | bytes 3145728 | tf_op jit(solution)/shard_map/broadcast_in_dim | solution.py:160
  86.1 0.2 select_select_fusion
  86.3 0.3 select_select_fusion.1
  86.5 1.4 %copy-done.1 = f32[4,24,32,256]{3,2,1,0:T(8,128)S(1)} copy-done((f32[4,24,32,256]{3,2,1,0:T(8,128)S(1)}, f32[4,24,32,256]{3,2,1,0:T(8,128)}, u32[]{:S(2)}) %copy-start.1) | copy-done | bytes 3145752
  88.0 0.5 copy-done.3
  88.4 2.5 %fusion = f32[4,24,32,256]{3,2,1,0:T(8,128)} fusion(f32[4,24,32,256]{3,2,1,0:T(8,128)S(1)} %copy-done.1, f32[2,24,32,256]{3,2,1,0:T(8,128)S(1)} %copy-done.4, f32[4,32,256]{2,1,0:T(8,128)S(1)} %select_select_fusion, f32[2,24,32,256]{3,2,1,0:T(8,128)S(1)} %copy-done.3, f32[4,32,256]{2,1,0:T(8,128)S(1)} %select_select_fusion.1), kind=kLoop, calls=%fused_computation.3 | loop fusion | flops 3145728 | bytes 9699328 | tf_op jit(solution)/shard_map/add | solution.py:460
  (55 shorter events, 0.4 us)
Async XLA Ops:
  6.5 20.4 %copy-start = (s32[128,2048]{1,0:T(8,128)S(1)}, s32[128,2048]{1,0:T(8,128)}, u32[]{:S(2)}) copy-start(s32[128,2048]{1,0:T(8,128)} %param.10) | copy-start | bytes 3145732
  6.5 77.9 %all-gather.3.cloned.1.call-start = ((), (), s32[]{:S(2)}) async-start(), calls=%async_computation | async-start | bytes 1310720 | tf_op jit(solution)/shard_map/all_gather | solution.py:425
  12.3 22.5 %collective-permute-start.2 = (f32[4,24,32]{2,1,0:T(8,128)S(1)}, f32[4,24,32]{2,1,0:T(8,128)S(1)}, u32[]{:S(2)}, u32[]{:S(2)}) collective-permute-start(f32[4,24,32]{2,1,0:T(8,128)S(1)} %bitcast.311), channel_id=1, source_target_pairs={{0,4},{4,8},{8,12},{12,16},{16,20},{20,24},{24,28},{28,0},{1,5},{5... | collective-permute-start | bytes 36872 | tf_op jit(solution)/shard_map/ppermute | solution.py:402
  16.1 18.7 %collective-permute-start.3 = (f32[4,24,32]{2,1,0:T(8,128)S(1)}, f32[4,24,32]{2,1,0:T(8,128)S(1)}, u32[]{:S(2)}, u32[]{:S(2)}) collective-permute-start(f32[4,24,32]{2,1,0:T(8,128)S(1)} %bitcast.310), channel_id=1, source_target_pairs={{4,0},{8,4},{12,8},{16,12},{20,16},{24,20},{28,24},{0,28},{5,1},{9... | collective-permute-start | bytes 36872 | tf_op jit(solution)/shard_map/ppermute | solution.py:403
  20.2 19.8 %collective-permute-start = (f32[4,24,256]{2,1,0:T(8,128)S(1)}, f32[4,24,256]{2,1,0:T(8,128)S(1)}, u32[]{:S(2)}, u32[]{:S(2)}) collective-permute-start(f32[4,24,256]{2,1,0:T(8,128)S(1)} %bitcast.308), channel_id=1, source_target_pairs={{0,32},{32,64},{64,96},{96,0},{1,33},{33,65},{65,97},{97,1},{2,34}... | collective-permute-start | bytes 294920 | tf_op jit(solution)/shard_map/ppermute | solution.py:400
  20.3 19.7 %collective-permute-start.1 = (f32[4,24,256]{2,1,0:T(8,128)S(1)}, f32[4,24,256]{2,1,0:T(8,128)S(1)}, u32[]{:S(2)}, u32[]{:S(2)}) collective-permute-start(f32[4,24,256]{2,1,0:T(8,128)S(1)} %bitcast.309), channel_id=1, source_target_pairs={{32,0},{64,32},{96,64},{0,96},{33,1},{65,33},{97,65},{1,97},{34,2}... | collective-permute-start | bytes 294920 | tf_op jit(solution)/shard_map/ppermute | solution.py:401
  22.9 12.1 %collective-permute-start.7 = (f32[2,32,256]{2,1,0:T(8,128)S(1)}, f32[2,32,256]{2,1,0:T(8,128)S(1)}, u32[]{:S(2)}, u32[]{:S(2)}) collective-permute-start(f32[2,32,256]{2,1,0:T(8,128)S(1)} %slice_bitcast_fusion.17), channel_id=1, source_target_pairs={{0,1},{1,2},{2,3},{4,5},{5,6},{6,7},{8,9},{9,10},{10,11},{12,13},{... | collective-permute-start | bytes 196616 | tf_op jit(solution)/shard_map/ppermute | solution.py:395
  29.2 3.6 %copy-start.2 = (f32[2,24,32,256]{3,2,1,0:T(8,128)S(1)}, f32[2,24,32,256]{3,2,1,0:T(8,128)}, u32[]{:S(2)}) copy-start(f32[2,24,32,256]{3,2,1,0:T(8,128)} %param.9) | copy-start | bytes 4718596
  30.8 3.3 %copy-start.5 = (s32[32,256]{1,0:T(8,128)}, s32[32,256]{1,0:T(8,128)S(1)}, u32[]{:S(2)}) copy-start(s32[32,256]{1,0:T(8,128)S(1)} %get-tuple-element.61.dc_ref) | copy-start | bytes 98308
  30.9 9.1 %copy-start.10 = (s32[1,256]{1,0:T(1,128)}, s32[1,256]{1,0:T(1,128)S(1)}, u32[]{:S(2)}) copy-start(s32[1,256]{1,0:T(1,128)S(1)} %get-tuple-element.56.dxw_ref) | copy-start | bytes 3076
  30.9 9.1 %copy-start.9 = (s32[1,256]{1,0:T(1,128)}, s32[1,256]{1,0:T(1,128)S(1)}, u32[]{:S(2)}) copy-start(s32[1,256]{1,0:T(1,128)S(1)} %get-tuple-element.55.dxe_ref) | copy-start | bytes 3076
  32.7 1.4 %copy-start.8 = (f32[2,32,256]{2,1,0:T(8,128)S(1)}, f32[2,32,256]{2,1,0:T(8,128)}, u32[]{:S(2)}) copy-start(f32[2,32,256]{2,1,0:T(8,128)} %param.11) | copy-start | bytes 196612
  40.0 15.8 %copy-start.6 = (f32[4,24,256]{2,1,0:T(8,128)}, f32[4,24,256]{2,1,0:T(8,128)S(1)}, u32[]{:S(2)}) copy-start(f32[4,24,256]{2,1,0:T(8,128)S(1)} %collective-permute-done.xw_ref) | copy-start | bytes 294916
  40.0 15.7 %copy-start.7 = (f32[4,24,256]{2,1,0:T(8,128)}, f32[4,24,256]{2,1,0:T(8,128)S(1)}, u32[]{:S(2)}) copy-start(f32[4,24,256]{2,1,0:T(8,128)S(1)} %collective-permute-done.1.xe_ref) | copy-start | bytes 294916
  40.1 13.1 %collective-permute-start.4 = (f32[36,256]{1,0:T(8,128)S(1)}, f32[36,256]{1,0:T(8,128)S(1)}, u32[]{:S(2)}, u32[]{:S(2)}) collective-permute-start(f32[36,256]{1,0:T(8,128)S(1)} %pad_maximum_fusion), channel_id=1, source_target_pairs={{0,1},{1,2},{2,3},{4,5},{5,6},{6,7},{8,9},{9,10},{10,11},{12,13},{... | collective-permute-start | bytes 110600 | tf_op jit(solution)/shard_map/ppermute | solution.py:439
  43.9 9.2 %collective-permute-start.5 = (f32[36,256]{1,0:T(8,128)S(1)}, f32[36,256]{1,0:T(8,128)S(1)}, u32[]{:S(2)}, u32[]{:S(2)}) collective-permute-start(f32[36,256]{1,0:T(8,128)S(1)} %pad_maximum_fusion), channel_id=1, source_target_pairs={{0,2},{1,3},{4,6},{5,7},{8,10},{9,11},{12,14},{13,15},{16,18},{17,... | collective-permute-start | bytes 110600 | tf_op jit(solution)/shard_map/ppermute | solution.py:439
  47.5 5.6 %collective-permute-start.6 = (f32[36,256]{1,0:T(8,128)S(1)}, f32[36,256]{1,0:T(8,128)S(1)}, u32[]{:S(2)}, u32[]{:S(2)}) collective-permute-start(f32[36,256]{1,0:T(8,128)S(1)} %pad_maximum_fusion), channel_id=1, source_target_pairs={{0,3},{4,7},{8,11},{12,15},{16,19},{20,23},{24,27},{28,31},{32,35}... | collective-permute-start | bytes 110600 | tf_op jit(solution)/shard_map/ppermute | solution.py:439
  68.6 14.6 %collective-permute-start.10 = (f32[8,32,256]{2,1,0:T(8,128)}, f32[8,32,256]{2,1,0:T(8,128)S(1)}, u32[]{:S(2)}, u32[]{:S(2)}) collective-permute-start(f32[8,32,256]{2,1,0:T(8,128)} %get-tuple-element.39), channel_id=1, source_target_pairs={{0,1},{1,2},{2,3},{3,0},{4,5},{5,6},{6,7},{7,4},{8,9},{9,10},{10,1... | collective-permute-start | bytes 786440 | tf_op jit(solution)/shard_map/ppermute | solution.py:201
  68.7 14.6 %collective-permute-start.8 = (f32[8,32,256]{2,1,0:T(8,128)}, f32[8,32,256]{2,1,0:T(8,128)S(1)}, u32[]{:S(2)}, u32[]{:S(2)}) collective-permute-start(f32[8,32,256]{2,1,0:T(8,128)} %get-tuple-element.39), channel_id=1, source_target_pairs={{0,3},{1,0},{2,1},{3,2},{4,7},{5,4},{6,5},{7,6},{8,11},{9,8},{10,9... | collective-permute-start | bytes 786440 | tf_op jit(solution)/shard_map/ppermute | solution.py:201
  71.9 11.3 %collective-permute-start.9 = (f32[8,32,256]{2,1,0:T(8,128)}, f32[8,32,256]{2,1,0:T(8,128)S(1)}, u32[]{:S(2)}, u32[]{:S(2)}) collective-permute-start(f32[8,32,256]{2,1,0:T(8,128)} %get-tuple-element.39), channel_id=1, source_target_pairs={{0,2},{1,3},{2,0},{3,1},{4,6},{5,7},{6,4},{7,5},{8,10},{9,11},{10,... | collective-permute-start | bytes 786440 | tf_op jit(solution)/shard_map/ppermute | solution.py:201
  84.4 2.1 %copy-start.4 = (f32[2,24,32,256]{3,2,1,0:T(8,128)S(1)}, f32[2,24,32,256]{3,2,1,0:T(8,128)}, u32[]{:S(2)}) copy-start(f32[2,24,32,256]{3,2,1,0:T(8,128)} %get-tuple-element.42) | copy-start | bytes 4718596
  86.0 1.9 %copy-start.1 = (f32[4,24,32,256]{3,2,1,0:T(8,128)S(1)}, f32[4,24,32,256]{3,2,1,0:T(8,128)}, u32[]{:S(2)}) copy-start(f32[4,24,32,256]{3,2,1,0:T(8,128)} %get-tuple-element.38) | copy-start | bytes 9437188
  86.0 2.4 %copy-start.3 = (f32[2,24,32,256]{3,2,1,0:T(8,128)S(1)}, f32[2,24,32,256]{3,2,1,0:T(8,128)}, u32[]{:S(2)}) copy-start(f32[2,24,32,256]{3,2,1,0:T(8,128)} %get-tuple-element.41) | copy-start | bytes 4718596
Sparse Core Ops, SparseCore 0:
  40.1 24.1 all-gather.2

commit v14 on v12

--- a/solution.py
+++ b/solution.py
@@ -124,7 +124,7 @@
 
 def coupling_solve(coupling, ctop):
     pairs, levels, cols_x, cols_y = coupling.shape
-    bx = 16 if cols_x % 16 == 0 else cols_x
+    bx = cols_x
     cspec = _specs(pairs, levels, bx, cols_y)
     full = jax.ShapeDtypeStruct(coupling.shape, jnp.float32)
     return pl.pallas_call(

time: 98.3 us -> 98.6 us (level)
  no operation moved by 1% of the time
where the time goes in v14:
time: 98.6 us; the launch traced here: 98.2 us
  starting transfers between devices  23.5 us (24%)
  local copies, waits for them, and re-layouts  23 us (23%)
  Pallas kernels  17.6 us (18%)
  between operations  13.8 us (14%)
  waiting for transfers between devices  11.4 us (12%)
  other arithmetic  8.86 us (9%)
    pallas_call x1, Pallas kernels, fused_solve(): pl.pallas_call(fused_kernel, grid=(levels // chunk,), in_specs=specs, out...  13 us
    ppermute x3, waiting for transfers between devices, gather_by_permutes(): received.append(lax.ppermute(part, axis, shift))  11.3 us
    ppermute x3, starting transfers between devices, per_device(): shallower = shallower + lax.ppermute(pack, 'gz', pairs_z)  8.7 us
    unnamed x26, local copies, waits for them, and re-layouts  4.58 us
    pallas_call x1, Pallas kernels, coupling_solve(): pl.pallas_call(coupling_kernel, grid=(cols_x // bx,), in_specs=[cspec, _p...  4.55 us
    ppermute x1, starting transfers between devices, per_device(): mix_above = lax.ppermute(mixing[:, lev_count - 1], 'gz', down_z)  3.93 us
    slice x1, local copies, waits for them, and re-layouts, per_device(): halo_yn = lax.ppermute(state[:, :, :, 0], 'gy', dn_y)  3.7 us
    ppermute x3, starting transfers between devices, gather_by_permutes(): received.append(lax.ppermute(part, axis, shift))  3.3 us
  transfers between devices with their start and end apart: 12, of which 1 were waited for; matrix products, arithmetic and copies ran while one was open for 20% of the time, Pallas kernels for 18%

profile of v14, /device:TPU:0, one launch (start us, length us, event | category | flops | bytes accessed | tf_op | source)
XLA Modules:
  0.0 98.2 jit_solution(5580241273219211710)
XLA Ops:
  6.5 3.7 %fusion.48 = (f32[4,24,32,1]{3,2,1,0:T(8,128)S(1)}, f32[4,24,32,1]{3,2,1,0:T(8,128)}) fusion(f32[4,24,32,256]{3,2,1,0:T(8,128)} %st_ref.1), kind=kLoop, calls=%fused_computation.140 | loop fusion | bytes 49152 | tf_op jit(solution)/shard_map/slice | solution.py:403
  10.2 2.0 %copy.49 = f32[4,24,32,1]{2,1,0,3:T(8,128)S(1)} copy(f32[4,24,32,1]{3,2,1,0:T(8,128)} %get-tuple-element.46) | data formatting | bytes 24576
  12.3 3.2 %collective-permute-start.2 = (f32[4,24,32]{2,1,0:T(8,128)S(1)}, f32[4,24,32]{2,1,0:T(8,128)S(1)}, u32[]{:S(2)}, u32[]{:S(2)}) collective-permute-start(f32[4,24,32]{2,1,0:T(8,128)S(1)} %bitcast.311), channel_id=1, source_target_pairs={{0,4},{4,8},{8,12},{12,16},{16,20},{20,24},{24,28},{28,0},{1,5},{5... | collective-permute-start | bytes 36872 | tf_op jit(solution)/shard_map/ppermute | solution.py:402
  15.5 0.6 copy.50
  16.1 2.6 %collective-permute-start.3 = (f32[4,24,32]{2,1,0:T(8,128)S(1)}, f32[4,24,32]{2,1,0:T(8,128)S(1)}, u32[]{:S(2)}, u32[]{:S(2)}) collective-permute-start(f32[4,24,32]{2,1,0:T(8,128)S(1)} %bitcast.310), channel_id=1, source_target_pairs={{4,0},{8,4},{12,8},{16,12},{20,16},{24,20},{28,24},{0,28},{5,1},{9... | collective-permute-start | bytes 36872 | tf_op jit(solution)/shard_map/ppermute | solution.py:403
  18.6 1.5 %fusion.49 = (f32[4,24,1,256]{3,2,1,0:T(1,128)S(1)}, f32[4,24,1,256]{3,2,1,0:T(1,128)S(1)}) fusion(f32[4,24,32,256]{3,2,1,0:T(8,128)} %st_ref.1), kind=kLoop, calls=%fused_computation.141 | loop fusion | bytes 393216 | tf_op jit(solution)/shard_map/slice | solution.py:401
  20.2 0.1 collective-permute-start
  20.3 1.8 %collective-permute-start.1 = (f32[4,24,256]{2,1,0:T(8,128)S(1)}, f32[4,24,256]{2,1,0:T(8,128)S(1)}, u32[]{:S(2)}, u32[]{:S(2)}) collective-permute-start(f32[4,24,256]{2,1,0:T(8,128)S(1)} %bitcast.309), channel_id=1, source_target_pairs={{32,0},{64,32},{96,64},{0,96},{33,1},{65,33},{97,65},{1,97},{34,2}... | collective-permute-start | bytes 294920 | tf_op jit(solution)/shard_map/ppermute | solution.py:401
  22.1 0.8 slice_bitcast_fusion.17
  22.9 3.9 %collective-permute-start.7 = (f32[2,32,256]{2,1,0:T(8,128)S(1)}, f32[2,32,256]{2,1,0:T(8,128)S(1)}, u32[]{:S(2)}, u32[]{:S(2)}) collective-permute-start(f32[2,32,256]{2,1,0:T(8,128)S(1)} %slice_bitcast_fusion.17), channel_id=1, source_target_pairs={{0,1},{1,2},{2,3},{4,5},{5,6},{6,7},{8,9},{9,10},{10,11},{12,13},{... | collective-permute-start | bytes 196616 | tf_op jit(solution)/shard_map/ppermute | solution.py:395
  27.0 0.7 gather_fusion
  27.6 0.1 broadcast_select_fusion
  27.7 0.4 copy.40
  28.1 1.0 %gather_fusion.1 = s32[258,34]{1,0:T(8,128)S(1)} fusion(s32[34,2048]{0,1:T(8,128)S(1)} %copy.40, s32[1024]{0:T(1024)S(1)} %pad_clamp_fusion), kind=kCustom, calls=%fused_computation.1 | custom fusion | bytes 71208 | tf_op jit(solution)/shard_map/jit(_take)/gather | solution.py:407
  29.2 0.1 copy.41
  29.3 0.8 slice_reduce_fusion
  30.1 0.7 fusion.51
  30.8 0.1 fusion.50
  30.9 0.1 fusion.5
  31.0 1.7 %compare_select_fusion = (f32[24,32,256]{2,1,0:T(8,128)S(1)}, f32[32,256]{1,0:T(8,128)S(1)}) fusion(s32[32,256]{1,0:T(8,128)S(1)} %get-tuple-element.61.dc_ref, s32[24]{0:T(128)S(1)} %iota_add_fusion.1, f32[4,24,32,256]{3,2,1,0:T(8,128)} %st_ref.1), kind=kLoop, calls=%fused_computation.15 | loop fusion | flops 2351104 | bytes 2424928 | tf_op jit(solution)/shard_map/mul | solution.py:420
  32.7 0.1 fusion.21
  32.8 1.3 %broadcast_multiply_fusion.c_ref = f32[2,24,32,256]{3,2,1,0:T(8,128)} fusion(f32[2,24,32,256]{3,2,1,0:T(8,128)S(1)} %copy-done.2, f32[24,32,256]{2,1,0:T(8,128)S(1)} %get-tuple-element.66), kind=kLoop, calls=%fused_computation.12 | loop fusion | flops 393216 | bytes 3932160 | tf_op jit(solution)/shard_map/mul | solution.py:420
  34.1 0.6 broadcast_select_fusion.1.wind_ref
  34.8 0.2 scatter.9
  35.0 0.6 multiply_select_fusion.ctop_ref
  35.7 4.5 %shard_map.46 = (f32[2,24,32,256]{3,2,1,0:T(8,128)}, f32[2,24,32,256]{3,2,1,0:T(8,128)}, f32[2,24,32,256]{3,2,1,0:T(8,128)}, f32[2,24,32,256]{3,2,1,0:T(8,128)}, f32[8,32,256]{2,1,0:T(8,128)}) custom-call(f32[2,24,32,256]{3,2,1,0:T(8,128)} %broadcast_multiply_fusion.c_ref, f32[2,32,256]{2,1,0:T(8,128)} %multiply_select_fusion.ctop_ref), custom_call_target="tpu_custom_call" | custom-call | tf_op jit(solution)/shard_map/pallas_call | solution.py:130
  40.4 3.8 %collective-permute-start.4 = (f32[36,256]{1,0:T(8,128)S(1)}, f32[36,256]{1,0:T(8,128)S(1)}, u32[]{:S(2)}, u32[]{:S(2)}) collective-permute-start(f32[36,256]{1,0:T(8,128)S(1)} %pad_maximum_fusion), channel_id=1, source_target_pairs={{0,1},{1,2},{2,3},{4,5},{5,6},{6,7},{8,9},{9,10},{10,11},{12,13},{... | collective-permute-start | bytes 110600 | tf_op jit(solution)/shard_map/ppermute | solution.py:439
  44.2 3.6 %collective-permute-start.5 = (f32[36,256]{1,0:T(8,128)S(1)}, f32[36,256]{1,0:T(8,128)S(1)}, u32[]{:S(2)}, u32[]{:S(2)}) collective-permute-start(f32[36,256]{1,0:T(8,128)S(1)} %pad_maximum_fusion), channel_id=1, source_target_pairs={{0,2},{1,3},{4,6},{5,7},{8,10},{9,11},{12,14},{13,15},{16,18},{17,... | collective-permute-start | bytes 110600 | tf_op jit(solution)/shard_map/ppermute | solution.py:439
  47.8 1.3 %collective-permute-start.6 = (f32[36,256]{1,0:T(8,128)S(1)}, f32[36,256]{1,0:T(8,128)S(1)}, u32[]{:S(2)}, u32[]{:S(2)}) collective-permute-start(f32[36,256]{1,0:T(8,128)S(1)} %pad_maximum_fusion), channel_id=1, source_target_pairs={{0,3},{4,7},{8,11},{12,15},{16,19},{20,23},{24,27},{28,31},{32,35}... | collective-permute-start | bytes 110600 | tf_op jit(solution)/shard_map/ppermute | solution.py:439
  49.1 0.6 stack.23.lane_ref
  49.7 1.9 %copy.43.ys_ref = f32[4,24,32,1]{3,2,1,0:T(8,128)} copy(f32[4,24,32,1]{2,1,0,3:T(8,128)S(1)} %bitcast.306) | data formatting | bytes 24576 | tf_op jit(solution)/shard_map/broadcast_in_dim | solution.py:451
  51.6 1.8 %copy.44.yn_ref = f32[4,24,32,1]{3,2,1,0:T(8,128)} copy(f32[4,24,32,1]{2,1,0,3:T(8,128)S(1)} %bitcast.307) | data formatting | bytes 24576 | tf_op jit(solution)/shard_map/broadcast_in_dim | solution.py:451
  53.5 0.6 slice.288.sc_ref
  54.1 0.7 copy.45.sys_ref
  54.7 0.7 copy.46.syn_ref
  55.4 0.6 fusion.52
  56.0 13.0 %shard_map.47 = (f32[4,24,32,256]{3,2,1,0:T(8,128)}, f32[8,32,256]{2,1,0:T(8,128)}) custom-call(f32[4,24,32,256]{3,2,1,0:T(8,128)} %st_ref.1, f32[4,24,256]{2,1,0:T(8,128)} %copy-done.6, f32[4,24,256]{2,1,0:T(8,128)} %copy-done.7, f32[4,24,32,1]{3,2,1,0:T(8,128)} %copy.43.ys_ref, f32[4,24,32,1]{3,2,1,0:T(8,128)} %copy.44.yn_ref, s32[32,256]{1,0:T(8,128)} %copy-done.5, ...), custom_call_target="tpu_custom_call" | custom-call | tf_op jit(solution)/shard_map/pallas_call | solution.py:368
  69.1 0.1 collective-permute-start.10
  69.1 3.2 %collective-permute-start.8 = (f32[8,32,256]{2,1,0:T(8,128)}, f32[8,32,256]{2,1,0:T(8,128)S(1)}, u32[]{:S(2)}, u32[]{:S(2)}) collective-permute-start(f32[8,32,256]{2,1,0:T(8,128)} %get-tuple-element.39), channel_id=1, source_target_pairs={{0,3},{1,0},{2,1},{3,2},{4,7},{5,4},{6,5},{7,6},{8,11},{9,8},{10,9... | collective-permute-start | bytes 786440 | tf_op jit(solution)/shard_map/ppermute | solution.py:201
  72.4 11.3 %collective-permute-done.10 = f32[8,32,256]{2,1,0:T(8,128)S(1)} collective-permute-done((f32[8,32,256]{2,1,0:T(8,128)}, f32[8,32,256]{2,1,0:T(8,128)S(1)}, u32[]{:S(2)}, u32[]{:S(2)}) %collective-permute-start.10) | collective-permute-done | bytes 262176 | tf_op jit(solution)/shard_map/ppermute | solution.py:201
  83.7 1.1 %select_bitcast_fusion.2 = (f32[1,8,32,256]{3,2,1,0:T(8,128)S(1)}, f32[1,8,32,256]{3,2,1,0:T(8,128)S(1)}, f32[1,8,32,256]{3,2,1,0:T(8,128)S(1)}, f32[1,8,32,256]{3,2,1,0:T(8,128)S(1)}) fusion(f32[8,32,256]{2,1,0:T(8,128)S(1)} %collective-permute-done.8, f32[8,32,256]{2,1,0:T(8,128)S(1)} %collective-permute-done.9, ...), kind=kLoop, calls=%fused_computation.18 | loop fusion | flops 786432 | bytes 2097164 | tf_op jit(solution)/shard_map/stack | solution.py:208
  84.8 0.0 all-gather.3.cloned.1.call-done
  84.9 1.6 %broadcast_in_dim.61 = f32[4,8,2,32,256]{4,3,2,1,0:T(8,128)S(1)} broadcast(f32[4,8,32,256]{3,2,1,0:T(8,128)} %bitcast.305), dimensions={0,1,3,4} | broadcast | bytes 3145728 | tf_op jit(solution)/shard_map/broadcast_in_dim | solution.py:160
  86.5 0.2 select_select_fusion
  86.7 0.3 select_select_fusion.1
  87.0 1.4 %copy-done.1 = f32[4,24,32,256]{3,2,1,0:T(8,128)S(1)} copy-done((f32[4,24,32,256]{3,2,1,0:T(8,128)S(1)}, f32[4,24,32,256]{3,2,1,0:T(8,128)}, u32[]{:S(2)}) %copy-start.1) | copy-done | bytes 3145752
  88.4 0.5 copy-done.3
  88.8 2.5 %fusion = f32[4,24,32,256]{3,2,1,0:T(8,128)} fusion(f32[4,24,32,256]{3,2,1,0:T(8,128)S(1)} %copy-done.1, f32[2,24,32,256]{3,2,1,0:T(8,128)S(1)} %copy-done.4, f32[4,32,256]{2,1,0:T(8,128)S(1)} %select_select_fusion, f32[2,24,32,256]{3,2,1,0:T(8,128)S(1)} %copy-done.3, f32[4,32,256]{2,1,0:T(8,128)S(1)} %select_select_fusion.1), kind=kLoop, calls=%fused_computation.3 | loop fusion | flops 3145728 | bytes 9699328 | tf_op jit(solution)/shard_map/add | solution.py:460
  (55 shorter events, 0.4 us)
Async XLA Ops:
  6.5 20.4 %copy-start = (s32[128,2048]{1,0:T(8,128)S(1)}, s32[128,2048]{1,0:T(8,128)}, u32[]{:S(2)}) copy-start(s32[128,2048]{1,0:T(8,128)} %param.10) | copy-start | bytes 3145732
  6.5 78.3 %all-gather.3.cloned.1.call-start = ((), (), s32[]{:S(2)}) async-start(), calls=%async_computation | async-start | bytes 1310720 | tf_op jit(solution)/shard_map/all_gather | solution.py:425
  12.3 22.5 %collective-permute-start.2 = (f32[4,24,32]{2,1,0:T(8,128)S(1)}, f32[4,24,32]{2,1,0:T(8,128)S(1)}, u32[]{:S(2)}, u32[]{:S(2)}) collective-permute-start(f32[4,24,32]{2,1,0:T(8,128)S(1)} %bitcast.311), channel_id=1, source_target_pairs={{0,4},{4,8},{8,12},{12,16},{16,20},{20,24},{24,28},{28,0},{1,5},{5... | collective-permute-start | bytes 36872 | tf_op jit(solution)/shard_map/ppermute | solution.py:402
  16.1 18.7 %collective-permute-start.3 = (f32[4,24,32]{2,1,0:T(8,128)S(1)}, f32[4,24,32]{2,1,0:T(8,128)S(1)}, u32[]{:S(2)}, u32[]{:S(2)}) collective-permute-start(f32[4,24,32]{2,1,0:T(8,128)S(1)} %bitcast.310), channel_id=1, source_target_pairs={{4,0},{8,4},{12,8},{16,12},{20,16},{24,20},{28,24},{0,28},{5,1},{9... | collective-permute-start | bytes 36872 | tf_op jit(solution)/shard_map/ppermute | solution.py:403
  20.2 20.1 %collective-permute-start = (f32[4,24,256]{2,1,0:T(8,128)S(1)}, f32[4,24,256]{2,1,0:T(8,128)S(1)}, u32[]{:S(2)}, u32[]{:S(2)}) collective-permute-start(f32[4,24,256]{2,1,0:T(8,128)S(1)} %bitcast.308), channel_id=1, source_target_pairs={{0,32},{32,64},{64,96},{96,0},{1,33},{33,65},{65,97},{97,1},{2,34}... | collective-permute-start | bytes 294920 | tf_op jit(solution)/shard_map/ppermute | solution.py:400
  20.3 20.0 %collective-permute-start.1 = (f32[4,24,256]{2,1,0:T(8,128)S(1)}, f32[4,24,256]{2,1,0:T(8,128)S(1)}, u32[]{:S(2)}, u32[]{:S(2)}) collective-permute-start(f32[4,24,256]{2,1,0:T(8,128)S(1)} %bitcast.309), channel_id=1, source_target_pairs={{32,0},{64,32},{96,64},{0,96},{33,1},{65,33},{97,65},{1,97},{34,2}... | collective-permute-start | bytes 294920 | tf_op jit(solution)/shard_map/ppermute | solution.py:401
  22.9 12.1 %collective-permute-start.7 = (f32[2,32,256]{2,1,0:T(8,128)S(1)}, f32[2,32,256]{2,1,0:T(8,128)S(1)}, u32[]{:S(2)}, u32[]{:S(2)}) collective-permute-start(f32[2,32,256]{2,1,0:T(8,128)S(1)} %slice_bitcast_fusion.17), channel_id=1, source_target_pairs={{0,1},{1,2},{2,3},{4,5},{5,6},{6,7},{8,9},{9,10},{10,11},{12,13},{... | collective-permute-start | bytes 196616 | tf_op jit(solution)/shard_map/ppermute | solution.py:395
  29.2 3.6 %copy-start.2 = (f32[2,24,32,256]{3,2,1,0:T(8,128)S(1)}, f32[2,24,32,256]{3,2,1,0:T(8,128)}, u32[]{:S(2)}) copy-start(f32[2,24,32,256]{3,2,1,0:T(8,128)} %param.9) | copy-start | bytes 4718596
  30.8 3.3 %copy-start.5 = (s32[32,256]{1,0:T(8,128)}, s32[32,256]{1,0:T(8,128)S(1)}, u32[]{:S(2)}) copy-start(s32[32,256]{1,0:T(8,128)S(1)} %get-tuple-element.61.dc_ref) | copy-start | bytes 98308
  30.9 9.4 %copy-start.10 = (s32[1,256]{1,0:T(1,128)}, s32[1,256]{1,0:T(1,128)S(1)}, u32[]{:S(2)}) copy-start(s32[1,256]{1,0:T(1,128)S(1)} %get-tuple-element.56.dxw_ref) | copy-start | bytes 3076
  30.9 9.4 %copy-start.9 = (s32[1,256]{1,0:T(1,128)}, s32[1,256]{1,0:T(1,128)S(1)}, u32[]{:S(2)}) copy-start(s32[1,256]{1,0:T(1,128)S(1)} %get-tuple-element.55.dxe_ref) | copy-start | bytes 3076
  32.7 1.4 %copy-start.8 = (f32[2,32,256]{2,1,0:T(8,128)S(1)}, f32[2,32,256]{2,1,0:T(8,128)}, u32[]{:S(2)}) copy-start(f32[2,32,256]{2,1,0:T(8,128)} %param.11) | copy-start | bytes 196612
  40.2 15.8 %copy-start.6 = (f32[4,24,256]{2,1,0:T(8,128)}, f32[4,24,256]{2,1,0:T(8,128)S(1)}, u32[]{:S(2)}) copy-start(f32[4,24,256]{2,1,0:T(8,128)S(1)} %collective-permute-done.xw_ref) | copy-start | bytes 294916
  40.3 15.7 %copy-start.7 = (f32[4,24,256]{2,1,0:T(8,128)}, f32[4,24,256]{2,1,0:T(8,128)S(1)}, u32[]{:S(2)}) copy-start(f32[4,24,256]{2,1,0:T(8,128)S(1)} %collective-permute-done.1.xe_ref) | copy-start | bytes 294916
  40.4 13.1 %collective-permute-start.4 = (f32[36,256]{1,0:T(8,128)S(1)}, f32[36,256]{1,0:T(8,128)S(1)}, u32[]{:S(2)}, u32[]{:S(2)}) collective-permute-start(f32[36,256]{1,0:T(8,128)S(1)} %pad_maximum_fusion), channel_id=1, source_target_pairs={{0,1},{1,2},{2,3},{4,5},{5,6},{6,7},{8,9},{9,10},{10,11},{12,13},{... | collective-permute-start | bytes 110600 | tf_op jit(solution)/shard_map/ppermute | solution.py:439
  44.2 9.2 %collective-permute-start.5 = (f32[36,256]{1,0:T(8,128)S(1)}, f32[36,256]{1,0:T(8,128)S(1)}, u32[]{:S(2)}, u32[]{:S(2)}) collective-permute-start(f32[36,256]{1,0:T(8,128)S(1)} %pad_maximum_fusion), channel_id=1, source_target_pairs={{0,2},{1,3},{4,6},{5,7},{8,10},{9,11},{12,14},{13,15},{16,18},{17,... | collective-permute-start | bytes 110600 | tf_op jit(solution)/shard_map/ppermute | solution.py:439
  47.8 5.6 %collective-permute-start.6 = (f32[36,256]{1,0:T(8,128)S(1)}, f32[36,256]{1,0:T(8,128)S(1)}, u32[]{:S(2)}, u32[]{:S(2)}) collective-permute-start(f32[36,256]{1,0:T(8,128)S(1)} %pad_maximum_fusion), channel_id=1, source_target_pairs={{0,3},{4,7},{8,11},{12,15},{16,19},{20,23},{24,27},{28,31},{32,35}... | collective-permute-start | bytes 110600 | tf_op jit(solution)/shard_map/ppermute | solution.py:439
  69.1 14.6 %collective-permute-start.10 = (f32[8,32,256]{2,1,0:T(8,128)}, f32[8,32,256]{2,1,0:T(8,128)S(1)}, u32[]{:S(2)}, u32[]{:S(2)}) collective-permute-start(f32[8,32,256]{2,1,0:T(8,128)} %get-tuple-element.39), channel_id=1, source_target_pairs={{0,1},{1,2},{2,3},{3,0},{4,5},{5,6},{6,7},{7,4},{8,9},{9,10},{10,1... | collective-permute-start | bytes 786440 | tf_op jit(solution)/shard_map/ppermute | solution.py:201
  69.1 14.6 %collective-permute-start.8 = (f32[8,32,256]{2,1,0:T(8,128)}, f32[8,32,256]{2,1,0:T(8,128)S(1)}, u32[]{:S(2)}, u32[]{:S(2)}) collective-permute-start(f32[8,32,256]{2,1,0:T(8,128)} %get-tuple-element.39), channel_id=1, source_target_pairs={{0,3},{1,0},{2,1},{3,2},{4,7},{5,4},{6,5},{7,6},{8,11},{9,8},{10,9... | collective-permute-start | bytes 786440 | tf_op jit(solution)/shard_map/ppermute | solution.py:201
  72.4 11.3 %collective-permute-start.9 = (f32[8,32,256]{2,1,0:T(8,128)}, f32[8,32,256]{2,1,0:T(8,128)S(1)}, u32[]{:S(2)}, u32[]{:S(2)}) collective-permute-start(f32[8,32,256]{2,1,0:T(8,128)} %get-tuple-element.39), channel_id=1, source_target_pairs={{0,2},{1,3},{2,0},{3,1},{4,6},{5,7},{6,4},{7,5},{8,10},{9,11},{10,... | collective-permute-start | bytes 786440 | tf_op jit(solution)/shard_map/ppermute | solution.py:201
  84.9 2.1 %copy-start.4 = (f32[2,24,32,256]{3,2,1,0:T(8,128)S(1)}, f32[2,24,32,256]{3,2,1,0:T(8,128)}, u32[]{:S(2)}) copy-start(f32[2,24,32,256]{3,2,1,0:T(8,128)} %get-tuple-element.42) | copy-start | bytes 4718596
  86.5 1.9 %copy-start.1 = (f32[4,24,32,256]{3,2,1,0:T(8,128)S(1)}, f32[4,24,32,256]{3,2,1,0:T(8,128)}, u32[]{:S(2)}) copy-start(f32[4,24,32,256]{3,2,1,0:T(8,128)} %get-tuple-element.38) | copy-start | bytes 9437188
  86.5 2.4 %copy-start.3 = (f32[2,24,32,256]{3,2,1,0:T(8,128)S(1)}, f32[2,24,32,256]{3,2,1,0:T(8,128)}, u32[]{:S(2)}) copy-start(f32[2,24,32,256]{3,2,1,0:T(8,128)} %get-tuple-element.41) | copy-start | bytes 4718596
Sparse Core Ops, SparseCore 0:
  40.4 24.1 all-gather.2

commit v15 on v12

--- a/solution.py
+++ b/solution.py
@@ -359,7 +359,7 @@
     st = operands[0]
     fields, levels, nx, ny = st.shape
     pairs = operands[21].shape[0]
-    chunk = 8 if levels % 8 == 0 else levels
+    chunk = 6 if levels % 6 == 0 else levels
     whole = [pl.BlockSpec(op.shape, (lambda i, n=op.ndim: (0,) * n)) for op in operands]
     by_level = lambda op: pl.BlockSpec((op.shape[0], chunk) + op.shape[2:], lambda i: (0, i, 0, 0))
     specs = list(whole)

time: 98.3 us -> 98.1 us (level)
  no operation moved by 1% of the time
where the time goes in v15:
time: 98.1 us; the launch traced here: 97.7 us
  starting transfers between devices  23.5 us (24%)
  local copies, waits for them, and re-layouts  23 us (23%)
  Pallas kernels  17.1 us (17%)
  between operations  13.8 us (14%)
  waiting for transfers between devices  11.4 us (12%)
  other arithmetic  8.86 us (9%)
    pallas_call x1, Pallas kernels, fused_solve(): pl.pallas_call(fused_kernel, grid=(levels // chunk,), in_specs=specs, out...  12.9 us
    ppermute x3, waiting for transfers between devices, gather_by_permutes(): received.append(lax.ppermute(part, axis, shift))  11.3 us
    ppermute x3, starting transfers between devices, per_device(): shallower = shallower + lax.ppermute(pack, 'gz', pairs_z)  8.7 us
    unnamed x26, local copies, waits for them, and re-layouts  4.58 us
    pallas_call x1, Pallas kernels, coupling_solve(): pl.pallas_call(coupling_kernel, grid=(cols_x // bx,), in_specs=[cspec, _p...  4.26 us
    ppermute x1, starting transfers between devices, per_device(): mix_above = lax.ppermute(mixing[:, lev_count - 1], 'gz', down_z)  3.93 us
    slice x1, local copies, waits for them, and re-layouts, per_device(): halo_yn = lax.ppermute(state[:, :, :, 0], 'gy', dn_y)  3.7 us
    ppermute x3, starting transfers between devices, gather_by_permutes(): received.append(lax.ppermute(part, axis, shift))  3.3 us
  transfers between devices with their start and end apart: 12, of which 1 were waited for; matrix products, arithmetic and copies ran while one was open for 20% of the time, Pallas kernels for 18%

profile of v15, /device:TPU:0, one launch (start us, length us, event | category | flops | bytes accessed | tf_op | source)
XLA Modules:
  0.0 97.7 jit_solution(7722994654173458695)
XLA Ops:
  6.5 3.7 %fusion.48 = (f32[4,24,32,1]{3,2,1,0:T(8,128)S(1)}, f32[4,24,32,1]{3,2,1,0:T(8,128)}) fusion(f32[4,24,32,256]{3,2,1,0:T(8,128)} %st_ref.1), kind=kLoop, calls=%fused_computation.140 | loop fusion | bytes 49152 | tf_op jit(solution)/shard_map/slice | solution.py:403
  10.2 2.0 %copy.49 = f32[4,24,32,1]{2,1,0,3:T(8,128)S(1)} copy(f32[4,24,32,1]{3,2,1,0:T(8,128)} %get-tuple-element.46) | data formatting | bytes 24576
  12.3 3.2 %collective-permute-start.2 = (f32[4,24,32]{2,1,0:T(8,128)S(1)}, f32[4,24,32]{2,1,0:T(8,128)S(1)}, u32[]{:S(2)}, u32[]{:S(2)}) collective-permute-start(f32[4,24,32]{2,1,0:T(8,128)S(1)} %bitcast.311), channel_id=1, source_target_pairs={{0,4},{4,8},{8,12},{12,16},{16,20},{20,24},{24,28},{28,0},{1,5},{5... | collective-permute-start | bytes 36872 | tf_op jit(solution)/shard_map/ppermute | solution.py:402
  15.5 0.6 copy.50
  16.1 2.6 %collective-permute-start.3 = (f32[4,24,32]{2,1,0:T(8,128)S(1)}, f32[4,24,32]{2,1,0:T(8,128)S(1)}, u32[]{:S(2)}, u32[]{:S(2)}) collective-permute-start(f32[4,24,32]{2,1,0:T(8,128)S(1)} %bitcast.310), channel_id=1, source_target_pairs={{4,0},{8,4},{12,8},{16,12},{20,16},{24,20},{28,24},{0,28},{5,1},{9... | collective-permute-start | bytes 36872 | tf_op jit(solution)/shard_map/ppermute | solution.py:403
  18.6 1.5 %fusion.49 = (f32[4,24,1,256]{3,2,1,0:T(1,128)S(1)}, f32[4,24,1,256]{3,2,1,0:T(1,128)S(1)}) fusion(f32[4,24,32,256]{3,2,1,0:T(8,128)} %st_ref.1), kind=kLoop, calls=%fused_computation.141 | loop fusion | bytes 393216 | tf_op jit(solution)/shard_map/slice | solution.py:401
  20.2 0.1 collective-permute-start
  20.3 1.8 %collective-permute-start.1 = (f32[4,24,256]{2,1,0:T(8,128)S(1)}, f32[4,24,256]{2,1,0:T(8,128)S(1)}, u32[]{:S(2)}, u32[]{:S(2)}) collective-permute-start(f32[4,24,256]{2,1,0:T(8,128)S(1)} %bitcast.309), channel_id=1, source_target_pairs={{32,0},{64,32},{96,64},{0,96},{33,1},{65,33},{97,65},{1,97},{34,2}... | collective-permute-start | bytes 294920 | tf_op jit(solution)/shard_map/ppermute | solution.py:401
  22.1 0.8 slice_bitcast_fusion.17
  22.9 3.9 %collective-permute-start.7 = (f32[2,32,256]{2,1,0:T(8,128)S(1)}, f32[2,32,256]{2,1,0:T(8,128)S(1)}, u32[]{:S(2)}, u32[]{:S(2)}) collective-permute-start(f32[2,32,256]{2,1,0:T(8,128)S(1)} %slice_bitcast_fusion.17), channel_id=1, source_target_pairs={{0,1},{1,2},{2,3},{4,5},{5,6},{6,7},{8,9},{9,10},{10,11},{12,13},{... | collective-permute-start | bytes 196616 | tf_op jit(solution)/shard_map/ppermute | solution.py:395
  27.0 0.7 gather_fusion
  27.6 0.1 broadcast_select_fusion
  27.7 0.4 copy.40
  28.1 1.0 %gather_fusion.1 = s32[258,34]{1,0:T(8,128)S(1)} fusion(s32[34,2048]{0,1:T(8,128)S(1)} %copy.40, s32[1024]{0:T(1024)S(1)} %pad_clamp_fusion), kind=kCustom, calls=%fused_computation.1 | custom fusion | bytes 71208 | tf_op jit(solution)/shard_map/jit(_take)/gather | solution.py:407
  29.2 0.1 copy.41
  29.3 0.8 slice_reduce_fusion
  30.1 0.7 fusion.51
  30.8 0.1 fusion.50
  30.9 0.1 fusion.5
  31.0 1.7 %compare_select_fusion = (f32[24,32,256]{2,1,0:T(8,128)S(1)}, f32[32,256]{1,0:T(8,128)S(1)}) fusion(s32[32,256]{1,0:T(8,128)S(1)} %get-tuple-element.61.dc_ref, s32[24]{0:T(128)S(1)} %iota_add_fusion.1, f32[4,24,32,256]{3,2,1,0:T(8,128)} %st_ref.1), kind=kLoop, calls=%fused_computation.15 | loop fusion | flops 2351104 | bytes 2424928 | tf_op jit(solution)/shard_map/mul | solution.py:420
  32.7 0.1 fusion.21
  32.8 1.3 %broadcast_multiply_fusion.c_ref = f32[2,24,32,256]{3,2,1,0:T(8,128)} fusion(f32[2,24,32,256]{3,2,1,0:T(8,128)S(1)} %copy-done.2, f32[24,32,256]{2,1,0:T(8,128)S(1)} %get-tuple-element.66), kind=kLoop, calls=%fused_computation.12 | loop fusion | flops 393216 | bytes 3932160 | tf_op jit(solution)/shard_map/mul | solution.py:420
  34.1 0.6 broadcast_select_fusion.1.wind_ref
  34.8 0.2 scatter.9
  35.0 0.6 multiply_select_fusion.ctop_ref
  35.7 4.3 %shard_map.46 = (f32[2,24,32,256]{3,2,1,0:T(8,128)}, f32[2,24,32,256]{3,2,1,0:T(8,128)}, f32[2,24,32,256]{3,2,1,0:T(8,128)}, f32[2,24,32,256]{3,2,1,0:T(8,128)}, f32[8,32,256]{2,1,0:T(8,128)}) custom-call(f32[2,24,32,256]{3,2,1,0:T(8,128)} %broadcast_multiply_fusion.c_ref, f32[2,32,256]{2,1,0:T(8,128)} %multiply_select_fusion.ctop_ref), custom_call_target="tpu_custom_call" | custom-call | tf_op jit(solution)/shard_map/pallas_call | solution.py:130
  40.1 3.8 %collective-permute-start.4 = (f32[36,256]{1,0:T(8,128)S(1)}, f32[36,256]{1,0:T(8,128)S(1)}, u32[]{:S(2)}, u32[]{:S(2)}) collective-permute-start(f32[36,256]{1,0:T(8,128)S(1)} %pad_maximum_fusion), channel_id=1, source_target_pairs={{0,1},{1,2},{2,3},{4,5},{5,6},{6,7},{8,9},{9,10},{10,11},{12,13},{... | collective-permute-start | bytes 110600 | tf_op jit(solution)/shard_map/ppermute | solution.py:439
  43.9 3.6 %collective-permute-start.5 = (f32[36,256]{1,0:T(8,128)S(1)}, f32[36,256]{1,0:T(8,128)S(1)}, u32[]{:S(2)}, u32[]{:S(2)}) collective-permute-start(f32[36,256]{1,0:T(8,128)S(1)} %pad_maximum_fusion), channel_id=1, source_target_pairs={{0,2},{1,3},{4,6},{5,7},{8,10},{9,11},{12,14},{13,15},{16,18},{17,... | collective-permute-start | bytes 110600 | tf_op jit(solution)/shard_map/ppermute | solution.py:439
  47.5 1.3 %collective-permute-start.6 = (f32[36,256]{1,0:T(8,128)S(1)}, f32[36,256]{1,0:T(8,128)S(1)}, u32[]{:S(2)}, u32[]{:S(2)}) collective-permute-start(f32[36,256]{1,0:T(8,128)S(1)} %pad_maximum_fusion), channel_id=1, source_target_pairs={{0,3},{4,7},{8,11},{12,15},{16,19},{20,23},{24,27},{28,31},{32,35}... | collective-permute-start | bytes 110600 | tf_op jit(solution)/shard_map/ppermute | solution.py:439
  48.8 0.6 stack.23.lane_ref
  49.5 1.9 %copy.43.ys_ref = f32[4,24,32,1]{3,2,1,0:T(8,128)} copy(f32[4,24,32,1]{2,1,0,3:T(8,128)S(1)} %bitcast.306) | data formatting | bytes 24576 | tf_op jit(solution)/shard_map/broadcast_in_dim | solution.py:451
  51.3 1.8 %copy.44.yn_ref = f32[4,24,32,1]{3,2,1,0:T(8,128)} copy(f32[4,24,32,1]{2,1,0,3:T(8,128)S(1)} %bitcast.307) | data formatting | bytes 24576 | tf_op jit(solution)/shard_map/broadcast_in_dim | solution.py:451
  53.2 0.6 slice.288.sc_ref
  53.8 0.7 copy.45.sys_ref
  54.5 0.7 copy.46.syn_ref
  55.1 0.6 fusion.52
  55.7 12.9 %shard_map.47 = (f32[4,24,32,256]{3,2,1,0:T(8,128)}, f32[8,32,256]{2,1,0:T(8,128)}) custom-call(f32[4,24,32,256]{3,2,1,0:T(8,128)} %st_ref.1, f32[4,24,256]{2,1,0:T(8,128)} %copy-done.6, f32[4,24,256]{2,1,0:T(8,128)} %copy-done.7, f32[4,24,32,1]{3,2,1,0:T(8,128)} %copy.43.ys_ref, f32[4,24,32,1]{3,2,1,0:T(8,128)} %copy.44.yn_ref, s32[32,256]{1,0:T(8,128)} %copy-done.5, ...), custom_call_target="tpu_custom_call" | custom-call | tf_op jit(solution)/shard_map/pallas_call | solution.py:368
  68.6 0.1 collective-permute-start.10
  68.7 3.2 %collective-permute-start.8 = (f32[8,32,256]{2,1,0:T(8,128)}, f32[8,32,256]{2,1,0:T(8,128)S(1)}, u32[]{:S(2)}, u32[]{:S(2)}) collective-permute-start(f32[8,32,256]{2,1,0:T(8,128)} %get-tuple-element.39), channel_id=1, source_target_pairs={{0,3},{1,0},{2,1},{3,2},{4,7},{5,4},{6,5},{7,6},{8,11},{9,8},{10,9... | collective-permute-start | bytes 786440 | tf_op jit(solution)/shard_map/ppermute | solution.py:201
  71.9 11.3 %collective-permute-done.10 = f32[8,32,256]{2,1,0:T(8,128)S(1)} collective-permute-done((f32[8,32,256]{2,1,0:T(8,128)}, f32[8,32,256]{2,1,0:T(8,128)S(1)}, u32[]{:S(2)}, u32[]{:S(2)}) %collective-permute-start.10) | collective-permute-done | bytes 262176 | tf_op jit(solution)/shard_map/ppermute | solution.py:201
  83.3 1.1 %select_bitcast_fusion.2 = (f32[1,8,32,256]{3,2,1,0:T(8,128)S(1)}, f32[1,8,32,256]{3,2,1,0:T(8,128)S(1)}, f32[1,8,32,256]{3,2,1,0:T(8,128)S(1)}, f32[1,8,32,256]{3,2,1,0:T(8,128)S(1)}) fusion(f32[8,32,256]{2,1,0:T(8,128)S(1)} %collective-permute-done.8, f32[8,32,256]{2,1,0:T(8,128)S(1)} %collective-permute-done.9, ...), kind=kLoop, calls=%fused_computation.18 | loop fusion | flops 786432 | bytes 2097164 | tf_op jit(solution)/shard_map/stack | solution.py:208
  84.4 0.0 all-gather.3.cloned.1.call-done
  84.4 1.6 %broadcast_in_dim.61 = f32[4,8,2,32,256]{4,3,2,1,0:T(8,128)S(1)} broadcast(f32[4,8,32,256]{3,2,1,0:T(8,128)} %bitcast.305), dimensions={0,1,3,4} | broadcast | bytes 3145728 | tf_op jit(solution)/shard_map/broadcast_in_dim | solution.py:160
  86.0 0.2 select_select_fusion
  86.3 0.3 select_select_fusion.1
  86.5 1.4 %copy-done.1 = f32[4,24,32,256]{3,2,1,0:T(8,128)S(1)} copy-done((f32[4,24,32,256]{3,2,1,0:T(8,128)S(1)}, f32[4,24,32,256]{3,2,1,0:T(8,128)}, u32[]{:S(2)}) %copy-start.1) | copy-done | bytes 3145752
  87.9 0.5 copy-done.3
  88.4 2.5 %fusion = f32[4,24,32,256]{3,2,1,0:T(8,128)} fusion(f32[4,24,32,256]{3,2,1,0:T(8,128)S(1)} %copy-done.1, f32[2,24,32,256]{3,2,1,0:T(8,128)S(1)} %copy-done.4, f32[4,32,256]{2,1,0:T(8,128)S(1)} %select_select_fusion, f32[2,24,32,256]{3,2,1,0:T(8,128)S(1)} %copy-done.3, f32[4,32,256]{2,1,0:T(8,128)S(1)} %select_select_fusion.1), kind=kLoop, calls=%fused_computation.3 | loop fusion | flops 3145728 | bytes 9699328 | tf_op jit(solution)/shard_map/add | solution.py:460
  (55 shorter events, 0.4 us)
Async XLA Ops:
  6.5 20.4 %copy-start = (s32[128,2048]{1,0:T(8,128)S(1)}, s32[128,2048]{1,0:T(8,128)}, u32[]{:S(2)}) copy-start(s32[128,2048]{1,0:T(8,128)} %param.10) | copy-start | bytes 3145732
  6.5 77.9 %all-gather.3.cloned.1.call-start = ((), (), s32[]{:S(2)}) async-start(), calls=%async_computation | async-start | bytes 1310720 | tf_op jit(solution)/shard_map/all_gather | solution.py:425
  12.3 22.5 %collective-permute-start.2 = (f32[4,24,32]{2,1,0:T(8,128)S(1)}, f32[4,24,32]{2,1,0:T(8,128)S(1)}, u32[]{:S(2)}, u32[]{:S(2)}) collective-permute-start(f32[4,24,32]{2,1,0:T(8,128)S(1)} %bitcast.311), channel_id=1, source_target_pairs={{0,4},{4,8},{8,12},{12,16},{16,20},{20,24},{24,28},{28,0},{1,5},{5... | collective-permute-start | bytes 36872 | tf_op jit(solution)/shard_map/ppermute | solution.py:402
  16.1 18.7 %collective-permute-start.3 = (f32[4,24,32]{2,1,0:T(8,128)S(1)}, f32[4,24,32]{2,1,0:T(8,128)S(1)}, u32[]{:S(2)}, u32[]{:S(2)}) collective-permute-start(f32[4,24,32]{2,1,0:T(8,128)S(1)} %bitcast.310), channel_id=1, source_target_pairs={{4,0},{8,4},{12,8},{16,12},{20,16},{24,20},{28,24},{0,28},{5,1},{9... | collective-permute-start | bytes 36872 | tf_op jit(solution)/shard_map/ppermute | solution.py:403
  20.2 19.8 %collective-permute-start = (f32[4,24,256]{2,1,0:T(8,128)S(1)}, f32[4,24,256]{2,1,0:T(8,128)S(1)}, u32[]{:S(2)}, u32[]{:S(2)}) collective-permute-start(f32[4,24,256]{2,1,0:T(8,128)S(1)} %bitcast.308), channel_id=1, source_target_pairs={{0,32},{32,64},{64,96},{96,0},{1,33},{33,65},{65,97},{97,1},{2,34}... | collective-permute-start | bytes 294920 | tf_op jit(solution)/shard_map/ppermute | solution.py:400
  20.3 19.7 %collective-permute-start.1 = (f32[4,24,256]{2,1,0:T(8,128)S(1)}, f32[4,24,256]{2,1,0:T(8,128)S(1)}, u32[]{:S(2)}, u32[]{:S(2)}) collective-permute-start(f32[4,24,256]{2,1,0:T(8,128)S(1)} %bitcast.309), channel_id=1, source_target_pairs={{32,0},{64,32},{96,64},{0,96},{33,1},{65,33},{97,65},{1,97},{34,2}... | collective-permute-start | bytes 294920 | tf_op jit(solution)/shard_map/ppermute | solution.py:401
  22.9 12.1 %collective-permute-start.7 = (f32[2,32,256]{2,1,0:T(8,128)S(1)}, f32[2,32,256]{2,1,0:T(8,128)S(1)}, u32[]{:S(2)}, u32[]{:S(2)}) collective-permute-start(f32[2,32,256]{2,1,0:T(8,128)S(1)} %slice_bitcast_fusion.17), channel_id=1, source_target_pairs={{0,1},{1,2},{2,3},{4,5},{5,6},{6,7},{8,9},{9,10},{10,11},{12,13},{... | collective-permute-start | bytes 196616 | tf_op jit(solution)/shard_map/ppermute | solution.py:395
  29.2 3.6 %copy-start.2 = (f32[2,24,32,256]{3,2,1,0:T(8,128)S(1)}, f32[2,24,32,256]{3,2,1,0:T(8,128)}, u32[]{:S(2)}) copy-start(f32[2,24,32,256]{3,2,1,0:T(8,128)} %param.9) | copy-start | bytes 4718596
  30.8 3.3 %copy-start.5 = (s32[32,256]{1,0:T(8,128)}, s32[32,256]{1,0:T(8,128)S(1)}, u32[]{:S(2)}) copy-start(s32[32,256]{1,0:T(8,128)S(1)} %get-tuple-element.61.dc_ref) | copy-start | bytes 98308
  30.9 9.1 %copy-start.10 = (s32[1,256]{1,0:T(1,128)}, s32[1,256]{1,0:T(1,128)S(1)}, u32[]{:S(2)}) copy-start(s32[1,256]{1,0:T(1,128)S(1)} %get-tuple-element.56.dxw_ref) | copy-start | bytes 3076
  30.9 9.1 %copy-start.9 = (s32[1,256]{1,0:T(1,128)}, s32[1,256]{1,0:T(1,128)S(1)}, u32[]{:S(2)}) copy-start(s32[1,256]{1,0:T(1,128)S(1)} %get-tuple-element.55.dxe_ref) | copy-start | bytes 3076
  32.7 1.4 %copy-start.8 = (f32[2,32,256]{2,1,0:T(8,128)S(1)}, f32[2,32,256]{2,1,0:T(8,128)}, u32[]{:S(2)}) copy-start(f32[2,32,256]{2,1,0:T(8,128)} %param.11) | copy-start | bytes 196612
  40.0 15.8 %copy-start.6 = (f32[4,24,256]{2,1,0:T(8,128)}, f32[4,24,256]{2,1,0:T(8,128)S(1)}, u32[]{:S(2)}) copy-start(f32[4,24,256]{2,1,0:T(8,128)S(1)} %collective-permute-done.xw_ref) | copy-start | bytes 294916
  40.0 15.7 %copy-start.7 = (f32[4,24,256]{2,1,0:T(8,128)}, f32[4,24,256]{2,1,0:T(8,128)S(1)}, u32[]{:S(2)}) copy-start(f32[4,24,256]{2,1,0:T(8,128)S(1)} %collective-permute-done.1.xe_ref) | copy-start | bytes 294916
  40.1 13.1 %collective-permute-start.4 = (f32[36,256]{1,0:T(8,128)S(1)}, f32[36,256]{1,0:T(8,128)S(1)}, u32[]{:S(2)}, u32[]{:S(2)}) collective-permute-start(f32[36,256]{1,0:T(8,128)S(1)} %pad_maximum_fusion), channel_id=1, source_target_pairs={{0,1},{1,2},{2,3},{4,5},{5,6},{6,7},{8,9},{9,10},{10,11},{12,13},{... | collective-permute-start | bytes 110600 | tf_op jit(solution)/shard_map/ppermute | solution.py:439
  43.9 9.2 %collective-permute-start.5 = (f32[36,256]{1,0:T(8,128)S(1)}, f32[36,256]{1,0:T(8,128)S(1)}, u32[]{:S(2)}, u32[]{:S(2)}) collective-permute-start(f32[36,256]{1,0:T(8,128)S(1)} %pad_maximum_fusion), channel_id=1, source_target_pairs={{0,2},{1,3},{4,6},{5,7},{8,10},{9,11},{12,14},{13,15},{16,18},{17,... | collective-permute-start | bytes 110600 | tf_op jit(solution)/shard_map/ppermute | solution.py:439
  47.5 5.6 %collective-permute-start.6 = (f32[36,256]{1,0:T(8,128)S(1)}, f32[36,256]{1,0:T(8,128)S(1)}, u32[]{:S(2)}, u32[]{:S(2)}) collective-permute-start(f32[36,256]{1,0:T(8,128)S(1)} %pad_maximum_fusion), channel_id=1, source_target_pairs={{0,3},{4,7},{8,11},{12,15},{16,19},{20,23},{24,27},{28,31},{32,35}... | collective-permute-start | bytes 110600 | tf_op jit(solution)/shard_map/ppermute | solution.py:439
  68.6 14.6 %collective-permute-start.10 = (f32[8,32,256]{2,1,0:T(8,128)}, f32[8,32,256]{2,1,0:T(8,128)S(1)}, u32[]{:S(2)}, u32[]{:S(2)}) collective-permute-start(f32[8,32,256]{2,1,0:T(8,128)} %get-tuple-element.39), channel_id=1, source_target_pairs={{0,1},{1,2},{2,3},{3,0},{4,5},{5,6},{6,7},{7,4},{8,9},{9,10},{10,1... | collective-permute-start | bytes 786440 | tf_op jit(solution)/shard_map/ppermute | solution.py:201
  68.7 14.6 %collective-permute-start.8 = (f32[8,32,256]{2,1,0:T(8,128)}, f32[8,32,256]{2,1,0:T(8,128)S(1)}, u32[]{:S(2)}, u32[]{:S(2)}) collective-permute-start(f32[8,32,256]{2,1,0:T(8,128)} %get-tuple-element.39), channel_id=1, source_target_pairs={{0,3},{1,0},{2,1},{3,2},{4,7},{5,4},{6,5},{7,6},{8,11},{9,8},{10,9... | collective-permute-start | bytes 786440 | tf_op jit(solution)/shard_map/ppermute | solution.py:201
  71.9 11.3 %collective-permute-start.9 = (f32[8,32,256]{2,1,0:T(8,128)}, f32[8,32,256]{2,1,0:T(8,128)S(1)}, u32[]{:S(2)}, u32[]{:S(2)}) collective-permute-start(f32[8,32,256]{2,1,0:T(8,128)} %get-tuple-element.39), channel_id=1, source_target_pairs={{0,2},{1,3},{2,0},{3,1},{4,6},{5,7},{6,4},{7,5},{8,10},{9,11},{10,... | collective-permute-start | bytes 786440 | tf_op jit(solution)/shard_map/ppermute | solution.py:201
  84.4 2.1 %copy-start.4 = (f32[2,24,32,256]{3,2,1,0:T(8,128)S(1)}, f32[2,24,32,256]{3,2,1,0:T(8,128)}, u32[]{:S(2)}) copy-start(f32[2,24,32,256]{3,2,1,0:T(8,128)} %get-tuple-element.42) | copy-start | bytes 4718596
  86.0 1.9 %copy-start.1 = (f32[4,24,32,256]{3,2,1,0:T(8,128)S(1)}, f32[4,24,32,256]{3,2,1,0:T(8,128)}, u32[]{:S(2)}) copy-start(f32[4,24,32,256]{3,2,1,0:T(8,128)} %get-tuple-element.38) | copy-start | bytes 9437188
  86.0 2.4 %copy-start.3 = (f32[2,24,32,256]{3,2,1,0:T(8,128)S(1)}, f32[2,24,32,256]{3,2,1,0:T(8,128)}, u32[]{:S(2)}) copy-start(f32[2,24,32,256]{3,2,1,0:T(8,128)} %get-tuple-element.41) | copy-start | bytes 4718596
Sparse Core Ops, SparseCore 0:
  40.1 24.1 all-gather.2

commit v16 on v15

--- a/solution.py
+++ b/solution.py
@@ -359,7 +359,7 @@
     st = operands[0]
     fields, levels, nx, ny = st.shape
     pairs = operands[21].shape[0]
-    chunk = 6 if levels % 6 == 0 else levels
+    chunk = 4 if levels % 4 == 0 else levels
     whole = [pl.BlockSpec(op.shape, (lambda i, n=op.ndim: (0,) * n)) for op in operands]
     by_level = lambda op: pl.BlockSpec((op.shape[0], chunk) + op.shape[2:], lambda i: (0, i, 0, 0))
     specs = list(whole)

time: 98.1 us -> 98.2 us (level)
  no operation moved by 1% of the time
where the time goes in v16:
time: 98.2 us; the launch traced here: 97.8 us
  starting transfers between devices  23.5 us (24%)
  local copies, waits for them, and re-layouts  23 us (23%)
  Pallas kernels  17.2 us (18%)
  between operations  13.8 us (14%)
  waiting for transfers between devices  11.4 us (12%)
  other arithmetic  8.86 us (9%)
    pallas_call x1, Pallas kernels, fused_solve(): pl.pallas_call(fused_kernel, grid=(levels // chunk,), in_specs=specs, out...  13 us
    ppermute x3, waiting for transfers between devices, gather_by_permutes(): received.append(lax.ppermute(part, axis, shift))  11.3 us
    ppermute x3, starting transfers between devices, per_device(): shallower = shallower + lax.ppermute(pack, 'gz', pairs_z)  8.7 us
    unnamed x26, local copies, waits for them, and re-layouts  4.58 us
    pallas_call x1, Pallas kernels, coupling_solve(): pl.pallas_call(coupling_kernel, grid=(cols_x // bx,), in_specs=[cspec, _p...  4.26 us
    ppermute x1, starting transfers between devices, per_device(): mix_above = lax.ppermute(mixing[:, lev_count - 1], 'gz', down_z)  3.93 us
    slice x1, local copies, waits for them, and re-layouts, per_device(): halo_yn = lax.ppermute(state[:, :, :, 0], 'gy', dn_y)  3.7 us
    ppermute x3, starting transfers between devices, gather_by_permutes(): received.append(lax.ppermute(part, axis, shift))  3.3 us
  transfers between devices with their start and end apart: 12, of which 1 were waited for; matrix products, arithmetic and copies ran while one was open for 20% of the time, Pallas kernels for 18%

profile of v16, /device:TPU:0, one launch (start us, length us, event | category | flops | bytes accessed | tf_op | source)
XLA Modules:
  0.0 97.8 jit_solution(16635034002041821562)
XLA Ops:
  6.5 3.7 %fusion.48 = (f32[4,24,32,1]{3,2,1,0:T(8,128)S(1)}, f32[4,24,32,1]{3,2,1,0:T(8,128)}) fusion(f32[4,24,32,256]{3,2,1,0:T(8,128)} %st_ref.1), kind=kLoop, calls=%fused_computation.140 | loop fusion | bytes 49152 | tf_op jit(solution)/shard_map/slice | solution.py:403
  10.2 2.0 %copy.49 = f32[4,24,32,1]{2,1,0,3:T(8,128)S(1)} copy(f32[4,24,32,1]{3,2,1,0:T(8,128)} %get-tuple-element.46) | data formatting | bytes 24576
  12.3 3.2 %collective-permute-start.2 = (f32[4,24,32]{2,1,0:T(8,128)S(1)}, f32[4,24,32]{2,1,0:T(8,128)S(1)}, u32[]{:S(2)}, u32[]{:S(2)}) collective-permute-start(f32[4,24,32]{2,1,0:T(8,128)S(1)} %bitcast.311), channel_id=1, source_target_pairs={{0,4},{4,8},{8,12},{12,16},{16,20},{20,24},{24,28},{28,0},{1,5},{5... | collective-permute-start | bytes 36872 | tf_op jit(solution)/shard_map/ppermute | solution.py:402
  15.5 0.6 copy.50
  16.1 2.6 %collective-permute-start.3 = (f32[4,24,32]{2,1,0:T(8,128)S(1)}, f32[4,24,32]{2,1,0:T(8,128)S(1)}, u32[]{:S(2)}, u32[]{:S(2)}) collective-permute-start(f32[4,24,32]{2,1,0:T(8,128)S(1)} %bitcast.310), channel_id=1, source_target_pairs={{4,0},{8,4},{12,8},{16,12},{20,16},{24,20},{28,24},{0,28},{5,1},{9... | collective-permute-start | bytes 36872 | tf_op jit(solution)/shard_map/ppermute | solution.py:403
  18.6 1.5 %fusion.49 = (f32[4,24,1,256]{3,2,1,0:T(1,128)S(1)}, f32[4,24,1,256]{3,2,1,0:T(1,128)S(1)}) fusion(f32[4,24,32,256]{3,2,1,0:T(8,128)} %st_ref.1), kind=kLoop, calls=%fused_computation.141 | loop fusion | bytes 393216 | tf_op jit(solution)/shard_map/slice | solution.py:401
  20.2 0.1 collective-permute-start
  20.3 1.8 %collective-permute-start.1 = (f32[4,24,256]{2,1,0:T(8,128)S(1)}, f32[4,24,256]{2,1,0:T(8,128)S(1)}, u32[]{:S(2)}, u32[]{:S(2)}) collective-permute-start(f32[4,24,256]{2,1,0:T(8,128)S(1)} %bitcast.309), channel_id=1, source_target_pairs={{32,0},{64,32},{96,64},{0,96},{33,1},{65,33},{97,65},{1,97},{34,2}... | collective-permute-start | bytes 294920 | tf_op jit(solution)/shard_map/ppermute | solution.py:401
  22.1 0.8 slice_bitcast_fusion.17
  22.9 3.9 %collective-permute-start.7 = (f32[2,32,256]{2,1,0:T(8,128)S(1)}, f32[2,32,256]{2,1,0:T(8,128)S(1)}, u32[]{:S(2)}, u32[]{:S(2)}) collective-permute-start(f32[2,32,256]{2,1,0:T(8,128)S(1)} %slice_bitcast_fusion.17), channel_id=1, source_target_pairs={{0,1},{1,2},{2,3},{4,5},{5,6},{6,7},{8,9},{9,10},{10,11},{12,13},{... | collective-permute-start | bytes 196616 | tf_op jit(solution)/shard_map/ppermute | solution.py:395
  27.0 0.7 gather_fusion
  27.6 0.1 broadcast_select_fusion
  27.7 0.4 copy.40
  28.1 1.0 %gather_fusion.1 = s32[258,34]{1,0:T(8,128)S(1)} fusion(s32[34,2048]{0,1:T(8,128)S(1)} %copy.40, s32[1024]{0:T(1024)S(1)} %pad_clamp_fusion), kind=kCustom, calls=%fused_computation.1 | custom fusion | bytes 71208 | tf_op jit(solution)/shard_map/jit(_take)/gather | solution.py:407
  29.2 0.1 copy.41
  29.3 0.8 slice_reduce_fusion
  30.1 0.7 fusion.51
  30.8 0.1 fusion.50
  30.9 0.1 fusion.5
  31.0 1.7 %compare_select_fusion = (f32[24,32,256]{2,1,0:T(8,128)S(1)}, f32[32,256]{1,0:T(8,128)S(1)}) fusion(s32[32,256]{1,0:T(8,128)S(1)} %get-tuple-element.61.dc_ref, s32[24]{0:T(128)S(1)} %iota_add_fusion.1, f32[4,24,32,256]{3,2,1,0:T(8,128)} %st_ref.1), kind=kLoop, calls=%fused_computation.15 | loop fusion | flops 2351104 | bytes 2424928 | tf_op jit(solution)/shard_map/mul | solution.py:420
  32.7 0.1 fusion.21
  32.8 1.3 %broadcast_multiply_fusion.c_ref = f32[2,24,32,256]{3,2,1,0:T(8,128)} fusion(f32[2,24,32,256]{3,2,1,0:T(8,128)S(1)} %copy-done.2, f32[24,32,256]{2,1,0:T(8,128)S(1)} %get-tuple-element.66), kind=kLoop, calls=%fused_computation.12 | loop fusion | flops 393216 | bytes 3932160 | tf_op jit(solution)/shard_map/mul | solution.py:420
  34.1 0.6 broadcast_select_fusion.1.wind_ref
  34.8 0.2 scatter.9
  35.0 0.6 multiply_select_fusion.ctop_ref
  35.7 4.3 %shard_map.46 = (f32[2,24,32,256]{3,2,1,0:T(8,128)}, f32[2,24,32,256]{3,2,1,0:T(8,128)}, f32[2,24,32,256]{3,2,1,0:T(8,128)}, f32[2,24,32,256]{3,2,1,0:T(8,128)}, f32[8,32,256]{2,1,0:T(8,128)}) custom-call(f32[2,24,32,256]{3,2,1,0:T(8,128)} %broadcast_multiply_fusion.c_ref, f32[2,32,256]{2,1,0:T(8,128)} %multiply_select_fusion.ctop_ref), custom_call_target="tpu_custom_call" | custom-call | tf_op jit(solution)/shard_map/pallas_call | solution.py:130
  40.1 3.8 %collective-permute-start.4 = (f32[36,256]{1,0:T(8,128)S(1)}, f32[36,256]{1,0:T(8,128)S(1)}, u32[]{:S(2)}, u32[]{:S(2)}) collective-permute-start(f32[36,256]{1,0:T(8,128)S(1)} %pad_maximum_fusion), channel_id=1, source_target_pairs={{0,1},{1,2},{2,3},{4,5},{5,6},{6,7},{8,9},{9,10},{10,11},{12,13},{... | collective-permute-start | bytes 110600 | tf_op jit(solution)/shard_map/ppermute | solution.py:439
  43.9 3.6 %collective-permute-start.5 = (f32[36,256]{1,0:T(8,128)S(1)}, f32[36,256]{1,0:T(8,128)S(1)}, u32[]{:S(2)}, u32[]{:S(2)}) collective-permute-start(f32[36,256]{1,0:T(8,128)S(1)} %pad_maximum_fusion), channel_id=1, source_target_pairs={{0,2},{1,3},{4,6},{5,7},{8,10},{9,11},{12,14},{13,15},{16,18},{17,... | collective-permute-start | bytes 110600 | tf_op jit(solution)/shard_map/ppermute | solution.py:439
  47.5 1.3 %collective-permute-start.6 = (f32[36,256]{1,0:T(8,128)S(1)}, f32[36,256]{1,0:T(8,128)S(1)}, u32[]{:S(2)}, u32[]{:S(2)}) collective-permute-start(f32[36,256]{1,0:T(8,128)S(1)} %pad_maximum_fusion), channel_id=1, source_target_pairs={{0,3},{4,7},{8,11},{12,15},{16,19},{20,23},{24,27},{28,31},{32,35}... | collective-permute-start | bytes 110600 | tf_op jit(solution)/shard_map/ppermute | solution.py:439
  48.8 0.6 stack.23.lane_ref
  49.5 1.9 %copy.43.ys_ref = f32[4,24,32,1]{3,2,1,0:T(8,128)} copy(f32[4,24,32,1]{2,1,0,3:T(8,128)S(1)} %bitcast.306) | data formatting | bytes 24576 | tf_op jit(solution)/shard_map/broadcast_in_dim | solution.py:451
  51.3 1.8 %copy.44.yn_ref = f32[4,24,32,1]{3,2,1,0:T(8,128)} copy(f32[4,24,32,1]{2,1,0,3:T(8,128)S(1)} %bitcast.307) | data formatting | bytes 24576 | tf_op jit(solution)/shard_map/broadcast_in_dim | solution.py:451
  53.2 0.6 slice.288.sc_ref
  53.8 0.7 copy.45.sys_ref
  54.5 0.7 copy.46.syn_ref
  55.1 0.6 fusion.52
  55.7 13.0 %shard_map.47 = (f32[4,24,32,256]{3,2,1,0:T(8,128)}, f32[8,32,256]{2,1,0:T(8,128)}) custom-call(f32[4,24,32,256]{3,2,1,0:T(8,128)} %st_ref.1, f32[4,24,256]{2,1,0:T(8,128)} %copy-done.6, f32[4,24,256]{2,1,0:T(8,128)} %copy-done.7, f32[4,24,32,1]{3,2,1,0:T(8,128)} %copy.43.ys_ref, f32[4,24,32,1]{3,2,1,0:T(8,128)} %copy.44.yn_ref, s32[32,256]{1,0:T(8,128)} %copy-done.5, ...), custom_call_target="tpu_custom_call" | custom-call | tf_op jit(solution)/shard_map/pallas_call | solution.py:368
  68.7 0.1 collective-permute-start.10
  68.8 3.2 %collective-permute-start.8 = (f32[8,32,256]{2,1,0:T(8,128)}, f32[8,32,256]{2,1,0:T(8,128)S(1)}, u32[]{:S(2)}, u32[]{:S(2)}) collective-permute-start(f32[8,32,256]{2,1,0:T(8,128)} %get-tuple-element.39), channel_id=1, source_target_pairs={{0,3},{1,0},{2,1},{3,2},{4,7},{5,4},{6,5},{7,6},{8,11},{9,8},{10,9... | collective-permute-start | bytes 786440 | tf_op jit(solution)/shard_map/ppermute | solution.py:201
  72.0 11.3 %collective-permute-done.10 = f32[8,32,256]{2,1,0:T(8,128)S(1)} collective-permute-done((f32[8,32,256]{2,1,0:T(8,128)}, f32[8,32,256]{2,1,0:T(8,128)S(1)}, u32[]{:S(2)}, u32[]{:S(2)}) %collective-permute-start.10) | collective-permute-done | bytes 262176 | tf_op jit(solution)/shard_map/ppermute | solution.py:201
  83.3 1.1 %select_bitcast_fusion.2 = (f32[1,8,32,256]{3,2,1,0:T(8,128)S(1)}, f32[1,8,32,256]{3,2,1,0:T(8,128)S(1)}, f32[1,8,32,256]{3,2,1,0:T(8,128)S(1)}, f32[1,8,32,256]{3,2,1,0:T(8,128)S(1)}) fusion(f32[8,32,256]{2,1,0:T(8,128)S(1)} %collective-permute-done.8, f32[8,32,256]{2,1,0:T(8,128)S(1)} %collective-permute-done.9, ...), kind=kLoop, calls=%fused_computation.18 | loop fusion | flops 786432 | bytes 2097164 | tf_op jit(solution)/shard_map/stack | solution.py:208
  84.5 0.0 all-gather.3.cloned.1.call-done
  84.5 1.6 %broadcast_in_dim.61 = f32[4,8,2,32,256]{4,3,2,1,0:T(8,128)S(1)} broadcast(f32[4,8,32,256]{3,2,1,0:T(8,128)} %bitcast.305), dimensions={0,1,3,4} | broadcast | bytes 3145728 | tf_op jit(solution)/shard_map/broadcast_in_dim | solution.py:160
  86.1 0.2 select_select_fusion
  86.3 0.3 select_select_fusion.1
  86.6 1.4 %copy-done.1 = f32[4,24,32,256]{3,2,1,0:T(8,128)S(1)} copy-done((f32[4,24,32,256]{3,2,1,0:T(8,128)S(1)}, f32[4,24,32,256]{3,2,1,0:T(8,128)}, u32[]{:S(2)}) %copy-start.1) | copy-done | bytes 3145752
  88.0 0.5 copy-done.3
  88.5 2.5 %fusion = f32[4,24,32,256]{3,2,1,0:T(8,128)} fusion(f32[4,24,32,256]{3,2,1,0:T(8,128)S(1)} %copy-done.1, f32[2,24,32,256]{3,2,1,0:T(8,128)S(1)} %copy-done.4, f32[4,32,256]{2,1,0:T(8,128)S(1)} %select_select_fusion, f32[2,24,32,256]{3,2,1,0:T(8,128)S(1)} %copy-done.3, f32[4,32,256]{2,1,0:T(8,128)S(1)} %select_select_fusion.1), kind=kLoop, calls=%fused_computation.3 | loop fusion | flops 3145728 | bytes 9699328 | tf_op jit(solution)/shard_map/add | solution.py:460
  (55 shorter events, 0.4 us)
Async XLA Ops:
  6.5 20.4 %copy-start = (s32[128,2048]{1,0:T(8,128)S(1)}, s32[128,2048]{1,0:T(8,128)}, u32[]{:S(2)}) copy-start(s32[128,2048]{1,0:T(8,128)} %param.10) | copy-start | bytes 3145732
  6.5 77.9 %all-gather.3.cloned.1.call-start = ((), (), s32[]{:S(2)}) async-start(), calls=%async_computation | async-start | bytes 1310720 | tf_op jit(solution)/shard_map/all_gather | solution.py:425
  12.3 22.5 %collective-permute-start.2 = (f32[4,24,32]{2,1,0:T(8,128)S(1)}, f32[4,24,32]{2,1,0:T(8,128)S(1)}, u32[]{:S(2)}, u32[]{:S(2)}) collective-permute-start(f32[4,24,32]{2,1,0:T(8,128)S(1)} %bitcast.311), channel_id=1, source_target_pairs={{0,4},{4,8},{8,12},{12,16},{16,20},{20,24},{24,28},{28,0},{1,5},{5... | collective-permute-start | bytes 36872 | tf_op jit(solution)/shard_map/ppermute | solution.py:402
  16.1 18.7 %collective-permute-start.3 = (f32[4,24,32]{2,1,0:T(8,128)S(1)}, f32[4,24,32]{2,1,0:T(8,128)S(1)}, u32[]{:S(2)}, u32[]{:S(2)}) collective-permute-start(f32[4,24,32]{2,1,0:T(8,128)S(1)} %bitcast.310), channel_id=1, source_target_pairs={{4,0},{8,4},{12,8},{16,12},{20,16},{24,20},{28,24},{0,28},{5,1},{9... | collective-permute-start | bytes 36872 | tf_op jit(solution)/shard_map/ppermute | solution.py:403
  20.2 19.8 %collective-permute-start = (f32[4,24,256]{2,1,0:T(8,128)S(1)}, f32[4,24,256]{2,1,0:T(8,128)S(1)}, u32[]{:S(2)}, u32[]{:S(2)}) collective-permute-start(f32[4,24,256]{2,1,0:T(8,128)S(1)} %bitcast.308), channel_id=1, source_target_pairs={{0,32},{32,64},{64,96},{96,0},{1,33},{33,65},{65,97},{97,1},{2,34}... | collective-permute-start | bytes 294920 | tf_op jit(solution)/shard_map/ppermute | solution.py:400
  20.3 19.7 %collective-permute-start.1 = (f32[4,24,256]{2,1,0:T(8,128)S(1)}, f32[4,24,256]{2,1,0:T(8,128)S(1)}, u32[]{:S(2)}, u32[]{:S(2)}) collective-permute-start(f32[4,24,256]{2,1,0:T(8,128)S(1)} %bitcast.309), channel_id=1, source_target_pairs={{32,0},{64,32},{96,64},{0,96},{33,1},{65,33},{97,65},{1,97},{34,2}... | collective-permute-start | bytes 294920 | tf_op jit(solution)/shard_map/ppermute | solution.py:401
  22.9 12.1 %collective-permute-start.7 = (f32[2,32,256]{2,1,0:T(8,128)S(1)}, f32[2,32,256]{2,1,0:T(8,128)S(1)}, u32[]{:S(2)}, u32[]{:S(2)}) collective-permute-start(f32[2,32,256]{2,1,0:T(8,128)S(1)} %slice_bitcast_fusion.17), channel_id=1, source_target_pairs={{0,1},{1,2},{2,3},{4,5},{5,6},{6,7},{8,9},{9,10},{10,11},{12,13},{... | collective-permute-start | bytes 196616 | tf_op jit(solution)/shard_map/ppermute | solution.py:395
  29.2 3.6 %copy-start.2 = (f32[2,24,32,256]{3,2,1,0:T(8,128)S(1)}, f32[2,24,32,256]{3,2,1,0:T(8,128)}, u32[]{:S(2)}) copy-start(f32[2,24,32,256]{3,2,1,0:T(8,128)} %param.9) | copy-start | bytes 4718596
  30.8 3.3 %copy-start.5 = (s32[32,256]{1,0:T(8,128)}, s32[32,256]{1,0:T(8,128)S(1)}, u32[]{:S(2)}) copy-start(s32[32,256]{1,0:T(8,128)S(1)} %get-tuple-element.61.dc_ref) | copy-start | bytes 98308
  30.9 9.1 %copy-start.10 = (s32[1,256]{1,0:T(1,128)}, s32[1,256]{1,0:T(1,128)S(1)}, u32[]{:S(2)}) copy-start(s32[1,256]{1,0:T(1,128)S(1)} %get-tuple-element.56.dxw_ref) | copy-start | bytes 3076
  30.9 9.1 %copy-start.9 = (s32[1,256]{1,0:T(1,128)}, s32[1,256]{1,0:T(1,128)S(1)}, u32[]{:S(2)}) copy-start(s32[1,256]{1,0:T(1,128)S(1)} %get-tuple-element.55.dxe_ref) | copy-start | bytes 3076
  32.7 1.4 %copy-start.8 = (f32[2,32,256]{2,1,0:T(8,128)S(1)}, f32[2,32,256]{2,1,0:T(8,128)}, u32[]{:S(2)}) copy-start(f32[2,32,256]{2,1,0:T(8,128)} %param.11) | copy-start | bytes 196612
  40.0 15.8 %copy-start.6 = (f32[4,24,256]{2,1,0:T(8,128)}, f32[4,24,256]{2,1,0:T(8,128)S(1)}, u32[]{:S(2)}) copy-start(f32[4,24,256]{2,1,0:T(8,128)S(1)} %collective-permute-done.xw_ref) | copy-start | bytes 294916
  40.0 15.7 %copy-start.7 = (f32[4,24,256]{2,1,0:T(8,128)}, f32[4,24,256]{2,1,0:T(8,128)S(1)}, u32[]{:S(2)}) copy-start(f32[4,24,256]{2,1,0:T(8,128)S(1)} %collective-permute-done.1.xe_ref) | copy-start | bytes 294916
  40.1 13.1 %collective-permute-start.4 = (f32[36,256]{1,0:T(8,128)S(1)}, f32[36,256]{1,0:T(8,128)S(1)}, u32[]{:S(2)}, u32[]{:S(2)}) collective-permute-start(f32[36,256]{1,0:T(8,128)S(1)} %pad_maximum_fusion), channel_id=1, source_target_pairs={{0,1},{1,2},{2,3},{4,5},{5,6},{6,7},{8,9},{9,10},{10,11},{12,13},{... | collective-permute-start | bytes 110600 | tf_op jit(solution)/shard_map/ppermute | solution.py:439
  43.9 9.2 %collective-permute-start.5 = (f32[36,256]{1,0:T(8,128)S(1)}, f32[36,256]{1,0:T(8,128)S(1)}, u32[]{:S(2)}, u32[]{:S(2)}) collective-permute-start(f32[36,256]{1,0:T(8,128)S(1)} %pad_maximum_fusion), channel_id=1, source_target_pairs={{0,2},{1,3},{4,6},{5,7},{8,10},{9,11},{12,14},{13,15},{16,18},{17,... | collective-permute-start | bytes 110600 | tf_op jit(solution)/shard_map/ppermute | solution.py:439
  47.5 5.6 %collective-permute-start.6 = (f32[36,256]{1,0:T(8,128)S(1)}, f32[36,256]{1,0:T(8,128)S(1)}, u32[]{:S(2)}, u32[]{:S(2)}) collective-permute-start(f32[36,256]{1,0:T(8,128)S(1)} %pad_maximum_fusion), channel_id=1, source_target_pairs={{0,3},{4,7},{8,11},{12,15},{16,19},{20,23},{24,27},{28,31},{32,35}... | collective-permute-start | bytes 110600 | tf_op jit(solution)/shard_map/ppermute | solution.py:439
  68.7 14.6 %collective-permute-start.10 = (f32[8,32,256]{2,1,0:T(8,128)}, f32[8,32,256]{2,1,0:T(8,128)S(1)}, u32[]{:S(2)}, u32[]{:S(2)}) collective-permute-start(f32[8,32,256]{2,1,0:T(8,128)} %get-tuple-element.39), channel_id=1, source_target_pairs={{0,1},{1,2},{2,3},{3,0},{4,5},{5,6},{6,7},{7,4},{8,9},{9,10},{10,1... | collective-permute-start | bytes 786440 | tf_op jit(solution)/shard_map/ppermute | solution.py:201
  68.8 14.6 %collective-permute-start.8 = (f32[8,32,256]{2,1,0:T(8,128)}, f32[8,32,256]{2,1,0:T(8,128)S(1)}, u32[]{:S(2)}, u32[]{:S(2)}) collective-permute-start(f32[8,32,256]{2,1,0:T(8,128)} %get-tuple-element.39), channel_id=1, source_target_pairs={{0,3},{1,0},{2,1},{3,2},{4,7},{5,4},{6,5},{7,6},{8,11},{9,8},{10,9... | collective-permute-start | bytes 786440 | tf_op jit(solution)/shard_map/ppermute | solution.py:201
  72.0 11.3 %collective-permute-start.9 = (f32[8,32,256]{2,1,0:T(8,128)}, f32[8,32,256]{2,1,0:T(8,128)S(1)}, u32[]{:S(2)}, u32[]{:S(2)}) collective-permute-start(f32[8,32,256]{2,1,0:T(8,128)} %get-tuple-element.39), channel_id=1, source_target_pairs={{0,2},{1,3},{2,0},{3,1},{4,6},{5,7},{6,4},{7,5},{8,10},{9,11},{10,... | collective-permute-start | bytes 786440 | tf_op jit(solution)/shard_map/ppermute | solution.py:201
  84.5 2.1 %copy-start.4 = (f32[2,24,32,256]{3,2,1,0:T(8,128)S(1)}, f32[2,24,32,256]{3,2,1,0:T(8,128)}, u32[]{:S(2)}) copy-start(f32[2,24,32,256]{3,2,1,0:T(8,128)} %get-tuple-element.42) | copy-start | bytes 4718596
  86.1 1.9 %copy-start.1 = (f32[4,24,32,256]{3,2,1,0:T(8,128)S(1)}, f32[4,24,32,256]{3,2,1,0:T(8,128)}, u32[]{:S(2)}) copy-start(f32[4,24,32,256]{3,2,1,0:T(8,128)} %get-tuple-element.38) | copy-start | bytes 9437188
  86.1 2.4 %copy-start.3 = (f32[2,24,32,256]{3,2,1,0:T(8,128)S(1)}, f32[2,24,32,256]{3,2,1,0:T(8,128)}, u32[]{:S(2)}) copy-start(f32[2,24,32,256]{3,2,1,0:T(8,128)} %get-tuple-element.41) | copy-start | bytes 4718596
Sparse Core Ops, SparseCore 0:
  40.1 24.1 all-gather.2
